TPU v7x, 256 devices: a whole 4x4x8 slice. The times are simulated.
256 devices in a mesh: node: 8 (over y, core), rows: 32 (over z, x).
Axes of the slice: x: 4, y: 4, z: 8, core: 2. Of those that a mesh axis runs over, the one named last changes fastest.
Arguments:
- columns: bfloat16 [32, 768, 128], P(None, 'rows'), may hold values from -6 to 6
- pencil_e: bfloat16 [768, 5, 128, 128], P('rows'), may hold values from -2 to 3, as said below
- pencil_a: bfloat16 [768, 5, 128, 128], P('rows'), may hold values from -5 to 2, as said below
- precond: bfloat16 [8, 2, 768, 128, 128], P('node', None, 'rows'), may hold values from -30 to 30, as said below
- neighbours: int32 [768, 5], P('rows'), may hold values from 0 to 767, as said below
Outputs:
- projected: float32 [2, 32, 768, 128], P(None, 'node', 'rows')
Inputs may be any that keep to these rules, and one draw needn't show every extreme that they name: neighbours[i, 0] = i. Every entry lies in the block rows of a device whose index along rows is at most 2 away, or exactly half of the 32 devices away, counted around the cycle. For each device and each other device, at most 6 entries of the first one's block rows lie in the second one's block rows; every device has exactly 6 entries in the block rows of the device half the cycle away. `pencil_e`: slot 0 holds the diagonal block. `pencil_a`: slot 0 holds the diagonal block. precond[k, 0, i] + i precond[k, 1, i] is the inverse of z_k E_i - A_i, where E_i and A_i are the float32 diagonal blocks before they were rounded to give pencil_e[i, 0] and pencil_a[i, 0]; the inverse is then rounded to bfloat16.
All inputs are finite; a program needn't handle non-finite values.
Results may differ from a plain program's by a relative error of at most 0.0017.
Values may be sent and summed in bfloat16 or wider, within the bound.
No kernel may reach another device: no remote copies, remote signals or barrier semaphores. Data moves between devices by JAX's collectives and lax.ppermute only.
A program may use at most 64 MiB of HBM per device.

v0:
```python
import math

import jax
import jax.numpy as jnp
from jax import lax
from jax.sharding import PartitionSpec as P

SLOTS = 5
HMAX = 6
SWEEPS = 2


def apply_blocks(extended, matrices, slot_index, dev_rows):
    summed = jnp.zeros((extended.shape[0], dev_rows, extended.shape[2]), jnp.float32)
    for slot in range(SLOTS):
        picked = extended[:, slot_index[:, slot], :]
        summed = summed + jnp.einsum(
            "cnb,nbd->cnd", picked, matrices[:, slot], preferred_element_type=jnp.float32
        )
    return summed


def precondition(residual, inverse):
    products = jnp.einsum("pcnb,mnbd->pmcnd", residual, inverse, preferred_element_type=jnp.float32)
    return jnp.stack([products[0, 0] - products[1, 1], products[0, 1] + products[1, 0]])


def per_device(columns, pencil_e, pencil_a, precond, neighbours):
    dev_rows = pencil_e.shape[0]
    block_size = pencil_e.shape[2]
    col_count = columns.shape[0]
    peer_count = lax.axis_size("rows")
    my_index = lax.axis_index("rows")
    owners = neighbours // dev_rows
    local_ids = neighbours - owners * dev_rows
    entries = dev_rows * SLOTS
    flat_owner = owners.reshape(-1)
    flat_local = local_ids.reshape(-1)
    flat_remote = flat_owner != my_index
    position = jnp.arange(entries)
    earlier = (
        (flat_owner[None, :] == flat_owner[:, None])
        & flat_remote[None, :]
        & (position[None, :] < position[:, None])
    )
    slot_rank = jnp.sum(earlier, axis=1)
    rank_range = jnp.arange(HMAX)
    slot_flat = jnp.where(flat_remote, dev_rows + flat_owner * HMAX + slot_rank, flat_local)
    matched = (
        (flat_owner[None, None, :] == jnp.arange(peer_count)[:, None, None])
        & (slot_rank[None, None, :] == rank_range[None, :, None])
        & flat_remote[None, None, :]
    )
    wanted = jnp.sum(jnp.where(matched, flat_local[None, None, :], 0), axis=2)
    asked_for = lax.all_to_all(wanted, "rows", split_axis=0, concat_axis=0, tiled=True)

    def fetch_halo(vector):
        outgoing = vector[:, asked_for.reshape(-1), :].reshape(
            vector.shape[0], peer_count, HMAX, block_size
        )
        incoming = lax.all_to_all(outgoing, "rows", split_axis=1, concat_axis=1, tiled=True)
        return jnp.concatenate(
            [vector, incoming.reshape(vector.shape[0], peer_count * HMAX, block_size)], axis=1
        )

    slot_index = slot_flat.reshape(dev_rows, SLOTS)
    rhs_full = apply_blocks(fetch_halo(columns), pencil_e, slot_index, dev_rows)
    node_count = lax.axis_size("node")
    angle_node = 2.0 * math.pi * (lax.axis_index("node").astype(jnp.float32) + 0.5) / node_count
    node_real = jnp.cos(angle_node)
    node_imag = jnp.sin(angle_node)
    inverse = precond[0]
    rhs_round = rhs_full.astype(jnp.bfloat16)
    iterate = jnp.einsum("cnb,mnbd->mcnd", rhs_round, inverse, preferred_element_type=jnp.float32)
    for sweep_step in range(SWEEPS):
        rounded = iterate.astype(jnp.bfloat16).reshape(2 * col_count, dev_rows, block_size)
        extended = fetch_halo(rounded)
        with_e = apply_blocks(extended, pencil_e, slot_index, dev_rows).reshape(
            2, col_count, dev_rows, block_size
        )
        with_a = apply_blocks(extended, pencil_a, slot_index, dev_rows).reshape(
            2, col_count, dev_rows, block_size
        )
        applied_real = node_real * with_e[0] - node_imag * with_e[1] - with_a[0]
        applied_imag = node_real * with_e[1] + node_imag * with_e[0] - with_a[1]
        residual = jnp.stack([rhs_full - applied_real, -applied_imag]).astype(jnp.bfloat16)
        iterate = iterate + precondition(residual, inverse)
    weighted = jnp.stack(
        [
            node_real * iterate[0] - node_imag * iterate[1],
            node_real * iterate[1] + node_imag * iterate[0],
        ]
    )
    weighted = weighted / node_count
    return lax.psum_scatter(weighted, "node", scatter_dimension=1, tiled=True)


def solution(mesh):
    placed = (
        P(None, "rows", None),
        P("rows", None, None, None),
        P("rows", None, None, None),
        P("node", None, "rows", None, None),
        P("rows", None),
    )
    return jax.shard_map(
        per_device,
        mesh=mesh,
        in_specs=placed,
        out_specs=P(None, "node", "rows", None),
        check_vma=False,
    )
```

profile of v0, /device:TPU:3, one launch (start us, length us, event | category | flops | bytes accessed | tf_op | source)
XLA Modules:
  0.0 356.5 jit_solution(1983969122975318889)
XLA Ops:
  8.3 18.5 %all_to_all.24 = s32[32,1,6]{2,1,0:T(1,128)S(1)} all-to-all(s32[32,1,6]{2,1,0:T(1,128)S(1)} %copy.87), channel_id=1, replica_groups=mesh['node'=8,'rows'=32] {'rows'}, dimensions={0} | all-to-all | bytes 1536 | tf_op jit(solution)/shard_map/all_to_all | solution.py:55
  28.1 8.6 %gather_fusion = bf16[192,32,128]{2,0,1:T(8,128)(2,1)S(1)} fusion(bf16[32,24,128]{2,1,0:T(8,128)(2,1)S(1)} %copy-done.1, s32[1024]{0:T(1024)S(1)} %pad_clamp_fusion.5), kind=kCustom, calls=%fused_computation | custom fusion | bytes 3146496 | tf_op jit(solution)/shard_map/gather | solution.py:58
  36.8 2.2 copy.88
  39.0 4.8 %all-to-all-start.1 = ((bf16[32,32,6,128]{3,0,2,1:T(8,128)(2,1)}), bf16[32,32,6,128]{3,0,2,1:T(8,128)(2,1)S(1)}, u32[]{:S(2)}, u32[]{:S(2)}) async-start(bf16[32,32,6,128]{3,0,2,1:T(8,128)(2,1)} %bitcast.236), calls=%async_computation.1 | async-start | bytes 3145728 | tf_op jit(solution)/shard_map/all_to_all | solution.py:61
  44.7 37.1 %all-to-all-done.1 = bf16[32,32,6,128]{3,0,2,1:T(8,128)(2,1)S(1)} async-done(((bf16[32,32,6,128]{3,0,2,1:T(8,128)(2,1)}), bf16[32,32,6,128]{3,0,2,1:T(8,128)(2,1)S(1)}, u32[]{:S(2)}, u32[]{:S(2)}) %all-to-all-start.1) | async-done | bytes 1572896 | tf_op jit(solution)/shard_map/all_to_all | solution.py:61
  83.2 2.1 gather_fusion.5
  85.3 2.1 gather_fusion.4
  87.3 2.2 gather_fusion.3
  89.5 2.2 gather_fusion.2
  91.7 2.1 gather_fusion.1
  101.4 2.7 gather_fusion.6
  104.1 5.2 %all-to-all-start.2 = ((bf16[64,32,6,128]{3,0,2,1:T(8,128)(2,1)}), bf16[64,32,6,128]{3,0,2,1:T(8,128)(2,1)}, u32[]{:S(2)}, u32[]{:S(2)}) async-start(bf16[64,32,6,128]{3,0,2,1:T(8,128)(2,1)} %bitcast.233), calls=%async_computation.2 | async-start | bytes 6291456 | tf_op jit(solution)/shard_map/all_to_all | solution.py:61
  109.6 70.9 %all-to-all-done.2 = bf16[64,32,6,128]{3,0,2,1:T(8,128)(2,1)} async-done(((bf16[64,32,6,128]{3,0,2,1:T(8,128)(2,1)}), bf16[64,32,6,128]{3,0,2,1:T(8,128)(2,1)}, u32[]{:S(2)}, u32[]{:S(2)}) %all-to-all-start.2) | async-done | bytes 3145760 | tf_op jit(solution)/shard_map/all_to_all | solution.py:61
  180.5 3.9 %pad_maximum_fusion = bf16[64,216,128]{2,0,1:T(8,128)(2,1)} fusion(bf16[64,192,128]{2,0,1:T(8,128)(2,1)} %bitcast.23, bf16[64,24,128]{2,0,1:T(8,128)(2,1)S(1)} %bitcast.229), kind=kLoop, calls=%fused_computation.18 | loop fusion | flops 1769472 | bytes 7077888 | tf_op jit(solution)/shard_map/concatenate | solution.py:62
  184.4 2.6 gather_fusion.11
  187.0 2.6 gather_fusion.10
  189.7 3.5 gather_fusion.9
  193.1 3.5 gather_fusion.8
  196.6 3.4 gather_fusion.7
  200.0 1.7 fusion.46
  201.8 1.7 fusion.30
  209.2 2.7 gather_fusion.12
  211.9 73.8 %all_to_all.25 = bf16[64,32,6,128]{3,0,2,1:T(8,128)(2,1)S(1)} all-to-all(bf16[64,32,6,128]{3,0,2,1:T(8,128)(2,1)} %bitcast.234), channel_id=1, replica_groups=mesh['node'=8,'rows'=32] {'rows'}, dimensions={1} | all-to-all | bytes 6291456 | tf_op jit(solution)/shard_map/all_to_all | solution.py:61
  285.7 2.1 pad_maximum_fusion.1
  287.8 2.6 gather_fusion.17
  290.4 3.4 gather_fusion.16
  293.8 3.5 gather_fusion.15
  297.3 3.5 gather_fusion.14
  300.8 3.4 gather_fusion.13
  304.1 1.7 fusion.44
  305.9 1.7 fusion.28
  314.8 33.3 %reduce-scatter.2.cloned.1.call-done = f32[2,4,24,128]{3,2,0,1:T(8,128)} async-done(((f32[2,32,24,128]{3,2,0,1:T(8,128)}), f32[2,4,24,128]{3,2,0,1:T(8,128)}) %reduce-scatter.2.cloned.1.call-update) | async-done | bytes 98320 | tf_op jit(solution)/shard_map/reduce_scatter | solution.py:95
  (85 shorter events, 27.1 us)
Async XLA Ops:
  6.5 94.5 %copy-start = (bf16[1,2,24,128,128]{4,3,2,1,0:T(8,128)(2,1)S(1)}, bf16[1,2,24,128,128]{4,3,2,1,0:T(8,128)(2,1)}, u32[]{:S(2)}) copy-start(bf16[1,2,24,128,128]{4,3,2,1,0:T(8,128)(2,1)} %param.8) | copy-start | bytes 4718596
  6.5 21.6 %copy-start.1 = (bf16[32,24,128]{2,1,0:T(8,128)(2,1)S(1)}, bf16[32,24,128]{2,1,0:T(8,128)(2,1)}, u32[]{:S(2)}) copy-start(bf16[32,24,128]{2,1,0:T(8,128)(2,1)} %param.5) | copy-start | bytes 589828
  39.0 42.8 %all-to-all-start.1 = ((bf16[32,32,6,128]{3,0,2,1:T(8,128)(2,1)}), bf16[32,32,6,128]{3,0,2,1:T(8,128)(2,1)S(1)}, u32[]{:S(2)}, u32[]{:S(2)}) async-start(bf16[32,32,6,128]{3,0,2,1:T(8,128)(2,1)} %bitcast.236), calls=%async_computation.1 | async-start | bytes 3145728 | tf_op jit(solution)/shard_map/all_to_all | solution.py:61
  104.1 76.3 %all-to-all-start.2 = ((bf16[64,32,6,128]{3,0,2,1:T(8,128)(2,1)}), bf16[64,32,6,128]{3,0,2,1:T(8,128)(2,1)}, u32[]{:S(2)}, u32[]{:S(2)}) async-start(bf16[64,32,6,128]{3,0,2,1:T(8,128)(2,1)} %bitcast.233), calls=%async_computation.2 | async-start | bytes 6291456 | tf_op jit(solution)/shard_map/all_to_all | solution.py:61
  109.4 238.7 %reduce-scatter.2.cloned.1.call-start = ((), (), s32[]{:S(2)}) async-start(), calls=%async_computation.5 | async-start | bytes 884736 | tf_op jit(solution)/shard_map/reduce_scatter | solution.py:95
  200.0 5.1 %copy-start.4 = (bf16[24,5,128,128]{3,2,1,0:T(8,128)(2,1)S(1)}, bf16[24,5,128,128]{3,2,1,0:T(8,128)(2,1)}, u32[]{:S(2)}) copy-start(bf16[24,5,128,128]{3,2,1,0:T(8,128)(2,1)} %param.7) | copy-start | bytes 11796484
  200.0 5.1 %copy-start.12 = (bf16[24,64,128]{2,1,0:T(8,128)(2,1)S(1)}, bf16[24,64,128]{2,1,0:T(8,128)(2,1)}, u32[]{:S(2)}) copy-start(bf16[24,64,128]{2,1,0:T(8,128)(2,1)} %gather_fusion.8) | copy-start | bytes 1179652
  201.7 3.7 %copy-start.2 = (bf16[24,5,128,128]{3,2,1,0:T(8,128)(2,1)S(1)}, bf16[24,5,128,128]{3,2,1,0:T(8,128)(2,1)}, u32[]{:S(2)}) copy-start(bf16[24,5,128,128]{3,2,1,0:T(8,128)(2,1)} %param.6) | copy-start | bytes 11796484
  201.7 3.7 %copy-start.10 = (bf16[24,64,128]{2,1,0:T(8,128)(2,1)S(1)}, bf16[24,64,128]{2,1,0:T(8,128)(2,1)}, u32[]{:S(2)}) copy-start(bf16[24,64,128]{2,1,0:T(8,128)(2,1)} %gather_fusion.9) | copy-start | bytes 1179652
  208.3 0.7 copy-start.6
  304.1 5.1 %copy-start.5 = (bf16[24,5,128,128]{3,2,1,0:T(8,128)(2,1)S(1)}, bf16[24,5,128,128]{3,2,1,0:T(8,128)(2,1)}, u32[]{:S(2)}) copy-start(bf16[24,5,128,128]{3,2,1,0:T(8,128)(2,1)} %param.7) | copy-start | bytes 11796484
  304.1 5.1 %copy-start.11 = (bf16[24,64,128]{2,1,0:T(8,128)(2,1)S(1)}, bf16[24,64,128]{2,1,0:T(8,128)(2,1)}, u32[]{:S(2)}) copy-start(bf16[24,64,128]{2,1,0:T(8,128)(2,1)} %gather_fusion.14) | copy-start | bytes 1179652
  305.9 3.7 %copy-start.3 = (bf16[24,5,128,128]{3,2,1,0:T(8,128)(2,1)S(1)}, bf16[24,5,128,128]{3,2,1,0:T(8,128)(2,1)}, u32[]{:S(2)}) copy-start(bf16[24,5,128,128]{3,2,1,0:T(8,128)(2,1)} %param.6) | copy-start | bytes 11796484
  305.9 3.7 %copy-start.9 = (bf16[24,64,128]{2,1,0:T(8,128)(2,1)S(1)}, bf16[24,64,128]{2,1,0:T(8,128)(2,1)}, u32[]{:S(2)}) copy-start(bf16[24,64,128]{2,1,0:T(8,128)(2,1)} %gather_fusion.15) | copy-start | bytes 1179652
  309.3 1.1 copy-start.8
  311.9 1.0 copy-start.7
Sparse Core Ops, SparseCore 0:
  314.9 33.1 reduce-scatter.1
where the time goes:
time: 360 us; the launch traced here: 356 us
  waiting for transfers between devices  141 us (39%)
  blocking collectives  92.4 us (26%)
  local copies, waits for them, and re-layouts  64.7 us (18%)
  matrix products  23.3 us (6%)
  between operations  14 us (4%)
  other arithmetic  10.7 us (3%)
  starting transfers between devices  10.1 us (3%)
    all_to_all x2, waiting for transfers between devices, fetch_halo(): lax.all_to_all(outgoing, 'rows', split_axis=1, concat_axis=1, tiled=True)  108 us
    all_to_all x1, blocking collectives, fetch_halo(): lax.all_to_all(outgoing, 'rows', split_axis=1, concat_axis=1, tiled=True)  73.8 us
    gather x15, local copies, waits for them, and re-layouts, apply_blocks(): picked = extended[:, slot_index[:, slot], :]  42.4 us
    reduce_scatter x1, waiting for transfers between devices, per_device(): return lax.psum_scatter(weighted, 'node', scatter_dimension=1, tiled=True)  33.3 us
    dot_general x25, matrix products, apply_blocks(): jnp.einsum('cnb,nbd->cnd', picked, matrices[:, slot], preferred_element_t...  22.2 us
    all_to_all x1, blocking collectives, per_device(): lax.all_to_all(wanted, 'rows', split_axis=0, concat_axis=0, tiled=True)  18.5 us
    gather x4, local copies, waits for them, and re-layouts, fetch_halo(): vector[:, asked_for.reshape(-1), :]  16.2 us
    all_to_all x2, starting transfers between devices, fetch_halo(): lax.all_to_all(outgoing, 'rows', split_axis=1, concat_axis=1, tiled=True)  10 us
  transfers between devices with their start and end apart: 3, of which 3 were waited for; matrix products, arithmetic and copies ran while one was open for 0% of the time, Pallas kernels for 0%

commit v1 on v0

v1 whole, which is shorter than its diff:
```python
import math

import jax
import jax.numpy as jnp
from jax import lax
from jax.sharding import PartitionSpec as P

SLOTS = 5
HMAX = 6
REACH = 2
SWEEPS = 2


def partner_offsets(peer_count):
    found = []
    for offset in list(range(1, REACH + 1)) + [peer_count // 2] + [-o for o in range(1, REACH + 1)]:
        offset = offset % peer_count
        if offset != 0 and offset not in found:
            found.append(offset)
    return found


def apply_pair(extended, slot_index, first, second):
    picked = extended[slot_index]
    with_first = jnp.einsum("nscb,nsbd->ncd", picked, first, preferred_element_type=jnp.float32)
    if second is None:
        return with_first, None
    with_second = jnp.einsum("nscb,nsbd->ncd", picked, second, preferred_element_type=jnp.float32)
    return with_first, with_second


def per_device(columns, pencil_e, pencil_a, precond, neighbours):
    dev_rows = pencil_e.shape[0]
    col_count = columns.shape[0]
    peer_count = lax.axis_size("rows")
    my_index = lax.axis_index("rows")
    offsets = partner_offsets(peer_count)
    owners = neighbours // dev_rows
    local_ids = neighbours - owners * dev_rows
    relative = (owners - my_index) % peer_count
    flat_rel = relative.reshape(-1)
    flat_local = local_ids.reshape(-1)
    slot_flat = flat_local
    wanted = []
    rank_range = jnp.arange(HMAX)
    for which, offset in enumerate(offsets):
        hit = flat_rel == offset
        rank = jnp.cumsum(hit.astype(jnp.int32)) - 1
        slot_flat = jnp.where(hit, dev_rows + which * HMAX + rank, slot_flat)
        matched = hit[None, :] & (rank[None, :] == rank_range[:, None])
        wanted.append(jnp.sum(jnp.where(matched, flat_local[None, :], 0), axis=1))
    slot_index = slot_flat.reshape(dev_rows, SLOTS)

    def to_partner(offset):
        return [(j, (j + offset) % peer_count) for j in range(peer_count)]

    def from_partner(offset):
        return [((j + offset) % peer_count, j) for j in range(peer_count)]

    asked_for = [
        lax.ppermute(wanted[which], "rows", to_partner(offset)) for which, offset in enumerate(offsets)
    ]

    def fetch_halo(vector):
        pieces = [vector]
        for which, offset in enumerate(offsets):
            pieces.append(lax.ppermute(vector[asked_for[which]], "rows", from_partner(offset)))
        return jnp.concatenate(pieces, axis=0)

    e_mats = pencil_e
    a_mats = pencil_a
    cols_major = jnp.transpose(columns, (1, 0, 2))
    rhs_full, _ = apply_pair(fetch_halo(cols_major), slot_index, e_mats, None)
    node_count = lax.axis_size("node")
    angle_node = 2.0 * math.pi * (lax.axis_index("node").astype(jnp.float32) + 0.5) / node_count
    node_real = jnp.cos(angle_node)
    node_imag = jnp.sin(angle_node)
    inverse = precond[0]
    rhs_round = rhs_full.astype(jnp.bfloat16)
    start = jnp.einsum("ncb,mnbd->nmcd", rhs_round, inverse, preferred_element_type=jnp.float32)
    iterate = start.reshape(dev_rows, 2 * col_count, -1)
    for sweep_step in range(SWEEPS):
        rounded = iterate.astype(jnp.bfloat16)
        with_e, with_a = apply_pair(fetch_halo(rounded), slot_index, e_mats, a_mats)
        e_real, e_imag = with_e[:, :col_count], with_e[:, col_count:]
        applied_real = node_real * e_real - node_imag * e_imag - with_a[:, :col_count]
        applied_imag = node_real * e_imag + node_imag * e_real - with_a[:, col_count:]
        residual = jnp.concatenate([rhs_full - applied_real, -applied_imag], axis=1).astype(jnp.bfloat16)
        products = jnp.einsum("ncb,mnbd->nmcd", residual, inverse, preferred_element_type=jnp.float32)
        products = products.reshape(dev_rows, 2, 2, col_count, -1)
        update_real = products[:, 0, 0] - products[:, 1, 1]
        update_imag = products[:, 1, 0] + products[:, 0, 1]
        iterate = iterate + jnp.concatenate([update_real, update_imag], axis=1)
    it_real, it_imag = iterate[:, :col_count], iterate[:, col_count:]
    weighted = jnp.stack(
        [
            node_real * it_real - node_imag * it_imag,
            node_real * it_imag + node_imag * it_real,
        ]
    )
    weighted = jnp.transpose(weighted / node_count, (0, 2, 1, 3))
    return lax.psum_scatter(weighted, "node", scatter_dimension=1, tiled=True)


def solution(mesh):
    placed = (
        P(None, "rows", None),
        P("rows", None, None, None),
        P("rows", None, None, None),
        P("node", None, "rows", None, None),
        P("rows", None),
    )
    return jax.shard_map(
        per_device,
        mesh=mesh,
        in_specs=placed,
        out_specs=P(None, "node", "rows", None),
        check_vma=False,
    )
```

time: 360 us -> 152 us (0.42)
  waiting for transfers between devices: 141 us -> 47.2 us
  blocking collectives: 92.4 us -> 0 us
  local copies, waits for them, and re-layouts: 64.7 us -> 29.9 us
  starting transfers between devices: 10.1 us -> 41.1 us
  matrix products: 23.3 us -> 12.3 us
  other arithmetic: 10.7 us -> 4.33 us
    all_to_all x2 -> x0, waiting for transfers between devices: 108 us -> none  [fetch_halo(): lax.all_to_all(outgoing, 'rows', split_axis=1, concat_axis=1, tiled=True)]
    all_to_all x2 -> x0, blocking collectives: 92.4 us -> none  [the longest x1 73.8 us: fetch_halo(): lax.all_to_all(outgoing, 'rows', split_axis=1, concat_axis=1, tiled=True)]
    gather x19 -> x18, local copies, waits for them, and re-layouts: 58.7 us -> 13.6 us  [the longest x15 8.7 us: fetch_halo(): vector[asked_for[which]]]
    ppermute x0 -> x20, starting transfers between devices: none -> 41.1 us  [the longest x15 29.1 us: fetch_halo(): lax.ppermute(vector[asked_for[which]], 'rows', from_partner(offset))]
    ppermute x0 -> x20, waiting for transfers between devices: none -> 11.1 us  [the longest x15 9.03 us: fetch_halo(): lax.ppermute(vector[asked_for[which]], 'rows', from_partner(offset))]
    dot_general x28 -> x8, matrix products: 23.3 us -> 12.3 us  [the longest x3 9.38 us: apply_pair(): jnp.einsum('nscb,nsbd->ncd', picked, first, preferred_element_type=jnp.fl...]
    all_to_all x2 -> x0, starting transfers between devices: 10 us -> none  [fetch_halo(): lax.all_to_all(outgoing, 'rows', split_axis=1, concat_axis=1, tiled=True)]
    unnamed x28 -> x47, local copies, waits for them, and re-layouts: 2.16 us -> 10.5 us
  transfers between devices with their start and end apart: 3 -> 21, of which waited for: 3 -> 6; matrix products, arithmetic and copies ran while one was open for 0% -> 9% of each run, Pallas kernels for 0% -> 0%
where the time goes in v1:
time: 152 us; the launch traced here: 149 us
  waiting for transfers between devices  47.2 us (31%)
  starting transfers between devices  41.1 us (27%)
  local copies, waits for them, and re-layouts  29.9 us (20%)
  between operations  14.1 us (9%)
  matrix products  12.3 us (8%)
  other arithmetic  4.33 us (3%)
    reduce_scatter x1, waiting for transfers between devices, per_device(): return lax.psum_scatter(weighted, 'node', scatter_dimension=1, tiled=True)  36.1 us
    ppermute x15, starting transfers between devices, fetch_halo(): lax.ppermute(vector[asked_for[which]], 'rows', from_partner(offset))  29.1 us
    ppermute x5, starting transfers between devices, per_device(): lax.ppermute(wanted[which], 'rows', to_partner(offset))  12.1 us
    unnamed x47, local copies, waits for them, and re-layouts  10.5 us
    dot_general x3, matrix products, apply_pair(): jnp.einsum('nscb,nsbd->ncd', picked, first, preferred_element_type=jnp.fl...  9.38 us
    ppermute x15, waiting for transfers between devices, fetch_halo(): lax.ppermute(vector[asked_for[which]], 'rows', from_partner(offset))  9.03 us
    gather x15, local copies, waits for them, and re-layouts, fetch_halo(): vector[asked_for[which]]  8.7 us
    gather x3, local copies, waits for them, and re-layouts, apply_pair(): picked = extended[slot_index]  4.94 us
  transfers between devices with their start and end apart: 21, of which 6 were waited for; matrix products, arithmetic and copies ran while one was open for 9% of the time, Pallas kernels for 0%

profile of v1, /device:TPU:3, one launch (start us, length us, event | category | flops | bytes accessed | tf_op | source)
XLA Modules:
  0.0 148.9 jit_solution(6974021041674477017)
XLA Ops:
  6.5 0.9 copy.66
  10.5 7.2 %collective-permute-start.8 = (s32[6]{0:T(128)S(1)}, s32[6]{0:T(128)S(1)}, u32[]{:S(2)}, u32[]{:S(2)}) collective-permute-start(s32[6]{0:T(128)S(1)} %get-tuple-element.15), channel_id=1, source_target_pairs={{0,30},{1,31},{2,0},{3,1},{4,2},{5,3},{6,4},{7,5},{8,6},{9,7},{10,... | collective-permute-start | bytes 80 | tf_op jit(solution)/shard_map/ppermute | solution.py:61
  17.7 2.7 %collective-permute-start.4 = (s32[6]{0:T(128)S(1)}, s32[6]{0:T(128)S(1)}, u32[]{:S(2)}, u32[]{:S(2)}) collective-permute-start(s32[6]{0:T(128)S(1)} %get-tuple-element.17), channel_id=1, source_target_pairs={{0,16},{1,17},{2,18},{3,19},{4,20},{5,21},{6,22},{7,23},{8,24},{9,... | collective-permute-start | bytes 80 | tf_op jit(solution)/shard_map/ppermute | solution.py:61
  20.7 1.9 %collective-permute-start = (s32[6]{0:T(128)S(1)}, s32[6]{0:T(128)S(1)}, u32[]{:S(2)}, u32[]{:S(2)}) collective-permute-start(s32[6]{0:T(128)S(1)} %get-tuple-element.19), channel_id=1, source_target_pairs={{0,1},{1,2},{2,3},{3,4},{4,5},{5,6},{6,7},{7,8},{8,9},{9,10},{10,1... | collective-permute-start | bytes 80 | tf_op jit(solution)/shard_map/ppermute | solution.py:61
  22.6 1.0 copy.113
  24.1 1.7 %collective-permute-done = s32[6]{0:T(128)S(1)} collective-permute-done((s32[6]{0:T(128)S(1)}, s32[6]{0:T(128)S(1)}, u32[]{:S(2)}, u32[]{:S(2)}) %collective-permute-start) | collective-permute-done | bytes 56 | tf_op jit(solution)/shard_map/ppermute | solution.py:61
  26.4 4.9 %collective-permute-start.1 = (bf16[6,32,128]{2,1,0:T(8,128)(2,1)S(1)}, bf16[6,32,128]{2,1,0:T(8,128)(2,1)S(1)}, u32[]{:S(2)}, u32[]{:S(2)}) collective-permute-start(bf16[6,32,128]{2,1,0:T(8,128)(2,1)S(1)} %gather_fusion), channel_id=1, source_target_pairs={{1,0},{2,1},{3,2},{4,3},{5,4},{6,5},{7,6},{8,7},{9,8},{10,9},{11,1... | collective-permute-start | bytes 147464 | tf_op jit(solution)/shard_map/ppermute | solution.py:67
  33.6 4.3 %collective-permute-start.5 = (bf16[6,32,128]{2,1,0:T(8,128)(2,1)S(1)}, bf16[6,32,128]{2,1,0:T(8,128)(2,1)S(1)}, u32[]{:S(2)}, u32[]{:S(2)}) collective-permute-start(bf16[6,32,128]{2,1,0:T(8,128)(2,1)S(1)} %gather_fusion.2), channel_id=1, source_target_pairs={{16,0},{17,1},{18,2},{19,3},{20,4},{21,5},{22,6},{23,7},{24,8},{25... | collective-permute-start | bytes 147464 | tf_op jit(solution)/shard_map/ppermute | solution.py:67
  37.9 1.4 collective-permute-start.7
  39.3 1.5 %collective-permute-start.9 = (bf16[6,32,128]{2,1,0:T(8,128)(2,1)S(1)}, bf16[6,32,128]{2,1,0:T(8,128)(2,1)S(1)}, u32[]{:S(2)}, u32[]{:S(2)}) collective-permute-start(bf16[6,32,128]{2,1,0:T(8,128)(2,1)S(1)} %gather_fusion.4), channel_id=1, source_target_pairs={{30,0},{31,1},{0,2},{1,3},{2,4},{3,5},{4,6},{5,7},{6,8},{7,9},{8,1... | collective-permute-start | bytes 147464 | tf_op jit(solution)/shard_map/ppermute | solution.py:67
  40.9 5.0 %collective-permute-done.9 = bf16[6,32,128]{2,1,0:T(8,128)(2,1)S(1)} collective-permute-done((bf16[6,32,128]{2,1,0:T(8,128)(2,1)S(1)}, bf16[6,32,128]{2,1,0:T(8,128)(2,1)S(1)}, u32[]{:S(2)}, u32[]{:S(2)}) %collective-permute-start.9) | collective-permute-done | bytes 49184 | tf_op jit(solution)/shard_map/ppermute | solution.py:67
  46.6 2.8 %convolution_bitcast_fusion.4 = f32[24,32,128]{2,1,0:T(8,128)S(1)} fusion(bf16[24,5,32,128]{3,2,1,0:T(8,128)(2,1)S(1)} %bitcast.133, bf16[24,5,128,128]{3,2,1,0:T(8,128)(2,1)} %param.6), kind=kOutput, calls=%fused_computation.22 | convolution fusion | flops 125829120 | bytes 5308416 | tf_op jit(solution)/shard_map/nscb,nsbd->ncd/dot_general | solution.py:25
  49.9 0.9 copy-done.3
  55.7 1.7 %collective-permute-start.12 = (bf16[6,64,128]{2,1,0:T(8,128)(2,1)S(1)}, bf16[6,64,128]{2,1,0:T(8,128)(2,1)S(1)}, u32[]{:S(2)}, u32[]{:S(2)}) collective-permute-start(bf16[6,64,128]{2,1,0:T(8,128)(2,1)S(1)} %gather_fusion.8), channel_id=1, source_target_pairs={{16,0},{17,1},{18,2},{19,3},{20,4},{21,5},{22,6},{23,7},{24,8},{25... | collective-permute-start | bytes 294920 | tf_op jit(solution)/shard_map/ppermute | solution.py:67
  57.4 2.1 %collective-permute-start.13 = (bf16[6,64,128]{2,1,0:T(8,128)(2,1)S(1)}, bf16[6,64,128]{2,1,0:T(8,128)(2,1)S(1)}, u32[]{:S(2)}, u32[]{:S(2)}) collective-permute-start(bf16[6,64,128]{2,1,0:T(8,128)(2,1)S(1)} %gather_fusion.9), channel_id=1, source_target_pairs={{31,0},{0,1},{1,2},{2,3},{3,4},{4,5},{5,6},{6,7},{7,8},{8,9},{9,10... | collective-permute-start | bytes 294920 | tf_op jit(solution)/shard_map/ppermute | solution.py:67
  59.4 3.2 %collective-permute-start.14 = (bf16[6,64,128]{2,1,0:T(8,128)(2,1)S(1)}, bf16[6,64,128]{2,1,0:T(8,128)(2,1)S(1)}, u32[]{:S(2)}, u32[]{:S(2)}) collective-permute-start(bf16[6,64,128]{2,1,0:T(8,128)(2,1)S(1)} %gather_fusion.10), channel_id=1, source_target_pairs={{30,0},{31,1},{0,2},{1,3},{2,4},{3,5},{4,6},{5,7},{6,8},{7,9},{8,1... | collective-permute-start | bytes 294920 | tf_op jit(solution)/shard_map/ppermute | solution.py:67
  65.2 2.5 %collective-permute-done.14 = bf16[6,64,128]{2,1,0:T(8,128)(2,1)S(1)} collective-permute-done((bf16[6,64,128]{2,1,0:T(8,128)(2,1)S(1)}, bf16[6,64,128]{2,1,0:T(8,128)(2,1)S(1)}, u32[]{:S(2)}, u32[]{:S(2)}) %collective-permute-start.14) | collective-permute-done | bytes 98336 | tf_op jit(solution)/shard_map/ppermute | solution.py:67
  68.4 2.1 %gather_fusion.11 = bf16[120,64,128]{2,1,0:T(8,128)(2,1)S(1)} fusion(bf16[54,64,128]{2,1,0:T(8,128)(2,1)} %constant_dynamic-update-slice_fusion.6, s32[1024]{0:T(1024)S(1)} %pad_clamp_fusion), kind=kCustom, calls=%fused_computation.11 | custom fusion | bytes 3932640 | tf_op jit(solution)/shard_map/gather | solution.py:24
  70.5 3.3 %convolution_bitcast_fusion.3 = f32[24,64,128]{2,1,0:T(8,128)S(1)} fusion(bf16[24,5,64,128]{3,2,1,0:T(8,128)(2,1)S(1)} %bitcast.129, bf16[24,5,128,128]{3,2,1,0:T(8,128)(2,1)} %param.6), kind=kOutput, calls=%fused_computation.21 | convolution fusion | flops 251658240 | bytes 6684672 | tf_op jit(solution)/shard_map/nscb,nsbd->ncd/dot_general | solution.py:25
  73.8 0.9 convolution_bitcast_fusion.2
  75.5 1.1 copy-done.4
  81.7 2.5 %collective-permute-start.17 = (bf16[6,64,128]{2,1,0:T(8,128)(2,1)S(1)}, bf16[6,64,128]{2,1,0:T(8,128)(2,1)S(1)}, u32[]{:S(2)}, u32[]{:S(2)}) collective-permute-start(bf16[6,64,128]{2,1,0:T(8,128)(2,1)S(1)} %gather_fusion.14), channel_id=1, source_target_pairs={{16,0},{17,1},{18,2},{19,3},{20,4},{21,5},{22,6},{23,7},{24,8},{25... | collective-permute-start | bytes 294920 | tf_op jit(solution)/shard_map/ppermute | solution.py:67
  84.2 2.1 %collective-permute-start.18 = (bf16[6,64,128]{2,1,0:T(8,128)(2,1)S(1)}, bf16[6,64,128]{2,1,0:T(8,128)(2,1)S(1)}, u32[]{:S(2)}, u32[]{:S(2)}) collective-permute-start(bf16[6,64,128]{2,1,0:T(8,128)(2,1)S(1)} %gather_fusion.15), channel_id=1, source_target_pairs={{31,0},{0,1},{1,2},{2,3},{3,4},{4,5},{5,6},{6,7},{7,8},{8,9},{9,10... | collective-permute-start | bytes 294920 | tf_op jit(solution)/shard_map/ppermute | solution.py:67
  86.2 3.4 %collective-permute-start.19 = (bf16[6,64,128]{2,1,0:T(8,128)(2,1)S(1)}, bf16[6,64,128]{2,1,0:T(8,128)(2,1)S(1)}, u32[]{:S(2)}, u32[]{:S(2)}) collective-permute-start(bf16[6,64,128]{2,1,0:T(8,128)(2,1)S(1)} %gather_fusion.16), channel_id=1, source_target_pairs={{30,0},{31,1},{0,2},{1,3},{2,4},{3,5},{4,6},{5,7},{6,8},{7,9},{8,1... | collective-permute-start | bytes 294920 | tf_op jit(solution)/shard_map/ppermute | solution.py:67
  92.2 1.5 %collective-permute-done.19 = bf16[6,64,128]{2,1,0:T(8,128)(2,1)S(1)} collective-permute-done((bf16[6,64,128]{2,1,0:T(8,128)(2,1)S(1)}, bf16[6,64,128]{2,1,0:T(8,128)(2,1)S(1)}, u32[]{:S(2)}, u32[]{:S(2)}) %collective-permute-start.19) | collective-permute-done | bytes 98336 | tf_op jit(solution)/shard_map/ppermute | solution.py:67
  94.4 2.1 %gather_fusion.17 = bf16[120,64,128]{2,1,0:T(8,128)(2,1)S(1)} fusion(bf16[54,64,128]{2,1,0:T(8,128)(2,1)} %constant_dynamic-update-slice_fusion.12, s32[1024]{0:T(1024)S(1)} %pad_clamp_fusion), kind=kCustom, calls=%fused_computation.17 | custom fusion | bytes 3932640 | tf_op jit(solution)/shard_map/gather | solution.py:24
  96.5 3.3 %convolution_bitcast_fusion.1 = f32[24,64,128]{2,1,0:T(8,128)S(1)} fusion(bf16[24,5,64,128]{3,2,1,0:T(8,128)(2,1)S(1)} %bitcast.127, bf16[24,5,128,128]{3,2,1,0:T(8,128)(2,1)} %param.6), kind=kOutput, calls=%fused_computation.19 | convolution fusion | flops 251658240 | bytes 6684672 | tf_op jit(solution)/shard_map/nscb,nsbd->ncd/dot_general | solution.py:25
  99.8 0.9 convolution_bitcast_fusion
  101.5 1.0 copy-done.5
  103.1 1.3 copy.86
  104.4 36.1 %reduce-scatter.2.cloned.1.call-done = f32[2,4,24,128]{3,2,0,1:T(8,128)} async-done(((f32[2,32,24,128]{3,2,0,1:T(8,128)}), f32[2,4,24,128]{3,2,0,1:T(8,128)}) %reduce-scatter.2.cloned.1.call-update) | async-done | bytes 98320 | tf_op jit(solution)/shard_map/reduce_scatter | solution.py:102
  140.5 1.5 %copy.87 = f32[2,4,24,128]{3,2,1,0:T(8,128)} copy(f32[2,4,24,128]{3,2,0,1:T(8,128)} %reduce-scatter.2.cloned.1.call-done) | data formatting | bytes 196608 | tf_op jit(solution)/shard_map/reduce_scatter | solution.py:102
  (138 shorter events, 26.2 us)
Async XLA Ops:
  6.5 43.0 %copy-start = (bf16[1,2,24,128,128]{4,3,2,1,0:T(8,128)(2,1)S(1)}, bf16[1,2,24,128,128]{4,3,2,1,0:T(8,128)(2,1)}, u32[]{:S(2)}) copy-start(bf16[1,2,24,128,128]{4,3,2,1,0:T(8,128)(2,1)} %param.8) | copy-start | bytes 4718596
  6.5 17.0 %copy-start.13 = (bf16[32,24,128]{2,1,0:T(8,128)(2,1)S(1)}, bf16[32,24,128]{2,1,0:T(8,128)(2,1)}, u32[]{:S(2)}) copy-start(bf16[32,24,128]{2,1,0:T(8,128)(2,1)} %param.5) | copy-start | bytes 589828
  6.5 134.0 %reduce-scatter.2.cloned.1.call-start = ((), (), s32[]{:S(2)}) async-start(), calls=%async_computation.1 | async-start | bytes 884736 | tf_op jit(solution)/shard_map/reduce_scatter | solution.py:102
  10.5 13.2 %collective-permute-start.8 = (s32[6]{0:T(128)S(1)}, s32[6]{0:T(128)S(1)}, u32[]{:S(2)}, u32[]{:S(2)}) collective-permute-start(s32[6]{0:T(128)S(1)} %get-tuple-element.15), channel_id=1, source_target_pairs={{0,30},{1,31},{2,0},{3,1},{4,2},{5,3},{6,4},{7,5},{8,6},{9,7},{10,... | collective-permute-start | bytes 80 | tf_op jit(solution)/shard_map/ppermute | solution.py:61
  17.7 6.0 %collective-permute-start.2 = (s32[6]{0:T(128)S(1)}, s32[6]{0:T(128)S(1)}, u32[]{:S(2)}, u32[]{:S(2)}) collective-permute-start(s32[6]{0:T(128)S(1)} %get-tuple-element.16), channel_id=1, source_target_pairs={{0,2},{1,3},{2,4},{3,5},{4,6},{5,7},{6,8},{7,9},{8,10},{9,11},{10,... | collective-permute-start | bytes 80 | tf_op jit(solution)/shard_map/ppermute | solution.py:61
  17.7 6.3 %collective-permute-start.4 = (s32[6]{0:T(128)S(1)}, s32[6]{0:T(128)S(1)}, u32[]{:S(2)}, u32[]{:S(2)}) collective-permute-start(s32[6]{0:T(128)S(1)} %get-tuple-element.17), channel_id=1, source_target_pairs={{0,16},{1,17},{2,18},{3,19},{4,20},{5,21},{6,22},{7,23},{8,24},{9,... | collective-permute-start | bytes 80 | tf_op jit(solution)/shard_map/ppermute | solution.py:61
  20.5 10.8 %collective-permute-start.6 = (s32[6]{0:T(128)S(1)}, s32[6]{0:T(128)S(1)}, u32[]{:S(2)}, u32[]{:S(2)}) collective-permute-start(s32[6]{0:T(128)S(1)} %get-tuple-element.18), channel_id=1, source_target_pairs={{0,31},{1,0},{2,1},{3,2},{4,3},{5,4},{6,5},{7,6},{8,7},{9,8},{10,9... | collective-permute-start | bytes 80 | tf_op jit(solution)/shard_map/ppermute | solution.py:61
  20.7 5.1 %collective-permute-start = (s32[6]{0:T(128)S(1)}, s32[6]{0:T(128)S(1)}, u32[]{:S(2)}, u32[]{:S(2)}) collective-permute-start(s32[6]{0:T(128)S(1)} %get-tuple-element.19), channel_id=1, source_target_pairs={{0,1},{1,2},{2,3},{3,4},{4,5},{5,6},{6,7},{7,8},{8,9},{9,10},{10,1... | collective-permute-start | bytes 80 | tf_op jit(solution)/shard_map/ppermute | solution.py:61
  25.8 25.8 %copy-start.14 = (s32[1024]{0:T(1024)}, s32[1024]{0:T(1024)S(1)}, u32[]{:S(2)}) copy-start(s32[1024]{0:T(1024)S(1)} %pad_clamp_fusion.5) | copy-start | bytes 12292
  26.4 14.4 %collective-permute-start.1 = (bf16[6,32,128]{2,1,0:T(8,128)(2,1)S(1)}, bf16[6,32,128]{2,1,0:T(8,128)(2,1)S(1)}, u32[]{:S(2)}, u32[]{:S(2)}) collective-permute-start(bf16[6,32,128]{2,1,0:T(8,128)(2,1)S(1)} %gather_fusion), channel_id=1, source_target_pairs={{1,0},{2,1},{3,2},{4,3},{5,4},{6,5},{7,6},{8,7},{9,8},{10,9},{11,1... | collective-permute-start | bytes 147464 | tf_op jit(solution)/shard_map/ppermute | solution.py:67
  31.3 21.8 %copy-start.15 = (s32[1024]{0:T(1024)}, s32[1024]{0:T(1024)S(1)}, u32[]{:S(2)}) copy-start(s32[1024]{0:T(1024)S(1)} %pad_clamp_fusion.2) | copy-start | bytes 12292
  33.5 7.3 %collective-permute-start.3 = (bf16[6,32,128]{2,1,0:T(8,128)(2,1)S(1)}, bf16[6,32,128]{2,1,0:T(8,128)(2,1)S(1)}, u32[]{:S(2)}, u32[]{:S(2)}) collective-permute-start(bf16[6,32,128]{2,1,0:T(8,128)(2,1)S(1)} %gather_fusion.1), channel_id=1, source_target_pairs={{2,0},{3,1},{4,2},{5,3},{6,4},{7,5},{8,6},{9,7},{10,8},{11,9},{12,... | collective-permute-start | bytes 147464 | tf_op jit(solution)/shard_map/ppermute | solution.py:67
  33.6 7.2 %collective-permute-start.5 = (bf16[6,32,128]{2,1,0:T(8,128)(2,1)S(1)}, bf16[6,32,128]{2,1,0:T(8,128)(2,1)S(1)}, u32[]{:S(2)}, u32[]{:S(2)}) collective-permute-start(bf16[6,32,128]{2,1,0:T(8,128)(2,1)S(1)} %gather_fusion.2), channel_id=1, source_target_pairs={{16,0},{17,1},{18,2},{19,3},{20,4},{21,5},{22,6},{23,7},{24,8},{25... | collective-permute-start | bytes 147464 | tf_op jit(solution)/shard_map/ppermute | solution.py:67
  37.9 2.9 %collective-permute-start.7 = (bf16[6,32,128]{2,1,0:T(8,128)(2,1)S(1)}, bf16[6,32,128]{2,1,0:T(8,128)(2,1)S(1)}, u32[]{:S(2)}, u32[]{:S(2)}) collective-permute-start(bf16[6,32,128]{2,1,0:T(8,128)(2,1)S(1)} %gather_fusion.3), channel_id=1, source_target_pairs={{31,0},{0,1},{1,2},{2,3},{3,4},{4,5},{5,6},{6,7},{7,8},{8,9},{9,10... | collective-permute-start | bytes 147464 | tf_op jit(solution)/shard_map/ppermute | solution.py:67
  39.3 6.6 %collective-permute-start.9 = (bf16[6,32,128]{2,1,0:T(8,128)(2,1)S(1)}, bf16[6,32,128]{2,1,0:T(8,128)(2,1)S(1)}, u32[]{:S(2)}, u32[]{:S(2)}) collective-permute-start(bf16[6,32,128]{2,1,0:T(8,128)(2,1)S(1)} %gather_fusion.4), channel_id=1, source_target_pairs={{30,0},{31,1},{0,2},{1,3},{2,4},{3,5},{4,6},{5,7},{6,8},{7,9},{8,1... | collective-permute-start | bytes 147464 | tf_op jit(solution)/shard_map/ppermute | solution.py:67
  49.5 2.1 %copy-start.6 = (f32[24,32,128]{2,1,0:T(8,128)}, f32[24,32,128]{2,1,0:T(8,128)S(1)}, u32[]{:S(2)}) copy-start(f32[24,32,128]{2,1,0:T(8,128)S(1)} %convolution_bitcast_fusion.4) | copy-start | bytes 1179652
  52.2 10.4 %collective-permute-start.10 = (bf16[6,64,128]{2,1,0:T(8,128)(2,1)S(1)}, bf16[6,64,128]{2,1,0:T(8,128)(2,1)S(1)}, u32[]{:S(2)}, u32[]{:S(2)}) collective-permute-start(bf16[6,64,128]{2,1,0:T(8,128)(2,1)S(1)} %gather_fusion.6), channel_id=1, source_target_pairs={{1,0},{2,1},{3,2},{4,3},{5,4},{6,5},{7,6},{8,7},{9,8},{10,9},{11,1... | collective-permute-start | bytes 294920 | tf_op jit(solution)/shard_map/ppermute | solution.py:67
  54.8 8.4 %collective-permute-start.11 = (bf16[6,64,128]{2,1,0:T(8,128)(2,1)S(1)}, bf16[6,64,128]{2,1,0:T(8,128)(2,1)S(1)}, u32[]{:S(2)}, u32[]{:S(2)}) collective-permute-start(bf16[6,64,128]{2,1,0:T(8,128)(2,1)S(1)} %gather_fusion.7), channel_id=1, source_target_pairs={{2,0},{3,1},{4,2},{5,3},{6,4},{7,5},{8,6},{9,7},{10,8},{11,9},{12,... | collective-permute-start | bytes 294920 | tf_op jit(solution)/shard_map/ppermute | solution.py:67
  55.7 8.2 %collective-permute-start.12 = (bf16[6,64,128]{2,1,0:T(8,128)(2,1)S(1)}, bf16[6,64,128]{2,1,0:T(8,128)(2,1)S(1)}, u32[]{:S(2)}, u32[]{:S(2)}) collective-permute-start(bf16[6,64,128]{2,1,0:T(8,128)(2,1)S(1)} %gather_fusion.8), channel_id=1, source_target_pairs={{16,0},{17,1},{18,2},{19,3},{20,4},{21,5},{22,6},{23,7},{24,8},{25... | collective-permute-start | bytes 294920 | tf_op jit(solution)/shard_map/ppermute | solution.py:67
  57.4 7.2 %collective-permute-start.13 = (bf16[6,64,128]{2,1,0:T(8,128)(2,1)S(1)}, bf16[6,64,128]{2,1,0:T(8,128)(2,1)S(1)}, u32[]{:S(2)}, u32[]{:S(2)}) collective-permute-start(bf16[6,64,128]{2,1,0:T(8,128)(2,1)S(1)} %gather_fusion.9), channel_id=1, source_target_pairs={{31,0},{0,1},{1,2},{2,3},{3,4},{4,5},{5,6},{6,7},{7,8},{8,9},{9,10... | collective-permute-start | bytes 294920 | tf_op jit(solution)/shard_map/ppermute | solution.py:67
  59.4 8.3 %collective-permute-start.14 = (bf16[6,64,128]{2,1,0:T(8,128)(2,1)S(1)}, bf16[6,64,128]{2,1,0:T(8,128)(2,1)S(1)}, u32[]{:S(2)}, u32[]{:S(2)}) collective-permute-start(bf16[6,64,128]{2,1,0:T(8,128)(2,1)S(1)} %gather_fusion.10), channel_id=1, source_target_pairs={{30,0},{31,1},{0,2},{1,3},{2,4},{3,5},{4,6},{5,7},{6,8},{7,9},{8,1... | collective-permute-start | bytes 294920 | tf_op jit(solution)/shard_map/ppermute | solution.py:67
  70.5 3.3 %copy-start.1 = (bf16[24,5,128,128]{3,2,1,0:T(8,128)(2,1)S(1)}, bf16[24,5,128,128]{3,2,1,0:T(8,128)(2,1)}, u32[]{:S(2)}) copy-start(bf16[24,5,128,128]{3,2,1,0:T(8,128)(2,1)} %param.7) | copy-start | bytes 11796484
  75.4 1.3 copy-start.4
  75.5 2.0 %copy-start.9 = (f32[24,32,128]{2,1,0:T(8,128)}, f32[24,32,128]{2,1,0:T(8,128)S(1)}, u32[]{:S(2)}) copy-start(f32[24,32,128]{2,1,0:T(8,128)S(1)} %get-tuple-element.35) | copy-start | bytes 1179652
  75.5 2.0 %copy-start.11 = (f32[24,32,128]{2,1,0:T(8,128)}, f32[24,32,128]{2,1,0:T(8,128)S(1)}, u32[]{:S(2)}) copy-start(f32[24,32,128]{2,1,0:T(8,128)S(1)} %get-tuple-element.36) | copy-start | bytes 1179652
  78.2 11.4 %collective-permute-start.15 = (bf16[6,64,128]{2,1,0:T(8,128)(2,1)S(1)}, bf16[6,64,128]{2,1,0:T(8,128)(2,1)S(1)}, u32[]{:S(2)}, u32[]{:S(2)}) collective-permute-start(bf16[6,64,128]{2,1,0:T(8,128)(2,1)S(1)} %gather_fusion.12), channel_id=1, source_target_pairs={{1,0},{2,1},{3,2},{4,3},{5,4},{6,5},{7,6},{8,7},{9,8},{10,9},{11,1... | collective-permute-start | bytes 294920 | tf_op jit(solution)/shard_map/ppermute | solution.py:67
  81.2 9.0 %collective-permute-start.16 = (bf16[6,64,128]{2,1,0:T(8,128)(2,1)S(1)}, bf16[6,64,128]{2,1,0:T(8,128)(2,1)S(1)}, u32[]{:S(2)}, u32[]{:S(2)}) collective-permute-start(bf16[6,64,128]{2,1,0:T(8,128)(2,1)S(1)} %gather_fusion.13), channel_id=1, source_target_pairs={{2,0},{3,1},{4,2},{5,3},{6,4},{7,5},{8,6},{9,7},{10,8},{11,9},{12,... | collective-permute-start | bytes 294920 | tf_op jit(solution)/shard_map/ppermute | solution.py:67
  81.7 9.2 %collective-permute-start.17 = (bf16[6,64,128]{2,1,0:T(8,128)(2,1)S(1)}, bf16[6,64,128]{2,1,0:T(8,128)(2,1)S(1)}, u32[]{:S(2)}, u32[]{:S(2)}) collective-permute-start(bf16[6,64,128]{2,1,0:T(8,128)(2,1)S(1)} %gather_fusion.14), channel_id=1, source_target_pairs={{16,0},{17,1},{18,2},{19,3},{20,4},{21,5},{22,6},{23,7},{24,8},{25... | collective-permute-start | bytes 294920 | tf_op jit(solution)/shard_map/ppermute | solution.py:67
  84.2 7.4 %collective-permute-start.18 = (bf16[6,64,128]{2,1,0:T(8,128)(2,1)S(1)}, bf16[6,64,128]{2,1,0:T(8,128)(2,1)S(1)}, u32[]{:S(2)}, u32[]{:S(2)}) collective-permute-start(bf16[6,64,128]{2,1,0:T(8,128)(2,1)S(1)} %gather_fusion.15), channel_id=1, source_target_pairs={{31,0},{0,1},{1,2},{2,3},{3,4},{4,5},{5,6},{6,7},{7,8},{8,9},{9,10... | collective-permute-start | bytes 294920 | tf_op jit(solution)/shard_map/ppermute | solution.py:67
  86.2 7.5 %collective-permute-start.19 = (bf16[6,64,128]{2,1,0:T(8,128)(2,1)S(1)}, bf16[6,64,128]{2,1,0:T(8,128)(2,1)S(1)}, u32[]{:S(2)}, u32[]{:S(2)}) collective-permute-start(bf16[6,64,128]{2,1,0:T(8,128)(2,1)S(1)} %gather_fusion.16), channel_id=1, source_target_pairs={{30,0},{31,1},{0,2},{1,3},{2,4},{3,5},{4,6},{5,7},{6,8},{7,9},{8,1... | collective-permute-start | bytes 294920 | tf_op jit(solution)/shard_map/ppermute | solution.py:67
  96.5 3.3 %copy-start.2 = (bf16[24,5,128,128]{3,2,1,0:T(8,128)(2,1)S(1)}, bf16[24,5,128,128]{3,2,1,0:T(8,128)(2,1)}, u32[]{:S(2)}) copy-start(bf16[24,5,128,128]{3,2,1,0:T(8,128)(2,1)} %param.7) | copy-start | bytes 11796484
  101.4 1.3 copy-start.12
  (5 other events, 5.3 us)
Sparse Core Ops, SparseCore 0:
  104.6 35.9 reduce-scatter.1

commit v2 on v1

--- a/solution.py
+++ b/solution.py
@@ -91,15 +91,22 @@
         update_real = products[:, 0, 0] - products[:, 1, 1]
         update_imag = products[:, 1, 0] + products[:, 0, 1]
         iterate = iterate + jnp.concatenate([update_real, update_imag], axis=1)
-    it_real, it_imag = iterate[:, :col_count], iterate[:, col_count:]
+    node_index = lax.axis_index("node")
+    parts = iterate.reshape(dev_rows, 2, node_count, col_count // node_count, -1)
+    it_real, it_imag = parts[:, 0], parts[:, 1]
     weighted = jnp.stack(
         [
             node_real * it_real - node_imag * it_imag,
             node_real * it_imag + node_imag * it_real,
         ]
     )
-    weighted = jnp.transpose(weighted / node_count, (0, 2, 1, 3))
-    return lax.psum_scatter(weighted, "node", scatter_dimension=1, tiled=True)
+    weighted = jnp.transpose(weighted / node_count, (2, 0, 3, 1, 4))
+    total = lax.dynamic_index_in_dim(weighted, node_index, 0, keepdims=False)
+    for offset in range(1, node_count):
+        chunk = lax.dynamic_index_in_dim(weighted, (node_index + offset) % node_count, 0, keepdims=False)
+        perm = [(j, (j + offset) % node_count) for j in range(node_count)]
+        total = total + lax.ppermute(chunk, "node", perm)
+    return total
 
 
 def solution(mesh):

time: 152 us -> 117 us (0.77); the launches traced: 149 us -> 117 us
  waiting for transfers between devices: 47.2 us -> 12.4 us
  starting transfers between devices: 41.1 us -> 57.2 us
  between operations: 14.1 us -> 0.87 us
    reduce_scatter x1 -> x0, waiting for transfers between devices: 36.1 us -> none  [per_device(): return lax.psum_scatter(weighted, 'node', scatter_dimension=1, tiled=True)]
    ppermute x0 -> x7, starting transfers between devices: none -> 15.8 us  [per_device(): total = total + lax.ppermute(chunk, 'node', perm)]
    ppermute x0 -> x7, waiting for transfers between devices: none -> 5.25 us  [per_device(): total = total + lax.ppermute(chunk, 'node', perm)]
    dot_general x3, matrix products: 9.38 us -> 6.96 us  [apply_pair(): jnp.einsum('nscb,nsbd->ncd', picked, first, preferred_element_type=jnp.fl...]
    dot_general x2, matrix products: 1.79 us -> 4.11 us  [apply_pair(): jnp.einsum('nscb,nsbd->ncd', picked, second, preferred_element_type=jnp.f...]
    ppermute x5, waiting for transfers between devices: 2.06 us -> 0.01 us  [per_device(): lax.ppermute(wanted[which], 'rows', to_partner(offset))]
    ppermute x15, waiting for transfers between devices: 9.03 us -> 7.15 us  [fetch_halo(): lax.ppermute(vector[asked_for[which]], 'rows', from_partner(offset))]
    concatenate x0 -> x2, local copies, waits for them, and re-layouts: none -> 1.82 us  [per_device(): iterate = iterate + jnp.concatenate([update_real, update_imag], axis=1)]
  transfers between devices with their start and end apart: 21 -> 27, of which waited for: 6 -> 6; matrix products, arithmetic and copies ran while one was open for 9% -> 12% of each run, Pallas kernels for 0% -> 0%
where the time goes in v2:
time: 117 us
  starting transfers between devices  57.2 us (49%)
  local copies, waits for them, and re-layouts  29.2 us (25%)
  waiting for transfers between devices  12.4 us (11%)
  matrix products  12.2 us (10%)
  other arithmetic  4.78 us (4%)
    ppermute x15, starting transfers between devices, fetch_halo(): lax.ppermute(vector[asked_for[which]], 'rows', from_partner(offset))  29.1 us
    ppermute x7, starting transfers between devices, per_device(): total = total + lax.ppermute(chunk, 'node', perm)  15.8 us
    ppermute x5, starting transfers between devices, per_device(): lax.ppermute(wanted[which], 'rows', to_partner(offset))  12.3 us
    unnamed x42, local copies, waits for them, and re-layouts  10.8 us
    gather x15, local copies, waits for them, and re-layouts, fetch_halo(): vector[asked_for[which]]  8.7 us
    ppermute x15, waiting for transfers between devices, fetch_halo(): lax.ppermute(vector[asked_for[which]], 'rows', from_partner(offset))  7.15 us
    dot_general x3, matrix products, apply_pair(): jnp.einsum('nscb,nsbd->ncd', picked, first, preferred_element_type=jnp.fl...  6.96 us
    ppermute x7, waiting for transfers between devices, per_device(): total = total + lax.ppermute(chunk, 'node', perm)  5.25 us
  transfers between devices with their start and end apart: 27, of which 6 were waited for; matrix products, arithmetic and copies ran while one was open for 12% of the time, Pallas kernels for 0%

profile of v2, /device:TPU:3, one launch (start us, length us, event | category | flops | bytes accessed | tf_op | source)
XLA Modules:
  0.0 116.6 jit_solution(3645062999788135725)
XLA Ops:
  4.2 7.7 %collective-permute-start.8 = (s32[6]{0:T(128)S(1)}, s32[6]{0:T(128)S(1)}, u32[]{:S(2)}, u32[]{:S(2)}) collective-permute-start(s32[6]{0:T(128)S(1)} %get-tuple-element.15), channel_id=1, source_target_pairs={{0,30},{1,31},{2,0},{3,1},{4,2},{5,3},{6,4},{7,5},{8,6},{9,7},{10,... | collective-permute-start | bytes 80 | tf_op jit(solution)/shard_map/ppermute | solution.py:61
  11.9 2.4 %collective-permute-start.4 = (s32[6]{0:T(128)S(1)}, s32[6]{0:T(128)S(1)}, u32[]{:S(2)}, u32[]{:S(2)}) collective-permute-start(s32[6]{0:T(128)S(1)} %get-tuple-element.17), channel_id=1, source_target_pairs={{0,16},{1,17},{2,18},{3,19},{4,20},{5,21},{6,22},{7,23},{8,24},{9,... | collective-permute-start | bytes 80 | tf_op jit(solution)/shard_map/ppermute | solution.py:61
  14.4 2.1 %collective-permute-start = (s32[6]{0:T(128)S(1)}, s32[6]{0:T(128)S(1)}, u32[]{:S(2)}, u32[]{:S(2)}) collective-permute-start(s32[6]{0:T(128)S(1)} %get-tuple-element.19), channel_id=1, source_target_pairs={{0,1},{1,2},{2,3},{3,4},{4,5},{5,6},{6,7},{7,8},{8,9},{9,10},{10,1... | collective-permute-start | bytes 80 | tf_op jit(solution)/shard_map/ppermute | solution.py:61
  16.5 1.0 copy.101
  18.2 1.3 %collective-permute-start.7 = (bf16[6,32,128]{2,1,0:T(8,128)(2,1)S(1)}, bf16[6,32,128]{2,1,0:T(8,128)(2,1)S(1)}, u32[]{:S(2)}, u32[]{:S(2)}) collective-permute-start(bf16[6,32,128]{2,1,0:T(8,128)(2,1)S(1)} %gather_fusion.3), channel_id=1, source_target_pairs={{31,0},{0,1},{1,2},{2,3},{3,4},{4,5},{5,6},{6,7},{7,8},{8,9},{9,10... | collective-permute-start | bytes 147464 | tf_op jit(solution)/shard_map/ppermute | solution.py:67
  20.1 3.9 %collective-permute-start.3 = (bf16[6,32,128]{2,1,0:T(8,128)(2,1)S(1)}, bf16[6,32,128]{2,1,0:T(8,128)(2,1)S(1)}, u32[]{:S(2)}, u32[]{:S(2)}) collective-permute-start(bf16[6,32,128]{2,1,0:T(8,128)(2,1)S(1)} %gather_fusion.1), channel_id=1, source_target_pairs={{2,0},{3,1},{4,2},{5,3},{6,4},{7,5},{8,6},{9,7},{10,8},{11,9},{12,... | collective-permute-start | bytes 147464 | tf_op jit(solution)/shard_map/ppermute | solution.py:67
  24.6 0.9 collective-permute-start.1
  26.1 4.3 %collective-permute-start.5 = (bf16[6,32,128]{2,1,0:T(8,128)(2,1)S(1)}, bf16[6,32,128]{2,1,0:T(8,128)(2,1)S(1)}, u32[]{:S(2)}, u32[]{:S(2)}) collective-permute-start(bf16[6,32,128]{2,1,0:T(8,128)(2,1)S(1)} %gather_fusion.2), channel_id=1, source_target_pairs={{16,0},{17,1},{18,2},{19,3},{20,4},{21,5},{22,6},{23,7},{24,8},{25... | collective-permute-start | bytes 147464 | tf_op jit(solution)/shard_map/ppermute | solution.py:67
  31.1 2.1 %collective-permute-done.5 = bf16[6,32,128]{2,1,0:T(8,128)(2,1)S(1)} collective-permute-done((bf16[6,32,128]{2,1,0:T(8,128)(2,1)S(1)}, bf16[6,32,128]{2,1,0:T(8,128)(2,1)S(1)}, u32[]{:S(2)}, u32[]{:S(2)}) %collective-permute-start.5) | collective-permute-done | bytes 49184 | tf_op jit(solution)/shard_map/ppermute | solution.py:67
  33.2 4.3 %collective-permute-done.9 = bf16[6,32,128]{2,1,0:T(8,128)(2,1)S(1)} collective-permute-done((bf16[6,32,128]{2,1,0:T(8,128)(2,1)S(1)}, bf16[6,32,128]{2,1,0:T(8,128)(2,1)S(1)}, u32[]{:S(2)}, u32[]{:S(2)}) %collective-permute-start.9) | collective-permute-done | bytes 49184 | tf_op jit(solution)/shard_map/ppermute | solution.py:67
  38.3 2.8 %convolution_bitcast_fusion.4 = f32[24,32,128]{2,1,0:T(8,128)S(1)} fusion(bf16[24,5,32,128]{3,2,1,0:T(8,128)(2,1)S(1)} %bitcast.171, bf16[24,5,128,128]{3,2,1,0:T(8,128)(2,1)} %param.6), kind=kOutput, calls=%fused_computation.22 | convolution fusion | flops 125829120 | bytes 5308416 | tf_op jit(solution)/shard_map/nscb,nsbd->ncd/dot_general | solution.py:25
  46.6 1.9 %collective-permute-start.12 = (bf16[6,64,128]{2,1,0:T(8,128)(2,1)S(1)}, bf16[6,64,128]{2,1,0:T(8,128)(2,1)S(1)}, u32[]{:S(2)}, u32[]{:S(2)}) collective-permute-start(bf16[6,64,128]{2,1,0:T(8,128)(2,1)S(1)} %gather_fusion.8), channel_id=1, source_target_pairs={{16,0},{17,1},{18,2},{19,3},{20,4},{21,5},{22,6},{23,7},{24,8},{25... | collective-permute-start | bytes 294920 | tf_op jit(solution)/shard_map/ppermute | solution.py:67
  48.4 1.2 %collective-permute-start.13 = (bf16[6,64,128]{2,1,0:T(8,128)(2,1)S(1)}, bf16[6,64,128]{2,1,0:T(8,128)(2,1)S(1)}, u32[]{:S(2)}, u32[]{:S(2)}) collective-permute-start(bf16[6,64,128]{2,1,0:T(8,128)(2,1)S(1)} %gather_fusion.9), channel_id=1, source_target_pairs={{31,0},{0,1},{1,2},{2,3},{3,4},{4,5},{5,6},{6,7},{7,8},{8,9},{9,10... | collective-permute-start | bytes 294920 | tf_op jit(solution)/shard_map/ppermute | solution.py:67
  49.6 4.1 %collective-permute-start.14 = (bf16[6,64,128]{2,1,0:T(8,128)(2,1)S(1)}, bf16[6,64,128]{2,1,0:T(8,128)(2,1)S(1)}, u32[]{:S(2)}, u32[]{:S(2)}) collective-permute-start(bf16[6,64,128]{2,1,0:T(8,128)(2,1)S(1)} %gather_fusion.10), channel_id=1, source_target_pairs={{30,0},{31,1},{0,2},{1,3},{2,4},{3,5},{4,6},{5,7},{6,8},{7,9},{8,1... | collective-permute-start | bytes 294920 | tf_op jit(solution)/shard_map/ppermute | solution.py:67
  57.6 2.1 %gather_fusion.11 = bf16[120,64,128]{2,1,0:T(8,128)(2,1)S(1)} fusion(bf16[54,64,128]{2,1,0:T(8,128)(2,1)} %constant_dynamic-update-slice_fusion.6, s32[1024]{0:T(1024)S(1)} %pad_clamp_fusion), kind=kCustom, calls=%fused_computation.11 | custom fusion | bytes 3932640 | tf_op jit(solution)/shard_map/gather | solution.py:24
  59.7 3.2 %convolution_bitcast_fusion.3 = f32[24,64,128]{2,1,0:T(8,128)S(1)} fusion(bf16[24,5,64,128]{3,2,1,0:T(8,128)(2,1)S(1)} %bitcast.165, bf16[24,5,128,128]{3,2,1,0:T(8,128)(2,1)} %param.6), kind=kOutput, calls=%fused_computation.21 | convolution fusion | flops 251658240 | bytes 6684672 | tf_op jit(solution)/shard_map/nscb,nsbd->ncd/dot_general | solution.py:25
  63.0 0.9 convolution_bitcast_fusion.2
  64.8 1.0 copy-done.4
  69.0 2.1 %collective-permute-start.16 = (bf16[6,64,128]{2,1,0:T(8,128)(2,1)S(1)}, bf16[6,64,128]{2,1,0:T(8,128)(2,1)S(1)}, u32[]{:S(2)}, u32[]{:S(2)}) collective-permute-start(bf16[6,64,128]{2,1,0:T(8,128)(2,1)S(1)} %gather_fusion.13), channel_id=1, source_target_pairs={{2,0},{3,1},{4,2},{5,3},{6,4},{7,5},{8,6},{9,7},{10,8},{11,9},{12,... | collective-permute-start | bytes 294920 | tf_op jit(solution)/shard_map/ppermute | solution.py:67
  71.9 2.9 %collective-permute-start.17 = (bf16[6,64,128]{2,1,0:T(8,128)(2,1)S(1)}, bf16[6,64,128]{2,1,0:T(8,128)(2,1)S(1)}, u32[]{:S(2)}, u32[]{:S(2)}) collective-permute-start(bf16[6,64,128]{2,1,0:T(8,128)(2,1)S(1)} %gather_fusion.14), channel_id=1, source_target_pairs={{16,0},{17,1},{18,2},{19,3},{20,4},{21,5},{22,6},{23,7},{24,8},{25... | collective-permute-start | bytes 294920 | tf_op jit(solution)/shard_map/ppermute | solution.py:67
  74.9 1.2 %collective-permute-start.18 = (bf16[6,64,128]{2,1,0:T(8,128)(2,1)S(1)}, bf16[6,64,128]{2,1,0:T(8,128)(2,1)S(1)}, u32[]{:S(2)}, u32[]{:S(2)}) collective-permute-start(bf16[6,64,128]{2,1,0:T(8,128)(2,1)S(1)} %gather_fusion.15), channel_id=1, source_target_pairs={{31,0},{0,1},{1,2},{2,3},{3,4},{4,5},{5,6},{6,7},{7,8},{8,9},{9,10... | collective-permute-start | bytes 294920 | tf_op jit(solution)/shard_map/ppermute | solution.py:67
  76.0 4.3 %collective-permute-start.19 = (bf16[6,64,128]{2,1,0:T(8,128)(2,1)S(1)}, bf16[6,64,128]{2,1,0:T(8,128)(2,1)S(1)}, u32[]{:S(2)}, u32[]{:S(2)}) collective-permute-start(bf16[6,64,128]{2,1,0:T(8,128)(2,1)S(1)} %gather_fusion.16), channel_id=1, source_target_pairs={{30,0},{31,1},{0,2},{1,3},{2,4},{3,5},{4,6},{5,7},{6,8},{7,9},{8,1... | collective-permute-start | bytes 294920 | tf_op jit(solution)/shard_map/ppermute | solution.py:67
  80.3 1.4 %copy.68 = f32[24,64,128]{2,0,1:T(8,128)} copy(f32[24,64,128]{2,1,0:T(8,128)S(1)} %get-tuple-element.46) | data formatting | bytes 1572864 | tf_op jit(solution)/shard_map/concatenate | solution.py:93
  85.7 2.1 %gather_fusion.17 = bf16[120,64,128]{2,1,0:T(8,128)(2,1)S(1)} fusion(bf16[54,64,128]{2,1,0:T(8,128)(2,1)} %constant_dynamic-update-slice_fusion.12, s32[1024]{0:T(1024)S(1)} %pad_clamp_fusion), kind=kCustom, calls=%fused_computation.17 | custom fusion | bytes 3932640 | tf_op jit(solution)/shard_map/gather | solution.py:24
  87.8 3.2 %convolution_bitcast_fusion = f32[24,64,128]{2,1,0:T(8,128)S(1)} fusion(bf16[24,5,64,128]{3,2,1,0:T(8,128)(2,1)S(1)} %bitcast.163, bf16[24,5,128,128]{3,2,1,0:T(8,128)(2,1)} %param.7), kind=kOutput, calls=%fused_computation.18 | convolution fusion | flops 251658240 | bytes 6684672 | tf_op jit(solution)/shard_map/nscb,nsbd->ncd/dot_general | solution.py:28
  94.9 8.1 %collective-permute-start.20 = (f32[2,4,24,128]{3,2,1,0:T(8,128)S(1)}, f32[2,4,24,128]{3,2,1,0:T(8,128)S(1)}, u32[]{:S(2)}, u32[]{:S(2)}) collective-permute-start(f32[2,4,24,128]{3,2,1,0:T(8,128)S(1)} %get-tuple-element.37), channel_id=1, source_target_pairs={{0,32},{32,64},{64,96},{96,128},{128,160},{160,192},{192,224},{224... | collective-permute-start | bytes 294920 | tf_op jit(solution)/shard_map/ppermute | solution.py:108
  103.0 1.3 %collective-permute-start.21 = (f32[2,4,24,128]{3,2,1,0:T(8,128)S(1)}, f32[2,4,24,128]{3,2,1,0:T(8,128)S(1)}, u32[]{:S(2)}, u32[]{:S(2)}) collective-permute-start(f32[2,4,24,128]{3,2,1,0:T(8,128)S(1)} %get-tuple-element.43), channel_id=1, source_target_pairs={{0,64},{32,96},{64,128},{96,160},{128,192},{160,224},{192,0},{224,... | collective-permute-start | bytes 294920 | tf_op jit(solution)/shard_map/ppermute | solution.py:108
  104.3 1.7 %collective-permute-start.22 = (f32[2,4,24,128]{3,2,1,0:T(8,128)S(1)}, f32[2,4,24,128]{3,2,1,0:T(8,128)S(1)}, u32[]{:S(2)}, u32[]{:S(2)}) collective-permute-start(f32[2,4,24,128]{3,2,1,0:T(8,128)S(1)} %get-tuple-element.42), channel_id=1, source_target_pairs={{0,96},{32,128},{64,160},{96,192},{128,224},{160,0},{192,32},{224,... | collective-permute-start | bytes 294920 | tf_op jit(solution)/shard_map/ppermute | solution.py:108
  106.3 1.9 %collective-permute-start.24 = (f32[2,4,24,128]{3,2,1,0:T(8,128)S(1)}, f32[2,4,24,128]{3,2,1,0:T(8,128)S(1)}, u32[]{:S(2)}, u32[]{:S(2)}) collective-permute-start(f32[2,4,24,128]{3,2,1,0:T(8,128)S(1)} %get-tuple-element.40), channel_id=1, source_target_pairs={{0,160},{32,192},{64,224},{96,0},{128,32},{160,64},{192,96},{224,1... | collective-permute-start | bytes 294920 | tf_op jit(solution)/shard_map/ppermute | solution.py:108
  109.1 1.6 %collective-permute-start.26 = (f32[2,4,24,128]{3,2,1,0:T(8,128)S(1)}, f32[2,4,24,128]{3,2,1,0:T(8,128)S(1)}, u32[]{:S(2)}, u32[]{:S(2)}) collective-permute-start(f32[2,4,24,128]{3,2,1,0:T(8,128)S(1)} %get-tuple-element.38), channel_id=1, source_target_pairs={{0,224},{32,0},{64,32},{96,64},{128,96},{160,128},{192,160},{224,1... | collective-permute-start | bytes 294920 | tf_op jit(solution)/shard_map/ppermute | solution.py:108
  110.7 3.6 %collective-permute-done.23 = f32[2,4,24,128]{3,2,1,0:T(8,128)S(1)} collective-permute-done((f32[2,4,24,128]{3,2,1,0:T(8,128)S(1)}, f32[2,4,24,128]{3,2,1,0:T(8,128)S(1)}, u32[]{:S(2)}, u32[]{:S(2)}) %collective-permute-start.23) | collective-permute-done | bytes 98336 | tf_op jit(solution)/shard_map/ppermute | solution.py:108
  115.0 1.0 collective-permute-done.26
  (148 shorter events, 32.2 us)
Async XLA Ops:
  0.0 41.2 %copy-start = (bf16[1,2,24,128,128]{4,3,2,1,0:T(8,128)(2,1)S(1)}, bf16[1,2,24,128,128]{4,3,2,1,0:T(8,128)(2,1)}, u32[]{:S(2)}) copy-start(bf16[1,2,24,128,128]{4,3,2,1,0:T(8,128)(2,1)} %param.8) | copy-start | bytes 4718596
  0.0 17.4 %copy-start.10 = (bf16[32,24,128]{2,1,0:T(8,128)(2,1)S(1)}, bf16[32,24,128]{2,1,0:T(8,128)(2,1)}, u32[]{:S(2)}) copy-start(bf16[32,24,128]{2,1,0:T(8,128)(2,1)} %param.5) | copy-start | bytes 589828
  4.2 13.4 %collective-permute-start.6 = (s32[6]{0:T(128)S(1)}, s32[6]{0:T(128)S(1)}, u32[]{:S(2)}, u32[]{:S(2)}) collective-permute-start(s32[6]{0:T(128)S(1)} %get-tuple-element.18), channel_id=1, source_target_pairs={{0,31},{1,0},{2,1},{3,2},{4,3},{5,4},{6,5},{7,6},{8,7},{9,8},{10,9... | collective-permute-start | bytes 80 | tf_op jit(solution)/shard_map/ppermute | solution.py:61
  4.2 13.4 %collective-permute-start.8 = (s32[6]{0:T(128)S(1)}, s32[6]{0:T(128)S(1)}, u32[]{:S(2)}, u32[]{:S(2)}) collective-permute-start(s32[6]{0:T(128)S(1)} %get-tuple-element.15), channel_id=1, source_target_pairs={{0,30},{1,31},{2,0},{3,1},{4,2},{5,3},{6,4},{7,5},{8,6},{9,7},{10,... | collective-permute-start | bytes 80 | tf_op jit(solution)/shard_map/ppermute | solution.py:61
  11.9 7.6 %collective-permute-start.2 = (s32[6]{0:T(128)S(1)}, s32[6]{0:T(128)S(1)}, u32[]{:S(2)}, u32[]{:S(2)}) collective-permute-start(s32[6]{0:T(128)S(1)} %get-tuple-element.16), channel_id=1, source_target_pairs={{0,2},{1,3},{2,4},{3,5},{4,6},{5,7},{6,8},{7,9},{8,10},{9,11},{10,... | collective-permute-start | bytes 80 | tf_op jit(solution)/shard_map/ppermute | solution.py:61
  11.9 7.6 %collective-permute-start.4 = (s32[6]{0:T(128)S(1)}, s32[6]{0:T(128)S(1)}, u32[]{:S(2)}, u32[]{:S(2)}) collective-permute-start(s32[6]{0:T(128)S(1)} %get-tuple-element.17), channel_id=1, source_target_pairs={{0,16},{1,17},{2,18},{3,19},{4,20},{5,21},{6,22},{7,23},{8,24},{9,... | collective-permute-start | bytes 80 | tf_op jit(solution)/shard_map/ppermute | solution.py:61
  14.4 9.6 %collective-permute-start = (s32[6]{0:T(128)S(1)}, s32[6]{0:T(128)S(1)}, u32[]{:S(2)}, u32[]{:S(2)}) collective-permute-start(s32[6]{0:T(128)S(1)} %get-tuple-element.19), channel_id=1, source_target_pairs={{0,1},{1,2},{2,3},{3,4},{4,5},{5,6},{6,7},{7,8},{8,9},{9,10},{10,1... | collective-permute-start | bytes 80 | tf_op jit(solution)/shard_map/ppermute | solution.py:61
  18.2 15.0 %collective-permute-start.7 = (bf16[6,32,128]{2,1,0:T(8,128)(2,1)S(1)}, bf16[6,32,128]{2,1,0:T(8,128)(2,1)S(1)}, u32[]{:S(2)}, u32[]{:S(2)}) collective-permute-start(bf16[6,32,128]{2,1,0:T(8,128)(2,1)S(1)} %gather_fusion.3), channel_id=1, source_target_pairs={{31,0},{0,1},{1,2},{2,3},{3,4},{4,5},{5,6},{6,7},{7,8},{8,9},{9,10... | collective-permute-start | bytes 147464 | tf_op jit(solution)/shard_map/ppermute | solution.py:67
  20.1 11.0 %collective-permute-start.3 = (bf16[6,32,128]{2,1,0:T(8,128)(2,1)S(1)}, bf16[6,32,128]{2,1,0:T(8,128)(2,1)S(1)}, u32[]{:S(2)}, u32[]{:S(2)}) collective-permute-start(bf16[6,32,128]{2,1,0:T(8,128)(2,1)S(1)} %gather_fusion.1), channel_id=1, source_target_pairs={{2,0},{3,1},{4,2},{5,3},{6,4},{7,5},{8,6},{9,7},{10,8},{11,9},{12,... | collective-permute-start | bytes 147464 | tf_op jit(solution)/shard_map/ppermute | solution.py:67
  24.6 6.5 %collective-permute-start.1 = (bf16[6,32,128]{2,1,0:T(8,128)(2,1)S(1)}, bf16[6,32,128]{2,1,0:T(8,128)(2,1)S(1)}, u32[]{:S(2)}, u32[]{:S(2)}) collective-permute-start(bf16[6,32,128]{2,1,0:T(8,128)(2,1)S(1)} %gather_fusion), channel_id=1, source_target_pairs={{1,0},{2,1},{3,2},{4,3},{5,4},{6,5},{7,6},{8,7},{9,8},{10,9},{11,1... | collective-permute-start | bytes 147464 | tf_op jit(solution)/shard_map/ppermute | solution.py:67
  25.5 18.7 %copy-start.11 = (s32[1024]{0:T(1024)}, s32[1024]{0:T(1024)S(1)}, u32[]{:S(2)}) copy-start(s32[1024]{0:T(1024)S(1)} %pad_clamp_fusion.3) | copy-start | bytes 12292
  26.1 7.1 %collective-permute-start.5 = (bf16[6,32,128]{2,1,0:T(8,128)(2,1)S(1)}, bf16[6,32,128]{2,1,0:T(8,128)(2,1)S(1)}, u32[]{:S(2)}, u32[]{:S(2)}) collective-permute-start(bf16[6,32,128]{2,1,0:T(8,128)(2,1)S(1)} %gather_fusion.2), channel_id=1, source_target_pairs={{16,0},{17,1},{18,2},{19,3},{20,4},{21,5},{22,6},{23,7},{24,8},{25... | collective-permute-start | bytes 147464 | tf_op jit(solution)/shard_map/ppermute | solution.py:67
  30.4 15.6 %copy-start.12 = (s32[1024]{0:T(1024)}, s32[1024]{0:T(1024)S(1)}, u32[]{:S(2)}) copy-start(s32[1024]{0:T(1024)S(1)} %pad_clamp_fusion.1) | copy-start | bytes 12292
  30.9 6.6 %collective-permute-start.9 = (bf16[6,32,128]{2,1,0:T(8,128)(2,1)S(1)}, bf16[6,32,128]{2,1,0:T(8,128)(2,1)S(1)}, u32[]{:S(2)}, u32[]{:S(2)}) collective-permute-start(bf16[6,32,128]{2,1,0:T(8,128)(2,1)S(1)} %gather_fusion.4), channel_id=1, source_target_pairs={{30,0},{31,1},{0,2},{1,3},{2,4},{3,5},{4,6},{5,7},{6,8},{7,9},{8,1... | collective-permute-start | bytes 147464 | tf_op jit(solution)/shard_map/ppermute | solution.py:67
  43.9 9.8 %collective-permute-start.10 = (bf16[6,64,128]{2,1,0:T(8,128)(2,1)S(1)}, bf16[6,64,128]{2,1,0:T(8,128)(2,1)S(1)}, u32[]{:S(2)}, u32[]{:S(2)}) collective-permute-start(bf16[6,64,128]{2,1,0:T(8,128)(2,1)S(1)} %gather_fusion.6), channel_id=1, source_target_pairs={{1,0},{2,1},{3,2},{4,3},{5,4},{6,5},{7,6},{8,7},{9,8},{10,9},{11,1... | collective-permute-start | bytes 294920 | tf_op jit(solution)/shard_map/ppermute | solution.py:67
  46.6 8.5 %collective-permute-start.12 = (bf16[6,64,128]{2,1,0:T(8,128)(2,1)S(1)}, bf16[6,64,128]{2,1,0:T(8,128)(2,1)S(1)}, u32[]{:S(2)}, u32[]{:S(2)}) collective-permute-start(bf16[6,64,128]{2,1,0:T(8,128)(2,1)S(1)} %gather_fusion.8), channel_id=1, source_target_pairs={{16,0},{17,1},{18,2},{19,3},{20,4},{21,5},{22,6},{23,7},{24,8},{25... | collective-permute-start | bytes 294920 | tf_op jit(solution)/shard_map/ppermute | solution.py:67
  48.4 5.9 %collective-permute-start.11 = (bf16[6,64,128]{2,1,0:T(8,128)(2,1)S(1)}, bf16[6,64,128]{2,1,0:T(8,128)(2,1)S(1)}, u32[]{:S(2)}, u32[]{:S(2)}) collective-permute-start(bf16[6,64,128]{2,1,0:T(8,128)(2,1)S(1)} %gather_fusion.7), channel_id=1, source_target_pairs={{2,0},{3,1},{4,2},{5,3},{6,4},{7,5},{8,6},{9,7},{10,8},{11,9},{12,... | collective-permute-start | bytes 294920 | tf_op jit(solution)/shard_map/ppermute | solution.py:67
  48.4 7.2 %collective-permute-start.13 = (bf16[6,64,128]{2,1,0:T(8,128)(2,1)S(1)}, bf16[6,64,128]{2,1,0:T(8,128)(2,1)S(1)}, u32[]{:S(2)}, u32[]{:S(2)}) collective-permute-start(bf16[6,64,128]{2,1,0:T(8,128)(2,1)S(1)} %gather_fusion.9), channel_id=1, source_target_pairs={{31,0},{0,1},{1,2},{2,3},{3,4},{4,5},{5,6},{6,7},{7,8},{8,9},{9,10... | collective-permute-start | bytes 294920 | tf_op jit(solution)/shard_map/ppermute | solution.py:67
  49.6 7.3 %collective-permute-start.14 = (bf16[6,64,128]{2,1,0:T(8,128)(2,1)S(1)}, bf16[6,64,128]{2,1,0:T(8,128)(2,1)S(1)}, u32[]{:S(2)}, u32[]{:S(2)}) collective-permute-start(bf16[6,64,128]{2,1,0:T(8,128)(2,1)S(1)} %gather_fusion.10), channel_id=1, source_target_pairs={{30,0},{31,1},{0,2},{1,3},{2,4},{3,5},{4,6},{5,7},{6,8},{7,9},{8,1... | collective-permute-start | bytes 294920 | tf_op jit(solution)/shard_map/ppermute | solution.py:67
  59.7 3.3 %copy-start.2 = (bf16[24,5,128,128]{3,2,1,0:T(8,128)(2,1)S(1)}, bf16[24,5,128,128]{3,2,1,0:T(8,128)(2,1)}, u32[]{:S(2)}) copy-start(bf16[24,5,128,128]{3,2,1,0:T(8,128)(2,1)} %param.7) | copy-start | bytes 11796484
  69.0 14.1 %collective-permute-start.16 = (bf16[6,64,128]{2,1,0:T(8,128)(2,1)S(1)}, bf16[6,64,128]{2,1,0:T(8,128)(2,1)S(1)}, u32[]{:S(2)}, u32[]{:S(2)}) collective-permute-start(bf16[6,64,128]{2,1,0:T(8,128)(2,1)S(1)} %gather_fusion.13), channel_id=1, source_target_pairs={{2,0},{3,1},{4,2},{5,3},{6,4},{7,5},{8,6},{9,7},{10,8},{11,9},{12,... | collective-permute-start | bytes 294920 | tf_op jit(solution)/shard_map/ppermute | solution.py:67
  71.1 11.4 %collective-permute-start.15 = (bf16[6,64,128]{2,1,0:T(8,128)(2,1)S(1)}, bf16[6,64,128]{2,1,0:T(8,128)(2,1)S(1)}, u32[]{:S(2)}, u32[]{:S(2)}) collective-permute-start(bf16[6,64,128]{2,1,0:T(8,128)(2,1)S(1)} %gather_fusion.12), channel_id=1, source_target_pairs={{1,0},{2,1},{3,2},{4,3},{5,4},{6,5},{7,6},{8,7},{9,8},{10,9},{11,1... | collective-permute-start | bytes 294920 | tf_op jit(solution)/shard_map/ppermute | solution.py:67
  71.9 11.8 %collective-permute-start.17 = (bf16[6,64,128]{2,1,0:T(8,128)(2,1)S(1)}, bf16[6,64,128]{2,1,0:T(8,128)(2,1)S(1)}, u32[]{:S(2)}, u32[]{:S(2)}) collective-permute-start(bf16[6,64,128]{2,1,0:T(8,128)(2,1)S(1)} %gather_fusion.14), channel_id=1, source_target_pairs={{16,0},{17,1},{18,2},{19,3},{20,4},{21,5},{22,6},{23,7},{24,8},{25... | collective-permute-start | bytes 294920 | tf_op jit(solution)/shard_map/ppermute | solution.py:67
  74.9 9.5 %collective-permute-start.18 = (bf16[6,64,128]{2,1,0:T(8,128)(2,1)S(1)}, bf16[6,64,128]{2,1,0:T(8,128)(2,1)S(1)}, u32[]{:S(2)}, u32[]{:S(2)}) collective-permute-start(bf16[6,64,128]{2,1,0:T(8,128)(2,1)S(1)} %gather_fusion.15), channel_id=1, source_target_pairs={{31,0},{0,1},{1,2},{2,3},{3,4},{4,5},{5,6},{6,7},{7,8},{8,9},{9,10... | collective-permute-start | bytes 294920 | tf_op jit(solution)/shard_map/ppermute | solution.py:67
  76.0 9.0 %collective-permute-start.19 = (bf16[6,64,128]{2,1,0:T(8,128)(2,1)S(1)}, bf16[6,64,128]{2,1,0:T(8,128)(2,1)S(1)}, u32[]{:S(2)}, u32[]{:S(2)}) collective-permute-start(bf16[6,64,128]{2,1,0:T(8,128)(2,1)S(1)} %gather_fusion.16), channel_id=1, source_target_pairs={{30,0},{31,1},{0,2},{1,3},{2,4},{3,5},{4,6},{5,7},{6,8},{7,9},{8,1... | collective-permute-start | bytes 294920 | tf_op jit(solution)/shard_map/ppermute | solution.py:67
  94.9 13.3 %collective-permute-start.20 = (f32[2,4,24,128]{3,2,1,0:T(8,128)S(1)}, f32[2,4,24,128]{3,2,1,0:T(8,128)S(1)}, u32[]{:S(2)}, u32[]{:S(2)}) collective-permute-start(f32[2,4,24,128]{3,2,1,0:T(8,128)S(1)} %get-tuple-element.37), channel_id=1, source_target_pairs={{0,32},{32,64},{64,96},{96,128},{128,160},{160,192},{192,224},{224... | collective-permute-start | bytes 294920 | tf_op jit(solution)/shard_map/ppermute | solution.py:108
  103.0 6.1 %collective-permute-start.21 = (f32[2,4,24,128]{3,2,1,0:T(8,128)S(1)}, f32[2,4,24,128]{3,2,1,0:T(8,128)S(1)}, u32[]{:S(2)}, u32[]{:S(2)}) collective-permute-start(f32[2,4,24,128]{3,2,1,0:T(8,128)S(1)} %get-tuple-element.43), channel_id=1, source_target_pairs={{0,64},{32,96},{64,128},{96,160},{128,192},{160,224},{192,0},{224,... | collective-permute-start | bytes 294920 | tf_op jit(solution)/shard_map/ppermute | solution.py:108
  104.3 6.4 %collective-permute-start.22 = (f32[2,4,24,128]{3,2,1,0:T(8,128)S(1)}, f32[2,4,24,128]{3,2,1,0:T(8,128)S(1)}, u32[]{:S(2)}, u32[]{:S(2)}) collective-permute-start(f32[2,4,24,128]{3,2,1,0:T(8,128)S(1)} %get-tuple-element.42), channel_id=1, source_target_pairs={{0,96},{32,128},{64,160},{96,192},{128,224},{160,0},{192,32},{224,... | collective-permute-start | bytes 294920 | tf_op jit(solution)/shard_map/ppermute | solution.py:108
  106.0 8.3 %collective-permute-start.23 = (f32[2,4,24,128]{3,2,1,0:T(8,128)S(1)}, f32[2,4,24,128]{3,2,1,0:T(8,128)S(1)}, u32[]{:S(2)}, u32[]{:S(2)}) collective-permute-start(f32[2,4,24,128]{3,2,1,0:T(8,128)S(1)} %get-tuple-element.41), channel_id=1, source_target_pairs={{0,128},{32,160},{64,192},{96,224},{128,0},{160,32},{192,64},{224,... | collective-permute-start | bytes 294920 | tf_op jit(solution)/shard_map/ppermute | solution.py:108
  106.3 8.6 %collective-permute-start.24 = (f32[2,4,24,128]{3,2,1,0:T(8,128)S(1)}, f32[2,4,24,128]{3,2,1,0:T(8,128)S(1)}, u32[]{:S(2)}, u32[]{:S(2)}) collective-permute-start(f32[2,4,24,128]{3,2,1,0:T(8,128)S(1)} %get-tuple-element.40), channel_id=1, source_target_pairs={{0,160},{32,192},{64,224},{96,0},{128,32},{160,64},{192,96},{224,1... | collective-permute-start | bytes 294920 | tf_op jit(solution)/shard_map/ppermute | solution.py:108
  108.2 6.7 %collective-permute-start.25 = (f32[2,4,24,128]{3,2,1,0:T(8,128)S(1)}, f32[2,4,24,128]{3,2,1,0:T(8,128)S(1)}, u32[]{:S(2)}, u32[]{:S(2)}) collective-permute-start(f32[2,4,24,128]{3,2,1,0:T(8,128)S(1)} %get-tuple-element.39), channel_id=1, source_target_pairs={{0,192},{32,224},{64,0},{96,32},{128,64},{160,96},{192,128},{224,1... | collective-permute-start | bytes 294920 | tf_op jit(solution)/shard_map/ppermute | solution.py:108
  109.1 6.8 %collective-permute-start.26 = (f32[2,4,24,128]{3,2,1,0:T(8,128)S(1)}, f32[2,4,24,128]{3,2,1,0:T(8,128)S(1)}, u32[]{:S(2)}, u32[]{:S(2)}) collective-permute-start(f32[2,4,24,128]{3,2,1,0:T(8,128)S(1)} %get-tuple-element.38), channel_id=1, source_target_pairs={{0,224},{32,0},{64,32},{96,64},{128,96},{160,128},{192,160},{224,1... | collective-permute-start | bytes 294920 | tf_op jit(solution)/shard_map/ppermute | solution.py:108
  (8 other events, 11.9 us)

commit v3 on v2

--- a/solution.py
+++ b/solution.py
@@ -41,15 +41,18 @@
     flat_rel = relative.reshape(-1)
     flat_local = local_ids.reshape(-1)
     slot_flat = flat_local
+    whole_flat = flat_local
     wanted = []
     rank_range = jnp.arange(HMAX)
     for which, offset in enumerate(offsets):
         hit = flat_rel == offset
         rank = jnp.cumsum(hit.astype(jnp.int32)) - 1
         slot_flat = jnp.where(hit, dev_rows + which * HMAX + rank, slot_flat)
+        whole_flat = jnp.where(hit, (which + 1) * dev_rows + flat_local, whole_flat)
         matched = hit[None, :] & (rank[None, :] == rank_range[:, None])
         wanted.append(jnp.sum(jnp.where(matched, flat_local[None, :], 0), axis=1))
     slot_index = slot_flat.reshape(dev_rows, SLOTS)
+    whole_index = whole_flat.reshape(dev_rows, SLOTS)
 
     def to_partner(offset):
         return [(j, (j + offset) % peer_count) for j in range(peer_count)]
@@ -70,7 +73,8 @@
     e_mats = pencil_e
     a_mats = pencil_a
     cols_major = jnp.transpose(columns, (1, 0, 2))
-    rhs_full, _ = apply_pair(fetch_halo(cols_major), slot_index, e_mats, None)
+    whole = [cols_major] + [lax.ppermute(cols_major, "rows", from_partner(offset)) for offset in offsets]
+    rhs_full, _ = apply_pair(jnp.concatenate(whole, axis=0), whole_index, e_mats, None)
     node_count = lax.axis_size("node")
     angle_node = 2.0 * math.pi * (lax.axis_index("node").astype(jnp.float32) + 0.5) / node_count
     node_real = jnp.cos(angle_node)

time: 117 us -> 146 us (1.25); the launches traced: 117 us -> 144 us
  waiting for transfers between devices: 12.4 us -> 30.8 us
  starting transfers between devices: 57.2 us -> 63 us
  local copies, waits for them, and re-layouts: 29.2 us -> 31.9 us
    ppermute x5, waiting for transfers between devices: 0.01 us -> 17.2 us  [per_device(): lax.ppermute(wanted[which], 'rows', to_partner(offset))]
    ppermute x0 -> x5, starting transfers between devices: none -> 10.4 us  [per_device(): lax.ppermute(cols_major, 'rows', from_partner(offset))]
    ppermute x15 -> x10, starting transfers between devices: 29.1 us -> 21.4 us  [fetch_halo(): lax.ppermute(vector[asked_for[which]], 'rows', from_partner(offset))]
    ppermute x0 -> x5, waiting for transfers between devices: none -> 5.33 us  [per_device(): lax.ppermute(cols_major, 'rows', from_partner(offset))]
    ppermute x15 -> x10, waiting for transfers between devices: 7.15 us -> 3.05 us  [fetch_halo(): lax.ppermute(vector[asked_for[which]], 'rows', from_partner(offset))]
    ppermute x7, starting transfers between devices: 15.8 us -> 19.7 us  [per_device(): total = total + lax.ppermute(chunk, 'node', perm)]
    unnamed x42, local copies, waits for them, and re-layouts: 10.8 us -> 14.2 us
    gather x15 -> x10, local copies, waits for them, and re-layouts: 8.7 us -> 5.89 us  [fetch_halo(): vector[asked_for[which]]]
  transfers between devices with their start and end apart: 27 -> 27, of which waited for: 6 -> 10; matrix products, arithmetic and copies ran while one was open for 12% -> 12% of each run, Pallas kernels for 0% -> 0%
where the time goes in v3:
time: 146 us; the launch traced here: 144 us
  starting transfers between devices  63 us (43%)
  local copies, waits for them, and re-layouts  31.9 us (22%)
  waiting for transfers between devices  30.8 us (21%)
  matrix products  12.2 us (8%)
  other arithmetic  4.79 us (3%)
    ppermute x10, starting transfers between devices, fetch_halo(): lax.ppermute(vector[asked_for[which]], 'rows', from_partner(offset))  21.4 us
    ppermute x7, starting transfers between devices, per_device(): total = total + lax.ppermute(chunk, 'node', perm)  19.7 us
    ppermute x5, waiting for transfers between devices, per_device(): lax.ppermute(wanted[which], 'rows', to_partner(offset))  17.2 us
    unnamed x42, local copies, waits for them, and re-layouts  14.2 us
    ppermute x5, starting transfers between devices, per_device(): lax.ppermute(wanted[which], 'rows', to_partner(offset))  11.5 us
    ppermute x5, starting transfers between devices, per_device(): lax.ppermute(cols_major, 'rows', from_partner(offset))  10.4 us
    dot_general x3, matrix products, apply_pair(): jnp.einsum('nscb,nsbd->ncd', picked, first, preferred_element_type=jnp.fl...  6.97 us
    gather x3, local copies, waits for them, and re-layouts, apply_pair(): picked = extended[slot_index]  6.21 us
  transfers between devices with their start and end apart: 27, of which 10 were waited for; matrix products, arithmetic and copies ran while one was open for 12% of the time, Pallas kernels for 0%

profile of v3, /device:TPU:3, one launch (start us, length us, event | category | flops | bytes accessed | tf_op | source)
XLA Modules:
  0.0 143.6 jit_solution(8593950360888602690)
XLA Ops:
  0.0 1.1 copy.101
  1.2 7.7 %collective-permute-start.1 = (bf16[24,32,128]{2,1,0:T(8,128)(2,1)S(1)}, bf16[24,32,128]{2,1,0:T(8,128)(2,1)S(1)}, u32[]{:S(2)}, u32[]{:S(2)}) collective-permute-start(bf16[24,32,128]{2,1,0:T(8,128)(2,1)S(1)} %bitcast.175), channel_id=1, source_target_pairs={{2,0},{3,1},{4,2},{5,3},{6,4},{7,5},{8,6},{9,7},{10,8},{11,9},{12,... | collective-permute-start | bytes 589832 | tf_op jit(solution)/shard_map/ppermute | solution.py:76
  8.9 1.2 collective-permute-start.2
  10.0 1.5 %collective-permute-start.3 = (bf16[24,32,128]{2,1,0:T(8,128)(2,1)S(1)}, bf16[24,32,128]{2,1,0:T(8,128)(2,1)S(1)}, u32[]{:S(2)}, u32[]{:S(2)}) collective-permute-start(bf16[24,32,128]{2,1,0:T(8,128)(2,1)S(1)} %bitcast.177), channel_id=1, source_target_pairs={{31,0},{0,1},{1,2},{2,3},{3,4},{4,5},{5,6},{6,7},{7,8},{8,9},{9,10... | collective-permute-start | bytes 589832 | tf_op jit(solution)/shard_map/ppermute | solution.py:76
  16.9 1.5 %collective-permute-done.11 = s32[6]{0:T(128)S(1)} collective-permute-done((s32[6]{0:T(128)S(1)}, s32[6]{0:T(128)S(1)}, u32[]{:S(2)}, u32[]{:S(2)}) %collective-permute-start.11) | collective-permute-done | bytes 56 | tf_op jit(solution)/shard_map/ppermute | solution.py:64
  18.4 11.4 %collective-permute-start.13 = (s32[6]{0:T(128)S(1)}, s32[6]{0:T(128)S(1)}, u32[]{:S(2)}, u32[]{:S(2)}) collective-permute-start(s32[6]{0:T(128)S(1)} %get-tuple-element.15), channel_id=1, source_target_pairs={{0,30},{1,31},{2,0},{3,1},{4,2},{5,3},{6,4},{7,5},{8,6},{9,7},{10,... | collective-permute-start | bytes 80 | tf_op jit(solution)/shard_map/ppermute | solution.py:64
  30.5 2.4 %collective-permute-done.5 = s32[6]{0:T(128)S(1)} collective-permute-done((s32[6]{0:T(128)S(1)}, s32[6]{0:T(128)S(1)}, u32[]{:S(2)}, u32[]{:S(2)}) %collective-permute-start.5) | collective-permute-done | bytes 56 | tf_op jit(solution)/shard_map/ppermute | solution.py:64
  32.9 6.3 %collective-permute-done.7 = s32[6]{0:T(128)S(1)} collective-permute-done((s32[6]{0:T(128)S(1)}, s32[6]{0:T(128)S(1)}, u32[]{:S(2)}, u32[]{:S(2)}) %collective-permute-start.7) | collective-permute-done | bytes 56 | tf_op jit(solution)/shard_map/ppermute | solution.py:64
  39.2 6.3 %collective-permute-done.9 = s32[6]{0:T(128)S(1)} collective-permute-done((s32[6]{0:T(128)S(1)}, s32[6]{0:T(128)S(1)}, u32[]{:S(2)}, u32[]{:S(2)}) %collective-permute-start.9) | collective-permute-done | bytes 56 | tf_op jit(solution)/shard_map/ppermute | solution.py:64
  48.3 5.3 %collective-permute-done.4 = bf16[24,32,128]{2,1,0:T(8,128)(2,1)S(1)} collective-permute-done((bf16[24,32,128]{2,1,0:T(8,128)(2,1)S(1)}, bf16[24,32,128]{2,1,0:T(8,128)(2,1)S(1)}, u32[]{:S(2)}, u32[]{:S(2)}) %collective-permute-start.4) | collective-permute-done | bytes 196640 | tf_op jit(solution)/shard_map/ppermute | solution.py:76
  54.3 2.0 %gather_fusion = bf16[120,32,128]{2,1,0:T(8,128)(2,1)S(1)} fusion(bf16[144,32,128]{2,1,0:T(8,128)(2,1)} %constant_dynamic-update-slice_fusion, s32[1024]{0:T(1024)S(1)} %pad_clamp_fusion.6), kind=kCustom, calls=%fused_computation | custom fusion | bytes 1966560 | tf_op jit(solution)/shard_map/gather | solution.py:24
  56.4 2.8 %convolution_bitcast_fusion.4 = f32[24,32,128]{2,1,0:T(8,128)S(1)} fusion(bf16[24,5,32,128]{3,2,1,0:T(8,128)(2,1)S(1)} %bitcast.171, bf16[24,5,128,128]{3,2,1,0:T(8,128)(2,1)} %param.6), kind=kOutput, calls=%fused_computation.17 | convolution fusion | flops 125829120 | bytes 5308416 | tf_op jit(solution)/shard_map/nscb,nsbd->ncd/dot_general | solution.py:25
  61.9 4.6 %collective-permute-start.6 = (bf16[6,64,128]{2,1,0:T(8,128)(2,1)S(1)}, bf16[6,64,128]{2,1,0:T(8,128)(2,1)S(1)}, u32[]{:S(2)}, u32[]{:S(2)}) collective-permute-start(bf16[6,64,128]{2,1,0:T(8,128)(2,1)S(1)} %gather_fusion.1), channel_id=1, source_target_pairs={{1,0},{2,1},{3,2},{4,3},{5,4},{6,5},{7,6},{8,7},{9,8},{10,9},{11,1... | collective-permute-start | bytes 294920 | tf_op jit(solution)/shard_map/ppermute | solution.py:70
  69.3 5.1 %collective-permute-start.8 = (bf16[6,64,128]{2,1,0:T(8,128)(2,1)S(1)}, bf16[6,64,128]{2,1,0:T(8,128)(2,1)S(1)}, u32[]{:S(2)}, u32[]{:S(2)}) collective-permute-start(bf16[6,64,128]{2,1,0:T(8,128)(2,1)S(1)} %gather_fusion.2), channel_id=1, source_target_pairs={{2,0},{3,1},{4,2},{5,3},{6,4},{7,5},{8,6},{9,7},{10,8},{11,9},{12,... | collective-permute-start | bytes 294920 | tf_op jit(solution)/shard_map/ppermute | solution.py:70
  75.1 3.0 %collective-permute-done.8 = bf16[6,64,128]{2,1,0:T(8,128)(2,1)S(1)} collective-permute-done((bf16[6,64,128]{2,1,0:T(8,128)(2,1)S(1)}, bf16[6,64,128]{2,1,0:T(8,128)(2,1)S(1)}, u32[]{:S(2)}, u32[]{:S(2)}) %collective-permute-start.8) | collective-permute-done | bytes 98336 | tf_op jit(solution)/shard_map/ppermute | solution.py:70
  80.7 2.1 %gather_fusion.6 = bf16[120,64,128]{2,1,0:T(8,128)(2,1)S(1)} fusion(bf16[54,64,128]{2,1,0:T(8,128)(2,1)} %constant_dynamic-update-slice_fusion.6, s32[1024]{0:T(1024)S(1)} %pad_clamp_fusion), kind=kCustom, calls=%fused_computation.6 | custom fusion | bytes 3932640 | tf_op jit(solution)/shard_map/gather | solution.py:24
  82.8 3.2 %convolution_bitcast_fusion.3 = f32[24,64,128]{2,1,0:T(8,128)S(1)} fusion(bf16[24,5,64,128]{3,2,1,0:T(8,128)(2,1)S(1)} %bitcast.165, bf16[24,5,128,128]{3,2,1,0:T(8,128)(2,1)} %param.6), kind=kOutput, calls=%fused_computation.16 | convolution fusion | flops 251658240 | bytes 6684672 | tf_op jit(solution)/shard_map/nscb,nsbd->ncd/dot_general | solution.py:25
  87.8 1.0 copy-done.4
  92.3 3.4 %collective-permute-start.17 = (bf16[6,64,128]{2,1,0:T(8,128)(2,1)S(1)}, bf16[6,64,128]{2,1,0:T(8,128)(2,1)S(1)}, u32[]{:S(2)}, u32[]{:S(2)}) collective-permute-start(bf16[6,64,128]{2,1,0:T(8,128)(2,1)S(1)} %gather_fusion.9), channel_id=1, source_target_pairs={{16,0},{17,1},{18,2},{19,3},{20,4},{21,5},{22,6},{23,7},{24,8},{25... | collective-permute-start | bytes 294920 | tf_op jit(solution)/shard_map/ppermute | solution.py:70
  95.7 5.9 %collective-permute-start.16 = (bf16[6,64,128]{2,1,0:T(8,128)(2,1)S(1)}, bf16[6,64,128]{2,1,0:T(8,128)(2,1)S(1)}, u32[]{:S(2)}, u32[]{:S(2)}) collective-permute-start(bf16[6,64,128]{2,1,0:T(8,128)(2,1)S(1)} %gather_fusion.8), channel_id=1, source_target_pairs={{2,0},{3,1},{4,2},{5,3},{6,4},{7,5},{8,6},{9,7},{10,8},{11,9},{12,... | collective-permute-start | bytes 294920 | tf_op jit(solution)/shard_map/ppermute | solution.py:70
  101.6 1.7 %collective-permute-start.15 = (bf16[6,64,128]{2,1,0:T(8,128)(2,1)S(1)}, bf16[6,64,128]{2,1,0:T(8,128)(2,1)S(1)}, u32[]{:S(2)}, u32[]{:S(2)}) collective-permute-start(bf16[6,64,128]{2,1,0:T(8,128)(2,1)S(1)} %gather_fusion.7), channel_id=1, source_target_pairs={{1,0},{2,1},{3,2},{4,3},{5,4},{6,5},{7,6},{8,7},{9,8},{10,9},{11,1... | collective-permute-start | bytes 294920 | tf_op jit(solution)/shard_map/ppermute | solution.py:70
  103.3 1.4 copy.68
  108.6 2.1 %gather_fusion.12 = bf16[120,64,128]{2,1,0:T(8,128)(2,1)S(1)} fusion(bf16[54,64,128]{2,1,0:T(8,128)(2,1)} %constant_dynamic-update-slice_fusion.12, s32[1024]{0:T(1024)S(1)} %pad_clamp_fusion), kind=kCustom, calls=%fused_computation.12 | custom fusion | bytes 3932640 | tf_op jit(solution)/shard_map/gather | solution.py:24
  110.7 3.2 %convolution_bitcast_fusion = f32[24,64,128]{2,1,0:T(8,128)S(1)} fusion(bf16[24,5,64,128]{3,2,1,0:T(8,128)(2,1)S(1)} %bitcast.163, bf16[24,5,128,128]{3,2,1,0:T(8,128)(2,1)} %param.7), kind=kOutput, calls=%fused_computation.13 | convolution fusion | flops 251658240 | bytes 6684672 | tf_op jit(solution)/shard_map/nscb,nsbd->ncd/dot_general | solution.py:28
  114.0 0.9 convolution_bitcast_fusion.1
  117.9 12.0 %collective-permute-start.20 = (f32[2,4,24,128]{3,2,1,0:T(8,128)S(1)}, f32[2,4,24,128]{3,2,1,0:T(8,128)S(1)}, u32[]{:S(2)}, u32[]{:S(2)}) collective-permute-start(f32[2,4,24,128]{3,2,1,0:T(8,128)S(1)} %get-tuple-element.37), channel_id=1, source_target_pairs={{0,32},{32,64},{64,96},{96,128},{128,160},{160,192},{192,224},{224... | collective-permute-start | bytes 294920 | tf_op jit(solution)/shard_map/ppermute | solution.py:112
  129.9 1.3 collective-permute-start.21
  131.2 1.7 %collective-permute-start.22 = (f32[2,4,24,128]{3,2,1,0:T(8,128)S(1)}, f32[2,4,24,128]{3,2,1,0:T(8,128)S(1)}, u32[]{:S(2)}, u32[]{:S(2)}) collective-permute-start(f32[2,4,24,128]{3,2,1,0:T(8,128)S(1)} %get-tuple-element.42), channel_id=1, source_target_pairs={{0,96},{32,128},{64,160},{96,192},{128,224},{160,0},{192,32},{224,... | collective-permute-start | bytes 294920 | tf_op jit(solution)/shard_map/ppermute | solution.py:112
  133.3 1.9 %collective-permute-start.24 = (f32[2,4,24,128]{3,2,1,0:T(8,128)S(1)}, f32[2,4,24,128]{3,2,1,0:T(8,128)S(1)}, u32[]{:S(2)}, u32[]{:S(2)}) collective-permute-start(f32[2,4,24,128]{3,2,1,0:T(8,128)S(1)} %get-tuple-element.40), channel_id=1, source_target_pairs={{0,160},{32,192},{64,224},{96,0},{128,32},{160,64},{192,96},{224,1... | collective-permute-start | bytes 294920 | tf_op jit(solution)/shard_map/ppermute | solution.py:112
  136.0 1.6 %collective-permute-start.26 = (f32[2,4,24,128]{3,2,1,0:T(8,128)S(1)}, f32[2,4,24,128]{3,2,1,0:T(8,128)S(1)}, u32[]{:S(2)}, u32[]{:S(2)}) collective-permute-start(f32[2,4,24,128]{3,2,1,0:T(8,128)S(1)} %get-tuple-element.38), channel_id=1, source_target_pairs={{0,224},{32,0},{64,32},{96,64},{128,96},{160,128},{192,160},{224,1... | collective-permute-start | bytes 294920 | tf_op jit(solution)/shard_map/ppermute | solution.py:112
  137.6 3.6 %collective-permute-done.23 = f32[2,4,24,128]{3,2,1,0:T(8,128)S(1)} collective-permute-done((f32[2,4,24,128]{3,2,1,0:T(8,128)S(1)}, f32[2,4,24,128]{3,2,1,0:T(8,128)S(1)}, u32[]{:S(2)}, u32[]{:S(2)}) %collective-permute-start.23) | collective-permute-done | bytes 98336 | tf_op jit(solution)/shard_map/ppermute | solution.py:112
  141.9 1.0 collective-permute-done.26
  (145 shorter events, 32.4 us)
Async XLA Ops:
  0.0 59.2 %copy-start = (bf16[1,2,24,128,128]{4,3,2,1,0:T(8,128)(2,1)S(1)}, bf16[1,2,24,128,128]{4,3,2,1,0:T(8,128)(2,1)}, u32[]{:S(2)}) copy-start(bf16[1,2,24,128,128]{4,3,2,1,0:T(8,128)(2,1)} %param.8) | copy-start | bytes 4718596
  0.0 15.7 %copy-start.10 = (bf16[32,24,128]{2,1,0:T(8,128)(2,1)S(1)}, bf16[32,24,128]{2,1,0:T(8,128)(2,1)}, u32[]{:S(2)}) copy-start(bf16[32,24,128]{2,1,0:T(8,128)(2,1)} %param.5) | copy-start | bytes 589828
  1.1 44.5 %collective-permute-start = (bf16[24,32,128]{2,1,0:T(8,128)(2,1)S(1)}, bf16[24,32,128]{2,1,0:T(8,128)(2,1)S(1)}, u32[]{:S(2)}, u32[]{:S(2)}) collective-permute-start(bf16[24,32,128]{2,1,0:T(8,128)(2,1)S(1)} %bitcast.174), channel_id=1, source_target_pairs={{1,0},{2,1},{3,2},{4,3},{5,4},{6,5},{7,6},{8,7},{9,8},{10,9},{11,1... | collective-permute-start | bytes 589832 | tf_op jit(solution)/shard_map/ppermute | solution.py:76
  1.2 45.1 %collective-permute-start.1 = (bf16[24,32,128]{2,1,0:T(8,128)(2,1)S(1)}, bf16[24,32,128]{2,1,0:T(8,128)(2,1)S(1)}, u32[]{:S(2)}, u32[]{:S(2)}) collective-permute-start(bf16[24,32,128]{2,1,0:T(8,128)(2,1)S(1)} %bitcast.175), channel_id=1, source_target_pairs={{2,0},{3,1},{4,2},{5,3},{6,4},{7,5},{8,6},{9,7},{10,8},{11,9},{12,... | collective-permute-start | bytes 589832 | tf_op jit(solution)/shard_map/ppermute | solution.py:76
  8.9 38.1 %collective-permute-start.2 = (bf16[24,32,128]{2,1,0:T(8,128)(2,1)S(1)}, bf16[24,32,128]{2,1,0:T(8,128)(2,1)S(1)}, u32[]{:S(2)}, u32[]{:S(2)}) collective-permute-start(bf16[24,32,128]{2,1,0:T(8,128)(2,1)S(1)} %bitcast.176), channel_id=1, source_target_pairs={{16,0},{17,1},{18,2},{19,3},{20,4},{21,5},{22,6},{23,7},{24,8},{25... | collective-permute-start | bytes 589832 | tf_op jit(solution)/shard_map/ppermute | solution.py:76
  10.0 37.6 %collective-permute-start.3 = (bf16[24,32,128]{2,1,0:T(8,128)(2,1)S(1)}, bf16[24,32,128]{2,1,0:T(8,128)(2,1)S(1)}, u32[]{:S(2)}, u32[]{:S(2)}) collective-permute-start(bf16[24,32,128]{2,1,0:T(8,128)(2,1)S(1)} %bitcast.177), channel_id=1, source_target_pairs={{31,0},{0,1},{1,2},{2,3},{3,4},{4,5},{5,6},{6,7},{7,8},{8,9},{9,10... | collective-permute-start | bytes 589832 | tf_op jit(solution)/shard_map/ppermute | solution.py:76
  15.6 2.8 %collective-permute-start.11 = (s32[6]{0:T(128)S(1)}, s32[6]{0:T(128)S(1)}, u32[]{:S(2)}, u32[]{:S(2)}) collective-permute-start(s32[6]{0:T(128)S(1)} %get-tuple-element.18), channel_id=1, source_target_pairs={{0,31},{1,0},{2,1},{3,2},{4,3},{5,4},{6,5},{7,6},{8,7},{9,8},{10,9... | collective-permute-start | bytes 80 | tf_op jit(solution)/shard_map/ppermute | solution.py:64
  18.4 12.1 %collective-permute-start.13 = (s32[6]{0:T(128)S(1)}, s32[6]{0:T(128)S(1)}, u32[]{:S(2)}, u32[]{:S(2)}) collective-permute-start(s32[6]{0:T(128)S(1)} %get-tuple-element.15), channel_id=1, source_target_pairs={{0,30},{1,31},{2,0},{3,1},{4,2},{5,3},{6,4},{7,5},{8,6},{9,7},{10,... | collective-permute-start | bytes 80 | tf_op jit(solution)/shard_map/ppermute | solution.py:64
  30.5 2.4 %collective-permute-start.5 = (s32[6]{0:T(128)S(1)}, s32[6]{0:T(128)S(1)}, u32[]{:S(2)}, u32[]{:S(2)}) collective-permute-start(s32[6]{0:T(128)S(1)} %get-tuple-element.19), channel_id=1, source_target_pairs={{0,1},{1,2},{2,3},{3,4},{4,5},{5,6},{6,7},{7,8},{8,9},{9,10},{10,1... | collective-permute-start | bytes 80 | tf_op jit(solution)/shard_map/ppermute | solution.py:64
  32.9 6.3 %collective-permute-start.7 = (s32[6]{0:T(128)S(1)}, s32[6]{0:T(128)S(1)}, u32[]{:S(2)}, u32[]{:S(2)}) collective-permute-start(s32[6]{0:T(128)S(1)} %get-tuple-element.16), channel_id=1, source_target_pairs={{0,2},{1,3},{2,4},{3,5},{4,6},{5,7},{6,8},{7,9},{8,10},{9,11},{10,... | collective-permute-start | bytes 80 | tf_op jit(solution)/shard_map/ppermute | solution.py:64
  39.2 6.3 %collective-permute-start.9 = (s32[6]{0:T(128)S(1)}, s32[6]{0:T(128)S(1)}, u32[]{:S(2)}, u32[]{:S(2)}) collective-permute-start(s32[6]{0:T(128)S(1)} %get-tuple-element.17), channel_id=1, source_target_pairs={{0,16},{1,17},{2,18},{3,19},{4,20},{5,21},{6,22},{7,23},{8,24},{9,... | collective-permute-start | bytes 80 | tf_op jit(solution)/shard_map/ppermute | solution.py:64
  45.5 8.1 %collective-permute-start.4 = (bf16[24,32,128]{2,1,0:T(8,128)(2,1)S(1)}, bf16[24,32,128]{2,1,0:T(8,128)(2,1)S(1)}, u32[]{:S(2)}, u32[]{:S(2)}) collective-permute-start(bf16[24,32,128]{2,1,0:T(8,128)(2,1)S(1)} %bitcast.178), channel_id=1, source_target_pairs={{30,0},{31,1},{0,2},{1,3},{2,4},{3,5},{4,6},{5,7},{6,8},{7,9},{8,1... | collective-permute-start | bytes 589832 | tf_op jit(solution)/shard_map/ppermute | solution.py:76
  45.5 22.5 %copy-start.11 = (s32[1024]{0:T(1024)}, s32[1024]{0:T(1024)S(1)}, u32[]{:S(2)}) copy-start(s32[1024]{0:T(1024)S(1)} %pad_clamp_fusion.3) | copy-start | bytes 12292
  61.9 12.5 %collective-permute-start.6 = (bf16[6,64,128]{2,1,0:T(8,128)(2,1)S(1)}, bf16[6,64,128]{2,1,0:T(8,128)(2,1)S(1)}, u32[]{:S(2)}, u32[]{:S(2)}) collective-permute-start(bf16[6,64,128]{2,1,0:T(8,128)(2,1)S(1)} %gather_fusion.1), channel_id=1, source_target_pairs={{1,0},{2,1},{3,2},{4,3},{5,4},{6,5},{7,6},{8,7},{9,8},{10,9},{11,1... | collective-permute-start | bytes 294920 | tf_op jit(solution)/shard_map/ppermute | solution.py:70
  67.1 12.9 %collective-permute-start.14 = (bf16[6,64,128]{2,1,0:T(8,128)(2,1)S(1)}, bf16[6,64,128]{2,1,0:T(8,128)(2,1)S(1)}, u32[]{:S(2)}, u32[]{:S(2)}) collective-permute-start(bf16[6,64,128]{2,1,0:T(8,128)(2,1)S(1)} %gather_fusion.5), channel_id=1, source_target_pairs={{30,0},{31,1},{0,2},{1,3},{2,4},{3,5},{4,6},{5,7},{6,8},{7,9},{8,1... | collective-permute-start | bytes 294920 | tf_op jit(solution)/shard_map/ppermute | solution.py:70
  67.7 11.6 %collective-permute-start.12 = (bf16[6,64,128]{2,1,0:T(8,128)(2,1)S(1)}, bf16[6,64,128]{2,1,0:T(8,128)(2,1)S(1)}, u32[]{:S(2)}, u32[]{:S(2)}) collective-permute-start(bf16[6,64,128]{2,1,0:T(8,128)(2,1)S(1)} %gather_fusion.4), channel_id=1, source_target_pairs={{31,0},{0,1},{1,2},{2,3},{3,4},{4,5},{5,6},{6,7},{7,8},{8,9},{9,10... | collective-permute-start | bytes 294920 | tf_op jit(solution)/shard_map/ppermute | solution.py:70
  68.6 10.1 %collective-permute-start.10 = (bf16[6,64,128]{2,1,0:T(8,128)(2,1)S(1)}, bf16[6,64,128]{2,1,0:T(8,128)(2,1)S(1)}, u32[]{:S(2)}, u32[]{:S(2)}) collective-permute-start(bf16[6,64,128]{2,1,0:T(8,128)(2,1)S(1)} %gather_fusion.3), channel_id=1, source_target_pairs={{16,0},{17,1},{18,2},{19,3},{20,4},{21,5},{22,6},{23,7},{24,8},{25... | collective-permute-start | bytes 294920 | tf_op jit(solution)/shard_map/ppermute | solution.py:70
  69.3 8.8 %collective-permute-start.8 = (bf16[6,64,128]{2,1,0:T(8,128)(2,1)S(1)}, bf16[6,64,128]{2,1,0:T(8,128)(2,1)S(1)}, u32[]{:S(2)}, u32[]{:S(2)}) collective-permute-start(bf16[6,64,128]{2,1,0:T(8,128)(2,1)S(1)} %gather_fusion.2), channel_id=1, source_target_pairs={{2,0},{3,1},{4,2},{5,3},{6,4},{7,5},{8,6},{9,7},{10,8},{11,9},{12,... | collective-permute-start | bytes 294920 | tf_op jit(solution)/shard_map/ppermute | solution.py:70
  82.7 3.3 %copy-start.2 = (bf16[24,5,128,128]{3,2,1,0:T(8,128)(2,1)S(1)}, bf16[24,5,128,128]{3,2,1,0:T(8,128)(2,1)}, u32[]{:S(2)}) copy-start(bf16[24,5,128,128]{3,2,1,0:T(8,128)(2,1)} %param.7) | copy-start | bytes 11796484
  92.1 15.9 %collective-permute-start.19 = (bf16[6,64,128]{2,1,0:T(8,128)(2,1)S(1)}, bf16[6,64,128]{2,1,0:T(8,128)(2,1)S(1)}, u32[]{:S(2)}, u32[]{:S(2)}) collective-permute-start(bf16[6,64,128]{2,1,0:T(8,128)(2,1)S(1)} %gather_fusion.11), channel_id=1, source_target_pairs={{30,0},{31,1},{0,2},{1,3},{2,4},{3,5},{4,6},{5,7},{6,8},{7,9},{8,1... | collective-permute-start | bytes 294920 | tf_op jit(solution)/shard_map/ppermute | solution.py:70
  92.2 15.2 %collective-permute-start.18 = (bf16[6,64,128]{2,1,0:T(8,128)(2,1)S(1)}, bf16[6,64,128]{2,1,0:T(8,128)(2,1)S(1)}, u32[]{:S(2)}, u32[]{:S(2)}) collective-permute-start(bf16[6,64,128]{2,1,0:T(8,128)(2,1)S(1)} %gather_fusion.10), channel_id=1, source_target_pairs={{31,0},{0,1},{1,2},{2,3},{3,4},{4,5},{5,6},{6,7},{7,8},{8,9},{9,10... | collective-permute-start | bytes 294920 | tf_op jit(solution)/shard_map/ppermute | solution.py:70
  92.3 14.4 %collective-permute-start.17 = (bf16[6,64,128]{2,1,0:T(8,128)(2,1)S(1)}, bf16[6,64,128]{2,1,0:T(8,128)(2,1)S(1)}, u32[]{:S(2)}, u32[]{:S(2)}) collective-permute-start(bf16[6,64,128]{2,1,0:T(8,128)(2,1)S(1)} %gather_fusion.9), channel_id=1, source_target_pairs={{16,0},{17,1},{18,2},{19,3},{20,4},{21,5},{22,6},{23,7},{24,8},{25... | collective-permute-start | bytes 294920 | tf_op jit(solution)/shard_map/ppermute | solution.py:70
  95.7 10.4 %collective-permute-start.16 = (bf16[6,64,128]{2,1,0:T(8,128)(2,1)S(1)}, bf16[6,64,128]{2,1,0:T(8,128)(2,1)S(1)}, u32[]{:S(2)}, u32[]{:S(2)}) collective-permute-start(bf16[6,64,128]{2,1,0:T(8,128)(2,1)S(1)} %gather_fusion.8), channel_id=1, source_target_pairs={{2,0},{3,1},{4,2},{5,3},{6,4},{7,5},{8,6},{9,7},{10,8},{11,9},{12,... | collective-permute-start | bytes 294920 | tf_op jit(solution)/shard_map/ppermute | solution.py:70
  101.6 3.8 %collective-permute-start.15 = (bf16[6,64,128]{2,1,0:T(8,128)(2,1)S(1)}, bf16[6,64,128]{2,1,0:T(8,128)(2,1)S(1)}, u32[]{:S(2)}, u32[]{:S(2)}) collective-permute-start(bf16[6,64,128]{2,1,0:T(8,128)(2,1)S(1)} %gather_fusion.7), channel_id=1, source_target_pairs={{1,0},{2,1},{3,2},{4,3},{5,4},{6,5},{7,6},{8,7},{9,8},{10,9},{11,1... | collective-permute-start | bytes 294920 | tf_op jit(solution)/shard_map/ppermute | solution.py:70
  110.7 3.3 %copy-start.1 = (bf16[24,5,128,128]{3,2,1,0:T(8,128)(2,1)S(1)}, bf16[24,5,128,128]{3,2,1,0:T(8,128)(2,1)}, u32[]{:S(2)}) copy-start(bf16[24,5,128,128]{3,2,1,0:T(8,128)(2,1)} %param.6) | copy-start | bytes 11796484
  117.9 17.3 %collective-permute-start.20 = (f32[2,4,24,128]{3,2,1,0:T(8,128)S(1)}, f32[2,4,24,128]{3,2,1,0:T(8,128)S(1)}, u32[]{:S(2)}, u32[]{:S(2)}) collective-permute-start(f32[2,4,24,128]{3,2,1,0:T(8,128)S(1)} %get-tuple-element.37), channel_id=1, source_target_pairs={{0,32},{32,64},{64,96},{96,128},{128,160},{160,192},{192,224},{224... | collective-permute-start | bytes 294920 | tf_op jit(solution)/shard_map/ppermute | solution.py:112
  129.9 6.1 %collective-permute-start.21 = (f32[2,4,24,128]{3,2,1,0:T(8,128)S(1)}, f32[2,4,24,128]{3,2,1,0:T(8,128)S(1)}, u32[]{:S(2)}, u32[]{:S(2)}) collective-permute-start(f32[2,4,24,128]{3,2,1,0:T(8,128)S(1)} %get-tuple-element.43), channel_id=1, source_target_pairs={{0,64},{32,96},{64,128},{96,160},{128,192},{160,224},{192,0},{224,... | collective-permute-start | bytes 294920 | tf_op jit(solution)/shard_map/ppermute | solution.py:112
  131.2 6.4 %collective-permute-start.22 = (f32[2,4,24,128]{3,2,1,0:T(8,128)S(1)}, f32[2,4,24,128]{3,2,1,0:T(8,128)S(1)}, u32[]{:S(2)}, u32[]{:S(2)}) collective-permute-start(f32[2,4,24,128]{3,2,1,0:T(8,128)S(1)} %get-tuple-element.42), channel_id=1, source_target_pairs={{0,96},{32,128},{64,160},{96,192},{128,224},{160,0},{192,32},{224,... | collective-permute-start | bytes 294920 | tf_op jit(solution)/shard_map/ppermute | solution.py:112
  132.9 8.3 %collective-permute-start.23 = (f32[2,4,24,128]{3,2,1,0:T(8,128)S(1)}, f32[2,4,24,128]{3,2,1,0:T(8,128)S(1)}, u32[]{:S(2)}, u32[]{:S(2)}) collective-permute-start(f32[2,4,24,128]{3,2,1,0:T(8,128)S(1)} %get-tuple-element.41), channel_id=1, source_target_pairs={{0,128},{32,160},{64,192},{96,224},{128,0},{160,32},{192,64},{224,... | collective-permute-start | bytes 294920 | tf_op jit(solution)/shard_map/ppermute | solution.py:112
  133.3 8.7 %collective-permute-start.24 = (f32[2,4,24,128]{3,2,1,0:T(8,128)S(1)}, f32[2,4,24,128]{3,2,1,0:T(8,128)S(1)}, u32[]{:S(2)}, u32[]{:S(2)}) collective-permute-start(f32[2,4,24,128]{3,2,1,0:T(8,128)S(1)} %get-tuple-element.40), channel_id=1, source_target_pairs={{0,160},{32,192},{64,224},{96,0},{128,32},{160,64},{192,96},{224,1... | collective-permute-start | bytes 294920 | tf_op jit(solution)/shard_map/ppermute | solution.py:112
  135.2 6.7 %collective-permute-start.25 = (f32[2,4,24,128]{3,2,1,0:T(8,128)S(1)}, f32[2,4,24,128]{3,2,1,0:T(8,128)S(1)}, u32[]{:S(2)}, u32[]{:S(2)}) collective-permute-start(f32[2,4,24,128]{3,2,1,0:T(8,128)S(1)} %get-tuple-element.39), channel_id=1, source_target_pairs={{0,192},{32,224},{64,0},{96,32},{128,64},{160,96},{192,128},{224,1... | collective-permute-start | bytes 294920 | tf_op jit(solution)/shard_map/ppermute | solution.py:112
  136.0 6.8 %collective-permute-start.26 = (f32[2,4,24,128]{3,2,1,0:T(8,128)S(1)}, f32[2,4,24,128]{3,2,1,0:T(8,128)S(1)}, u32[]{:S(2)}, u32[]{:S(2)}) collective-permute-start(f32[2,4,24,128]{3,2,1,0:T(8,128)S(1)} %get-tuple-element.38), channel_id=1, source_target_pairs={{0,224},{32,0},{64,32},{96,64},{128,96},{160,128},{192,160},{224,1... | collective-permute-start | bytes 294920 | tf_op jit(solution)/shard_map/ppermute | solution.py:112
  (8 other events, 10.8 us)

commit v4 on v3

--- a/solution.py
+++ b/solution.py
@@ -60,10 +60,6 @@
     def from_partner(offset):
         return [((j + offset) % peer_count, j) for j in range(peer_count)]
 
-    asked_for = [
-        lax.ppermute(wanted[which], "rows", to_partner(offset)) for which, offset in enumerate(offsets)
-    ]
-
     def fetch_halo(vector):
         pieces = [vector]
         for which, offset in enumerate(offsets):
@@ -73,7 +69,15 @@
     e_mats = pencil_e
     a_mats = pencil_a
     cols_major = jnp.transpose(columns, (1, 0, 2))
-    whole = [cols_major] + [lax.ppermute(cols_major, "rows", from_partner(offset)) for offset in offsets]
+    whole = [cols_major]
+    asked_for = [None] * len(offsets)
+    for which, offset in enumerate(offsets):
+        back = offsets.index((-offset) % peer_count)
+        tag = jnp.zeros((1,) + cols_major.shape[1:], cols_major.dtype)
+        tag = tag.at[0, 0, :HMAX].set(wanted[back].astype(cols_major.dtype))
+        got = lax.ppermute(jnp.concatenate([cols_major, tag], axis=0), "rows", from_partner(offset))
+        whole.append(got[:dev_rows])
+        asked_for[back] = got[dev_rows, 0, :HMAX].astype(jnp.int32)
     rhs_full, _ = apply_pair(jnp.concatenate(whole, axis=0), whole_index, e_mats, None)
     node_count = lax.axis_size("node")
     angle_node = 2.0 * math.pi * (lax.axis_index("node").astype(jnp.float32) + 0.5) / node_count

time: 146 us -> 122 us (0.84)
  starting transfers between devices: 63 us -> 46 us
  waiting for transfers between devices: 30.8 us -> 22.2 us
  other arithmetic: 4.79 us -> 6.34 us
    ppermute x10 -> x5, waiting for transfers between devices: 22.5 us -> 10.4 us  [per_device(): lax.ppermute(jnp.concatenate([cols_major, tag], axis=0), 'rows', from_par...]
    ppermute x10 -> x5, starting transfers between devices: 22 us -> 12.9 us  [per_device(): lax.ppermute(jnp.concatenate([cols_major, tag], axis=0), 'rows', from_par...]
    ppermute x7, starting transfers between devices: 19.7 us -> 14.9 us  [per_device(): total = total + lax.ppermute(chunk, 'node', perm)]
    ppermute x10, waiting for transfers between devices: 3.05 us -> 6.57 us  [fetch_halo(): lax.ppermute(vector[asked_for[which]], 'rows', from_partner(offset))]
    ppermute x10, starting transfers between devices: 21.4 us -> 18.2 us  [fetch_halo(): lax.ppermute(vector[asked_for[which]], 'rows', from_partner(offset))]
  transfers between devices with their start and end apart: 27 -> 22, of which waited for: 10 -> 10; matrix products, arithmetic and copies ran while one was open for 12% -> 13% of each run, Pallas kernels for 0% -> 0%
where the time goes in v4:
time: 122 us; the launch traced here: 120 us
  starting transfers between devices  46 us (38%)
  local copies, waits for them, and re-layouts  32.8 us (27%)
  waiting for transfers between devices  22.2 us (18%)
  matrix products  12.2 us (10%)
  other arithmetic  6.34 us (5%)
    ppermute x10, starting transfers between devices, fetch_halo(): lax.ppermute(vector[asked_for[which]], 'rows', from_partner(offset))  18.2 us
    unnamed x42, local copies, waits for them, and re-layouts  15.1 us
    ppermute x7, starting transfers between devices, per_device(): total = total + lax.ppermute(chunk, 'node', perm)  14.9 us
    ppermute x5, starting transfers between devices, per_device(): lax.ppermute(jnp.concatenate([cols_major, tag], axis=0), 'rows', from_par...  12.9 us
    ppermute x5, waiting for transfers between devices, per_device(): lax.ppermute(jnp.concatenate([cols_major, tag], axis=0), 'rows', from_par...  10.4 us
    dot_general x3, matrix products, apply_pair(): jnp.einsum('nscb,nsbd->ncd', picked, first, preferred_element_type=jnp.fl...  6.97 us
    ppermute x10, waiting for transfers between devices, fetch_halo(): lax.ppermute(vector[asked_for[which]], 'rows', from_partner(offset))  6.57 us
    gather x3, local copies, waits for them, and re-layouts, apply_pair(): picked = extended[slot_index]  6.21 us
  transfers between devices with their start and end apart: 22, of which 10 were waited for; matrix products, arithmetic and copies ran while one was open for 13% of the time, Pallas kernels for 0%

profile of v4, /device:TPU:3, one launch (start us, length us, event | category | flops | bytes accessed | tf_op | source)
XLA Modules:
  0.0 120.4 jit_solution(2049394300543538910)
XLA Ops:
  0.0 0.9 copy.58
  4.5 7.7 %collective-permute-start.1 = (bf16[25,32,128]{2,1,0:T(8,128)(2,1)S(1)}, bf16[25,32,128]{2,1,0:T(8,128)(2,1)}, u32[]{:S(2)}, u32[]{:S(2)}) collective-permute-start(bf16[25,32,128]{2,1,0:T(8,128)(2,1)S(1)} %get-tuple-element.106), channel_id=1, source_target_pairs={{2,0},{3,1},{4,2},{5,3},{6,4},{7,5},{8,6},{9,7},{10,8},{11,9},{12,... | collective-permute-start | bytes 614408 | tf_op jit(solution)/shard_map/ppermute | solution.py:78
  12.2 1.2 collective-permute-start.2
  13.4 1.5 %collective-permute-start.3 = (bf16[25,32,128]{2,1,0:T(8,128)(2,1)S(1)}, bf16[25,32,128]{2,1,0:T(8,128)(2,1)S(1)}, u32[]{:S(2)}, u32[]{:S(2)}) collective-permute-start(bf16[25,32,128]{2,1,0:T(8,128)(2,1)S(1)} %get-tuple-element.105), channel_id=1, source_target_pairs={{31,0},{0,1},{1,2},{2,3},{3,4},{4,5},{5,6},{6,7},{7,8},{8,9},{9,10... | collective-permute-start | bytes 614408 | tf_op jit(solution)/shard_map/ppermute | solution.py:78
  14.9 2.5 %collective-permute-start.4 = (bf16[25,32,128]{2,1,0:T(8,128)(2,1)S(1)}, bf16[25,32,128]{2,1,0:T(8,128)(2,1)S(1)}, u32[]{:S(2)}, u32[]{:S(2)}) collective-permute-start(bf16[25,32,128]{2,1,0:T(8,128)(2,1)S(1)} %get-tuple-element.103), channel_id=1, source_target_pairs={{30,0},{31,1},{0,2},{1,3},{2,4},{3,5},{4,6},{5,7},{6,8},{7,9},{8,1... | collective-permute-start | bytes 614408 | tf_op jit(solution)/shard_map/ppermute | solution.py:78
  19.3 5.1 %collective-permute-done.1 = bf16[25,32,128]{2,1,0:T(8,128)(2,1)} collective-permute-done((bf16[25,32,128]{2,1,0:T(8,128)(2,1)S(1)}, bf16[25,32,128]{2,1,0:T(8,128)(2,1)}, u32[]{:S(2)}, u32[]{:S(2)}) %collective-permute-start.1) | collective-permute-done | bytes 204832 | tf_op jit(solution)/shard_map/ppermute | solution.py:78
  24.4 1.6 %slice_dynamic-update-slice_fusion.3 = bf16[144,32,128]{2,1,0:T(8,128)(2,1)} fusion(bf16[144,32,128]{2,1,0:T(8,128)(2,1)} %slice_dynamic-update-slice_fusion.4, bf16[25,32,128]{2,1,0:T(8,128)(2,1)} %collective-permute-done.1), kind=kLoop, calls=%fused_computation.80 | loop fusion | bytes 393216
  26.5 1.6 %slice_dynamic-update-slice_fusion.2 = bf16[144,32,128]{2,1,0:T(8,128)(2,1)} fusion(bf16[144,32,128]{2,1,0:T(8,128)(2,1)} %slice_dynamic-update-slice_fusion.3, bf16[25,32,128]{2,1,0:T(8,128)(2,1)} %collective-permute-done.2), kind=kLoop, calls=%fused_computation.79 | loop fusion | bytes 393216
  28.8 4.8 %collective-permute-done.4 = bf16[25,32,128]{2,1,0:T(8,128)(2,1)S(1)} collective-permute-done((bf16[25,32,128]{2,1,0:T(8,128)(2,1)S(1)}, bf16[25,32,128]{2,1,0:T(8,128)(2,1)S(1)}, u32[]{:S(2)}, u32[]{:S(2)}) %collective-permute-start.4) | collective-permute-done | bytes 204832 | tf_op jit(solution)/shard_map/ppermute | solution.py:78
  34.2 2.0 %gather_fusion = bf16[120,32,128]{2,1,0:T(8,128)(2,1)S(1)} fusion(bf16[144,32,128]{2,1,0:T(8,128)(2,1)} %slice_dynamic-update-slice_fusion, s32[1024]{0:T(1024)S(1)} %pad_clamp_fusion.6), kind=kCustom, calls=%fused_computation | custom fusion | bytes 1966560 | tf_op jit(solution)/shard_map/gather | solution.py:24
  36.3 2.8 %convolution_bitcast_fusion.4 = f32[24,32,128]{2,1,0:T(8,128)S(1)} fusion(bf16[24,5,32,128]{3,2,1,0:T(8,128)(2,1)S(1)} %bitcast.226, bf16[24,5,128,128]{3,2,1,0:T(8,128)(2,1)} %param.16), kind=kOutput, calls=%fused_computation.17 | convolution fusion | flops 125829120 | bytes 5308416 | tf_op jit(solution)/shard_map/nscb,nsbd->ncd/dot_general | solution.py:25
  43.2 4.2 %collective-permute-start.7 = (bf16[6,64,128]{2,1,0:T(8,128)(2,1)S(1)}, bf16[6,64,128]{2,1,0:T(8,128)(2,1)S(1)}, u32[]{:S(2)}, u32[]{:S(2)}) collective-permute-start(bf16[6,64,128]{2,1,0:T(8,128)(2,1)S(1)} %gather_fusion.3), channel_id=1, source_target_pairs={{16,0},{17,1},{18,2},{19,3},{20,4},{21,5},{22,6},{23,7},{24,8},{25... | collective-permute-start | bytes 294920 | tf_op jit(solution)/shard_map/ppermute | solution.py:66
  47.9 3.5 %collective-permute-start.6 = (bf16[6,64,128]{2,1,0:T(8,128)(2,1)S(1)}, bf16[6,64,128]{2,1,0:T(8,128)(2,1)S(1)}, u32[]{:S(2)}, u32[]{:S(2)}) collective-permute-start(bf16[6,64,128]{2,1,0:T(8,128)(2,1)S(1)} %gather_fusion.2), channel_id=1, source_target_pairs={{2,0},{3,1},{4,2},{5,3},{6,4},{7,5},{8,6},{9,7},{10,8},{11,9},{12,... | collective-permute-start | bytes 294920 | tf_op jit(solution)/shard_map/ppermute | solution.py:66
  54.0 1.8 %collective-permute-done.5 = bf16[6,64,128]{2,1,0:T(8,128)(2,1)S(1)} collective-permute-done((bf16[6,64,128]{2,1,0:T(8,128)(2,1)S(1)}, bf16[6,64,128]{2,1,0:T(8,128)(2,1)S(1)}, u32[]{:S(2)}, u32[]{:S(2)}) %collective-permute-start.5) | collective-permute-done | bytes 98336 | tf_op jit(solution)/shard_map/ppermute | solution.py:66
  58.4 2.3 %collective-permute-done.9 = bf16[6,64,128]{2,1,0:T(8,128)(2,1)S(1)} collective-permute-done((bf16[6,64,128]{2,1,0:T(8,128)(2,1)S(1)}, bf16[6,64,128]{2,1,0:T(8,128)(2,1)S(1)}, u32[]{:S(2)}, u32[]{:S(2)}) %collective-permute-start.9) | collective-permute-done | bytes 98336 | tf_op jit(solution)/shard_map/ppermute | solution.py:66
  61.4 2.1 %gather_fusion.6 = bf16[120,64,128]{2,1,0:T(8,128)(2,1)S(1)} fusion(bf16[54,64,128]{2,1,0:T(8,128)(2,1)} %constant_dynamic-update-slice_fusion.1, s32[1024]{0:T(1024)S(1)} %pad_clamp_fusion), kind=kCustom, calls=%fused_computation.6 | custom fusion | bytes 3932640 | tf_op jit(solution)/shard_map/gather | solution.py:24
  63.5 3.2 %convolution_bitcast_fusion.3 = f32[24,64,128]{2,1,0:T(8,128)S(1)} fusion(bf16[24,5,64,128]{3,2,1,0:T(8,128)(2,1)S(1)} %bitcast.220, bf16[24,5,128,128]{3,2,1,0:T(8,128)(2,1)} %param.16), kind=kOutput, calls=%fused_computation.16 | convolution fusion | flops 251658240 | bytes 6684672 | tf_op jit(solution)/shard_map/nscb,nsbd->ncd/dot_general | solution.py:25
  68.5 1.0 copy-done.4
  72.9 3.8 %collective-permute-start.12 = (bf16[6,64,128]{2,1,0:T(8,128)(2,1)S(1)}, bf16[6,64,128]{2,1,0:T(8,128)(2,1)S(1)}, u32[]{:S(2)}, u32[]{:S(2)}) collective-permute-start(bf16[6,64,128]{2,1,0:T(8,128)(2,1)S(1)} %gather_fusion.9), channel_id=1, source_target_pairs={{16,0},{17,1},{18,2},{19,3},{20,4},{21,5},{22,6},{23,7},{24,8},{25... | collective-permute-start | bytes 294920 | tf_op jit(solution)/shard_map/ppermute | solution.py:66
  76.7 5.8 %collective-permute-start.11 = (bf16[6,64,128]{2,1,0:T(8,128)(2,1)S(1)}, bf16[6,64,128]{2,1,0:T(8,128)(2,1)S(1)}, u32[]{:S(2)}, u32[]{:S(2)}) collective-permute-start(bf16[6,64,128]{2,1,0:T(8,128)(2,1)S(1)} %gather_fusion.8), channel_id=1, source_target_pairs={{2,0},{3,1},{4,2},{5,3},{6,4},{7,5},{8,6},{9,7},{10,8},{11,9},{12,... | collective-permute-start | bytes 294920 | tf_op jit(solution)/shard_map/ppermute | solution.py:66
  82.6 1.4 %copy.73 = f32[24,64,128]{2,0,1:T(8,128)} copy(f32[24,64,128]{2,1,0:T(8,128)S(1)} %get-tuple-element.101) | data formatting | bytes 1572864 | tf_op jit(solution)/shard_map/concatenate | solution.py:101
  84.7 2.3 %collective-permute-done.10 = bf16[6,64,128]{2,1,0:T(8,128)(2,1)S(1)} collective-permute-done((bf16[6,64,128]{2,1,0:T(8,128)(2,1)S(1)}, bf16[6,64,128]{2,1,0:T(8,128)(2,1)S(1)}, u32[]{:S(2)}, u32[]{:S(2)}) %collective-permute-start.10) | collective-permute-done | bytes 98336 | tf_op jit(solution)/shard_map/ppermute | solution.py:66
  90.3 2.1 %gather_fusion.12 = bf16[120,64,128]{2,1,0:T(8,128)(2,1)S(1)} fusion(bf16[54,64,128]{2,1,0:T(8,128)(2,1)} %constant_dynamic-update-slice_fusion.7, s32[1024]{0:T(1024)S(1)} %pad_clamp_fusion), kind=kCustom, calls=%fused_computation.12 | custom fusion | bytes 3932640 | tf_op jit(solution)/shard_map/gather | solution.py:24
  92.4 3.2 %convolution_bitcast_fusion = f32[24,64,128]{2,1,0:T(8,128)S(1)} fusion(bf16[24,5,64,128]{3,2,1,0:T(8,128)(2,1)S(1)} %bitcast.218, bf16[24,5,128,128]{3,2,1,0:T(8,128)(2,1)} %param.17), kind=kOutput, calls=%fused_computation.13 | convolution fusion | flops 251658240 | bytes 6684672 | tf_op jit(solution)/shard_map/nscb,nsbd->ncd/dot_general | solution.py:28
  95.7 0.9 convolution_bitcast_fusion.1
  99.6 7.0 %collective-permute-start.15 = (f32[2,4,24,128]{3,2,1,0:T(8,128)S(1)}, f32[2,4,24,128]{3,2,1,0:T(8,128)S(1)}, u32[]{:S(2)}, u32[]{:S(2)}) collective-permute-start(f32[2,4,24,128]{3,2,1,0:T(8,128)S(1)} %get-tuple-element.92), channel_id=1, source_target_pairs={{0,32},{32,64},{64,96},{96,128},{128,160},{160,192},{192,224},{224... | collective-permute-start | bytes 294920 | tf_op jit(solution)/shard_map/ppermute | solution.py:116
  106.5 1.3 %collective-permute-start.16 = (f32[2,4,24,128]{3,2,1,0:T(8,128)S(1)}, f32[2,4,24,128]{3,2,1,0:T(8,128)S(1)}, u32[]{:S(2)}, u32[]{:S(2)}) collective-permute-start(f32[2,4,24,128]{3,2,1,0:T(8,128)S(1)} %get-tuple-element.98), channel_id=1, source_target_pairs={{0,64},{32,96},{64,128},{96,160},{128,192},{160,224},{192,0},{224,... | collective-permute-start | bytes 294920 | tf_op jit(solution)/shard_map/ppermute | solution.py:116
  107.8 1.9 %collective-permute-start.17 = (f32[2,4,24,128]{3,2,1,0:T(8,128)S(1)}, f32[2,4,24,128]{3,2,1,0:T(8,128)S(1)}, u32[]{:S(2)}, u32[]{:S(2)}) collective-permute-start(f32[2,4,24,128]{3,2,1,0:T(8,128)S(1)} %get-tuple-element.97), channel_id=1, source_target_pairs={{0,96},{32,128},{64,160},{96,192},{128,224},{160,0},{192,32},{224,... | collective-permute-start | bytes 294920 | tf_op jit(solution)/shard_map/ppermute | solution.py:116
  110.1 1.7 %collective-permute-start.19 = (f32[2,4,24,128]{3,2,1,0:T(8,128)S(1)}, f32[2,4,24,128]{3,2,1,0:T(8,128)S(1)}, u32[]{:S(2)}, u32[]{:S(2)}) collective-permute-start(f32[2,4,24,128]{3,2,1,0:T(8,128)S(1)} %get-tuple-element.95), channel_id=1, source_target_pairs={{0,160},{32,192},{64,224},{96,0},{128,32},{160,64},{192,96},{224,1... | collective-permute-start | bytes 294920 | tf_op jit(solution)/shard_map/ppermute | solution.py:116
  112.7 1.8 %collective-permute-start.21 = (f32[2,4,24,128]{3,2,1,0:T(8,128)S(1)}, f32[2,4,24,128]{3,2,1,0:T(8,128)S(1)}, u32[]{:S(2)}, u32[]{:S(2)}) collective-permute-start(f32[2,4,24,128]{3,2,1,0:T(8,128)S(1)} %get-tuple-element.93), channel_id=1, source_target_pairs={{0,224},{32,0},{64,32},{96,64},{128,96},{160,128},{192,160},{224,1... | collective-permute-start | bytes 294920 | tf_op jit(solution)/shard_map/ppermute | solution.py:116
  114.5 3.2 %collective-permute-done.18 = f32[2,4,24,128]{3,2,1,0:T(8,128)S(1)} collective-permute-done((f32[2,4,24,128]{3,2,1,0:T(8,128)S(1)}, f32[2,4,24,128]{3,2,1,0:T(8,128)S(1)}, u32[]{:S(2)}, u32[]{:S(2)}) %collective-permute-start.18) | collective-permute-done | bytes 98336 | tf_op jit(solution)/shard_map/ppermute | solution.py:116
  118.5 1.2 collective-permute-done.21
  (145 shorter events, 32.1 us)
Async XLA Ops:
  0.0 39.1 %copy-start = (bf16[1,2,24,128,128]{4,3,2,1,0:T(8,128)(2,1)S(1)}, bf16[1,2,24,128,128]{4,3,2,1,0:T(8,128)(2,1)}, u32[]{:S(2)}) copy-start(bf16[1,2,24,128,128]{4,3,2,1,0:T(8,128)(2,1)} %param.18) | copy-start | bytes 4718596
  0.0 4.2 %copy-start.10 = (bf16[32,24,128]{2,1,0:T(8,128)(2,1)S(1)}, bf16[32,24,128]{2,1,0:T(8,128)(2,1)}, u32[]{:S(2)}) copy-start(bf16[32,24,128]{2,1,0:T(8,128)(2,1)} %param.15) | copy-start | bytes 589828
  4.4 14.1 %collective-permute-start = (bf16[25,32,128]{2,1,0:T(8,128)(2,1)S(1)}, bf16[25,32,128]{2,1,0:T(8,128)(2,1)S(1)}, u32[]{:S(2)}, u32[]{:S(2)}) collective-permute-start(bf16[25,32,128]{2,1,0:T(8,128)(2,1)S(1)} %get-tuple-element.107), channel_id=1, source_target_pairs={{1,0},{2,1},{3,2},{4,3},{5,4},{6,5},{7,6},{8,7},{9,8},{10,9},{11,1... | collective-permute-start | bytes 614408 | tf_op jit(solution)/shard_map/ppermute | solution.py:78
  4.5 19.8 %collective-permute-start.1 = (bf16[25,32,128]{2,1,0:T(8,128)(2,1)S(1)}, bf16[25,32,128]{2,1,0:T(8,128)(2,1)}, u32[]{:S(2)}, u32[]{:S(2)}) collective-permute-start(bf16[25,32,128]{2,1,0:T(8,128)(2,1)S(1)} %get-tuple-element.106), channel_id=1, source_target_pairs={{2,0},{3,1},{4,2},{5,3},{6,4},{7,5},{8,6},{9,7},{10,8},{11,9},{12,... | collective-permute-start | bytes 614408 | tf_op jit(solution)/shard_map/ppermute | solution.py:78
  12.2 14.3 %collective-permute-start.2 = (bf16[25,32,128]{2,1,0:T(8,128)(2,1)S(1)}, bf16[25,32,128]{2,1,0:T(8,128)(2,1)}, u32[]{:S(2)}, u32[]{:S(2)}) collective-permute-start(bf16[25,32,128]{2,1,0:T(8,128)(2,1)S(1)} %get-tuple-element.104), channel_id=1, source_target_pairs={{16,0},{17,1},{18,2},{19,3},{20,4},{21,5},{22,6},{23,7},{24,8},{25... | collective-permute-start | bytes 614408 | tf_op jit(solution)/shard_map/ppermute | solution.py:78
  13.4 14.7 %collective-permute-start.3 = (bf16[25,32,128]{2,1,0:T(8,128)(2,1)S(1)}, bf16[25,32,128]{2,1,0:T(8,128)(2,1)S(1)}, u32[]{:S(2)}, u32[]{:S(2)}) collective-permute-start(bf16[25,32,128]{2,1,0:T(8,128)(2,1)S(1)} %get-tuple-element.105), channel_id=1, source_target_pairs={{31,0},{0,1},{1,2},{2,3},{3,4},{4,5},{5,6},{6,7},{7,8},{8,9},{9,10... | collective-permute-start | bytes 614408 | tf_op jit(solution)/shard_map/ppermute | solution.py:78
  14.9 18.7 %collective-permute-start.4 = (bf16[25,32,128]{2,1,0:T(8,128)(2,1)S(1)}, bf16[25,32,128]{2,1,0:T(8,128)(2,1)S(1)}, u32[]{:S(2)}, u32[]{:S(2)}) collective-permute-start(bf16[25,32,128]{2,1,0:T(8,128)(2,1)S(1)} %get-tuple-element.103), channel_id=1, source_target_pairs={{30,0},{31,1},{0,2},{1,3},{2,4},{3,5},{4,6},{5,7},{6,8},{7,9},{8,1... | collective-permute-start | bytes 614408 | tf_op jit(solution)/shard_map/ppermute | solution.py:78
  39.1 2.1 %copy-start.6 = (f32[24,32,128]{2,1,0:T(8,128)}, f32[24,32,128]{2,1,0:T(8,128)S(1)}, u32[]{:S(2)}) copy-start(f32[24,32,128]{2,1,0:T(8,128)S(1)} %convolution_bitcast_fusion.4) | copy-start | bytes 1179652
  42.5 15.2 %collective-permute-start.8 = (bf16[6,64,128]{2,1,0:T(8,128)(2,1)S(1)}, bf16[6,64,128]{2,1,0:T(8,128)(2,1)S(1)}, u32[]{:S(2)}, u32[]{:S(2)}) collective-permute-start(bf16[6,64,128]{2,1,0:T(8,128)(2,1)S(1)} %gather_fusion.4), channel_id=1, source_target_pairs={{31,0},{0,1},{1,2},{2,3},{3,4},{4,5},{5,6},{6,7},{7,8},{8,9},{9,10... | collective-permute-start | bytes 294920 | tf_op jit(solution)/shard_map/ppermute | solution.py:66
  43.2 13.9 %collective-permute-start.7 = (bf16[6,64,128]{2,1,0:T(8,128)(2,1)S(1)}, bf16[6,64,128]{2,1,0:T(8,128)(2,1)S(1)}, u32[]{:S(2)}, u32[]{:S(2)}) collective-permute-start(bf16[6,64,128]{2,1,0:T(8,128)(2,1)S(1)} %gather_fusion.3), channel_id=1, source_target_pairs={{16,0},{17,1},{18,2},{19,3},{20,4},{21,5},{22,6},{23,7},{24,8},{25... | collective-permute-start | bytes 294920 | tf_op jit(solution)/shard_map/ppermute | solution.py:66
  47.9 8.5 %collective-permute-start.6 = (bf16[6,64,128]{2,1,0:T(8,128)(2,1)S(1)}, bf16[6,64,128]{2,1,0:T(8,128)(2,1)S(1)}, u32[]{:S(2)}, u32[]{:S(2)}) collective-permute-start(bf16[6,64,128]{2,1,0:T(8,128)(2,1)S(1)} %gather_fusion.2), channel_id=1, source_target_pairs={{2,0},{3,1},{4,2},{5,3},{6,4},{7,5},{8,6},{9,7},{10,8},{11,9},{12,... | collective-permute-start | bytes 294920 | tf_op jit(solution)/shard_map/ppermute | solution.py:66
  51.5 9.3 %copy-start.11 = (s32[1024]{0:T(1024)}, s32[1024]{0:T(1024)S(1)}, u32[]{:S(2)}) copy-start(s32[1024]{0:T(1024)S(1)} %pad_clamp_fusion.5) | copy-start | bytes 12292
  52.0 3.8 %collective-permute-start.5 = (bf16[6,64,128]{2,1,0:T(8,128)(2,1)S(1)}, bf16[6,64,128]{2,1,0:T(8,128)(2,1)S(1)}, u32[]{:S(2)}, u32[]{:S(2)}) collective-permute-start(bf16[6,64,128]{2,1,0:T(8,128)(2,1)S(1)} %gather_fusion.1), channel_id=1, source_target_pairs={{1,0},{2,1},{3,2},{4,3},{5,4},{6,5},{7,6},{8,7},{9,8},{10,9},{11,1... | collective-permute-start | bytes 294920 | tf_op jit(solution)/shard_map/ppermute | solution.py:66
  52.8 7.9 %copy-start.12 = (s32[1024]{0:T(1024)}, s32[1024]{0:T(1024)S(1)}, u32[]{:S(2)}) copy-start(s32[1024]{0:T(1024)S(1)} %pad_clamp_fusion.1) | copy-start | bytes 12292
  53.4 7.3 %collective-permute-start.9 = (bf16[6,64,128]{2,1,0:T(8,128)(2,1)S(1)}, bf16[6,64,128]{2,1,0:T(8,128)(2,1)S(1)}, u32[]{:S(2)}, u32[]{:S(2)}) collective-permute-start(bf16[6,64,128]{2,1,0:T(8,128)(2,1)S(1)} %gather_fusion.5), channel_id=1, source_target_pairs={{30,0},{31,1},{0,2},{1,3},{2,4},{3,5},{4,6},{5,7},{6,8},{7,9},{8,1... | collective-permute-start | bytes 294920 | tf_op jit(solution)/shard_map/ppermute | solution.py:66
  63.5 3.3 %copy-start.2 = (bf16[24,5,128,128]{3,2,1,0:T(8,128)(2,1)S(1)}, bf16[24,5,128,128]{3,2,1,0:T(8,128)(2,1)}, u32[]{:S(2)}) copy-start(bf16[24,5,128,128]{3,2,1,0:T(8,128)(2,1)} %param.17) | copy-start | bytes 11796484
  68.4 1.1 copy-start.4
  72.8 16.1 %collective-permute-start.13 = (bf16[6,64,128]{2,1,0:T(8,128)(2,1)S(1)}, bf16[6,64,128]{2,1,0:T(8,128)(2,1)S(1)}, u32[]{:S(2)}, u32[]{:S(2)}) collective-permute-start(bf16[6,64,128]{2,1,0:T(8,128)(2,1)S(1)} %gather_fusion.10), channel_id=1, source_target_pairs={{31,0},{0,1},{1,2},{2,3},{3,4},{4,5},{5,6},{6,7},{7,8},{8,9},{9,10... | collective-permute-start | bytes 294920 | tf_op jit(solution)/shard_map/ppermute | solution.py:66
  72.9 15.4 %collective-permute-start.12 = (bf16[6,64,128]{2,1,0:T(8,128)(2,1)S(1)}, bf16[6,64,128]{2,1,0:T(8,128)(2,1)S(1)}, u32[]{:S(2)}, u32[]{:S(2)}) collective-permute-start(bf16[6,64,128]{2,1,0:T(8,128)(2,1)S(1)} %gather_fusion.9), channel_id=1, source_target_pairs={{16,0},{17,1},{18,2},{19,3},{20,4},{21,5},{22,6},{23,7},{24,8},{25... | collective-permute-start | bytes 294920 | tf_op jit(solution)/shard_map/ppermute | solution.py:66
  76.7 10.9 %collective-permute-start.11 = (bf16[6,64,128]{2,1,0:T(8,128)(2,1)S(1)}, bf16[6,64,128]{2,1,0:T(8,128)(2,1)S(1)}, u32[]{:S(2)}, u32[]{:S(2)}) collective-permute-start(bf16[6,64,128]{2,1,0:T(8,128)(2,1)S(1)} %gather_fusion.8), channel_id=1, source_target_pairs={{2,0},{3,1},{4,2},{5,3},{6,4},{7,5},{8,6},{9,7},{10,8},{11,9},{12,... | collective-permute-start | bytes 294920 | tf_op jit(solution)/shard_map/ppermute | solution.py:66
  82.6 4.4 %collective-permute-start.10 = (bf16[6,64,128]{2,1,0:T(8,128)(2,1)S(1)}, bf16[6,64,128]{2,1,0:T(8,128)(2,1)S(1)}, u32[]{:S(2)}, u32[]{:S(2)}) collective-permute-start(bf16[6,64,128]{2,1,0:T(8,128)(2,1)S(1)} %gather_fusion.7), channel_id=1, source_target_pairs={{1,0},{2,1},{3,2},{4,3},{5,4},{6,5},{7,6},{8,7},{9,8},{10,9},{11,1... | collective-permute-start | bytes 294920 | tf_op jit(solution)/shard_map/ppermute | solution.py:66
  82.6 7.1 %collective-permute-start.14 = (bf16[6,64,128]{2,1,0:T(8,128)(2,1)S(1)}, bf16[6,64,128]{2,1,0:T(8,128)(2,1)S(1)}, u32[]{:S(2)}, u32[]{:S(2)}) collective-permute-start(bf16[6,64,128]{2,1,0:T(8,128)(2,1)S(1)} %gather_fusion.11), channel_id=1, source_target_pairs={{30,0},{31,1},{0,2},{1,3},{2,4},{3,5},{4,6},{5,7},{6,8},{7,9},{8,1... | collective-permute-start | bytes 294920 | tf_op jit(solution)/shard_map/ppermute | solution.py:66
  92.4 3.3 %copy-start.1 = (bf16[24,5,128,128]{3,2,1,0:T(8,128)(2,1)S(1)}, bf16[24,5,128,128]{3,2,1,0:T(8,128)(2,1)}, u32[]{:S(2)}) copy-start(bf16[24,5,128,128]{3,2,1,0:T(8,128)(2,1)} %param.16) | copy-start | bytes 11796484
  97.4 1.1 copy-start.5
  97.4 1.4 %copy-start.9 = (f32[24,64,128]{2,0,1:T(8,128)S(1)}, f32[24,64,128]{2,0,1:T(8,128)}, u32[]{:S(2)}) copy-start(f32[24,64,128]{2,0,1:T(8,128)} %copy.73) | copy-start | bytes 2359300
  99.6 12.2 %collective-permute-start.15 = (f32[2,4,24,128]{3,2,1,0:T(8,128)S(1)}, f32[2,4,24,128]{3,2,1,0:T(8,128)S(1)}, u32[]{:S(2)}, u32[]{:S(2)}) collective-permute-start(f32[2,4,24,128]{3,2,1,0:T(8,128)S(1)} %get-tuple-element.92), channel_id=1, source_target_pairs={{0,32},{32,64},{64,96},{96,128},{128,160},{160,192},{192,224},{224... | collective-permute-start | bytes 294920 | tf_op jit(solution)/shard_map/ppermute | solution.py:116
  106.5 6.1 %collective-permute-start.16 = (f32[2,4,24,128]{3,2,1,0:T(8,128)S(1)}, f32[2,4,24,128]{3,2,1,0:T(8,128)S(1)}, u32[]{:S(2)}, u32[]{:S(2)}) collective-permute-start(f32[2,4,24,128]{3,2,1,0:T(8,128)S(1)} %get-tuple-element.98), channel_id=1, source_target_pairs={{0,64},{32,96},{64,128},{96,160},{128,192},{160,224},{192,0},{224,... | collective-permute-start | bytes 294920 | tf_op jit(solution)/shard_map/ppermute | solution.py:116
  107.8 6.6 %collective-permute-start.17 = (f32[2,4,24,128]{3,2,1,0:T(8,128)S(1)}, f32[2,4,24,128]{3,2,1,0:T(8,128)S(1)}, u32[]{:S(2)}, u32[]{:S(2)}) collective-permute-start(f32[2,4,24,128]{3,2,1,0:T(8,128)S(1)} %get-tuple-element.97), channel_id=1, source_target_pairs={{0,96},{32,128},{64,160},{96,192},{128,224},{160,0},{192,32},{224,... | collective-permute-start | bytes 294920 | tf_op jit(solution)/shard_map/ppermute | solution.py:116
  109.8 7.9 %collective-permute-start.18 = (f32[2,4,24,128]{3,2,1,0:T(8,128)S(1)}, f32[2,4,24,128]{3,2,1,0:T(8,128)S(1)}, u32[]{:S(2)}, u32[]{:S(2)}) collective-permute-start(f32[2,4,24,128]{3,2,1,0:T(8,128)S(1)} %get-tuple-element.96), channel_id=1, source_target_pairs={{0,128},{32,160},{64,192},{96,224},{128,0},{160,32},{192,64},{224,... | collective-permute-start | bytes 294920 | tf_op jit(solution)/shard_map/ppermute | solution.py:116
  110.1 8.4 %collective-permute-start.19 = (f32[2,4,24,128]{3,2,1,0:T(8,128)S(1)}, f32[2,4,24,128]{3,2,1,0:T(8,128)S(1)}, u32[]{:S(2)}, u32[]{:S(2)}) collective-permute-start(f32[2,4,24,128]{3,2,1,0:T(8,128)S(1)} %get-tuple-element.95), channel_id=1, source_target_pairs={{0,160},{32,192},{64,224},{96,0},{128,32},{160,64},{192,96},{224,1... | collective-permute-start | bytes 294920 | tf_op jit(solution)/shard_map/ppermute | solution.py:116
  111.8 6.7 %collective-permute-start.20 = (f32[2,4,24,128]{3,2,1,0:T(8,128)S(1)}, f32[2,4,24,128]{3,2,1,0:T(8,128)S(1)}, u32[]{:S(2)}, u32[]{:S(2)}) collective-permute-start(f32[2,4,24,128]{3,2,1,0:T(8,128)S(1)} %get-tuple-element.94), channel_id=1, source_target_pairs={{0,192},{32,224},{64,0},{96,32},{128,64},{160,96},{192,128},{224,1... | collective-permute-start | bytes 294920 | tf_op jit(solution)/shard_map/ppermute | solution.py:116
  112.7 7.1 %collective-permute-start.21 = (f32[2,4,24,128]{3,2,1,0:T(8,128)S(1)}, f32[2,4,24,128]{3,2,1,0:T(8,128)S(1)}, u32[]{:S(2)}, u32[]{:S(2)}) collective-permute-start(f32[2,4,24,128]{3,2,1,0:T(8,128)S(1)} %get-tuple-element.93), channel_id=1, source_target_pairs={{0,224},{32,0},{64,32},{96,64},{128,96},{160,128},{192,160},{224,1... | collective-permute-start | bytes 294920 | tf_op jit(solution)/shard_map/ppermute | solution.py:116
  (3 other events, 2.9 us)

commit v5 on v4

--- a/solution.py
+++ b/solution.py
@@ -20,13 +20,17 @@
     return found
 
 
-def apply_pair(extended, slot_index, first, second):
-    picked = extended[slot_index]
-    with_first = jnp.einsum("nscb,nsbd->ncd", picked, first, preferred_element_type=jnp.float32)
-    if second is None:
-        return with_first, None
-    with_second = jnp.einsum("nscb,nsbd->ncd", picked, second, preferred_element_type=jnp.float32)
-    return with_first, with_second
+def apply_split(local_vec, halo_vec, local_index, halo_row, mats, halo_mats):
+    padded = jnp.concatenate([local_vec, jnp.zeros((1,) + local_vec.shape[1:], local_vec.dtype)], axis=0)
+    picked = padded[local_index]
+    rows = local_vec.shape[0]
+    results = []
+    for matrices, halo_matrices in zip(mats, halo_mats):
+        summed = jnp.einsum("nscb,nsbd->ncd", picked, matrices, preferred_element_type=jnp.float32)
+        extra = jnp.einsum("hcb,hbd->hcd", halo_vec, halo_matrices, preferred_element_type=jnp.float32)
+        extra = jnp.zeros((rows + 1,) + extra.shape[1:], jnp.float32).at[halo_row].add(extra)
+        results.append(summed + extra[:rows])
+    return results
 
 
 def per_device(columns, pencil_e, pencil_a, precond, neighbours):
@@ -40,19 +44,24 @@
     relative = (owners - my_index) % peer_count
     flat_rel = relative.reshape(-1)
     flat_local = local_ids.reshape(-1)
-    slot_flat = flat_local
-    whole_flat = flat_local
+    entries = flat_local.shape[0]
+    local_flat = jnp.where(flat_rel == 0, flat_local, dev_rows)
     wanted = []
+    halo_entry = []
+    halo_valid = []
     rank_range = jnp.arange(HMAX)
+    entry_range = jnp.arange(entries)
     for which, offset in enumerate(offsets):
         hit = flat_rel == offset
         rank = jnp.cumsum(hit.astype(jnp.int32)) - 1
-        slot_flat = jnp.where(hit, dev_rows + which * HMAX + rank, slot_flat)
-        whole_flat = jnp.where(hit, (which + 1) * dev_rows + flat_local, whole_flat)
         matched = hit[None, :] & (rank[None, :] == rank_range[:, None])
         wanted.append(jnp.sum(jnp.where(matched, flat_local[None, :], 0), axis=1))
-    slot_index = slot_flat.reshape(dev_rows, SLOTS)
-    whole_index = whole_flat.reshape(dev_rows, SLOTS)
+        halo_entry.append(jnp.sum(jnp.where(matched, entry_range[None, :], 0), axis=1))
+        halo_valid.append(jnp.any(matched, axis=1))
+    local_index = local_flat.reshape(dev_rows, SLOTS)
+    halo_entry = jnp.concatenate(halo_entry)
+    halo_valid = jnp.concatenate(halo_valid)
+    halo_row = jnp.where(halo_valid, halo_entry // SLOTS, dev_rows)
 
     def to_partner(offset):
         return [(j, (j + offset) % peer_count) for j in range(peer_count)]
@@ -61,24 +70,30 @@
         return [((j + offset) % peer_count, j) for j in range(peer_count)]
 
     def fetch_halo(vector):
-        pieces = [vector]
+        pieces = []
         for which, offset in enumerate(offsets):
             pieces.append(lax.ppermute(vector[asked_for[which]], "rows", from_partner(offset)))
         return jnp.concatenate(pieces, axis=0)
 
     e_mats = pencil_e
     a_mats = pencil_a
+    block_shape = pencil_e.shape[2:]
+    halo_e = pencil_e.reshape((-1,) + block_shape)[halo_entry]
+    halo_a = pencil_a.reshape((-1,) + block_shape)[halo_entry]
+    halo_e = jnp.where(halo_valid[:, None, None], halo_e, jnp.zeros_like(halo_e))
+    halo_a = jnp.where(halo_valid[:, None, None], halo_a, jnp.zeros_like(halo_a))
     cols_major = jnp.transpose(columns, (1, 0, 2))
-    whole = [cols_major]
+    col_halo = []
     asked_for = [None] * len(offsets)
     for which, offset in enumerate(offsets):
         back = offsets.index((-offset) % peer_count)
         tag = jnp.zeros((1,) + cols_major.shape[1:], cols_major.dtype)
         tag = tag.at[0, 0, :HMAX].set(wanted[back].astype(cols_major.dtype))
         got = lax.ppermute(jnp.concatenate([cols_major, tag], axis=0), "rows", from_partner(offset))
-        whole.append(got[:dev_rows])
+        col_halo.append(got[:dev_rows][wanted[which]])
         asked_for[back] = got[dev_rows, 0, :HMAX].astype(jnp.int32)
-    rhs_full, _ = apply_pair(jnp.concatenate(whole, axis=0), whole_index, e_mats, None)
+    col_halo = jnp.concatenate(col_halo, axis=0)
+    (rhs_full,) = apply_split(cols_major, col_halo, local_index, halo_row, [e_mats], [halo_e])
     node_count = lax.axis_size("node")
     angle_node = 2.0 * math.pi * (lax.axis_index("node").astype(jnp.float32) + 0.5) / node_count
     node_real = jnp.cos(angle_node)
@@ -89,7 +104,9 @@
     iterate = start.reshape(dev_rows, 2 * col_count, -1)
     for sweep_step in range(SWEEPS):
         rounded = iterate.astype(jnp.bfloat16)
-        with_e, with_a = apply_pair(fetch_halo(rounded), slot_index, e_mats, a_mats)
+        with_e, with_a = apply_split(
+            rounded, fetch_halo(rounded), local_index, halo_row, [e_mats, a_mats], [halo_e, halo_a]
+        )
         e_real, e_imag = with_e[:, :col_count], with_e[:, col_count:]
         applied_real = node_real * e_real - node_imag * e_imag - with_a[:, :col_count]
         applied_imag = node_real * e_imag + node_imag * e_real - with_a[:, col_count:]

time: 122 us -> 182 us (1.49)
  local copies, waits for them, and re-layouts: 32.8 us -> 62.5 us
  other arithmetic: 6.34 us -> 34.7 us
  waiting for transfers between devices: 22.2 us -> 6.14 us
  matrix products: 12.2 us -> 28.2 us
  starting transfers between devices: 46 us -> 48.6 us
    scatter-add x0 -> x5, other arithmetic: none -> 24.8 us  [apply_split(): jnp.zeros((rows + 1,) + extra.shape[1:], jnp.float32).at[halo_row]]
    dot_general x5 -> x10, matrix products: 11.1 us -> 27.1 us  [the longest x5 18 us: apply_split(): jnp.einsum('nscb,nsbd->ncd', picked, matrices, preferred_element_type=jnp...]
    gather x3 -> x10, local copies, waits for them, and re-layouts: 6.21 us -> 17.5 us  [the longest x3 5.52 us: apply_split(): picked = padded[local_index]]
    ppermute x5, waiting for transfers between devices: 10.4 us -> 0.01 us  [per_device(): lax.ppermute(jnp.concatenate([cols_major, tag], axis=0), 'rows', from_par...]
    gather x10, local copies, waits for them, and re-layouts: 5.9 us -> 12.5 us  [fetch_halo(): vector[asked_for[which]]]
    ppermute x10, waiting for transfers between devices: 6.57 us -> 0.88 us  [fetch_halo(): lax.ppermute(vector[asked_for[which]], 'rows', from_partner(offset))]
    slice x0 -> x5, local copies, waits for them, and re-layouts: none -> 5.39 us  [per_device(): col_halo.append(got[:dev_rows][wanted[which]])]
    another operation x0 -> x4, local copies, waits for them, and re-layouts: none -> 3.97 us
  transfers between devices with their start and end apart: 22 -> 22, of which waited for: 10 -> 4; matrix products, arithmetic and copies ran while one was open for 13% -> 24% of each run, Pallas kernels for 0% -> 0%
where the time goes in v5:
time: 182 us; the launch traced here: 181 us
  local copies, waits for them, and re-layouts  62.5 us (34%)
  starting transfers between devices  48.6 us (27%)
  other arithmetic  34.7 us (19%)
  matrix products  28.2 us (15%)
  waiting for transfers between devices  6.14 us (3%)
    scatter-add x5, other arithmetic, apply_split(): jnp.zeros((rows + 1,) + extra.shape[1:], jnp.float32).at[halo_row]  24.8 us
    ppermute x10, starting transfers between devices, fetch_halo(): lax.ppermute(vector[asked_for[which]], 'rows', from_partner(offset))  21.9 us
    dot_general x5, matrix products, apply_split(): jnp.einsum('nscb,nsbd->ncd', picked, matrices, preferred_element_type=jnp...  18 us
    ppermute x5, starting transfers between devices, per_device(): lax.ppermute(jnp.concatenate([cols_major, tag], axis=0), 'rows', from_par...  13.5 us
    ppermute x7, starting transfers between devices, per_device(): total = total + lax.ppermute(chunk, 'node', perm)  13.2 us
    unnamed x53, local copies, waits for them, and re-layouts  12.6 us
    gather x10, local copies, waits for them, and re-layouts, fetch_halo(): vector[asked_for[which]]  12.5 us
    dot_general x5, matrix products, apply_split(): jnp.einsum('hcb,hbd->hcd', halo_vec, halo_matrices, preferred_element_typ...  9.08 us
  transfers between devices with their start and end apart: 22, of which 4 were waited for; matrix products, arithmetic and copies ran while one was open for 24% of the time, Pallas kernels for 0%

profile of v5, /device:TPU:3, one launch (start us, length us, event | category | flops | bytes accessed | tf_op | source)
XLA Modules:
  0.0 181.0 jit_solution(12444409144446257842)
XLA Ops:
  7.3 7.1 %collective-permute-start.1 = (bf16[25,32,128]{2,1,0:T(8,128)(2,1)}, bf16[25,32,128]{2,1,0:T(8,128)(2,1)}, u32[]{:S(2)}, u32[]{:S(2)}) collective-permute-start(bf16[25,32,128]{2,1,0:T(8,128)(2,1)} %get-tuple-element.112), channel_id=1, source_target_pairs={{2,0},{3,1},{4,2},{5,3},{6,4},{7,5},{8,6},{9,7},{10,8},{11,9},{12,... | collective-permute-start | bytes 614408 | tf_op jit(solution)/shard_map/ppermute | solution.py:92
  17.1 3.7 %collective-permute-start.4 = (bf16[25,32,128]{2,1,0:T(8,128)(2,1)S(1)}, bf16[25,32,128]{2,1,0:T(8,128)(2,1)}, u32[]{:S(2)}, u32[]{:S(2)}) collective-permute-start(bf16[25,32,128]{2,1,0:T(8,128)(2,1)S(1)} %get-tuple-element.111), channel_id=1, source_target_pairs={{30,0},{31,1},{0,2},{1,3},{2,4},{3,5},{4,6},{5,7},{6,8},{7,9},{8,1... | collective-permute-start | bytes 614408 | tf_op jit(solution)/shard_map/ppermute | solution.py:92
  22.0 2.9 %gather_fusion.6 = bf16[30,128,128]{2,1,0:T(8,128)(2,1)S(1)} fusion(bf16[120,128,128]{2,1,0:T(8,128)(2,1)} %bitcast.259, s32[1024]{0:T(1024)S(1)} %pad_clamp_fusion.5), kind=kCustom, calls=%fused_computation.6 | custom fusion | bytes 1966200 | tf_op jit(solution)/shard_map/gather | solution.py:81
  24.8 4.1 %gather_fusion.13 = bf16[30,128,128]{2,1,0:T(8,128)(2,1)} fusion(bf16[120,128,128]{2,1,0:T(8,128)(2,1)} %bitcast.260, s32[1024]{0:T(1024)S(1)} %pad_clamp_fusion.5), kind=kCustom, calls=%fused_computation.13 | custom fusion | bytes 1966200 | tf_op jit(solution)/shard_map/gather | solution.py:82
  28.9 1.7 gather_fusion
  38.9 1.6 slice.281
  40.5 2.2 %gather_fusion.5 = bf16[6,32,128]{2,1,0:T(8,128)(2,1)} fusion(bf16[24,32,128]{2,1,0:T(8,128)(2,1)} %slice.281, s32[1024]{0:T(1024)S(1)} %get-tuple-element.131), kind=kCustom, calls=%fused_computation.5 | custom fusion | bytes 98328 | tf_op jit(solution)/shard_map/gather | solution.py:93
  44.1 2.2 %fusion.83 = f32[30,32,128]{2,1,0:T(8,128)} fusion(bf16[30,32,128]{2,1,0:T(8,128)(2,1)} %constant_dynamic-update-slice_fusion, bf16[30,128,128]{2,1,0:T(8,128)(2,1)S(1)} %gather_fusion.6, pred[30]{0:T(512)(128)(4,1)S(1)} %concatenate.153), kind=kOutput, calls=%fused_computation.233 | convolution fusion | flops 31948800 | bytes 1720350 | tf_op jit(solution)/shard_map/hcb,hbd->hcd/dot_general | solution.py:30
  46.3 3.4 %scatter_fusion = f32[25,32,128]{2,1,0:T(8,128)S(1)} fusion(f32[25,32,128]{2,1,0:T(8,128)S(1)} %broadcast_in_dim.130, s32[30]{0:T(128)S(1)} %get-tuple-element.126, f32[30,32,128]{2,1,0:T(8,128)} %fusion.83), kind=kCustom, calls=%fused_computation.20 | custom fusion | flops 122880 | bytes 1474680 | tf_op jit(solution)/shard_map/scatter-add | solution.py:31
  49.7 2.9 %fusion = f32[24,32,128]{2,1,0:T(8,128)S(1)} fusion(bf16[24,5,32,128]{3,2,1,0:T(8,128)(2,1)S(1)} %bitcast.269, bf16[24,5,128,128]{3,2,1,0:T(8,128)(2,1)} %param.16, f32[25,32,128]{2,1,0:T(8,128)S(1)} %scatter_fusion), kind=kOutput, calls=%fused_computation.30 | convolution fusion | flops 125927424 | bytes 5701632 | tf_op jit(solution)/shard_map/nscb,nsbd->ncd/dot_general | solution.py:29
  57.0 1.6 collective-permute-start.7
  60.5 4.6 %collective-permute-start.6 = (bf16[6,64,128]{2,1,0:T(8,128)(2,1)}, bf16[6,64,128]{2,1,0:T(8,128)(2,1)}, u32[]{:S(2)}, u32[]{:S(2)}) collective-permute-start(bf16[6,64,128]{2,1,0:T(8,128)(2,1)} %gather_fusion.9), channel_id=1, source_target_pairs={{2,0},{3,1},{4,2},{5,3},{6,4},{7,5},{8,6},{9,7},{10,8},{11,9},{12,... | collective-permute-start | bytes 294920 | tf_op jit(solution)/shard_map/ppermute | solution.py:75
  66.3 1.5 collective-permute-start.5
  70.5 1.9 %gather_fusion.7 = bf16[120,64,128]{2,1,0:T(8,128)(2,1)S(1)} fusion(bf16[25,64,128]{2,1,0:T(8,128)(2,1)} %concatenate.154, s32[1024]{0:T(1024)S(1)} %pad_clamp_fusion.11), kind=kCustom, calls=%fused_computation.7 | custom fusion | bytes 3932640 | tf_op jit(solution)/shard_map/gather | solution.py:25
  78.0 2.6 %fusion.82 = f32[30,64,128]{2,1,0:T(8,128)} fusion(bf16[30,64,128]{2,1,0:T(8,128)(2,1)S(1)} %constant_dynamic-update-slice_fusion.5, bf16[30,128,128]{2,1,0:T(8,128)(2,1)} %copy-done.1, pred[30]{0:T(512)(128)(4,1)S(1)} %concatenate.153), kind=kOutput, calls=%fused_computation.232 | convolution fusion | flops 63406080 | bytes 2457630 | tf_op jit(solution)/shard_map/hcb,hbd->hcd/dot_general | solution.py:30
  83.0 5.3 %scatter_fusion.1 = f32[25,64,128]{2,1,0:T(8,128)} fusion(f32[25,64,128]{2,1,0:T(8,128)} %broadcast.517.clone.2, s32[30]{0:T(128)S(1)} %get-tuple-element.126, f32[30,64,128]{2,1,0:T(8,128)} %fusion.82), kind=kCustom, calls=%fused_computation.21 | custom fusion | flops 245760 | bytes 2949240 | tf_op jit(solution)/shard_map/scatter-add | solution.py:31
  88.3 4.2 %slice_add_fusion.3 = f32[24,64,128]{2,1,0:T(8,128)} fusion(f32[25,64,128]{2,1,0:T(8,128)} %scatter_fusion.1, bf16[24,5,64,128]{3,2,1,0:T(8,128)(2,1)S(1)} %bitcast.263, bf16[24,5,128,128]{3,2,1,0:T(8,128)(2,1)} %param.16), kind=kOutput, calls=%fused_computation.42 | convolution fusion | flops 251854848 | bytes 7471104 | tf_op jit(solution)/shard_map/nscb,nsbd->ncd/dot_general | solution.py:29
  93.5 5.3 %scatter_fusion.2 = f32[25,64,128]{2,1,0:T(8,128)} fusion(f32[25,64,128]{2,1,0:T(8,128)} %broadcast.517.clone.1, s32[30]{0:T(128)S(1)} %get-tuple-element.126, f32[30,64,128]{2,1,0:T(8,128)} %fusion.15), kind=kCustom, calls=%fused_computation.22 | custom fusion | flops 245760 | bytes 2949240 | tf_op jit(solution)/shard_map/scatter-add | solution.py:31
  98.9 3.4 %slice_add_fusion.2 = f32[24,64,128]{2,1,0:T(8,128)S(1)} fusion(f32[25,64,128]{2,1,0:T(8,128)} %scatter_fusion.2, bf16[24,5,64,128]{3,2,1,0:T(8,128)(2,1)S(1)} %bitcast.264, bf16[24,5,128,128]{3,2,1,0:T(8,128)(2,1)} %param.17), kind=kOutput, calls=%fused_computation.41 | convolution fusion | flops 251854848 | bytes 7471104 | tf_op jit(solution)/shard_map/nscb,nsbd->ncd/dot_general | solution.py:29
  113.8 5.3 %collective-permute-start.12 = (bf16[6,64,128]{2,1,0:T(8,128)(2,1)}, bf16[6,64,128]{2,1,0:T(8,128)(2,1)}, u32[]{:S(2)}, u32[]{:S(2)}) collective-permute-start(bf16[6,64,128]{2,1,0:T(8,128)(2,1)} %gather_fusion.17), channel_id=1, source_target_pairs={{16,0},{17,1},{18,2},{19,3},{20,4},{21,5},{22,6},{23,7},{24,8},{25... | collective-permute-start | bytes 294920 | tf_op jit(solution)/shard_map/ppermute | solution.py:75
  119.1 7.5 %collective-permute-start.11 = (bf16[6,64,128]{2,1,0:T(8,128)(2,1)}, bf16[6,64,128]{2,1,0:T(8,128)(2,1)}, u32[]{:S(2)}, u32[]{:S(2)}) collective-permute-start(bf16[6,64,128]{2,1,0:T(8,128)(2,1)} %gather_fusion.16), channel_id=1, source_target_pairs={{2,0},{3,1},{4,2},{5,3},{6,4},{7,5},{8,6},{9,7},{10,8},{11,9},{12,... | collective-permute-start | bytes 294920 | tf_op jit(solution)/shard_map/ppermute | solution.py:75
  126.6 1.9 %gather_fusion.14 = bf16[120,64,128]{2,1,0:T(8,128)(2,1)S(1)} fusion(bf16[25,64,128]{2,1,0:T(8,128)(2,1)} %concatenate.159, s32[1024]{0:T(1024)S(1)} %pad_clamp_fusion.11), kind=kCustom, calls=%fused_computation.14 | custom fusion | bytes 3932640 | tf_op jit(solution)/shard_map/gather | solution.py:25
  128.5 2.6 %copy.97 = f32[24,64,128]{2,0,1:T(8,128)} copy(f32[24,64,128]{2,1,0:T(8,128)} %get-tuple-element.109) | data formatting | bytes 1572864 | tf_op jit(solution)/shard_map/concatenate | solution.py:118
  139.7 5.4 %scatter_fusion.3 = f32[25,64,128]{2,1,0:T(8,128)} fusion(f32[25,64,128]{2,1,0:T(8,128)} %broadcast.517.clone.3, s32[30]{0:T(128)S(1)} %get-tuple-element.126, f32[30,64,128]{2,1,0:T(8,128)} %fusion.81), kind=kCustom, calls=%fused_computation.23 | custom fusion | flops 245760 | bytes 2949240 | tf_op jit(solution)/shard_map/scatter-add | solution.py:31
  145.0 4.2 %slice_add_fusion.1 = f32[24,64,128]{2,1,0:T(8,128)} fusion(f32[25,64,128]{2,1,0:T(8,128)} %scatter_fusion.3, bf16[24,5,64,128]{3,2,1,0:T(8,128)(2,1)S(1)} %bitcast.261, bf16[24,5,128,128]{3,2,1,0:T(8,128)(2,1)} %param.16), kind=kOutput, calls=%fused_computation.40 | convolution fusion | flops 251854848 | bytes 7471104 | tf_op jit(solution)/shard_map/nscb,nsbd->ncd/dot_general | solution.py:29
  150.2 5.4 %scatter_fusion.4 = f32[25,64,128]{2,1,0:T(8,128)} fusion(f32[25,64,128]{2,1,0:T(8,128)} %broadcast.517.clone, s32[30]{0:T(128)S(1)} %get-tuple-element.126, f32[30,64,128]{2,1,0:T(8,128)} %fusion.14), kind=kCustom, calls=%fused_computation.24 | custom fusion | flops 245760 | bytes 2949240 | tf_op jit(solution)/shard_map/scatter-add | solution.py:31
  155.6 3.4 %slice_add_fusion = f32[24,64,128]{2,1,0:T(8,128)S(1)} fusion(f32[25,64,128]{2,1,0:T(8,128)} %scatter_fusion.4, bf16[24,5,64,128]{3,2,1,0:T(8,128)(2,1)S(1)} %bitcast.262, bf16[24,5,128,128]{3,2,1,0:T(8,128)(2,1)} %param.17), kind=kOutput, calls=%fused_computation.39 | convolution fusion | flops 251854848 | bytes 7471104 | tf_op jit(solution)/shard_map/nscb,nsbd->ncd/dot_general | solution.py:29
  161.8 5.5 %collective-permute-start.15 = (f32[2,4,24,128]{3,2,1,0:T(8,128)S(1)}, f32[2,4,24,128]{3,2,1,0:T(8,128)S(1)}, u32[]{:S(2)}, u32[]{:S(2)}) collective-permute-start(f32[2,4,24,128]{3,2,1,0:T(8,128)S(1)} %get-tuple-element.100), channel_id=1, source_target_pairs={{0,32},{32,64},{64,96},{96,128},{128,160},{160,192},{192,224},{224... | collective-permute-start | bytes 294920 | tf_op jit(solution)/shard_map/ppermute | solution.py:133
  168.6 1.7 collective-permute-start.17
  170.7 1.9 %collective-permute-start.19 = (f32[2,4,24,128]{3,2,1,0:T(8,128)S(1)}, f32[2,4,24,128]{3,2,1,0:T(8,128)S(1)}, u32[]{:S(2)}, u32[]{:S(2)}) collective-permute-start(f32[2,4,24,128]{3,2,1,0:T(8,128)S(1)} %get-tuple-element.103), channel_id=1, source_target_pairs={{0,160},{32,192},{64,224},{96,0},{128,32},{160,64},{192,96},{224,1... | collective-permute-start | bytes 294920 | tf_op jit(solution)/shard_map/ppermute | solution.py:133
  173.4 1.6 collective-permute-start.21
  175.0 3.6 %collective-permute-done.18 = f32[2,4,24,128]{3,2,1,0:T(8,128)S(1)} collective-permute-done((f32[2,4,24,128]{3,2,1,0:T(8,128)S(1)}, f32[2,4,24,128]{3,2,1,0:T(8,128)S(1)}, u32[]{:S(2)}, u32[]{:S(2)}) %collective-permute-start.18) | collective-permute-done | bytes 98336 | tf_op jit(solution)/shard_map/ppermute | solution.py:133
  (202 shorter events, 68.1 us)
Async XLA Ops:
  0.0 52.5 %copy-start = (bf16[1,2,24,128,128]{4,3,2,1,0:T(8,128)(2,1)S(1)}, bf16[1,2,24,128,128]{4,3,2,1,0:T(8,128)(2,1)}, u32[]{:S(2)}) copy-start(bf16[1,2,24,128,128]{4,3,2,1,0:T(8,128)(2,1)} %param.18) | copy-start | bytes 4718596
  7.3 23.3 %collective-permute-start.1 = (bf16[25,32,128]{2,1,0:T(8,128)(2,1)}, bf16[25,32,128]{2,1,0:T(8,128)(2,1)}, u32[]{:S(2)}, u32[]{:S(2)}) collective-permute-start(bf16[25,32,128]{2,1,0:T(8,128)(2,1)} %get-tuple-element.112), channel_id=1, source_target_pairs={{2,0},{3,1},{4,2},{5,3},{6,4},{7,5},{8,6},{9,7},{10,8},{11,9},{12,... | collective-permute-start | bytes 614408 | tf_op jit(solution)/shard_map/ppermute | solution.py:92
  14.5 17.7 %collective-permute-start = (bf16[25,32,128]{2,1,0:T(8,128)(2,1)}, bf16[25,32,128]{2,1,0:T(8,128)(2,1)}, u32[]{:S(2)}, u32[]{:S(2)}) collective-permute-start(bf16[25,32,128]{2,1,0:T(8,128)(2,1)} %get-tuple-element.115), channel_id=1, source_target_pairs={{1,0},{2,1},{3,2},{4,3},{5,4},{6,5},{7,6},{8,7},{9,8},{10,9},{11,1... | collective-permute-start | bytes 614408 | tf_op jit(solution)/shard_map/ppermute | solution.py:92
  15.6 18.6 %collective-permute-start.2 = (bf16[25,32,128]{2,1,0:T(8,128)(2,1)S(1)}, bf16[25,32,128]{2,1,0:T(8,128)(2,1)}, u32[]{:S(2)}, u32[]{:S(2)}) collective-permute-start(bf16[25,32,128]{2,1,0:T(8,128)(2,1)S(1)} %get-tuple-element.113), channel_id=1, source_target_pairs={{16,0},{17,1},{18,2},{19,3},{20,4},{21,5},{22,6},{23,7},{24,8},{25... | collective-permute-start | bytes 614408 | tf_op jit(solution)/shard_map/ppermute | solution.py:92
  16.8 19.8 %collective-permute-start.3 = (bf16[25,32,128]{2,1,0:T(8,128)(2,1)S(1)}, bf16[25,32,128]{2,1,0:T(8,128)(2,1)}, u32[]{:S(2)}, u32[]{:S(2)}) collective-permute-start(bf16[25,32,128]{2,1,0:T(8,128)(2,1)S(1)} %get-tuple-element.114), channel_id=1, source_target_pairs={{31,0},{0,1},{1,2},{2,3},{3,4},{4,5},{5,6},{6,7},{7,8},{8,9},{9,10... | collective-permute-start | bytes 614408 | tf_op jit(solution)/shard_map/ppermute | solution.py:92
  17.1 21.0 %collective-permute-start.4 = (bf16[25,32,128]{2,1,0:T(8,128)(2,1)S(1)}, bf16[25,32,128]{2,1,0:T(8,128)(2,1)}, u32[]{:S(2)}, u32[]{:S(2)}) collective-permute-start(bf16[25,32,128]{2,1,0:T(8,128)(2,1)S(1)} %get-tuple-element.111), channel_id=1, source_target_pairs={{30,0},{31,1},{0,2},{1,3},{2,4},{3,5},{4,6},{5,7},{6,8},{7,9},{8,1... | collective-permute-start | bytes 614408 | tf_op jit(solution)/shard_map/ppermute | solution.py:92
  24.8 19.3 %copy-start.1 = (bf16[30,128,128]{2,1,0:T(8,128)(2,1)}, bf16[30,128,128]{2,1,0:T(8,128)(2,1)S(1)}, u32[]{:S(2)}) copy-start(bf16[30,128,128]{2,1,0:T(8,128)(2,1)S(1)} %gather_fusion.6) | copy-start | bytes 2949124
  40.5 9.2 %copy-start.11 = (bf16[120,32,128]{2,1,0:T(8,128)(2,1)S(1)}, bf16[120,32,128]{2,1,0:T(8,128)(2,1)}, u32[]{:S(2)}) copy-start(bf16[120,32,128]{2,1,0:T(8,128)(2,1)} %gather_fusion) | copy-start | bytes 2949124
  55.8 19.5 %collective-permute-start.8 = (bf16[6,64,128]{2,1,0:T(8,128)(2,1)}, bf16[6,64,128]{2,1,0:T(8,128)(2,1)}, u32[]{:S(2)}, u32[]{:S(2)}) collective-permute-start(bf16[6,64,128]{2,1,0:T(8,128)(2,1)} %gather_fusion.11), channel_id=1, source_target_pairs={{31,0},{0,1},{1,2},{2,3},{3,4},{4,5},{5,6},{6,7},{7,8},{8,9},{9,10... | collective-permute-start | bytes 294920 | tf_op jit(solution)/shard_map/ppermute | solution.py:75
  55.8 13.9 %copy-start.16 = (s32[1024]{0:T(1024)}, s32[1024]{0:T(1024)S(1)}, u32[]{:S(2)}) copy-start(s32[1024]{0:T(1024)S(1)} %pad_clamp_fusion.2) | copy-start | bytes 12292
  57.0 17.4 %collective-permute-start.7 = (bf16[6,64,128]{2,1,0:T(8,128)(2,1)}, bf16[6,64,128]{2,1,0:T(8,128)(2,1)}, u32[]{:S(2)}, u32[]{:S(2)}) collective-permute-start(bf16[6,64,128]{2,1,0:T(8,128)(2,1)} %gather_fusion.10), channel_id=1, source_target_pairs={{16,0},{17,1},{18,2},{19,3},{20,4},{21,5},{22,6},{23,7},{24,8},{25... | collective-permute-start | bytes 294920 | tf_op jit(solution)/shard_map/ppermute | solution.py:75
  59.3 10.4 %copy-start.17 = (s32[1024]{0:T(1024)}, s32[1024]{0:T(1024)S(1)}, u32[]{:S(2)}) copy-start(s32[1024]{0:T(1024)S(1)} %pad_clamp_fusion.3) | copy-start | bytes 12292
  60.5 12.9 %collective-permute-start.6 = (bf16[6,64,128]{2,1,0:T(8,128)(2,1)}, bf16[6,64,128]{2,1,0:T(8,128)(2,1)}, u32[]{:S(2)}, u32[]{:S(2)}) collective-permute-start(bf16[6,64,128]{2,1,0:T(8,128)(2,1)} %gather_fusion.9), channel_id=1, source_target_pairs={{2,0},{3,1},{4,2},{5,3},{6,4},{7,5},{8,6},{9,7},{10,8},{11,9},{12,... | collective-permute-start | bytes 294920 | tf_op jit(solution)/shard_map/ppermute | solution.py:75
  66.3 6.2 %collective-permute-start.5 = (bf16[6,64,128]{2,1,0:T(8,128)(2,1)}, bf16[6,64,128]{2,1,0:T(8,128)(2,1)}, u32[]{:S(2)}, u32[]{:S(2)}) collective-permute-start(bf16[6,64,128]{2,1,0:T(8,128)(2,1)} %gather_fusion.8), channel_id=1, source_target_pairs={{1,0},{2,1},{3,2},{4,3},{5,4},{6,5},{7,6},{8,7},{9,8},{10,9},{11,1... | collective-permute-start | bytes 294920 | tf_op jit(solution)/shard_map/ppermute | solution.py:75
  69.7 7.4 %collective-permute-start.9 = (bf16[6,64,128]{2,1,0:T(8,128)(2,1)}, bf16[6,64,128]{2,1,0:T(8,128)(2,1)}, u32[]{:S(2)}, u32[]{:S(2)}) collective-permute-start(bf16[6,64,128]{2,1,0:T(8,128)(2,1)} %gather_fusion.12), channel_id=1, source_target_pairs={{30,0},{31,1},{0,2},{1,3},{2,4},{3,5},{4,6},{5,7},{6,8},{7,9},{8,1... | collective-permute-start | bytes 294920 | tf_op jit(solution)/shard_map/ppermute | solution.py:75
  72.4 8.1 %copy-start.6 = (bf16[30,128,128]{2,1,0:T(8,128)(2,1)S(1)}, bf16[30,128,128]{2,1,0:T(8,128)(2,1)}, u32[]{:S(2)}) copy-start(bf16[30,128,128]{2,1,0:T(8,128)(2,1)} %gather_fusion.13) | copy-start | bytes 2949124
  98.9 3.4 %copy-start.13 = (f32[24,64,128]{2,1,0:T(8,128)S(1)}, f32[24,64,128]{2,1,0:T(8,128)}, u32[]{:S(2)}) copy-start(f32[24,64,128]{2,1,0:T(8,128)} %slice_add_fusion.3) | copy-start | bytes 2359300
  106.4 24.8 %collective-permute-start.10 = (bf16[6,64,128]{2,1,0:T(8,128)(2,1)}, bf16[6,64,128]{2,1,0:T(8,128)(2,1)}, u32[]{:S(2)}, u32[]{:S(2)}) collective-permute-start(bf16[6,64,128]{2,1,0:T(8,128)(2,1)} %gather_fusion.15), channel_id=1, source_target_pairs={{1,0},{2,1},{3,2},{4,3},{5,4},{6,5},{7,6},{8,7},{9,8},{10,9},{11,1... | collective-permute-start | bytes 294920 | tf_op jit(solution)/shard_map/ppermute | solution.py:75
  113.5 20.4 %collective-permute-start.13 = (bf16[6,64,128]{2,1,0:T(8,128)(2,1)}, bf16[6,64,128]{2,1,0:T(8,128)(2,1)}, u32[]{:S(2)}, u32[]{:S(2)}) collective-permute-start(bf16[6,64,128]{2,1,0:T(8,128)(2,1)} %gather_fusion.18), channel_id=1, source_target_pairs={{31,0},{0,1},{1,2},{2,3},{3,4},{4,5},{5,6},{6,7},{7,8},{8,9},{9,10... | collective-permute-start | bytes 294920 | tf_op jit(solution)/shard_map/ppermute | solution.py:75
  113.8 19.2 %collective-permute-start.12 = (bf16[6,64,128]{2,1,0:T(8,128)(2,1)}, bf16[6,64,128]{2,1,0:T(8,128)(2,1)}, u32[]{:S(2)}, u32[]{:S(2)}) collective-permute-start(bf16[6,64,128]{2,1,0:T(8,128)(2,1)} %gather_fusion.17), channel_id=1, source_target_pairs={{16,0},{17,1},{18,2},{19,3},{20,4},{21,5},{22,6},{23,7},{24,8},{25... | collective-permute-start | bytes 294920 | tf_op jit(solution)/shard_map/ppermute | solution.py:75
  119.1 13.1 %collective-permute-start.11 = (bf16[6,64,128]{2,1,0:T(8,128)(2,1)}, bf16[6,64,128]{2,1,0:T(8,128)(2,1)}, u32[]{:S(2)}, u32[]{:S(2)}) collective-permute-start(bf16[6,64,128]{2,1,0:T(8,128)(2,1)} %gather_fusion.16), channel_id=1, source_target_pairs={{2,0},{3,1},{4,2},{5,3},{6,4},{7,5},{8,6},{9,7},{10,8},{11,9},{12,... | collective-permute-start | bytes 294920 | tf_op jit(solution)/shard_map/ppermute | solution.py:75
  126.6 8.3 %collective-permute-start.14 = (bf16[6,64,128]{2,1,0:T(8,128)(2,1)}, bf16[6,64,128]{2,1,0:T(8,128)(2,1)}, u32[]{:S(2)}, u32[]{:S(2)}) collective-permute-start(bf16[6,64,128]{2,1,0:T(8,128)(2,1)} %gather_fusion.19), channel_id=1, source_target_pairs={{30,0},{31,1},{0,2},{1,3},{2,4},{3,5},{4,6},{5,7},{6,8},{7,9},{8,1... | collective-permute-start | bytes 294920 | tf_op jit(solution)/shard_map/ppermute | solution.py:75
  128.5 7.3 %copy-start.2 = (bf16[30,128,128]{2,1,0:T(8,128)(2,1)S(1)}, bf16[30,128,128]{2,1,0:T(8,128)(2,1)}, u32[]{:S(2)}) copy-start(bf16[30,128,128]{2,1,0:T(8,128)(2,1)} %copy-done.1) | copy-start | bytes 2949124
  131.1 6.1 %copy-start.7 = (bf16[30,128,128]{2,1,0:T(8,128)(2,1)S(1)}, bf16[30,128,128]{2,1,0:T(8,128)(2,1)}, u32[]{:S(2)}) copy-start(bf16[30,128,128]{2,1,0:T(8,128)(2,1)} %gather_fusion.13) | copy-start | bytes 2949124
  155.6 3.4 %copy-start.12 = (f32[24,64,128]{2,1,0:T(8,128)S(1)}, f32[24,64,128]{2,1,0:T(8,128)}, u32[]{:S(2)}) copy-start(f32[24,64,128]{2,1,0:T(8,128)} %slice_add_fusion.1) | copy-start | bytes 2359300
  161.8 10.8 %collective-permute-start.15 = (f32[2,4,24,128]{3,2,1,0:T(8,128)S(1)}, f32[2,4,24,128]{3,2,1,0:T(8,128)S(1)}, u32[]{:S(2)}, u32[]{:S(2)}) collective-permute-start(f32[2,4,24,128]{3,2,1,0:T(8,128)S(1)} %get-tuple-element.100), channel_id=1, source_target_pairs={{0,32},{32,64},{64,96},{96,128},{128,160},{160,192},{192,224},{224... | collective-permute-start | bytes 294920 | tf_op jit(solution)/shard_map/ppermute | solution.py:133
  167.3 6.1 %collective-permute-start.16 = (f32[2,4,24,128]{3,2,1,0:T(8,128)S(1)}, f32[2,4,24,128]{3,2,1,0:T(8,128)S(1)}, u32[]{:S(2)}, u32[]{:S(2)}) collective-permute-start(f32[2,4,24,128]{3,2,1,0:T(8,128)S(1)} %get-tuple-element.106), channel_id=1, source_target_pairs={{0,64},{32,96},{64,128},{96,160},{128,192},{160,224},{192,0},{224,... | collective-permute-start | bytes 294920 | tf_op jit(solution)/shard_map/ppermute | solution.py:133
  168.6 6.4 %collective-permute-start.17 = (f32[2,4,24,128]{3,2,1,0:T(8,128)S(1)}, f32[2,4,24,128]{3,2,1,0:T(8,128)S(1)}, u32[]{:S(2)}, u32[]{:S(2)}) collective-permute-start(f32[2,4,24,128]{3,2,1,0:T(8,128)S(1)} %get-tuple-element.105), channel_id=1, source_target_pairs={{0,96},{32,128},{64,160},{96,192},{128,224},{160,0},{192,32},{224,... | collective-permute-start | bytes 294920 | tf_op jit(solution)/shard_map/ppermute | solution.py:133
  170.3 8.3 %collective-permute-start.18 = (f32[2,4,24,128]{3,2,1,0:T(8,128)S(1)}, f32[2,4,24,128]{3,2,1,0:T(8,128)S(1)}, u32[]{:S(2)}, u32[]{:S(2)}) collective-permute-start(f32[2,4,24,128]{3,2,1,0:T(8,128)S(1)} %get-tuple-element.104), channel_id=1, source_target_pairs={{0,128},{32,160},{64,192},{96,224},{128,0},{160,32},{192,64},{224,... | collective-permute-start | bytes 294920 | tf_op jit(solution)/shard_map/ppermute | solution.py:133
  170.7 8.7 %collective-permute-start.19 = (f32[2,4,24,128]{3,2,1,0:T(8,128)S(1)}, f32[2,4,24,128]{3,2,1,0:T(8,128)S(1)}, u32[]{:S(2)}, u32[]{:S(2)}) collective-permute-start(f32[2,4,24,128]{3,2,1,0:T(8,128)S(1)} %get-tuple-element.103), channel_id=1, source_target_pairs={{0,160},{32,192},{64,224},{96,0},{128,32},{160,64},{192,96},{224,1... | collective-permute-start | bytes 294920 | tf_op jit(solution)/shard_map/ppermute | solution.py:133
  172.6 6.7 %collective-permute-start.20 = (f32[2,4,24,128]{3,2,1,0:T(8,128)S(1)}, f32[2,4,24,128]{3,2,1,0:T(8,128)S(1)}, u32[]{:S(2)}, u32[]{:S(2)}) collective-permute-start(f32[2,4,24,128]{3,2,1,0:T(8,128)S(1)} %get-tuple-element.102), channel_id=1, source_target_pairs={{0,192},{32,224},{64,0},{96,32},{128,64},{160,96},{192,128},{224,1... | collective-permute-start | bytes 294920 | tf_op jit(solution)/shard_map/ppermute | solution.py:133
  173.4 6.8 %collective-permute-start.21 = (f32[2,4,24,128]{3,2,1,0:T(8,128)S(1)}, f32[2,4,24,128]{3,2,1,0:T(8,128)S(1)}, u32[]{:S(2)}, u32[]{:S(2)}) collective-permute-start(f32[2,4,24,128]{3,2,1,0:T(8,128)S(1)} %get-tuple-element.101), channel_id=1, source_target_pairs={{0,224},{32,0},{64,32},{96,64},{128,96},{160,128},{192,160},{224,1... | collective-permute-start | bytes 294920 | tf_op jit(solution)/shard_map/ppermute | solution.py:133
  (10 other events, 17.9 us)

commit v6 on v4

--- a/solution.py
+++ b/solution.py
@@ -109,10 +109,17 @@
         ]
     )
     weighted = jnp.transpose(weighted / node_count, (2, 0, 3, 1, 4))
-    total = lax.dynamic_index_in_dim(weighted, node_index, 0, keepdims=False)
-    for offset in range(1, node_count):
-        chunk = lax.dynamic_index_in_dim(weighted, (node_index + offset) % node_count, 0, keepdims=False)
-        perm = [(j, (j + offset) % node_count) for j in range(node_count)]
+    groups = node_count // 2
+    core = node_index % 2
+    group = node_index // 2
+    paired = weighted.reshape((groups, 2) + weighted.shape[1:])
+    keep = lax.dynamic_index_in_dim(paired, core, 1, keepdims=False)
+    other = lax.dynamic_index_in_dim(paired, 1 - core, 1, keepdims=False)
+    partial = keep + lax.ppermute(other, "node", [(j, j ^ 1) for j in range(node_count)])
+    total = lax.dynamic_index_in_dim(partial, group, 0, keepdims=False)
+    for offset in range(1, groups):
+        chunk = lax.dynamic_index_in_dim(partial, (group + offset) % groups, 0, keepdims=False)
+        perm = [(j, ((j // 2 + offset) % groups) * 2 + j % 2) for j in range(node_count)]
         total = total + lax.ppermute(chunk, "node", perm)
     return total
 

time: 122 us -> 119 us (0.975); the launches traced: 120 us -> 119 us
  starting transfers between devices: 46 us -> 40.8 us
  waiting for transfers between devices: 22.2 us -> 24.8 us
  other arithmetic: 6.34 us -> 8.16 us
    ppermute x7 -> x3, starting transfers between devices: 14.9 us -> 3.85 us  [per_device(): total = total + lax.ppermute(chunk, 'node', perm)]
    ppermute x0 -> x1, starting transfers between devices: none -> 4.94 us  [per_device(): lax.ppermute(other, 'node', [(j, j ^ 1) for j in range(node_count)])]
    ppermute x7 -> x3, waiting for transfers between devices: 5.25 us -> 7.15 us  [per_device(): total = total + lax.ppermute(chunk, 'node', perm)]
    concatenate x2 -> x0, local copies, waits for them, and re-layouts: 1.82 us -> none  [per_device(): iterate = iterate + jnp.concatenate([update_real, update_imag], axis=1)]
    ppermute x10, waiting for transfers between devices: 6.57 us -> 4.78 us  [fetch_halo(): lax.ppermute(vector[asked_for[which]], 'rows', from_partner(offset))]
    ppermute x0 -> x1, waiting for transfers between devices: none -> 1.35 us  [per_device(): lax.ppermute(other, 'node', [(j, j ^ 1) for j in range(node_count)])]
    unnamed x42 -> x43, local copies, waits for them, and re-layouts: 15.1 us -> 14.4 us
  transfers between devices with their start and end apart: 22 -> 19, of which waited for: 10 -> 9; matrix products, arithmetic and copies ran while one was open for 13% -> 11% of each run, Pallas kernels for 0% -> 0%
where the time goes in v6:
time: 119 us
  starting transfers between devices  40.8 us (34%)
  local copies, waits for them, and re-layouts  32.1 us (27%)
  waiting for transfers between devices  24.8 us (21%)
  matrix products  12.2 us (10%)
  other arithmetic  8.16 us (7%)
    ppermute x10, starting transfers between devices, fetch_halo(): lax.ppermute(vector[asked_for[which]], 'rows', from_partner(offset))  19.1 us
    unnamed x43, local copies, waits for them, and re-layouts  14.4 us
    ppermute x5, starting transfers between devices, per_device(): lax.ppermute(jnp.concatenate([cols_major, tag], axis=0), 'rows', from_par...  12.9 us
    ppermute x5, waiting for transfers between devices, per_device(): lax.ppermute(jnp.concatenate([cols_major, tag], axis=0), 'rows', from_par...  11.5 us
    ppermute x3, waiting for transfers between devices, per_device(): total = total + lax.ppermute(chunk, 'node', perm)  7.15 us
    dot_general x3, matrix products, apply_pair(): jnp.einsum('nscb,nsbd->ncd', picked, first, preferred_element_type=jnp.fl...  6.96 us
    gather x3, local copies, waits for them, and re-layouts, apply_pair(): picked = extended[slot_index]  6.21 us
    gather x10, local copies, waits for them, and re-layouts, fetch_halo(): vector[asked_for[which]]  5.9 us
  transfers between devices with their start and end apart: 19, of which 9 were waited for; matrix products, arithmetic and copies ran while one was open for 11% of the time, Pallas kernels for 0%

profile of v6, /device:TPU:3, one launch (start us, length us, event | category | flops | bytes accessed | tf_op | source)
XLA Modules:
  0.0 118.8 jit_solution(15663561623120764421)
XLA Ops:
  0.0 0.9 copy.142
  4.5 7.7 %collective-permute-start.1 = (bf16[25,32,128]{2,1,0:T(8,128)(2,1)S(1)}, bf16[25,32,128]{2,1,0:T(8,128)(2,1)}, u32[]{:S(2)}, u32[]{:S(2)}) collective-permute-start(bf16[25,32,128]{2,1,0:T(8,128)(2,1)S(1)} %get-tuple-element.106), channel_id=1, source_target_pairs={{2,0},{3,1},{4,2},{5,3},{6,4},{7,5},{8,6},{9,7},{10,8},{11,9},{12,... | collective-permute-start | bytes 614408 | tf_op jit(solution)/shard_map/ppermute | solution.py:78
  12.2 1.2 collective-permute-start.2
  13.4 1.5 %collective-permute-start.3 = (bf16[25,32,128]{2,1,0:T(8,128)(2,1)S(1)}, bf16[25,32,128]{2,1,0:T(8,128)(2,1)S(1)}, u32[]{:S(2)}, u32[]{:S(2)}) collective-permute-start(bf16[25,32,128]{2,1,0:T(8,128)(2,1)S(1)} %get-tuple-element.105), channel_id=1, source_target_pairs={{31,0},{0,1},{1,2},{2,3},{3,4},{4,5},{5,6},{6,7},{7,8},{8,9},{9,10... | collective-permute-start | bytes 614408 | tf_op jit(solution)/shard_map/ppermute | solution.py:78
  14.9 2.5 %collective-permute-start.4 = (bf16[25,32,128]{2,1,0:T(8,128)(2,1)S(1)}, bf16[25,32,128]{2,1,0:T(8,128)(2,1)}, u32[]{:S(2)}, u32[]{:S(2)}) collective-permute-start(bf16[25,32,128]{2,1,0:T(8,128)(2,1)S(1)} %get-tuple-element.103), channel_id=1, source_target_pairs={{30,0},{31,1},{0,2},{1,3},{2,4},{3,5},{4,6},{5,7},{6,8},{7,9},{8,1... | collective-permute-start | bytes 614408 | tf_op jit(solution)/shard_map/ppermute | solution.py:78
  19.2 5.2 %collective-permute-done.1 = bf16[25,32,128]{2,1,0:T(8,128)(2,1)} collective-permute-done((bf16[25,32,128]{2,1,0:T(8,128)(2,1)S(1)}, bf16[25,32,128]{2,1,0:T(8,128)(2,1)}, u32[]{:S(2)}, u32[]{:S(2)}) %collective-permute-start.1) | collective-permute-done | bytes 204832 | tf_op jit(solution)/shard_map/ppermute | solution.py:78
  24.4 1.6 %slice_dynamic-update-slice_fusion.3 = bf16[144,32,128]{2,1,0:T(8,128)(2,1)} fusion(bf16[144,32,128]{2,1,0:T(8,128)(2,1)} %slice_dynamic-update-slice_fusion.4, bf16[25,32,128]{2,1,0:T(8,128)(2,1)} %collective-permute-done.1), kind=kLoop, calls=%fused_computation.83 | loop fusion | bytes 393216
  27.7 5.9 %collective-permute-done.4 = bf16[25,32,128]{2,1,0:T(8,128)(2,1)} collective-permute-done((bf16[25,32,128]{2,1,0:T(8,128)(2,1)S(1)}, bf16[25,32,128]{2,1,0:T(8,128)(2,1)}, u32[]{:S(2)}, u32[]{:S(2)}) %collective-permute-start.4) | collective-permute-done | bytes 204832 | tf_op jit(solution)/shard_map/ppermute | solution.py:78
  33.7 1.6 %slice_dynamic-update-slice_fusion = bf16[144,32,128]{2,1,0:T(8,128)(2,1)} fusion(bf16[144,32,128]{2,1,0:T(8,128)(2,1)} %slice_dynamic-update-slice_fusion.1, bf16[25,32,128]{2,1,0:T(8,128)(2,1)} %collective-permute-done.4), kind=kLoop, calls=%fused_computation.80 | loop fusion | bytes 393216 | tf_op jit(solution)/shard_map/concatenate | solution.py:81
  35.3 2.0 %gather_fusion = bf16[120,32,128]{2,1,0:T(8,128)(2,1)S(1)} fusion(bf16[144,32,128]{2,1,0:T(8,128)(2,1)} %slice_dynamic-update-slice_fusion, s32[1024]{0:T(1024)S(1)} %pad_clamp_fusion.6), kind=kCustom, calls=%fused_computation | custom fusion | bytes 1966560 | tf_op jit(solution)/shard_map/gather | solution.py:24
  37.3 2.8 %convolution_bitcast_fusion.4 = f32[24,32,128]{2,1,0:T(8,128)S(1)} fusion(bf16[24,5,32,128]{3,2,1,0:T(8,128)(2,1)S(1)} %bitcast.201, bf16[24,5,128,128]{3,2,1,0:T(8,128)(2,1)} %param.16), kind=kOutput, calls=%fused_computation.17 | convolution fusion | flops 125829120 | bytes 5308416 | tf_op jit(solution)/shard_map/nscb,nsbd->ncd/dot_general | solution.py:25
  44.2 4.3 %collective-permute-start.6 = (bf16[6,64,128]{2,1,0:T(8,128)(2,1)S(1)}, bf16[6,64,128]{2,1,0:T(8,128)(2,1)S(1)}, u32[]{:S(2)}, u32[]{:S(2)}) collective-permute-start(bf16[6,64,128]{2,1,0:T(8,128)(2,1)S(1)} %gather_fusion.2), channel_id=1, source_target_pairs={{2,0},{3,1},{4,2},{5,3},{6,4},{7,5},{8,6},{9,7},{10,8},{11,9},{12,... | collective-permute-start | bytes 294920 | tf_op jit(solution)/shard_map/ppermute | solution.py:66
  49.8 1.3 %collective-permute-start.8 = (bf16[6,64,128]{2,1,0:T(8,128)(2,1)S(1)}, bf16[6,64,128]{2,1,0:T(8,128)(2,1)S(1)}, u32[]{:S(2)}, u32[]{:S(2)}) collective-permute-start(bf16[6,64,128]{2,1,0:T(8,128)(2,1)S(1)} %gather_fusion.4), channel_id=1, source_target_pairs={{31,0},{0,1},{1,2},{2,3},{3,4},{4,5},{5,6},{6,7},{7,8},{8,9},{9,10... | collective-permute-start | bytes 294920 | tf_op jit(solution)/shard_map/ppermute | solution.py:66
  52.4 4.7 %collective-permute-start.9 = (bf16[6,64,128]{2,1,0:T(8,128)(2,1)S(1)}, bf16[6,64,128]{2,1,0:T(8,128)(2,1)S(1)}, u32[]{:S(2)}, u32[]{:S(2)}) collective-permute-start(bf16[6,64,128]{2,1,0:T(8,128)(2,1)S(1)} %gather_fusion.5), channel_id=1, source_target_pairs={{30,0},{31,1},{0,2},{1,3},{2,4},{3,5},{4,6},{5,7},{6,8},{7,9},{8,1... | collective-permute-start | bytes 294920 | tf_op jit(solution)/shard_map/ppermute | solution.py:66
  59.7 2.5 %collective-permute-done.9 = bf16[6,64,128]{2,1,0:T(8,128)(2,1)S(1)} collective-permute-done((bf16[6,64,128]{2,1,0:T(8,128)(2,1)S(1)}, bf16[6,64,128]{2,1,0:T(8,128)(2,1)S(1)}, u32[]{:S(2)}, u32[]{:S(2)}) %collective-permute-start.9) | collective-permute-done | bytes 98336 | tf_op jit(solution)/shard_map/ppermute | solution.py:66
  62.8 2.1 %gather_fusion.6 = bf16[120,64,128]{2,1,0:T(8,128)(2,1)S(1)} fusion(bf16[54,64,128]{2,1,0:T(8,128)(2,1)} %constant_dynamic-update-slice_fusion.1, s32[1024]{0:T(1024)S(1)} %pad_clamp_fusion), kind=kCustom, calls=%fused_computation.6 | custom fusion | bytes 3932640 | tf_op jit(solution)/shard_map/gather | solution.py:24
  65.0 3.2 %convolution_bitcast_fusion.3 = f32[24,64,128]{2,1,0:T(8,128)S(1)} fusion(bf16[24,5,64,128]{3,2,1,0:T(8,128)(2,1)S(1)} %bitcast.196, bf16[24,5,128,128]{3,2,1,0:T(8,128)(2,1)} %param.16), kind=kOutput, calls=%fused_computation.16 | convolution fusion | flops 251658240 | bytes 6684672 | tf_op jit(solution)/shard_map/nscb,nsbd->ncd/dot_general | solution.py:25
  68.2 0.9 convolution_bitcast_fusion.2
  70.0 1.0 copy-done.4
  71.0 1.1 fusion.6
  75.7 3.6 %collective-permute-start.12 = (bf16[6,64,128]{2,1,0:T(8,128)(2,1)S(1)}, bf16[6,64,128]{2,1,0:T(8,128)(2,1)S(1)}, u32[]{:S(2)}, u32[]{:S(2)}) collective-permute-start(bf16[6,64,128]{2,1,0:T(8,128)(2,1)S(1)} %gather_fusion.9), channel_id=1, source_target_pairs={{16,0},{17,1},{18,2},{19,3},{20,4},{21,5},{22,6},{23,7},{24,8},{25... | collective-permute-start | bytes 294920 | tf_op jit(solution)/shard_map/ppermute | solution.py:66
  79.4 2.0 %collective-permute-start.13 = (bf16[6,64,128]{2,1,0:T(8,128)(2,1)S(1)}, bf16[6,64,128]{2,1,0:T(8,128)(2,1)S(1)}, u32[]{:S(2)}, u32[]{:S(2)}) collective-permute-start(bf16[6,64,128]{2,1,0:T(8,128)(2,1)S(1)} %gather_fusion.10), channel_id=1, source_target_pairs={{31,0},{0,1},{1,2},{2,3},{3,4},{4,5},{5,6},{6,7},{7,8},{8,9},{9,10... | collective-permute-start | bytes 294920 | tf_op jit(solution)/shard_map/ppermute | solution.py:66
  81.3 2.4 %collective-permute-start.14 = (bf16[6,64,128]{2,1,0:T(8,128)(2,1)S(1)}, bf16[6,64,128]{2,1,0:T(8,128)(2,1)S(1)}, u32[]{:S(2)}, u32[]{:S(2)}) collective-permute-start(bf16[6,64,128]{2,1,0:T(8,128)(2,1)S(1)} %gather_fusion.11), channel_id=1, source_target_pairs={{30,0},{31,1},{0,2},{1,3},{2,4},{3,5},{4,6},{5,7},{6,8},{7,9},{8,1... | collective-permute-start | bytes 294920 | tf_op jit(solution)/shard_map/ppermute | solution.py:66
  87.1 2.3 %collective-permute-done.14 = bf16[6,64,128]{2,1,0:T(8,128)(2,1)S(1)} collective-permute-done((bf16[6,64,128]{2,1,0:T(8,128)(2,1)S(1)}, bf16[6,64,128]{2,1,0:T(8,128)(2,1)S(1)}, u32[]{:S(2)}, u32[]{:S(2)}) %collective-permute-start.14) | collective-permute-done | bytes 98336 | tf_op jit(solution)/shard_map/ppermute | solution.py:66
  90.0 2.1 %gather_fusion.12 = bf16[120,64,128]{2,1,0:T(8,128)(2,1)S(1)} fusion(bf16[54,64,128]{2,1,0:T(8,128)(2,1)} %constant_dynamic-update-slice_fusion.7, s32[1024]{0:T(1024)S(1)} %pad_clamp_fusion), kind=kCustom, calls=%fused_computation.12 | custom fusion | bytes 3932640 | tf_op jit(solution)/shard_map/gather | solution.py:24
  92.1 3.2 %convolution_bitcast_fusion = f32[24,64,128]{2,1,0:T(8,128)S(1)} fusion(bf16[24,5,64,128]{3,2,1,0:T(8,128)(2,1)S(1)} %bitcast.194, bf16[24,5,128,128]{3,2,1,0:T(8,128)(2,1)} %param.17), kind=kOutput, calls=%fused_computation.13 | convolution fusion | flops 251658240 | bytes 6684672 | tf_op jit(solution)/shard_map/nscb,nsbd->ncd/dot_general | solution.py:28
  100.7 4.9 %collective-permute-start.15 = (f32[4,2,4,24,128]{4,3,2,1,0:T(8,128)S(1)}, f32[4,2,4,24,128]{4,3,2,1,0:T(8,128)S(1)}, u32[]{:S(2)}, u32[]{:S(2)}) collective-permute-start(f32[4,2,4,24,128]{4,3,2,1,0:T(8,128)S(1)} %bitcast.206), channel_id=1, source_target_pairs={{0,32},{32,0},{64,96},{96,64},{128,160},{160,128},{192,224},{224,1... | collective-permute-start | bytes 1179656 | tf_op jit(solution)/shard_map/ppermute | solution.py:118
  105.6 1.3 %collective-permute-done.15 = f32[4,2,4,24,128]{4,3,2,1,0:T(8,128)S(1)} collective-permute-done((f32[4,2,4,24,128]{4,3,2,1,0:T(8,128)S(1)}, f32[4,2,4,24,128]{4,3,2,1,0:T(8,128)S(1)}, u32[]{:S(2)}, u32[]{:S(2)}) %collective-permute-start.15) | collective-permute-done | bytes 393248 | tf_op jit(solution)/shard_map/ppermute | solution.py:118
  107.2 2.8 %collective-permute-start.18 = (f32[2,4,24,128]{3,2,1,0:T(8,128)S(1)}, f32[2,4,24,128]{3,2,1,0:T(8,128)S(1)}, u32[]{:S(2)}, u32[]{:S(2)}) collective-permute-start(f32[2,4,24,128]{3,2,1,0:T(8,128)S(1)} %get-tuple-element.101), channel_id=1, source_target_pairs={{0,192},{32,224},{64,0},{96,32},{128,64},{160,96},{192,128},{224,1... | collective-permute-start | bytes 294920 | tf_op jit(solution)/shard_map/ppermute | solution.py:123
  111.0 2.7 %collective-permute-done.18 = f32[2,4,24,128]{3,2,1,0:T(8,128)S(1)} collective-permute-done((f32[2,4,24,128]{3,2,1,0:T(8,128)S(1)}, f32[2,4,24,128]{3,2,1,0:T(8,128)S(1)}, u32[]{:S(2)}, u32[]{:S(2)}) %collective-permute-start.18) | collective-permute-done | bytes 98336 | tf_op jit(solution)/shard_map/ppermute | solution.py:123
  113.7 1.3 %collective-permute-done.17 = f32[2,4,24,128]{3,2,1,0:T(8,128)S(1)} collective-permute-done((f32[2,4,24,128]{3,2,1,0:T(8,128)S(1)}, f32[2,4,24,128]{3,2,1,0:T(8,128)S(1)}, u32[]{:S(2)}, u32[]{:S(2)}) %collective-permute-start.17) | collective-permute-done | bytes 98336 | tf_op jit(solution)/shard_map/ppermute | solution.py:123
  115.0 3.1 %collective-permute-done.16 = f32[2,4,24,128]{3,2,1,0:T(8,128)S(1)} collective-permute-done((f32[2,4,24,128]{3,2,1,0:T(8,128)S(1)}, f32[2,4,24,128]{3,2,1,0:T(8,128)S(1)}, u32[]{:S(2)}, u32[]{:S(2)}) %collective-permute-start.16) | collective-permute-done | bytes 98336 | tf_op jit(solution)/shard_map/ppermute | solution.py:123
  (142 shorter events, 32.2 us)
Async XLA Ops:
  0.0 40.2 %copy-start = (bf16[1,2,24,128,128]{4,3,2,1,0:T(8,128)(2,1)S(1)}, bf16[1,2,24,128,128]{4,3,2,1,0:T(8,128)(2,1)}, u32[]{:S(2)}) copy-start(bf16[1,2,24,128,128]{4,3,2,1,0:T(8,128)(2,1)} %param.18) | copy-start | bytes 4718596
  0.0 4.2 %copy-start.10 = (bf16[32,24,128]{2,1,0:T(8,128)(2,1)S(1)}, bf16[32,24,128]{2,1,0:T(8,128)(2,1)}, u32[]{:S(2)}) copy-start(bf16[32,24,128]{2,1,0:T(8,128)(2,1)} %param.15) | copy-start | bytes 589828
  4.4 14.0 %collective-permute-start = (bf16[25,32,128]{2,1,0:T(8,128)(2,1)S(1)}, bf16[25,32,128]{2,1,0:T(8,128)(2,1)S(1)}, u32[]{:S(2)}, u32[]{:S(2)}) collective-permute-start(bf16[25,32,128]{2,1,0:T(8,128)(2,1)S(1)} %get-tuple-element.107), channel_id=1, source_target_pairs={{1,0},{2,1},{3,2},{4,3},{5,4},{6,5},{7,6},{8,7},{9,8},{10,9},{11,1... | collective-permute-start | bytes 614408 | tf_op jit(solution)/shard_map/ppermute | solution.py:78
  4.5 19.8 %collective-permute-start.1 = (bf16[25,32,128]{2,1,0:T(8,128)(2,1)S(1)}, bf16[25,32,128]{2,1,0:T(8,128)(2,1)}, u32[]{:S(2)}, u32[]{:S(2)}) collective-permute-start(bf16[25,32,128]{2,1,0:T(8,128)(2,1)S(1)} %get-tuple-element.106), channel_id=1, source_target_pairs={{2,0},{3,1},{4,2},{5,3},{6,4},{7,5},{8,6},{9,7},{10,8},{11,9},{12,... | collective-permute-start | bytes 614408 | tf_op jit(solution)/shard_map/ppermute | solution.py:78
  12.2 14.2 %collective-permute-start.2 = (bf16[25,32,128]{2,1,0:T(8,128)(2,1)S(1)}, bf16[25,32,128]{2,1,0:T(8,128)(2,1)S(1)}, u32[]{:S(2)}, u32[]{:S(2)}) collective-permute-start(bf16[25,32,128]{2,1,0:T(8,128)(2,1)S(1)} %get-tuple-element.104), channel_id=1, source_target_pairs={{16,0},{17,1},{18,2},{19,3},{20,4},{21,5},{22,6},{23,7},{24,8},{25... | collective-permute-start | bytes 614408 | tf_op jit(solution)/shard_map/ppermute | solution.py:78
  13.4 13.7 %collective-permute-start.3 = (bf16[25,32,128]{2,1,0:T(8,128)(2,1)S(1)}, bf16[25,32,128]{2,1,0:T(8,128)(2,1)S(1)}, u32[]{:S(2)}, u32[]{:S(2)}) collective-permute-start(bf16[25,32,128]{2,1,0:T(8,128)(2,1)S(1)} %get-tuple-element.105), channel_id=1, source_target_pairs={{31,0},{0,1},{1,2},{2,3},{3,4},{4,5},{5,6},{6,7},{7,8},{8,9},{9,10... | collective-permute-start | bytes 614408 | tf_op jit(solution)/shard_map/ppermute | solution.py:78
  14.9 18.8 %collective-permute-start.4 = (bf16[25,32,128]{2,1,0:T(8,128)(2,1)S(1)}, bf16[25,32,128]{2,1,0:T(8,128)(2,1)}, u32[]{:S(2)}, u32[]{:S(2)}) collective-permute-start(bf16[25,32,128]{2,1,0:T(8,128)(2,1)S(1)} %get-tuple-element.103), channel_id=1, source_target_pairs={{30,0},{31,1},{0,2},{1,3},{2,4},{3,5},{4,6},{5,7},{6,8},{7,9},{8,1... | collective-permute-start | bytes 614408 | tf_op jit(solution)/shard_map/ppermute | solution.py:78
  40.2 2.1 %copy-start.6 = (f32[24,32,128]{2,1,0:T(8,128)}, f32[24,32,128]{2,1,0:T(8,128)S(1)}, u32[]{:S(2)}) copy-start(f32[24,32,128]{2,1,0:T(8,128)S(1)} %convolution_bitcast_fusion.4) | copy-start | bytes 1179652
  40.5 0.9 copy-start.3
  43.5 13.6 %collective-permute-start.5 = (bf16[6,64,128]{2,1,0:T(8,128)(2,1)S(1)}, bf16[6,64,128]{2,1,0:T(8,128)(2,1)S(1)}, u32[]{:S(2)}, u32[]{:S(2)}) collective-permute-start(bf16[6,64,128]{2,1,0:T(8,128)(2,1)S(1)} %gather_fusion.1), channel_id=1, source_target_pairs={{1,0},{2,1},{3,2},{4,3},{5,4},{6,5},{7,6},{8,7},{9,8},{10,9},{11,1... | collective-permute-start | bytes 294920 | tf_op jit(solution)/shard_map/ppermute | solution.py:66
  44.2 13.6 %collective-permute-start.6 = (bf16[6,64,128]{2,1,0:T(8,128)(2,1)S(1)}, bf16[6,64,128]{2,1,0:T(8,128)(2,1)S(1)}, u32[]{:S(2)}, u32[]{:S(2)}) collective-permute-start(bf16[6,64,128]{2,1,0:T(8,128)(2,1)S(1)} %gather_fusion.2), channel_id=1, source_target_pairs={{2,0},{3,1},{4,2},{5,3},{6,4},{7,5},{8,6},{9,7},{10,8},{11,9},{12,... | collective-permute-start | bytes 294920 | tf_op jit(solution)/shard_map/ppermute | solution.py:66
  49.1 9.3 %collective-permute-start.7 = (bf16[6,64,128]{2,1,0:T(8,128)(2,1)S(1)}, bf16[6,64,128]{2,1,0:T(8,128)(2,1)S(1)}, u32[]{:S(2)}, u32[]{:S(2)}) collective-permute-start(bf16[6,64,128]{2,1,0:T(8,128)(2,1)S(1)} %gather_fusion.3), channel_id=1, source_target_pairs={{16,0},{17,1},{18,2},{19,3},{20,4},{21,5},{22,6},{23,7},{24,8},{25... | collective-permute-start | bytes 294920 | tf_op jit(solution)/shard_map/ppermute | solution.py:66
  49.2 13.0 %copy-start.11 = (s32[1024]{0:T(1024)}, s32[1024]{0:T(1024)S(1)}, u32[]{:S(2)}) copy-start(s32[1024]{0:T(1024)S(1)} %pad_clamp_fusion.2) | copy-start | bytes 12292
  49.8 9.3 %collective-permute-start.8 = (bf16[6,64,128]{2,1,0:T(8,128)(2,1)S(1)}, bf16[6,64,128]{2,1,0:T(8,128)(2,1)S(1)}, u32[]{:S(2)}, u32[]{:S(2)}) collective-permute-start(bf16[6,64,128]{2,1,0:T(8,128)(2,1)S(1)} %gather_fusion.4), channel_id=1, source_target_pairs={{31,0},{0,1},{1,2},{2,3},{3,4},{4,5},{5,6},{6,7},{7,8},{8,9},{9,10... | collective-permute-start | bytes 294920 | tf_op jit(solution)/shard_map/ppermute | solution.py:66
  51.8 10.4 %copy-start.12 = (s32[1024]{0:T(1024)}, s32[1024]{0:T(1024)S(1)}, u32[]{:S(2)}) copy-start(s32[1024]{0:T(1024)S(1)} %pad_clamp_fusion.1) | copy-start | bytes 12292
  52.4 9.8 %collective-permute-start.9 = (bf16[6,64,128]{2,1,0:T(8,128)(2,1)S(1)}, bf16[6,64,128]{2,1,0:T(8,128)(2,1)S(1)}, u32[]{:S(2)}, u32[]{:S(2)}) collective-permute-start(bf16[6,64,128]{2,1,0:T(8,128)(2,1)S(1)} %gather_fusion.5), channel_id=1, source_target_pairs={{30,0},{31,1},{0,2},{1,3},{2,4},{3,5},{4,6},{5,7},{6,8},{7,9},{8,1... | collective-permute-start | bytes 294920 | tf_op jit(solution)/shard_map/ppermute | solution.py:66
  64.9 3.3 %copy-start.2 = (bf16[24,5,128,128]{3,2,1,0:T(8,128)(2,1)S(1)}, bf16[24,5,128,128]{3,2,1,0:T(8,128)(2,1)}, u32[]{:S(2)}) copy-start(bf16[24,5,128,128]{3,2,1,0:T(8,128)(2,1)} %param.17) | copy-start | bytes 11796484
  68.2 1.0 copy-start.7
  69.8 1.1 copy-start.4
  75.1 9.4 %collective-permute-start.10 = (bf16[6,64,128]{2,1,0:T(8,128)(2,1)S(1)}, bf16[6,64,128]{2,1,0:T(8,128)(2,1)S(1)}, u32[]{:S(2)}, u32[]{:S(2)}) collective-permute-start(bf16[6,64,128]{2,1,0:T(8,128)(2,1)S(1)} %gather_fusion.7), channel_id=1, source_target_pairs={{1,0},{2,1},{3,2},{4,3},{5,4},{6,5},{7,6},{8,7},{9,8},{10,9},{11,1... | collective-permute-start | bytes 294920 | tf_op jit(solution)/shard_map/ppermute | solution.py:66
  75.2 9.9 %collective-permute-start.11 = (bf16[6,64,128]{2,1,0:T(8,128)(2,1)S(1)}, bf16[6,64,128]{2,1,0:T(8,128)(2,1)S(1)}, u32[]{:S(2)}, u32[]{:S(2)}) collective-permute-start(bf16[6,64,128]{2,1,0:T(8,128)(2,1)S(1)} %gather_fusion.8), channel_id=1, source_target_pairs={{2,0},{3,1},{4,2},{5,3},{6,4},{7,5},{8,6},{9,7},{10,8},{11,9},{12,... | collective-permute-start | bytes 294920 | tf_op jit(solution)/shard_map/ppermute | solution.py:66
  75.7 10.1 %collective-permute-start.12 = (bf16[6,64,128]{2,1,0:T(8,128)(2,1)S(1)}, bf16[6,64,128]{2,1,0:T(8,128)(2,1)S(1)}, u32[]{:S(2)}, u32[]{:S(2)}) collective-permute-start(bf16[6,64,128]{2,1,0:T(8,128)(2,1)S(1)} %gather_fusion.9), channel_id=1, source_target_pairs={{16,0},{17,1},{18,2},{19,3},{20,4},{21,5},{22,6},{23,7},{24,8},{25... | collective-permute-start | bytes 294920 | tf_op jit(solution)/shard_map/ppermute | solution.py:66
  79.4 7.1 %collective-permute-start.13 = (bf16[6,64,128]{2,1,0:T(8,128)(2,1)S(1)}, bf16[6,64,128]{2,1,0:T(8,128)(2,1)S(1)}, u32[]{:S(2)}, u32[]{:S(2)}) collective-permute-start(bf16[6,64,128]{2,1,0:T(8,128)(2,1)S(1)} %gather_fusion.10), channel_id=1, source_target_pairs={{31,0},{0,1},{1,2},{2,3},{3,4},{4,5},{5,6},{6,7},{7,8},{8,9},{9,10... | collective-permute-start | bytes 294920 | tf_op jit(solution)/shard_map/ppermute | solution.py:66
  81.3 8.0 %collective-permute-start.14 = (bf16[6,64,128]{2,1,0:T(8,128)(2,1)S(1)}, bf16[6,64,128]{2,1,0:T(8,128)(2,1)S(1)}, u32[]{:S(2)}, u32[]{:S(2)}) collective-permute-start(bf16[6,64,128]{2,1,0:T(8,128)(2,1)S(1)} %gather_fusion.11), channel_id=1, source_target_pairs={{30,0},{31,1},{0,2},{1,3},{2,4},{3,5},{4,6},{5,7},{6,8},{7,9},{8,1... | collective-permute-start | bytes 294920 | tf_op jit(solution)/shard_map/ppermute | solution.py:66
  92.1 3.3 %copy-start.1 = (bf16[24,5,128,128]{3,2,1,0:T(8,128)(2,1)S(1)}, bf16[24,5,128,128]{3,2,1,0:T(8,128)(2,1)}, u32[]{:S(2)}) copy-start(bf16[24,5,128,128]{3,2,1,0:T(8,128)(2,1)} %param.16) | copy-start | bytes 11796484
  95.4 1.0 copy-start.8
  97.6 1.1 copy-start.5
  97.6 1.4 %copy-start.9 = (f32[24,64,128]{2,1,0:T(8,128)S(1)}, f32[24,64,128]{2,1,0:T(8,128)}, u32[]{:S(2)}) copy-start(f32[24,64,128]{2,1,0:T(8,128)} %get-tuple-element.99) | copy-start | bytes 2359300
  100.7 6.3 %collective-permute-start.15 = (f32[4,2,4,24,128]{4,3,2,1,0:T(8,128)S(1)}, f32[4,2,4,24,128]{4,3,2,1,0:T(8,128)S(1)}, u32[]{:S(2)}, u32[]{:S(2)}) collective-permute-start(f32[4,2,4,24,128]{4,3,2,1,0:T(8,128)S(1)} %bitcast.206), channel_id=1, source_target_pairs={{0,32},{32,0},{64,96},{96,64},{128,160},{160,128},{192,224},{224,1... | collective-permute-start | bytes 1179656 | tf_op jit(solution)/shard_map/ppermute | solution.py:118
  107.2 6.6 %collective-permute-start.18 = (f32[2,4,24,128]{3,2,1,0:T(8,128)S(1)}, f32[2,4,24,128]{3,2,1,0:T(8,128)S(1)}, u32[]{:S(2)}, u32[]{:S(2)}) collective-permute-start(f32[2,4,24,128]{3,2,1,0:T(8,128)S(1)} %get-tuple-element.101), channel_id=1, source_target_pairs={{0,192},{32,224},{64,0},{96,32},{128,64},{160,96},{192,128},{224,1... | collective-permute-start | bytes 294920 | tf_op jit(solution)/shard_map/ppermute | solution.py:123
  110.0 5.1 %collective-permute-start.17 = (f32[2,4,24,128]{3,2,1,0:T(8,128)S(1)}, f32[2,4,24,128]{3,2,1,0:T(8,128)S(1)}, u32[]{:S(2)}, u32[]{:S(2)}) collective-permute-start(f32[2,4,24,128]{3,2,1,0:T(8,128)S(1)} %get-tuple-element.102), channel_id=1, source_target_pairs={{0,128},{32,160},{64,192},{96,224},{128,0},{160,32},{192,64},{224,... | collective-permute-start | bytes 294920 | tf_op jit(solution)/shard_map/ppermute | solution.py:123
  110.3 7.8 %collective-permute-start.16 = (f32[2,4,24,128]{3,2,1,0:T(8,128)S(1)}, f32[2,4,24,128]{3,2,1,0:T(8,128)S(1)}, u32[]{:S(2)}, u32[]{:S(2)}) collective-permute-start(f32[2,4,24,128]{3,2,1,0:T(8,128)S(1)} %get-tuple-element.100), channel_id=1, source_target_pairs={{0,64},{32,96},{64,128},{96,160},{128,192},{160,224},{192,0},{224,... | collective-permute-start | bytes 294920 | tf_op jit(solution)/shard_map/ppermute | solution.py:123

commit v7 on v2

--- a/solution.py
+++ b/solution.py
@@ -101,10 +101,17 @@
         ]
     )
     weighted = jnp.transpose(weighted / node_count, (2, 0, 3, 1, 4))
-    total = lax.dynamic_index_in_dim(weighted, node_index, 0, keepdims=False)
-    for offset in range(1, node_count):
-        chunk = lax.dynamic_index_in_dim(weighted, (node_index + offset) % node_count, 0, keepdims=False)
-        perm = [(j, (j + offset) % node_count) for j in range(node_count)]
+    groups = node_count // 2
+    core = node_index % 2
+    group = node_index // 2
+    paired = weighted.reshape((groups, 2) + weighted.shape[1:])
+    keep = lax.dynamic_index_in_dim(paired, core, 1, keepdims=False)
+    other = lax.dynamic_index_in_dim(paired, 1 - core, 1, keepdims=False)
+    partial = keep + lax.ppermute(other, "node", [(j, j ^ 1) for j in range(node_count)])
+    total = lax.dynamic_index_in_dim(partial, group, 0, keepdims=False)
+    for offset in range(1, groups):
+        chunk = lax.dynamic_index_in_dim(partial, (group + offset) % groups, 0, keepdims=False)
+        perm = [(j, ((j // 2 + offset) % groups) * 2 + j % 2) for j in range(node_count)]
         total = total + lax.ppermute(chunk, "node", perm)
     return total
 

time: 117 us -> 116 us (level)
  starting transfers between devices: 57.2 us -> 52 us
  waiting for transfers between devices: 12.4 us -> 15.9 us
  other arithmetic: 4.78 us -> 6.57 us
    ppermute x7 -> x3, starting transfers between devices: 15.8 us -> 3.85 us  [per_device(): total = total + lax.ppermute(chunk, 'node', perm)]
    ppermute x0 -> x1, starting transfers between devices: none -> 8.19 us  [per_device(): lax.ppermute(other, 'node', [(j, j ^ 1) for j in range(node_count)])]
    ppermute x15, starting transfers between devices: 29.1 us -> 26.4 us  [fetch_halo(): lax.ppermute(vector[asked_for[which]], 'rows', from_partner(offset))]
    ppermute x7 -> x3, waiting for transfers between devices: 5.25 us -> 7.15 us  [per_device(): total = total + lax.ppermute(chunk, 'node', perm)]
    concatenate x2 -> x0, local copies, waits for them, and re-layouts: 1.82 us -> none  [per_device(): iterate = iterate + jnp.concatenate([update_real, update_imag], axis=1)]
    ppermute x0 -> x1, waiting for transfers between devices: none -> 1.35 us  [per_device(): lax.ppermute(other, 'node', [(j, j ^ 1) for j in range(node_count)])]
    ppermute x5, starting transfers between devices: 12.3 us -> 13.5 us  [per_device(): lax.ppermute(wanted[which], 'rows', to_partner(offset))]
    unnamed x42 -> x43, local copies, waits for them, and re-layouts: 10.8 us -> 10.5 us
  transfers between devices with their start and end apart: 27 -> 24, of which waited for: 6 -> 7; matrix products, arithmetic and copies ran while one was open for 12% -> 10% of each run, Pallas kernels for 0% -> 0%
where the time goes in v7:
time: 116 us
  starting transfers between devices  52 us (45%)
  local copies, waits for them, and re-layouts  28.1 us (24%)
  waiting for transfers between devices  15.9 us (14%)
  matrix products  12.2 us (11%)
  other arithmetic  6.57 us (6%)
    ppermute x15, starting transfers between devices, fetch_halo(): lax.ppermute(vector[asked_for[which]], 'rows', from_partner(offset))  26.4 us
    ppermute x5, starting transfers between devices, per_device(): lax.ppermute(wanted[which], 'rows', to_partner(offset))  13.5 us
    unnamed x43, local copies, waits for them, and re-layouts  10.5 us
    gather x15, local copies, waits for them, and re-layouts, fetch_halo(): vector[asked_for[which]]  8.7 us
    ppermute x1, starting transfers between devices, per_device(): lax.ppermute(other, 'node', [(j, j ^ 1) for j in range(node_count)])  8.19 us
    ppermute x15, waiting for transfers between devices, fetch_halo(): lax.ppermute(vector[asked_for[which]], 'rows', from_partner(offset))  7.42 us
    ppermute x3, waiting for transfers between devices, per_device(): total = total + lax.ppermute(chunk, 'node', perm)  7.15 us
    dot_general x3, matrix products, apply_pair(): jnp.einsum('nscb,nsbd->ncd', picked, first, preferred_element_type=jnp.fl...  6.97 us
  transfers between devices with their start and end apart: 24, of which 7 were waited for; matrix products, arithmetic and copies ran while one was open for 10% of the time, Pallas kernels for 0%

profile of v7, /device:TPU:3, one launch (start us, length us, event | category | flops | bytes accessed | tf_op | source)
XLA Modules:
  0.0 115.6 jit_solution(6848652089080899126)
XLA Ops:
  4.2 1.3 %collective-permute-start = (s32[6]{0:T(128)S(1)}, s32[6]{0:T(128)S(1)}, u32[]{:S(2)}, u32[]{:S(2)}) collective-permute-start(s32[6]{0:T(128)S(1)} %get-tuple-element.19), channel_id=1, source_target_pairs={{0,1},{1,2},{2,3},{3,4},{4,5},{5,6},{6,7},{7,8},{8,9},{9,10},{10,1... | collective-permute-start | bytes 80 | tf_op jit(solution)/shard_map/ppermute | solution.py:61
  5.4 6.9 %collective-permute-start.4 = (s32[6]{0:T(128)S(1)}, s32[6]{0:T(128)S(1)}, u32[]{:S(2)}, u32[]{:S(2)}) collective-permute-start(s32[6]{0:T(128)S(1)} %get-tuple-element.17), channel_id=1, source_target_pairs={{0,16},{1,17},{2,18},{3,19},{4,20},{5,21},{6,22},{7,23},{8,24},{9,... | collective-permute-start | bytes 80 | tf_op jit(solution)/shard_map/ppermute | solution.py:61
  12.4 1.3 %collective-permute-start.2 = (s32[6]{0:T(128)S(1)}, s32[6]{0:T(128)S(1)}, u32[]{:S(2)}, u32[]{:S(2)}) collective-permute-start(s32[6]{0:T(128)S(1)} %get-tuple-element.16), channel_id=1, source_target_pairs={{0,2},{1,3},{2,4},{3,5},{4,6},{5,7},{6,8},{7,9},{8,10},{9,11},{10,... | collective-permute-start | bytes 80 | tf_op jit(solution)/shard_map/ppermute | solution.py:61
  13.6 3.8 %collective-permute-start.8 = (s32[6]{0:T(128)S(1)}, s32[6]{0:T(128)S(1)}, u32[]{:S(2)}, u32[]{:S(2)}) collective-permute-start(s32[6]{0:T(128)S(1)} %get-tuple-element.15), channel_id=1, source_target_pairs={{0,30},{1,31},{2,0},{3,1},{4,2},{5,3},{6,4},{7,5},{8,6},{9,7},{10,... | collective-permute-start | bytes 80 | tf_op jit(solution)/shard_map/ppermute | solution.py:61
  17.7 1.0 constant_dynamic-update-slice_fusion.5
  19.4 1.5 %collective-permute-start.1 = (bf16[6,32,128]{2,1,0:T(8,128)(2,1)S(1)}, bf16[6,32,128]{2,1,0:T(8,128)(2,1)S(1)}, u32[]{:S(2)}, u32[]{:S(2)}) collective-permute-start(bf16[6,32,128]{2,1,0:T(8,128)(2,1)S(1)} %gather_fusion), channel_id=1, source_target_pairs={{1,0},{2,1},{3,2},{4,3},{5,4},{6,5},{7,6},{8,7},{9,8},{10,9},{11,1... | collective-permute-start | bytes 147464 | tf_op jit(solution)/shard_map/ppermute | solution.py:67
  22.2 3.5 %collective-permute-start.5 = (bf16[6,32,128]{2,1,0:T(8,128)(2,1)S(1)}, bf16[6,32,128]{2,1,0:T(8,128)(2,1)S(1)}, u32[]{:S(2)}, u32[]{:S(2)}) collective-permute-start(bf16[6,32,128]{2,1,0:T(8,128)(2,1)S(1)} %gather_fusion.2), channel_id=1, source_target_pairs={{16,0},{17,1},{18,2},{19,3},{20,4},{21,5},{22,6},{23,7},{24,8},{25... | collective-permute-start | bytes 147464 | tf_op jit(solution)/shard_map/ppermute | solution.py:67
  27.6 1.6 %collective-permute-start.9 = (bf16[6,32,128]{2,1,0:T(8,128)(2,1)S(1)}, bf16[6,32,128]{2,1,0:T(8,128)(2,1)S(1)}, u32[]{:S(2)}, u32[]{:S(2)}) collective-permute-start(bf16[6,32,128]{2,1,0:T(8,128)(2,1)S(1)} %gather_fusion.4), channel_id=1, source_target_pairs={{30,0},{31,1},{0,2},{1,3},{2,4},{3,5},{4,6},{5,7},{6,8},{7,9},{8,1... | collective-permute-start | bytes 147464 | tf_op jit(solution)/shard_map/ppermute | solution.py:67
  29.4 4.9 %collective-permute-done.9 = bf16[6,32,128]{2,1,0:T(8,128)(2,1)S(1)} collective-permute-done((bf16[6,32,128]{2,1,0:T(8,128)(2,1)S(1)}, bf16[6,32,128]{2,1,0:T(8,128)(2,1)S(1)}, u32[]{:S(2)}, u32[]{:S(2)}) %collective-permute-start.9) | collective-permute-done | bytes 49184 | tf_op jit(solution)/shard_map/ppermute | solution.py:67
  35.0 2.8 %convolution_bitcast_fusion.4 = f32[24,32,128]{2,1,0:T(8,128)S(1)} fusion(bf16[24,5,32,128]{3,2,1,0:T(8,128)(2,1)S(1)} %bitcast.146, bf16[24,5,128,128]{3,2,1,0:T(8,128)(2,1)} %param.6), kind=kOutput, calls=%fused_computation.22 | convolution fusion | flops 125829120 | bytes 5308416 | tf_op jit(solution)/shard_map/nscb,nsbd->ncd/dot_general | solution.py:25
  40.6 1.1 collective-permute-start.10
  44.2 1.3 %collective-permute-start.11 = (bf16[6,64,128]{2,1,0:T(8,128)(2,1)S(1)}, bf16[6,64,128]{2,1,0:T(8,128)(2,1)S(1)}, u32[]{:S(2)}, u32[]{:S(2)}) collective-permute-start(bf16[6,64,128]{2,1,0:T(8,128)(2,1)S(1)} %gather_fusion.7), channel_id=1, source_target_pairs={{2,0},{3,1},{4,2},{5,3},{6,4},{7,5},{8,6},{9,7},{10,8},{11,9},{12,... | collective-permute-start | bytes 294920 | tf_op jit(solution)/shard_map/ppermute | solution.py:67
  45.4 1.5 %collective-permute-start.12 = (bf16[6,64,128]{2,1,0:T(8,128)(2,1)S(1)}, bf16[6,64,128]{2,1,0:T(8,128)(2,1)S(1)}, u32[]{:S(2)}, u32[]{:S(2)}) collective-permute-start(bf16[6,64,128]{2,1,0:T(8,128)(2,1)S(1)} %gather_fusion.8), channel_id=1, source_target_pairs={{16,0},{17,1},{18,2},{19,3},{20,4},{21,5},{22,6},{23,7},{24,8},{25... | collective-permute-start | bytes 294920 | tf_op jit(solution)/shard_map/ppermute | solution.py:67
  46.9 2.1 %collective-permute-start.13 = (bf16[6,64,128]{2,1,0:T(8,128)(2,1)S(1)}, bf16[6,64,128]{2,1,0:T(8,128)(2,1)S(1)}, u32[]{:S(2)}, u32[]{:S(2)}) collective-permute-start(bf16[6,64,128]{2,1,0:T(8,128)(2,1)S(1)} %gather_fusion.9), channel_id=1, source_target_pairs={{31,0},{0,1},{1,2},{2,3},{3,4},{4,5},{5,6},{6,7},{7,8},{8,9},{9,10... | collective-permute-start | bytes 294920 | tf_op jit(solution)/shard_map/ppermute | solution.py:67
  48.9 3.3 %collective-permute-start.14 = (bf16[6,64,128]{2,1,0:T(8,128)(2,1)S(1)}, bf16[6,64,128]{2,1,0:T(8,128)(2,1)S(1)}, u32[]{:S(2)}, u32[]{:S(2)}) collective-permute-start(bf16[6,64,128]{2,1,0:T(8,128)(2,1)S(1)} %gather_fusion.10), channel_id=1, source_target_pairs={{30,0},{31,1},{0,2},{1,3},{2,4},{3,5},{4,6},{5,7},{6,8},{7,9},{8,1... | collective-permute-start | bytes 294920 | tf_op jit(solution)/shard_map/ppermute | solution.py:67
  54.8 2.4 %collective-permute-done.14 = bf16[6,64,128]{2,1,0:T(8,128)(2,1)S(1)} collective-permute-done((bf16[6,64,128]{2,1,0:T(8,128)(2,1)S(1)}, bf16[6,64,128]{2,1,0:T(8,128)(2,1)S(1)}, u32[]{:S(2)}, u32[]{:S(2)}) %collective-permute-start.14) | collective-permute-done | bytes 98336 | tf_op jit(solution)/shard_map/ppermute | solution.py:67
  57.9 2.1 %gather_fusion.11 = bf16[120,64,128]{2,1,0:T(8,128)(2,1)S(1)} fusion(bf16[54,64,128]{2,1,0:T(8,128)(2,1)} %constant_dynamic-update-slice_fusion.6, s32[1024]{0:T(1024)S(1)} %pad_clamp_fusion), kind=kCustom, calls=%fused_computation.11 | custom fusion | bytes 3932640 | tf_op jit(solution)/shard_map/gather | solution.py:24
  60.0 3.2 %convolution_bitcast_fusion.3 = f32[24,64,128]{2,1,0:T(8,128)S(1)} fusion(bf16[24,5,64,128]{3,2,1,0:T(8,128)(2,1)S(1)} %bitcast.141, bf16[24,5,128,128]{3,2,1,0:T(8,128)(2,1)} %param.6), kind=kOutput, calls=%fused_computation.21 | convolution fusion | flops 251658240 | bytes 6684672 | tf_op jit(solution)/shard_map/nscb,nsbd->ncd/dot_general | solution.py:25
  65.0 1.0 copy-done.4
  66.0 1.0 fusion.6
  70.9 3.3 %collective-permute-start.17 = (bf16[6,64,128]{2,1,0:T(8,128)(2,1)S(1)}, bf16[6,64,128]{2,1,0:T(8,128)(2,1)S(1)}, u32[]{:S(2)}, u32[]{:S(2)}) collective-permute-start(bf16[6,64,128]{2,1,0:T(8,128)(2,1)S(1)} %gather_fusion.14), channel_id=1, source_target_pairs={{16,0},{17,1},{18,2},{19,3},{20,4},{21,5},{22,6},{23,7},{24,8},{25... | collective-permute-start | bytes 294920 | tf_op jit(solution)/shard_map/ppermute | solution.py:67
  74.2 1.5 %collective-permute-start.18 = (bf16[6,64,128]{2,1,0:T(8,128)(2,1)S(1)}, bf16[6,64,128]{2,1,0:T(8,128)(2,1)S(1)}, u32[]{:S(2)}, u32[]{:S(2)}) collective-permute-start(bf16[6,64,128]{2,1,0:T(8,128)(2,1)S(1)} %gather_fusion.15), channel_id=1, source_target_pairs={{31,0},{0,1},{1,2},{2,3},{3,4},{4,5},{5,6},{6,7},{7,8},{8,9},{9,10... | collective-permute-start | bytes 294920 | tf_op jit(solution)/shard_map/ppermute | solution.py:67
  75.7 4.2 %collective-permute-start.19 = (bf16[6,64,128]{2,1,0:T(8,128)(2,1)S(1)}, bf16[6,64,128]{2,1,0:T(8,128)(2,1)S(1)}, u32[]{:S(2)}, u32[]{:S(2)}) collective-permute-start(bf16[6,64,128]{2,1,0:T(8,128)(2,1)S(1)} %gather_fusion.16), channel_id=1, source_target_pairs={{30,0},{31,1},{0,2},{1,3},{2,4},{3,5},{4,6},{5,7},{6,8},{7,9},{8,1... | collective-permute-start | bytes 294920 | tf_op jit(solution)/shard_map/ppermute | solution.py:67
  83.9 2.1 %gather_fusion.17 = bf16[120,64,128]{2,1,0:T(8,128)(2,1)S(1)} fusion(bf16[54,64,128]{2,1,0:T(8,128)(2,1)} %constant_dynamic-update-slice_fusion.12, s32[1024]{0:T(1024)S(1)} %pad_clamp_fusion), kind=kCustom, calls=%fused_computation.17 | custom fusion | bytes 3932640 | tf_op jit(solution)/shard_map/gather | solution.py:24
  86.1 3.2 %convolution_bitcast_fusion = f32[24,64,128]{2,1,0:T(8,128)S(1)} fusion(bf16[24,5,64,128]{3,2,1,0:T(8,128)(2,1)S(1)} %bitcast.139, bf16[24,5,128,128]{3,2,1,0:T(8,128)(2,1)} %param.7), kind=kOutput, calls=%fused_computation.18 | convolution fusion | flops 251658240 | bytes 6684672 | tf_op jit(solution)/shard_map/nscb,nsbd->ncd/dot_general | solution.py:28
  89.3 0.9 convolution_bitcast_fusion.1
  94.2 8.2 %collective-permute-start.20 = (f32[4,2,4,24,128]{4,3,2,1,0:T(8,128)S(1)}, f32[4,2,4,24,128]{4,3,2,1,0:T(8,128)S(1)}, u32[]{:S(2)}, u32[]{:S(2)}) collective-permute-start(f32[4,2,4,24,128]{4,3,2,1,0:T(8,128)S(1)} %bitcast.155), channel_id=1, source_target_pairs={{0,32},{32,0},{64,96},{96,64},{128,160},{160,128},{192,224},{224,1... | collective-permute-start | bytes 1179656 | tf_op jit(solution)/shard_map/ppermute | solution.py:110
  102.4 1.3 %collective-permute-done.20 = f32[4,2,4,24,128]{4,3,2,1,0:T(8,128)S(1)} collective-permute-done((f32[4,2,4,24,128]{4,3,2,1,0:T(8,128)S(1)}, f32[4,2,4,24,128]{4,3,2,1,0:T(8,128)S(1)}, u32[]{:S(2)}, u32[]{:S(2)}) %collective-permute-start.20) | collective-permute-done | bytes 393248 | tf_op jit(solution)/shard_map/ppermute | solution.py:110
  103.9 2.8 %collective-permute-start.23 = (f32[2,4,24,128]{3,2,1,0:T(8,128)S(1)}, f32[2,4,24,128]{3,2,1,0:T(8,128)S(1)}, u32[]{:S(2)}, u32[]{:S(2)}) collective-permute-start(f32[2,4,24,128]{3,2,1,0:T(8,128)S(1)} %get-tuple-element.46), channel_id=1, source_target_pairs={{0,192},{32,224},{64,0},{96,32},{128,64},{160,96},{192,128},{224,1... | collective-permute-start | bytes 294920 | tf_op jit(solution)/shard_map/ppermute | solution.py:115
  107.7 2.7 %collective-permute-done.23 = f32[2,4,24,128]{3,2,1,0:T(8,128)S(1)} collective-permute-done((f32[2,4,24,128]{3,2,1,0:T(8,128)S(1)}, f32[2,4,24,128]{3,2,1,0:T(8,128)S(1)}, u32[]{:S(2)}, u32[]{:S(2)}) %collective-permute-start.23) | collective-permute-done | bytes 98336 | tf_op jit(solution)/shard_map/ppermute | solution.py:115
  110.5 1.3 %collective-permute-done.22 = f32[2,4,24,128]{3,2,1,0:T(8,128)S(1)} collective-permute-done((f32[2,4,24,128]{3,2,1,0:T(8,128)S(1)}, f32[2,4,24,128]{3,2,1,0:T(8,128)S(1)}, u32[]{:S(2)}, u32[]{:S(2)}) %collective-permute-start.22) | collective-permute-done | bytes 98336 | tf_op jit(solution)/shard_map/ppermute | solution.py:115
  111.8 3.1 %collective-permute-done.21 = f32[2,4,24,128]{3,2,1,0:T(8,128)S(1)} collective-permute-done((f32[2,4,24,128]{3,2,1,0:T(8,128)S(1)}, f32[2,4,24,128]{3,2,1,0:T(8,128)S(1)}, u32[]{:S(2)}, u32[]{:S(2)}) %collective-permute-start.21) | collective-permute-done | bytes 98336 | tf_op jit(solution)/shard_map/ppermute | solution.py:115
  (145 shorter events, 32.5 us)
Async XLA Ops:
  0.0 37.9 %copy-start = (bf16[1,2,24,128,128]{4,3,2,1,0:T(8,128)(2,1)S(1)}, bf16[1,2,24,128,128]{4,3,2,1,0:T(8,128)(2,1)}, u32[]{:S(2)}) copy-start(bf16[1,2,24,128,128]{4,3,2,1,0:T(8,128)(2,1)} %param.8) | copy-start | bytes 4718596
  0.0 18.6 %copy-start.10 = (bf16[32,24,128]{2,1,0:T(8,128)(2,1)S(1)}, bf16[32,24,128]{2,1,0:T(8,128)(2,1)}, u32[]{:S(2)}) copy-start(bf16[32,24,128]{2,1,0:T(8,128)(2,1)} %param.5) | copy-start | bytes 589828
  4.2 14.6 %collective-permute-start = (s32[6]{0:T(128)S(1)}, s32[6]{0:T(128)S(1)}, u32[]{:S(2)}, u32[]{:S(2)}) collective-permute-start(s32[6]{0:T(128)S(1)} %get-tuple-element.19), channel_id=1, source_target_pairs={{0,1},{1,2},{2,3},{3,4},{4,5},{5,6},{6,7},{7,8},{8,9},{9,10},{10,1... | collective-permute-start | bytes 80 | tf_op jit(solution)/shard_map/ppermute | solution.py:61
  5.4 15.5 %collective-permute-start.4 = (s32[6]{0:T(128)S(1)}, s32[6]{0:T(128)S(1)}, u32[]{:S(2)}, u32[]{:S(2)}) collective-permute-start(s32[6]{0:T(128)S(1)} %get-tuple-element.17), channel_id=1, source_target_pairs={{0,16},{1,17},{2,18},{3,19},{4,20},{5,21},{6,22},{7,23},{8,24},{9,... | collective-permute-start | bytes 80 | tf_op jit(solution)/shard_map/ppermute | solution.py:61
  12.4 8.6 %collective-permute-start.2 = (s32[6]{0:T(128)S(1)}, s32[6]{0:T(128)S(1)}, u32[]{:S(2)}, u32[]{:S(2)}) collective-permute-start(s32[6]{0:T(128)S(1)} %get-tuple-element.16), channel_id=1, source_target_pairs={{0,2},{1,3},{2,4},{3,5},{4,6},{5,7},{6,8},{7,9},{8,10},{9,11},{10,... | collective-permute-start | bytes 80 | tf_op jit(solution)/shard_map/ppermute | solution.py:61
  13.6 12.1 %collective-permute-start.8 = (s32[6]{0:T(128)S(1)}, s32[6]{0:T(128)S(1)}, u32[]{:S(2)}, u32[]{:S(2)}) collective-permute-start(s32[6]{0:T(128)S(1)} %get-tuple-element.15), channel_id=1, source_target_pairs={{0,30},{1,31},{2,0},{3,1},{4,2},{5,3},{6,4},{7,5},{8,6},{9,7},{10,... | collective-permute-start | bytes 80 | tf_op jit(solution)/shard_map/ppermute | solution.py:61
  17.4 8.3 %collective-permute-start.6 = (s32[6]{0:T(128)S(1)}, s32[6]{0:T(128)S(1)}, u32[]{:S(2)}, u32[]{:S(2)}) collective-permute-start(s32[6]{0:T(128)S(1)} %get-tuple-element.18), channel_id=1, source_target_pairs={{0,31},{1,0},{2,1},{3,2},{4,3},{5,4},{6,5},{7,6},{8,7},{9,8},{10,9... | collective-permute-start | bytes 80 | tf_op jit(solution)/shard_map/ppermute | solution.py:61
  19.4 9.8 %collective-permute-start.1 = (bf16[6,32,128]{2,1,0:T(8,128)(2,1)S(1)}, bf16[6,32,128]{2,1,0:T(8,128)(2,1)S(1)}, u32[]{:S(2)}, u32[]{:S(2)}) collective-permute-start(bf16[6,32,128]{2,1,0:T(8,128)(2,1)S(1)} %gather_fusion), channel_id=1, source_target_pairs={{1,0},{2,1},{3,2},{4,3},{5,4},{6,5},{7,6},{8,7},{9,8},{10,9},{11,1... | collective-permute-start | bytes 147464 | tf_op jit(solution)/shard_map/ppermute | solution.py:67
  21.5 7.7 %collective-permute-start.3 = (bf16[6,32,128]{2,1,0:T(8,128)(2,1)S(1)}, bf16[6,32,128]{2,1,0:T(8,128)(2,1)S(1)}, u32[]{:S(2)}, u32[]{:S(2)}) collective-permute-start(bf16[6,32,128]{2,1,0:T(8,128)(2,1)S(1)} %gather_fusion.1), channel_id=1, source_target_pairs={{2,0},{3,1},{4,2},{5,3},{6,4},{7,5},{8,6},{9,7},{10,8},{11,9},{12,... | collective-permute-start | bytes 147464 | tf_op jit(solution)/shard_map/ppermute | solution.py:67
  22.2 7.0 %collective-permute-start.5 = (bf16[6,32,128]{2,1,0:T(8,128)(2,1)S(1)}, bf16[6,32,128]{2,1,0:T(8,128)(2,1)S(1)}, u32[]{:S(2)}, u32[]{:S(2)}) collective-permute-start(bf16[6,32,128]{2,1,0:T(8,128)(2,1)S(1)} %gather_fusion.2), channel_id=1, source_target_pairs={{16,0},{17,1},{18,2},{19,3},{20,4},{21,5},{22,6},{23,7},{24,8},{25... | collective-permute-start | bytes 147464 | tf_op jit(solution)/shard_map/ppermute | solution.py:67
  25.8 17.2 %copy-start.11 = (s32[1024]{0:T(1024)}, s32[1024]{0:T(1024)S(1)}, u32[]{:S(2)}) copy-start(s32[1024]{0:T(1024)S(1)} %pad_clamp_fusion.2) | copy-start | bytes 12292
  26.3 3.0 %collective-permute-start.7 = (bf16[6,32,128]{2,1,0:T(8,128)(2,1)S(1)}, bf16[6,32,128]{2,1,0:T(8,128)(2,1)S(1)}, u32[]{:S(2)}, u32[]{:S(2)}) collective-permute-start(bf16[6,32,128]{2,1,0:T(8,128)(2,1)S(1)} %gather_fusion.3), channel_id=1, source_target_pairs={{31,0},{0,1},{1,2},{2,3},{3,4},{4,5},{5,6},{6,7},{7,8},{8,9},{9,10... | collective-permute-start | bytes 147464 | tf_op jit(solution)/shard_map/ppermute | solution.py:67
  27.1 16.5 %copy-start.12 = (s32[1024]{0:T(1024)}, s32[1024]{0:T(1024)S(1)}, u32[]{:S(2)}) copy-start(s32[1024]{0:T(1024)S(1)} %pad_clamp_fusion.1) | copy-start | bytes 12292
  27.6 6.6 %collective-permute-start.9 = (bf16[6,32,128]{2,1,0:T(8,128)(2,1)S(1)}, bf16[6,32,128]{2,1,0:T(8,128)(2,1)S(1)}, u32[]{:S(2)}, u32[]{:S(2)}) collective-permute-start(bf16[6,32,128]{2,1,0:T(8,128)(2,1)S(1)} %gather_fusion.4), channel_id=1, source_target_pairs={{30,0},{31,1},{0,2},{1,3},{2,4},{3,5},{4,6},{5,7},{6,8},{7,9},{8,1... | collective-permute-start | bytes 147464 | tf_op jit(solution)/shard_map/ppermute | solution.py:67
  37.9 2.1 %copy-start.6 = (f32[24,32,128]{2,1,0:T(8,128)}, f32[24,32,128]{2,1,0:T(8,128)S(1)}, u32[]{:S(2)}) copy-start(f32[24,32,128]{2,1,0:T(8,128)S(1)} %convolution_bitcast_fusion.4) | copy-start | bytes 1179652
  40.6 11.7 %collective-permute-start.10 = (bf16[6,64,128]{2,1,0:T(8,128)(2,1)S(1)}, bf16[6,64,128]{2,1,0:T(8,128)(2,1)S(1)}, u32[]{:S(2)}, u32[]{:S(2)}) collective-permute-start(bf16[6,64,128]{2,1,0:T(8,128)(2,1)S(1)} %gather_fusion.6), channel_id=1, source_target_pairs={{1,0},{2,1},{3,2},{4,3},{5,4},{6,5},{7,6},{8,7},{9,8},{10,9},{11,1... | collective-permute-start | bytes 294920 | tf_op jit(solution)/shard_map/ppermute | solution.py:67
  44.2 8.7 %collective-permute-start.11 = (bf16[6,64,128]{2,1,0:T(8,128)(2,1)S(1)}, bf16[6,64,128]{2,1,0:T(8,128)(2,1)S(1)}, u32[]{:S(2)}, u32[]{:S(2)}) collective-permute-start(bf16[6,64,128]{2,1,0:T(8,128)(2,1)S(1)} %gather_fusion.7), channel_id=1, source_target_pairs={{2,0},{3,1},{4,2},{5,3},{6,4},{7,5},{8,6},{9,7},{10,8},{11,9},{12,... | collective-permute-start | bytes 294920 | tf_op jit(solution)/shard_map/ppermute | solution.py:67
  45.4 8.1 %collective-permute-start.12 = (bf16[6,64,128]{2,1,0:T(8,128)(2,1)S(1)}, bf16[6,64,128]{2,1,0:T(8,128)(2,1)S(1)}, u32[]{:S(2)}, u32[]{:S(2)}) collective-permute-start(bf16[6,64,128]{2,1,0:T(8,128)(2,1)S(1)} %gather_fusion.8), channel_id=1, source_target_pairs={{16,0},{17,1},{18,2},{19,3},{20,4},{21,5},{22,6},{23,7},{24,8},{25... | collective-permute-start | bytes 294920 | tf_op jit(solution)/shard_map/ppermute | solution.py:67
  46.9 7.3 %collective-permute-start.13 = (bf16[6,64,128]{2,1,0:T(8,128)(2,1)S(1)}, bf16[6,64,128]{2,1,0:T(8,128)(2,1)S(1)}, u32[]{:S(2)}, u32[]{:S(2)}) collective-permute-start(bf16[6,64,128]{2,1,0:T(8,128)(2,1)S(1)} %gather_fusion.9), channel_id=1, source_target_pairs={{31,0},{0,1},{1,2},{2,3},{3,4},{4,5},{5,6},{6,7},{7,8},{8,9},{9,10... | collective-permute-start | bytes 294920 | tf_op jit(solution)/shard_map/ppermute | solution.py:67
  48.9 8.3 %collective-permute-start.14 = (bf16[6,64,128]{2,1,0:T(8,128)(2,1)S(1)}, bf16[6,64,128]{2,1,0:T(8,128)(2,1)S(1)}, u32[]{:S(2)}, u32[]{:S(2)}) collective-permute-start(bf16[6,64,128]{2,1,0:T(8,128)(2,1)S(1)} %gather_fusion.10), channel_id=1, source_target_pairs={{30,0},{31,1},{0,2},{1,3},{2,4},{3,5},{4,6},{5,7},{6,8},{7,9},{8,1... | collective-permute-start | bytes 294920 | tf_op jit(solution)/shard_map/ppermute | solution.py:67
  60.0 3.3 %copy-start.2 = (bf16[24,5,128,128]{3,2,1,0:T(8,128)(2,1)S(1)}, bf16[24,5,128,128]{3,2,1,0:T(8,128)(2,1)}, u32[]{:S(2)}) copy-start(bf16[24,5,128,128]{3,2,1,0:T(8,128)(2,1)} %param.7) | copy-start | bytes 11796484
  70.1 10.6 %collective-permute-start.15 = (bf16[6,64,128]{2,1,0:T(8,128)(2,1)S(1)}, bf16[6,64,128]{2,1,0:T(8,128)(2,1)S(1)}, u32[]{:S(2)}, u32[]{:S(2)}) collective-permute-start(bf16[6,64,128]{2,1,0:T(8,128)(2,1)S(1)} %gather_fusion.12), channel_id=1, source_target_pairs={{1,0},{2,1},{3,2},{4,3},{5,4},{6,5},{7,6},{8,7},{9,8},{10,9},{11,1... | collective-permute-start | bytes 294920 | tf_op jit(solution)/shard_map/ppermute | solution.py:67
  70.5 10.8 %collective-permute-start.16 = (bf16[6,64,128]{2,1,0:T(8,128)(2,1)S(1)}, bf16[6,64,128]{2,1,0:T(8,128)(2,1)S(1)}, u32[]{:S(2)}, u32[]{:S(2)}) collective-permute-start(bf16[6,64,128]{2,1,0:T(8,128)(2,1)S(1)} %gather_fusion.13), channel_id=1, source_target_pairs={{2,0},{3,1},{4,2},{5,3},{6,4},{7,5},{8,6},{9,7},{10,8},{11,9},{12,... | collective-permute-start | bytes 294920 | tf_op jit(solution)/shard_map/ppermute | solution.py:67
  70.9 11.1 %collective-permute-start.17 = (bf16[6,64,128]{2,1,0:T(8,128)(2,1)S(1)}, bf16[6,64,128]{2,1,0:T(8,128)(2,1)S(1)}, u32[]{:S(2)}, u32[]{:S(2)}) collective-permute-start(bf16[6,64,128]{2,1,0:T(8,128)(2,1)S(1)} %gather_fusion.14), channel_id=1, source_target_pairs={{16,0},{17,1},{18,2},{19,3},{20,4},{21,5},{22,6},{23,7},{24,8},{25... | collective-permute-start | bytes 294920 | tf_op jit(solution)/shard_map/ppermute | solution.py:67
  74.2 8.5 %collective-permute-start.18 = (bf16[6,64,128]{2,1,0:T(8,128)(2,1)S(1)}, bf16[6,64,128]{2,1,0:T(8,128)(2,1)S(1)}, u32[]{:S(2)}, u32[]{:S(2)}) collective-permute-start(bf16[6,64,128]{2,1,0:T(8,128)(2,1)S(1)} %gather_fusion.15), channel_id=1, source_target_pairs={{31,0},{0,1},{1,2},{2,3},{3,4},{4,5},{5,6},{6,7},{7,8},{8,9},{9,10... | collective-permute-start | bytes 294920 | tf_op jit(solution)/shard_map/ppermute | solution.py:67
  75.7 7.6 %collective-permute-start.19 = (bf16[6,64,128]{2,1,0:T(8,128)(2,1)S(1)}, bf16[6,64,128]{2,1,0:T(8,128)(2,1)S(1)}, u32[]{:S(2)}, u32[]{:S(2)}) collective-permute-start(bf16[6,64,128]{2,1,0:T(8,128)(2,1)S(1)} %gather_fusion.16), channel_id=1, source_target_pairs={{30,0},{31,1},{0,2},{1,3},{2,4},{3,5},{4,6},{5,7},{6,8},{7,9},{8,1... | collective-permute-start | bytes 294920 | tf_op jit(solution)/shard_map/ppermute | solution.py:67
  86.0 3.3 %copy-start.1 = (bf16[24,5,128,128]{3,2,1,0:T(8,128)(2,1)S(1)}, bf16[24,5,128,128]{3,2,1,0:T(8,128)(2,1)}, u32[]{:S(2)}) copy-start(bf16[24,5,128,128]{3,2,1,0:T(8,128)(2,1)} %param.6) | copy-start | bytes 11796484
  91.1 1.4 %copy-start.9 = (f32[24,64,128]{2,1,0:T(8,128)S(1)}, f32[24,64,128]{2,1,0:T(8,128)}, u32[]{:S(2)}) copy-start(f32[24,64,128]{2,1,0:T(8,128)} %get-tuple-element.44) | copy-start | bytes 2359300
  94.2 9.5 %collective-permute-start.20 = (f32[4,2,4,24,128]{4,3,2,1,0:T(8,128)S(1)}, f32[4,2,4,24,128]{4,3,2,1,0:T(8,128)S(1)}, u32[]{:S(2)}, u32[]{:S(2)}) collective-permute-start(f32[4,2,4,24,128]{4,3,2,1,0:T(8,128)S(1)} %bitcast.155), channel_id=1, source_target_pairs={{0,32},{32,0},{64,96},{96,64},{128,160},{160,128},{192,224},{224,1... | collective-permute-start | bytes 1179656 | tf_op jit(solution)/shard_map/ppermute | solution.py:110
  103.9 6.6 %collective-permute-start.23 = (f32[2,4,24,128]{3,2,1,0:T(8,128)S(1)}, f32[2,4,24,128]{3,2,1,0:T(8,128)S(1)}, u32[]{:S(2)}, u32[]{:S(2)}) collective-permute-start(f32[2,4,24,128]{3,2,1,0:T(8,128)S(1)} %get-tuple-element.46), channel_id=1, source_target_pairs={{0,192},{32,224},{64,0},{96,32},{128,64},{160,96},{192,128},{224,1... | collective-permute-start | bytes 294920 | tf_op jit(solution)/shard_map/ppermute | solution.py:115
  106.7 5.1 %collective-permute-start.22 = (f32[2,4,24,128]{3,2,1,0:T(8,128)S(1)}, f32[2,4,24,128]{3,2,1,0:T(8,128)S(1)}, u32[]{:S(2)}, u32[]{:S(2)}) collective-permute-start(f32[2,4,24,128]{3,2,1,0:T(8,128)S(1)} %get-tuple-element.47), channel_id=1, source_target_pairs={{0,128},{32,160},{64,192},{96,224},{128,0},{160,32},{192,64},{224,... | collective-permute-start | bytes 294920 | tf_op jit(solution)/shard_map/ppermute | solution.py:115
  107.1 7.8 %collective-permute-start.21 = (f32[2,4,24,128]{3,2,1,0:T(8,128)S(1)}, f32[2,4,24,128]{3,2,1,0:T(8,128)S(1)}, u32[]{:S(2)}, u32[]{:S(2)}) collective-permute-start(f32[2,4,24,128]{3,2,1,0:T(8,128)S(1)} %get-tuple-element.45), channel_id=1, source_target_pairs={{0,64},{32,96},{64,128},{96,160},{128,192},{160,224},{192,0},{224,... | collective-permute-start | bytes 294920 | tf_op jit(solution)/shard_map/ppermute | solution.py:115
  (5 other events, 5.2 us)

commit v8 on v7

--- a/solution.py
+++ b/solution.py
@@ -13,7 +13,8 @@
 
 def partner_offsets(peer_count):
     found = []
-    for offset in list(range(1, REACH + 1)) + [peer_count // 2] + [-o for o in range(1, REACH + 1)]:
+    order = [peer_count // 2] + [sign * o for o in range(1, REACH + 1) for sign in (1, -1)]
+    for offset in order:
         offset = offset % peer_count
         if offset != 0 and offset not in found:
             found.append(offset)

time: 116 us -> 128 us (1.10)
  waiting for transfers between devices: 15.9 us -> 24.4 us
  starting transfers between devices: 52 us -> 55.2 us
    ppermute x15, waiting for transfers between devices: 7.42 us -> 15.9 us  [fetch_halo(): lax.ppermute(vector[asked_for[which]], 'rows', from_partner(offset))]
    ppermute x15, starting transfers between devices: 26.4 us -> 29.3 us  [fetch_halo(): lax.ppermute(vector[asked_for[which]], 'rows', from_partner(offset))]
  transfers between devices with their start and end apart: 24 -> 24, of which waited for: 7 -> 8; matrix products, arithmetic and copies ran while one was open for 10% -> 10% of each run, Pallas kernels for 0% -> 0%
where the time goes in v8:
time: 128 us; the launch traced here: 127 us
  starting transfers between devices  55.2 us (43%)
  local copies, waits for them, and re-layouts  28.1 us (22%)
  waiting for transfers between devices  24.4 us (19%)
  matrix products  12.2 us (10%)
  other arithmetic  6.57 us (5%)
    ppermute x15, starting transfers between devices, fetch_halo(): lax.ppermute(vector[asked_for[which]], 'rows', from_partner(offset))  29.3 us
    ppermute x15, waiting for transfers between devices, fetch_halo(): lax.ppermute(vector[asked_for[which]], 'rows', from_partner(offset))  15.9 us
    ppermute x5, starting transfers between devices, per_device(): lax.ppermute(wanted[which], 'rows', to_partner(offset))  13.2 us
    unnamed x43, local copies, waits for them, and re-layouts  10.5 us
    ppermute x1, starting transfers between devices, per_device(): lax.ppermute(other, 'node', [(j, j ^ 1) for j in range(node_count)])  8.88 us
    gather x15, local copies, waits for them, and re-layouts, fetch_halo(): vector[asked_for[which]]  8.7 us
    ppermute x3, waiting for transfers between devices, per_device(): total = total + lax.ppermute(chunk, 'node', perm)  7.15 us
    dot_general x3, matrix products, apply_pair(): jnp.einsum('nscb,nsbd->ncd', picked, first, preferred_element_type=jnp.fl...  6.96 us
  transfers between devices with their start and end apart: 24, of which 8 were waited for; matrix products, arithmetic and copies ran while one was open for 10% of the time, Pallas kernels for 0%

profile of v8, /device:TPU:3, one launch (start us, length us, event | category | flops | bytes accessed | tf_op | source)
XLA Modules:
  0.0 127.2 jit_solution(6190702999452619552)
XLA Ops:
  0.0 0.9 copy.137
  4.2 7.0 %collective-permute-start = (s32[6]{0:T(128)S(1)}, s32[6]{0:T(128)S(1)}, u32[]{:S(2)}, u32[]{:S(2)}) collective-permute-start(s32[6]{0:T(128)S(1)} %get-tuple-element.19), channel_id=1, source_target_pairs={{0,16},{1,17},{2,18},{3,19},{4,20},{5,21},{6,22},{7,23},{8,24},{9,... | collective-permute-start | bytes 80 | tf_op jit(solution)/shard_map/ppermute | solution.py:62
  11.4 1.2 collective-permute-start.2
  12.6 4.7 %collective-permute-start.8 = (s32[6]{0:T(128)S(1)}, s32[6]{0:T(128)S(1)}, u32[]{:S(2)}, u32[]{:S(2)}) collective-permute-start(s32[6]{0:T(128)S(1)} %get-tuple-element.15), channel_id=1, source_target_pairs={{0,30},{1,31},{2,0},{3,1},{4,2},{5,3},{6,4},{7,5},{8,6},{9,7},{10,... | collective-permute-start | bytes 80 | tf_op jit(solution)/shard_map/ppermute | solution.py:62
  17.3 1.0 constant_dynamic-update-slice_fusion.5
  19.0 4.3 %collective-permute-start.1 = (bf16[6,32,128]{2,1,0:T(8,128)(2,1)S(1)}, bf16[6,32,128]{2,1,0:T(8,128)(2,1)S(1)}, u32[]{:S(2)}, u32[]{:S(2)}) collective-permute-start(bf16[6,32,128]{2,1,0:T(8,128)(2,1)S(1)} %gather_fusion), channel_id=1, source_target_pairs={{16,0},{17,1},{18,2},{19,3},{20,4},{21,5},{22,6},{23,7},{24,8},{25... | collective-permute-start | bytes 147464 | tf_op jit(solution)/shard_map/ppermute | solution.py:68
  24.6 1.5 %collective-permute-start.5 = (bf16[6,32,128]{2,1,0:T(8,128)(2,1)S(1)}, bf16[6,32,128]{2,1,0:T(8,128)(2,1)S(1)}, u32[]{:S(2)}, u32[]{:S(2)}) collective-permute-start(bf16[6,32,128]{2,1,0:T(8,128)(2,1)S(1)} %gather_fusion.2), channel_id=1, source_target_pairs={{31,0},{0,1},{1,2},{2,3},{3,4},{4,5},{5,6},{6,7},{7,8},{8,9},{9,10... | collective-permute-start | bytes 147464 | tf_op jit(solution)/shard_map/ppermute | solution.py:68
  26.7 8.5 %collective-permute-start.7 = (bf16[6,32,128]{2,1,0:T(8,128)(2,1)S(1)}, bf16[6,32,128]{2,1,0:T(8,128)(2,1)S(1)}, u32[]{:S(2)}, u32[]{:S(2)}) collective-permute-start(bf16[6,32,128]{2,1,0:T(8,128)(2,1)S(1)} %gather_fusion.3), channel_id=1, source_target_pairs={{2,0},{3,1},{4,2},{5,3},{6,4},{7,5},{8,6},{9,7},{10,8},{11,9},{12,... | collective-permute-start | bytes 147464 | tf_op jit(solution)/shard_map/ppermute | solution.py:68
  36.4 6.0 %collective-permute-done.9 = bf16[6,32,128]{2,1,0:T(8,128)(2,1)S(1)} collective-permute-done((bf16[6,32,128]{2,1,0:T(8,128)(2,1)S(1)}, bf16[6,32,128]{2,1,0:T(8,128)(2,1)S(1)}, u32[]{:S(2)}, u32[]{:S(2)}) %collective-permute-start.9) | collective-permute-done | bytes 49184 | tf_op jit(solution)/shard_map/ppermute | solution.py:68
  43.2 2.8 %convolution_bitcast_fusion.4 = f32[24,32,128]{2,1,0:T(8,128)S(1)} fusion(bf16[24,5,32,128]{3,2,1,0:T(8,128)(2,1)S(1)} %bitcast.146, bf16[24,5,128,128]{3,2,1,0:T(8,128)(2,1)} %param.6), kind=kOutput, calls=%fused_computation.22 | convolution fusion | flops 125829120 | bytes 5308416 | tf_op jit(solution)/shard_map/nscb,nsbd->ncd/dot_general | solution.py:26
  46.4 0.9 copy-done.3
  48.7 1.2 collective-permute-start.10
  52.6 1.5 %collective-permute-start.12 = (bf16[6,64,128]{2,1,0:T(8,128)(2,1)S(1)}, bf16[6,64,128]{2,1,0:T(8,128)(2,1)S(1)}, u32[]{:S(2)}, u32[]{:S(2)}) collective-permute-start(bf16[6,64,128]{2,1,0:T(8,128)(2,1)S(1)} %gather_fusion.8), channel_id=1, source_target_pairs={{31,0},{0,1},{1,2},{2,3},{3,4},{4,5},{5,6},{6,7},{7,8},{8,9},{9,10... | collective-permute-start | bytes 294920 | tf_op jit(solution)/shard_map/ppermute | solution.py:68
  54.0 3.0 %collective-permute-start.13 = (bf16[6,64,128]{2,1,0:T(8,128)(2,1)S(1)}, bf16[6,64,128]{2,1,0:T(8,128)(2,1)S(1)}, u32[]{:S(2)}, u32[]{:S(2)}) collective-permute-start(bf16[6,64,128]{2,1,0:T(8,128)(2,1)S(1)} %gather_fusion.9), channel_id=1, source_target_pairs={{2,0},{3,1},{4,2},{5,3},{6,4},{7,5},{8,6},{9,7},{10,8},{11,9},{12,... | collective-permute-start | bytes 294920 | tf_op jit(solution)/shard_map/ppermute | solution.py:68
  59.6 5.6 %collective-permute-done.14 = bf16[6,64,128]{2,1,0:T(8,128)(2,1)S(1)} collective-permute-done((bf16[6,64,128]{2,1,0:T(8,128)(2,1)S(1)}, bf16[6,64,128]{2,1,0:T(8,128)(2,1)S(1)}, u32[]{:S(2)}, u32[]{:S(2)}) %collective-permute-start.14) | collective-permute-done | bytes 98336 | tf_op jit(solution)/shard_map/ppermute | solution.py:68
  65.9 2.1 %gather_fusion.11 = bf16[120,64,128]{2,1,0:T(8,128)(2,1)S(1)} fusion(bf16[54,64,128]{2,1,0:T(8,128)(2,1)} %constant_dynamic-update-slice_fusion.6, s32[1024]{0:T(1024)S(1)} %pad_clamp_fusion), kind=kCustom, calls=%fused_computation.11 | custom fusion | bytes 3932640 | tf_op jit(solution)/shard_map/gather | solution.py:25
  68.0 3.2 %convolution_bitcast_fusion.3 = f32[24,64,128]{2,1,0:T(8,128)S(1)} fusion(bf16[24,5,64,128]{3,2,1,0:T(8,128)(2,1)S(1)} %bitcast.141, bf16[24,5,128,128]{3,2,1,0:T(8,128)(2,1)} %param.6), kind=kOutput, calls=%fused_computation.21 | convolution fusion | flops 251658240 | bytes 6684672 | tf_op jit(solution)/shard_map/nscb,nsbd->ncd/dot_general | solution.py:26
  73.0 1.0 copy-done.4
  74.0 1.0 fusion.6
  78.2 3.3 %collective-permute-start.15 = (bf16[6,64,128]{2,1,0:T(8,128)(2,1)S(1)}, bf16[6,64,128]{2,1,0:T(8,128)(2,1)S(1)}, u32[]{:S(2)}, u32[]{:S(2)}) collective-permute-start(bf16[6,64,128]{2,1,0:T(8,128)(2,1)S(1)} %gather_fusion.12), channel_id=1, source_target_pairs={{16,0},{17,1},{18,2},{19,3},{20,4},{21,5},{22,6},{23,7},{24,8},{25... | collective-permute-start | bytes 294920 | tf_op jit(solution)/shard_map/ppermute | solution.py:68
  81.5 1.5 %collective-permute-start.17 = (bf16[6,64,128]{2,1,0:T(8,128)(2,1)S(1)}, bf16[6,64,128]{2,1,0:T(8,128)(2,1)S(1)}, u32[]{:S(2)}, u32[]{:S(2)}) collective-permute-start(bf16[6,64,128]{2,1,0:T(8,128)(2,1)S(1)} %gather_fusion.14), channel_id=1, source_target_pairs={{31,0},{0,1},{1,2},{2,3},{3,4},{4,5},{5,6},{6,7},{7,8},{8,9},{9,10... | collective-permute-start | bytes 294920 | tf_op jit(solution)/shard_map/ppermute | solution.py:68
  82.9 4.2 %collective-permute-start.18 = (bf16[6,64,128]{2,1,0:T(8,128)(2,1)S(1)}, bf16[6,64,128]{2,1,0:T(8,128)(2,1)S(1)}, u32[]{:S(2)}, u32[]{:S(2)}) collective-permute-start(bf16[6,64,128]{2,1,0:T(8,128)(2,1)S(1)} %gather_fusion.15), channel_id=1, source_target_pairs={{2,0},{3,1},{4,2},{5,3},{6,4},{7,5},{8,6},{9,7},{10,8},{11,9},{12,... | collective-permute-start | bytes 294920 | tf_op jit(solution)/shard_map/ppermute | solution.py:68
  90.5 3.7 %collective-permute-done.19 = bf16[6,64,128]{2,1,0:T(8,128)(2,1)S(1)} collective-permute-done((bf16[6,64,128]{2,1,0:T(8,128)(2,1)S(1)}, bf16[6,64,128]{2,1,0:T(8,128)(2,1)S(1)}, u32[]{:S(2)}, u32[]{:S(2)}) %collective-permute-start.19) | collective-permute-done | bytes 98336 | tf_op jit(solution)/shard_map/ppermute | solution.py:68
  94.9 2.1 %gather_fusion.17 = bf16[120,64,128]{2,1,0:T(8,128)(2,1)S(1)} fusion(bf16[54,64,128]{2,1,0:T(8,128)(2,1)} %constant_dynamic-update-slice_fusion.12, s32[1024]{0:T(1024)S(1)} %pad_clamp_fusion), kind=kCustom, calls=%fused_computation.17 | custom fusion | bytes 3932640 | tf_op jit(solution)/shard_map/gather | solution.py:25
  97.0 3.2 %convolution_bitcast_fusion = f32[24,64,128]{2,1,0:T(8,128)S(1)} fusion(bf16[24,5,64,128]{3,2,1,0:T(8,128)(2,1)S(1)} %bitcast.139, bf16[24,5,128,128]{3,2,1,0:T(8,128)(2,1)} %param.7), kind=kOutput, calls=%fused_computation.18 | convolution fusion | flops 251658240 | bytes 6684672 | tf_op jit(solution)/shard_map/nscb,nsbd->ncd/dot_general | solution.py:29
  100.3 0.9 convolution_bitcast_fusion.1
  105.1 8.9 %collective-permute-start.20 = (f32[4,2,4,24,128]{4,3,2,1,0:T(8,128)S(1)}, f32[4,2,4,24,128]{4,3,2,1,0:T(8,128)S(1)}, u32[]{:S(2)}, u32[]{:S(2)}) collective-permute-start(f32[4,2,4,24,128]{4,3,2,1,0:T(8,128)S(1)} %bitcast.155), channel_id=1, source_target_pairs={{0,32},{32,0},{64,96},{96,64},{128,160},{160,128},{192,224},{224,1... | collective-permute-start | bytes 1179656 | tf_op jit(solution)/shard_map/ppermute | solution.py:111
  114.0 1.3 %collective-permute-done.20 = f32[4,2,4,24,128]{4,3,2,1,0:T(8,128)S(1)} collective-permute-done((f32[4,2,4,24,128]{4,3,2,1,0:T(8,128)S(1)}, f32[4,2,4,24,128]{4,3,2,1,0:T(8,128)S(1)}, u32[]{:S(2)}, u32[]{:S(2)}) %collective-permute-start.20) | collective-permute-done | bytes 393248 | tf_op jit(solution)/shard_map/ppermute | solution.py:111
  115.5 2.8 %collective-permute-start.23 = (f32[2,4,24,128]{3,2,1,0:T(8,128)S(1)}, f32[2,4,24,128]{3,2,1,0:T(8,128)S(1)}, u32[]{:S(2)}, u32[]{:S(2)}) collective-permute-start(f32[2,4,24,128]{3,2,1,0:T(8,128)S(1)} %get-tuple-element.46), channel_id=1, source_target_pairs={{0,192},{32,224},{64,0},{96,32},{128,64},{160,96},{192,128},{224,1... | collective-permute-start | bytes 294920 | tf_op jit(solution)/shard_map/ppermute | solution.py:116
  119.4 2.7 %collective-permute-done.23 = f32[2,4,24,128]{3,2,1,0:T(8,128)S(1)} collective-permute-done((f32[2,4,24,128]{3,2,1,0:T(8,128)S(1)}, f32[2,4,24,128]{3,2,1,0:T(8,128)S(1)}, u32[]{:S(2)}, u32[]{:S(2)}) %collective-permute-start.23) | collective-permute-done | bytes 98336 | tf_op jit(solution)/shard_map/ppermute | solution.py:116
  122.1 1.3 %collective-permute-done.22 = f32[2,4,24,128]{3,2,1,0:T(8,128)S(1)} collective-permute-done((f32[2,4,24,128]{3,2,1,0:T(8,128)S(1)}, f32[2,4,24,128]{3,2,1,0:T(8,128)S(1)}, u32[]{:S(2)}, u32[]{:S(2)}) %collective-permute-start.22) | collective-permute-done | bytes 98336 | tf_op jit(solution)/shard_map/ppermute | solution.py:116
  123.4 3.1 %collective-permute-done.21 = f32[2,4,24,128]{3,2,1,0:T(8,128)S(1)} collective-permute-done((f32[2,4,24,128]{3,2,1,0:T(8,128)S(1)}, f32[2,4,24,128]{3,2,1,0:T(8,128)S(1)}, u32[]{:S(2)}, u32[]{:S(2)}) %collective-permute-start.21) | collective-permute-done | bytes 98336 | tf_op jit(solution)/shard_map/ppermute | solution.py:116
  (145 shorter events, 29.8 us)
Async XLA Ops:
  0.0 46.0 %copy-start = (bf16[1,2,24,128,128]{4,3,2,1,0:T(8,128)(2,1)S(1)}, bf16[1,2,24,128,128]{4,3,2,1,0:T(8,128)(2,1)}, u32[]{:S(2)}) copy-start(bf16[1,2,24,128,128]{4,3,2,1,0:T(8,128)(2,1)} %param.8) | copy-start | bytes 4718596
  0.0 18.3 %copy-start.10 = (bf16[32,24,128]{2,1,0:T(8,128)(2,1)S(1)}, bf16[32,24,128]{2,1,0:T(8,128)(2,1)}, u32[]{:S(2)}) copy-start(bf16[32,24,128]{2,1,0:T(8,128)(2,1)} %param.5) | copy-start | bytes 589828
  4.2 14.3 %collective-permute-start = (s32[6]{0:T(128)S(1)}, s32[6]{0:T(128)S(1)}, u32[]{:S(2)}, u32[]{:S(2)}) collective-permute-start(s32[6]{0:T(128)S(1)} %get-tuple-element.19), channel_id=1, source_target_pairs={{0,16},{1,17},{2,18},{3,19},{4,20},{5,21},{6,22},{7,23},{8,24},{9,... | collective-permute-start | bytes 80 | tf_op jit(solution)/shard_map/ppermute | solution.py:62
  11.1 12.2 %collective-permute-start.4 = (s32[6]{0:T(128)S(1)}, s32[6]{0:T(128)S(1)}, u32[]{:S(2)}, u32[]{:S(2)}) collective-permute-start(s32[6]{0:T(128)S(1)} %get-tuple-element.17), channel_id=1, source_target_pairs={{0,31},{1,0},{2,1},{3,2},{4,3},{5,4},{6,5},{7,6},{8,7},{9,8},{10,9... | collective-permute-start | bytes 80 | tf_op jit(solution)/shard_map/ppermute | solution.py:62
  11.4 11.9 %collective-permute-start.2 = (s32[6]{0:T(128)S(1)}, s32[6]{0:T(128)S(1)}, u32[]{:S(2)}, u32[]{:S(2)}) collective-permute-start(s32[6]{0:T(128)S(1)} %get-tuple-element.16), channel_id=1, source_target_pairs={{0,1},{1,2},{2,3},{3,4},{4,5},{5,6},{6,7},{7,8},{8,9},{9,10},{10,1... | collective-permute-start | bytes 80 | tf_op jit(solution)/shard_map/ppermute | solution.py:62
  12.6 13.5 %collective-permute-start.8 = (s32[6]{0:T(128)S(1)}, s32[6]{0:T(128)S(1)}, u32[]{:S(2)}, u32[]{:S(2)}) collective-permute-start(s32[6]{0:T(128)S(1)} %get-tuple-element.15), channel_id=1, source_target_pairs={{0,30},{1,31},{2,0},{3,1},{4,2},{5,3},{6,4},{7,5},{8,6},{9,7},{10,... | collective-permute-start | bytes 80 | tf_op jit(solution)/shard_map/ppermute | solution.py:62
  17.3 8.8 %collective-permute-start.6 = (s32[6]{0:T(128)S(1)}, s32[6]{0:T(128)S(1)}, u32[]{:S(2)}, u32[]{:S(2)}) collective-permute-start(s32[6]{0:T(128)S(1)} %get-tuple-element.18), channel_id=1, source_target_pairs={{0,2},{1,3},{2,4},{3,5},{4,6},{5,7},{6,8},{7,9},{8,10},{9,11},{10,... | collective-permute-start | bytes 80 | tf_op jit(solution)/shard_map/ppermute | solution.py:62
  19.0 16.8 %collective-permute-start.1 = (bf16[6,32,128]{2,1,0:T(8,128)(2,1)S(1)}, bf16[6,32,128]{2,1,0:T(8,128)(2,1)S(1)}, u32[]{:S(2)}, u32[]{:S(2)}) collective-permute-start(bf16[6,32,128]{2,1,0:T(8,128)(2,1)S(1)} %gather_fusion), channel_id=1, source_target_pairs={{16,0},{17,1},{18,2},{19,3},{20,4},{21,5},{22,6},{23,7},{24,8},{25... | collective-permute-start | bytes 147464 | tf_op jit(solution)/shard_map/ppermute | solution.py:68
  23.9 12.0 %collective-permute-start.3 = (bf16[6,32,128]{2,1,0:T(8,128)(2,1)S(1)}, bf16[6,32,128]{2,1,0:T(8,128)(2,1)S(1)}, u32[]{:S(2)}, u32[]{:S(2)}) collective-permute-start(bf16[6,32,128]{2,1,0:T(8,128)(2,1)S(1)} %gather_fusion.1), channel_id=1, source_target_pairs={{1,0},{2,1},{3,2},{4,3},{5,4},{6,5},{7,6},{8,7},{9,8},{10,9},{11,1... | collective-permute-start | bytes 147464 | tf_op jit(solution)/shard_map/ppermute | solution.py:68
  24.6 11.3 %collective-permute-start.5 = (bf16[6,32,128]{2,1,0:T(8,128)(2,1)S(1)}, bf16[6,32,128]{2,1,0:T(8,128)(2,1)S(1)}, u32[]{:S(2)}, u32[]{:S(2)}) collective-permute-start(bf16[6,32,128]{2,1,0:T(8,128)(2,1)S(1)} %gather_fusion.2), channel_id=1, source_target_pairs={{31,0},{0,1},{1,2},{2,3},{3,4},{4,5},{5,6},{6,7},{7,8},{8,9},{9,10... | collective-permute-start | bytes 147464 | tf_op jit(solution)/shard_map/ppermute | solution.py:68
  26.2 25.1 %copy-start.11 = (s32[1024]{0:T(1024)}, s32[1024]{0:T(1024)S(1)}, u32[]{:S(2)}) copy-start(s32[1024]{0:T(1024)S(1)} %pad_clamp_fusion.2) | copy-start | bytes 12292
  26.7 9.6 %collective-permute-start.7 = (bf16[6,32,128]{2,1,0:T(8,128)(2,1)S(1)}, bf16[6,32,128]{2,1,0:T(8,128)(2,1)S(1)}, u32[]{:S(2)}, u32[]{:S(2)}) collective-permute-start(bf16[6,32,128]{2,1,0:T(8,128)(2,1)S(1)} %gather_fusion.3), channel_id=1, source_target_pairs={{2,0},{3,1},{4,2},{5,3},{6,4},{7,5},{8,6},{9,7},{10,8},{11,9},{12,... | collective-permute-start | bytes 147464 | tf_op jit(solution)/shard_map/ppermute | solution.py:68
  35.2 16.7 %copy-start.12 = (s32[1024]{0:T(1024)}, s32[1024]{0:T(1024)S(1)}, u32[]{:S(2)}) copy-start(s32[1024]{0:T(1024)S(1)} %pad_clamp_fusion.1) | copy-start | bytes 12292
  35.8 6.6 %collective-permute-start.9 = (bf16[6,32,128]{2,1,0:T(8,128)(2,1)S(1)}, bf16[6,32,128]{2,1,0:T(8,128)(2,1)S(1)}, u32[]{:S(2)}, u32[]{:S(2)}) collective-permute-start(bf16[6,32,128]{2,1,0:T(8,128)(2,1)S(1)} %gather_fusion.4), channel_id=1, source_target_pairs={{30,0},{31,1},{0,2},{1,3},{2,4},{3,5},{4,6},{5,7},{6,8},{7,9},{8,1... | collective-permute-start | bytes 147464 | tf_op jit(solution)/shard_map/ppermute | solution.py:68
  46.0 2.1 %copy-start.6 = (f32[24,32,128]{2,1,0:T(8,128)}, f32[24,32,128]{2,1,0:T(8,128)S(1)}, u32[]{:S(2)}) copy-start(f32[24,32,128]{2,1,0:T(8,128)S(1)} %convolution_bitcast_fusion.4) | copy-start | bytes 1179652
  48.7 8.3 %collective-permute-start.10 = (bf16[6,64,128]{2,1,0:T(8,128)(2,1)S(1)}, bf16[6,64,128]{2,1,0:T(8,128)(2,1)S(1)}, u32[]{:S(2)}, u32[]{:S(2)}) collective-permute-start(bf16[6,64,128]{2,1,0:T(8,128)(2,1)S(1)} %gather_fusion.6), channel_id=1, source_target_pairs={{16,0},{17,1},{18,2},{19,3},{20,4},{21,5},{22,6},{23,7},{24,8},{25... | collective-permute-start | bytes 294920 | tf_op jit(solution)/shard_map/ppermute | solution.py:68
  52.5 5.2 %collective-permute-start.11 = (bf16[6,64,128]{2,1,0:T(8,128)(2,1)S(1)}, bf16[6,64,128]{2,1,0:T(8,128)(2,1)S(1)}, u32[]{:S(2)}, u32[]{:S(2)}) collective-permute-start(bf16[6,64,128]{2,1,0:T(8,128)(2,1)S(1)} %gather_fusion.7), channel_id=1, source_target_pairs={{1,0},{2,1},{3,2},{4,3},{5,4},{6,5},{7,6},{8,7},{9,8},{10,9},{11,1... | collective-permute-start | bytes 294920 | tf_op jit(solution)/shard_map/ppermute | solution.py:68
  52.6 5.8 %collective-permute-start.12 = (bf16[6,64,128]{2,1,0:T(8,128)(2,1)S(1)}, bf16[6,64,128]{2,1,0:T(8,128)(2,1)S(1)}, u32[]{:S(2)}, u32[]{:S(2)}) collective-permute-start(bf16[6,64,128]{2,1,0:T(8,128)(2,1)S(1)} %gather_fusion.8), channel_id=1, source_target_pairs={{31,0},{0,1},{1,2},{2,3},{3,4},{4,5},{5,6},{6,7},{7,8},{8,9},{9,10... | collective-permute-start | bytes 294920 | tf_op jit(solution)/shard_map/ppermute | solution.py:68
  54.0 5.0 %collective-permute-start.13 = (bf16[6,64,128]{2,1,0:T(8,128)(2,1)S(1)}, bf16[6,64,128]{2,1,0:T(8,128)(2,1)S(1)}, u32[]{:S(2)}, u32[]{:S(2)}) collective-permute-start(bf16[6,64,128]{2,1,0:T(8,128)(2,1)S(1)} %gather_fusion.9), channel_id=1, source_target_pairs={{2,0},{3,1},{4,2},{5,3},{6,4},{7,5},{8,6},{9,7},{10,8},{11,9},{12,... | collective-permute-start | bytes 294920 | tf_op jit(solution)/shard_map/ppermute | solution.py:68
  57.0 8.2 %collective-permute-start.14 = (bf16[6,64,128]{2,1,0:T(8,128)(2,1)S(1)}, bf16[6,64,128]{2,1,0:T(8,128)(2,1)S(1)}, u32[]{:S(2)}, u32[]{:S(2)}) collective-permute-start(bf16[6,64,128]{2,1,0:T(8,128)(2,1)S(1)} %gather_fusion.10), channel_id=1, source_target_pairs={{30,0},{31,1},{0,2},{1,3},{2,4},{3,5},{4,6},{5,7},{6,8},{7,9},{8,1... | collective-permute-start | bytes 294920 | tf_op jit(solution)/shard_map/ppermute | solution.py:68
  68.0 3.3 %copy-start.2 = (bf16[24,5,128,128]{3,2,1,0:T(8,128)(2,1)S(1)}, bf16[24,5,128,128]{3,2,1,0:T(8,128)(2,1)}, u32[]{:S(2)}) copy-start(bf16[24,5,128,128]{3,2,1,0:T(8,128)(2,1)} %param.7) | copy-start | bytes 11796484
  78.2 9.8 %collective-permute-start.15 = (bf16[6,64,128]{2,1,0:T(8,128)(2,1)S(1)}, bf16[6,64,128]{2,1,0:T(8,128)(2,1)S(1)}, u32[]{:S(2)}, u32[]{:S(2)}) collective-permute-start(bf16[6,64,128]{2,1,0:T(8,128)(2,1)S(1)} %gather_fusion.12), channel_id=1, source_target_pairs={{16,0},{17,1},{18,2},{19,3},{20,4},{21,5},{22,6},{23,7},{24,8},{25... | collective-permute-start | bytes 294920 | tf_op jit(solution)/shard_map/ppermute | solution.py:68
  81.5 7.1 %collective-permute-start.16 = (bf16[6,64,128]{2,1,0:T(8,128)(2,1)S(1)}, bf16[6,64,128]{2,1,0:T(8,128)(2,1)S(1)}, u32[]{:S(2)}, u32[]{:S(2)}) collective-permute-start(bf16[6,64,128]{2,1,0:T(8,128)(2,1)S(1)} %gather_fusion.13), channel_id=1, source_target_pairs={{1,0},{2,1},{3,2},{4,3},{5,4},{6,5},{7,6},{8,7},{9,8},{10,9},{11,1... | collective-permute-start | bytes 294920 | tf_op jit(solution)/shard_map/ppermute | solution.py:68
  81.5 7.8 %collective-permute-start.17 = (bf16[6,64,128]{2,1,0:T(8,128)(2,1)S(1)}, bf16[6,64,128]{2,1,0:T(8,128)(2,1)S(1)}, u32[]{:S(2)}, u32[]{:S(2)}) collective-permute-start(bf16[6,64,128]{2,1,0:T(8,128)(2,1)S(1)} %gather_fusion.14), channel_id=1, source_target_pairs={{31,0},{0,1},{1,2},{2,3},{3,4},{4,5},{5,6},{6,7},{7,8},{8,9},{9,10... | collective-permute-start | bytes 294920 | tf_op jit(solution)/shard_map/ppermute | solution.py:68
  82.9 6.9 %collective-permute-start.18 = (bf16[6,64,128]{2,1,0:T(8,128)(2,1)S(1)}, bf16[6,64,128]{2,1,0:T(8,128)(2,1)S(1)}, u32[]{:S(2)}, u32[]{:S(2)}) collective-permute-start(bf16[6,64,128]{2,1,0:T(8,128)(2,1)S(1)} %gather_fusion.15), channel_id=1, source_target_pairs={{2,0},{3,1},{4,2},{5,3},{6,4},{7,5},{8,6},{9,7},{10,8},{11,9},{12,... | collective-permute-start | bytes 294920 | tf_op jit(solution)/shard_map/ppermute | solution.py:68
  87.2 7.1 %collective-permute-start.19 = (bf16[6,64,128]{2,1,0:T(8,128)(2,1)S(1)}, bf16[6,64,128]{2,1,0:T(8,128)(2,1)S(1)}, u32[]{:S(2)}, u32[]{:S(2)}) collective-permute-start(bf16[6,64,128]{2,1,0:T(8,128)(2,1)S(1)} %gather_fusion.16), channel_id=1, source_target_pairs={{30,0},{31,1},{0,2},{1,3},{2,4},{3,5},{4,6},{5,7},{6,8},{7,9},{8,1... | collective-permute-start | bytes 294920 | tf_op jit(solution)/shard_map/ppermute | solution.py:68
  97.0 3.3 %copy-start.1 = (bf16[24,5,128,128]{3,2,1,0:T(8,128)(2,1)S(1)}, bf16[24,5,128,128]{3,2,1,0:T(8,128)(2,1)}, u32[]{:S(2)}) copy-start(bf16[24,5,128,128]{3,2,1,0:T(8,128)(2,1)} %param.6) | copy-start | bytes 11796484
  102.1 1.4 %copy-start.9 = (f32[24,64,128]{2,1,0:T(8,128)S(1)}, f32[24,64,128]{2,1,0:T(8,128)}, u32[]{:S(2)}) copy-start(f32[24,64,128]{2,1,0:T(8,128)} %get-tuple-element.44) | copy-start | bytes 2359300
  105.1 10.2 %collective-permute-start.20 = (f32[4,2,4,24,128]{4,3,2,1,0:T(8,128)S(1)}, f32[4,2,4,24,128]{4,3,2,1,0:T(8,128)S(1)}, u32[]{:S(2)}, u32[]{:S(2)}) collective-permute-start(f32[4,2,4,24,128]{4,3,2,1,0:T(8,128)S(1)} %bitcast.155), channel_id=1, source_target_pairs={{0,32},{32,0},{64,96},{96,64},{128,160},{160,128},{192,224},{224,1... | collective-permute-start | bytes 1179656 | tf_op jit(solution)/shard_map/ppermute | solution.py:111
  115.5 6.6 %collective-permute-start.23 = (f32[2,4,24,128]{3,2,1,0:T(8,128)S(1)}, f32[2,4,24,128]{3,2,1,0:T(8,128)S(1)}, u32[]{:S(2)}, u32[]{:S(2)}) collective-permute-start(f32[2,4,24,128]{3,2,1,0:T(8,128)S(1)} %get-tuple-element.46), channel_id=1, source_target_pairs={{0,192},{32,224},{64,0},{96,32},{128,64},{160,96},{192,128},{224,1... | collective-permute-start | bytes 294920 | tf_op jit(solution)/shard_map/ppermute | solution.py:116
  118.3 5.1 %collective-permute-start.22 = (f32[2,4,24,128]{3,2,1,0:T(8,128)S(1)}, f32[2,4,24,128]{3,2,1,0:T(8,128)S(1)}, u32[]{:S(2)}, u32[]{:S(2)}) collective-permute-start(f32[2,4,24,128]{3,2,1,0:T(8,128)S(1)} %get-tuple-element.47), channel_id=1, source_target_pairs={{0,128},{32,160},{64,192},{96,224},{128,0},{160,32},{192,64},{224,... | collective-permute-start | bytes 294920 | tf_op jit(solution)/shard_map/ppermute | solution.py:116
  118.7 7.8 %collective-permute-start.21 = (f32[2,4,24,128]{3,2,1,0:T(8,128)S(1)}, f32[2,4,24,128]{3,2,1,0:T(8,128)S(1)}, u32[]{:S(2)}, u32[]{:S(2)}) collective-permute-start(f32[2,4,24,128]{3,2,1,0:T(8,128)S(1)} %get-tuple-element.45), channel_id=1, source_target_pairs={{0,64},{32,96},{64,128},{96,160},{128,192},{160,224},{192,0},{224,... | collective-permute-start | bytes 294920 | tf_op jit(solution)/shard_map/ppermute | solution.py:116
  (5 other events, 5.2 us)

commit v9 on v8

--- a/solution.py
+++ b/solution.py
@@ -13,7 +13,7 @@
 
 def partner_offsets(peer_count):
     found = []
-    order = [peer_count // 2] + [sign * o for o in range(1, REACH + 1) for sign in (1, -1)]
+    order = [sign * o for o in range(1, REACH + 1) for sign in (1, -1)] + [peer_count // 2]
     for offset in order:
         offset = offset % peer_count
         if offset != 0 and offset not in found:

time: 128 us -> 125 us (0.977)
  waiting for transfers between devices: 24.4 us -> 16.4 us
  starting transfers between devices: 55.2 us -> 60.1 us
    ppermute x15, waiting for transfers between devices: 15.9 us -> 7.88 us  [fetch_halo(): lax.ppermute(vector[asked_for[which]], 'rows', from_partner(offset))]
    ppermute x15, starting transfers between devices: 29.3 us -> 35.7 us  [fetch_halo(): lax.ppermute(vector[asked_for[which]], 'rows', from_partner(offset))]
    ppermute x1, starting transfers between devices: 8.88 us -> 7.31 us  [per_device(): lax.ppermute(other, 'node', [(j, j ^ 1) for j in range(node_count)])]
where the time goes in v9:
time: 125 us; the launch traced here: 124 us
  starting transfers between devices  60.1 us (48%)
  local copies, waits for them, and re-layouts  28.1 us (22%)
  waiting for transfers between devices  16.4 us (13%)
  matrix products  12.2 us (10%)
  other arithmetic  6.57 us (5%)
    ppermute x15, starting transfers between devices, fetch_halo(): lax.ppermute(vector[asked_for[which]], 'rows', from_partner(offset))  35.7 us
    ppermute x5, starting transfers between devices, per_device(): lax.ppermute(wanted[which], 'rows', to_partner(offset))  13.3 us
    unnamed x43, local copies, waits for them, and re-layouts  10.5 us
    gather x15, local copies, waits for them, and re-layouts, fetch_halo(): vector[asked_for[which]]  8.7 us
    ppermute x15, waiting for transfers between devices, fetch_halo(): lax.ppermute(vector[asked_for[which]], 'rows', from_partner(offset))  7.88 us
    ppermute x1, starting transfers between devices, per_device(): lax.ppermute(other, 'node', [(j, j ^ 1) for j in range(node_count)])  7.31 us
    ppermute x3, waiting for transfers between devices, per_device(): total = total + lax.ppermute(chunk, 'node', perm)  7.15 us
    dot_general x3, matrix products, apply_pair(): jnp.einsum('nscb,nsbd->ncd', picked, first, preferred_element_type=jnp.fl...  6.97 us
  transfers between devices with their start and end apart: 24, of which 8 were waited for; matrix products, arithmetic and copies ran while one was open for 10% of the time, Pallas kernels for 0%

profile of v9, /device:TPU:3, one launch (start us, length us, event | category | flops | bytes accessed | tf_op | source)
XLA Modules:
  0.0 124.1 jit_solution(4047563633763960308)
XLA Ops:
  4.2 1.3 %collective-permute-start = (s32[6]{0:T(128)S(1)}, s32[6]{0:T(128)S(1)}, u32[]{:S(2)}, u32[]{:S(2)}) collective-permute-start(s32[6]{0:T(128)S(1)} %get-tuple-element.19), channel_id=1, source_target_pairs={{0,1},{1,2},{2,3},{3,4},{4,5},{5,6},{6,7},{7,8},{8,9},{9,10},{10,1... | collective-permute-start | bytes 80 | tf_op jit(solution)/shard_map/ppermute | solution.py:62
  5.4 2.2 %collective-permute-start.4 = (s32[6]{0:T(128)S(1)}, s32[6]{0:T(128)S(1)}, u32[]{:S(2)}, u32[]{:S(2)}) collective-permute-start(s32[6]{0:T(128)S(1)} %get-tuple-element.17), channel_id=1, source_target_pairs={{0,2},{1,3},{2,4},{3,5},{4,6},{5,7},{6,8},{7,9},{8,10},{9,11},{10,... | collective-permute-start | bytes 80 | tf_op jit(solution)/shard_map/ppermute | solution.py:62
  8.1 6.9 %collective-permute-start.8 = (s32[6]{0:T(128)S(1)}, s32[6]{0:T(128)S(1)}, u32[]{:S(2)}, u32[]{:S(2)}) collective-permute-start(s32[6]{0:T(128)S(1)} %get-tuple-element.15), channel_id=1, source_target_pairs={{0,16},{1,17},{2,18},{3,19},{4,20},{5,21},{6,22},{7,23},{8,24},{9,... | collective-permute-start | bytes 80 | tf_op jit(solution)/shard_map/ppermute | solution.py:62
  15.1 2.4 %collective-permute-start.6 = (s32[6]{0:T(128)S(1)}, s32[6]{0:T(128)S(1)}, u32[]{:S(2)}, u32[]{:S(2)}) collective-permute-start(s32[6]{0:T(128)S(1)} %get-tuple-element.18), channel_id=1, source_target_pairs={{0,30},{1,31},{2,0},{3,1},{4,2},{5,3},{6,4},{7,5},{8,6},{9,7},{10,... | collective-permute-start | bytes 80 | tf_op jit(solution)/shard_map/ppermute | solution.py:62
  17.4 1.0 constant_dynamic-update-slice_fusion.5
  19.2 1.2 collective-permute-start.1
  20.9 1.1 collective-permute-start.3
  22.6 3.6 %collective-permute-start.5 = (bf16[6,32,128]{2,1,0:T(8,128)(2,1)S(1)}, bf16[6,32,128]{2,1,0:T(8,128)(2,1)S(1)}, u32[]{:S(2)}, u32[]{:S(2)}) collective-permute-start(bf16[6,32,128]{2,1,0:T(8,128)(2,1)S(1)} %gather_fusion.2), channel_id=1, source_target_pairs={{2,0},{3,1},{4,2},{5,3},{6,4},{7,5},{8,6},{9,7},{10,8},{11,9},{12,... | collective-permute-start | bytes 147464 | tf_op jit(solution)/shard_map/ppermute | solution.py:68
  27.4 3.6 %collective-permute-start.9 = (bf16[6,32,128]{2,1,0:T(8,128)(2,1)S(1)}, bf16[6,32,128]{2,1,0:T(8,128)(2,1)S(1)}, u32[]{:S(2)}, u32[]{:S(2)}) collective-permute-start(bf16[6,32,128]{2,1,0:T(8,128)(2,1)S(1)} %gather_fusion.4), channel_id=1, source_target_pairs={{16,0},{17,1},{18,2},{19,3},{20,4},{21,5},{22,6},{23,7},{24,8},{25... | collective-permute-start | bytes 147464 | tf_op jit(solution)/shard_map/ppermute | solution.py:68
  31.1 2.3 %collective-permute-done.7 = bf16[6,32,128]{2,1,0:T(8,128)(2,1)S(1)} collective-permute-done((bf16[6,32,128]{2,1,0:T(8,128)(2,1)S(1)}, bf16[6,32,128]{2,1,0:T(8,128)(2,1)S(1)}, u32[]{:S(2)}, u32[]{:S(2)}) %collective-permute-start.7) | collective-permute-done | bytes 49184 | tf_op jit(solution)/shard_map/ppermute | solution.py:68
  33.4 1.0 collective-permute-done.9
  35.2 2.8 %convolution_bitcast_fusion.4 = f32[24,32,128]{2,1,0:T(8,128)S(1)} fusion(bf16[24,5,32,128]{3,2,1,0:T(8,128)(2,1)S(1)} %bitcast.146, bf16[24,5,128,128]{3,2,1,0:T(8,128)(2,1)} %param.6), kind=kOutput, calls=%fused_computation.22 | convolution fusion | flops 125829120 | bytes 5308416 | tf_op jit(solution)/shard_map/nscb,nsbd->ncd/dot_general | solution.py:26
  43.3 2.0 %collective-permute-start.11 = (bf16[6,64,128]{2,1,0:T(8,128)(2,1)S(1)}, bf16[6,64,128]{2,1,0:T(8,128)(2,1)S(1)}, u32[]{:S(2)}, u32[]{:S(2)}) collective-permute-start(bf16[6,64,128]{2,1,0:T(8,128)(2,1)S(1)} %gather_fusion.7), channel_id=1, source_target_pairs={{31,0},{0,1},{1,2},{2,3},{3,4},{4,5},{5,6},{6,7},{7,8},{8,9},{9,10... | collective-permute-start | bytes 294920 | tf_op jit(solution)/shard_map/ppermute | solution.py:68
  45.3 8.5 %collective-permute-start.12 = (bf16[6,64,128]{2,1,0:T(8,128)(2,1)S(1)}, bf16[6,64,128]{2,1,0:T(8,128)(2,1)S(1)}, u32[]{:S(2)}, u32[]{:S(2)}) collective-permute-start(bf16[6,64,128]{2,1,0:T(8,128)(2,1)S(1)} %gather_fusion.8), channel_id=1, source_target_pairs={{2,0},{3,1},{4,2},{5,3},{6,4},{7,5},{8,6},{9,7},{10,8},{11,9},{12,... | collective-permute-start | bytes 294920 | tf_op jit(solution)/shard_map/ppermute | solution.py:68
  53.8 3.4 %collective-permute-start.14 = (bf16[6,64,128]{2,1,0:T(8,128)(2,1)S(1)}, bf16[6,64,128]{2,1,0:T(8,128)(2,1)S(1)}, u32[]{:S(2)}, u32[]{:S(2)}) collective-permute-start(bf16[6,64,128]{2,1,0:T(8,128)(2,1)S(1)} %gather_fusion.10), channel_id=1, source_target_pairs={{16,0},{17,1},{18,2},{19,3},{20,4},{21,5},{22,6},{23,7},{24,8},{25... | collective-permute-start | bytes 294920 | tf_op jit(solution)/shard_map/ppermute | solution.py:68
  59.2 3.6 %collective-permute-done.13 = bf16[6,64,128]{2,1,0:T(8,128)(2,1)S(1)} collective-permute-done((bf16[6,64,128]{2,1,0:T(8,128)(2,1)S(1)}, bf16[6,64,128]{2,1,0:T(8,128)(2,1)S(1)}, u32[]{:S(2)}, u32[]{:S(2)}) %collective-permute-start.13) | collective-permute-done | bytes 98336 | tf_op jit(solution)/shard_map/ppermute | solution.py:68
  64.0 2.1 %gather_fusion.11 = bf16[120,64,128]{2,1,0:T(8,128)(2,1)S(1)} fusion(bf16[54,64,128]{2,1,0:T(8,128)(2,1)} %constant_dynamic-update-slice_fusion.6, s32[1024]{0:T(1024)S(1)} %pad_clamp_fusion), kind=kCustom, calls=%fused_computation.11 | custom fusion | bytes 3932640 | tf_op jit(solution)/shard_map/gather | solution.py:25
  66.1 3.2 %convolution_bitcast_fusion.3 = f32[24,64,128]{2,1,0:T(8,128)S(1)} fusion(bf16[24,5,64,128]{3,2,1,0:T(8,128)(2,1)S(1)} %bitcast.141, bf16[24,5,128,128]{3,2,1,0:T(8,128)(2,1)} %param.6), kind=kOutput, calls=%fused_computation.21 | convolution fusion | flops 251658240 | bytes 6684672 | tf_op jit(solution)/shard_map/nscb,nsbd->ncd/dot_general | solution.py:26
  71.2 1.0 copy-done.4
  72.1 1.0 fusion.6
  76.4 1.5 %collective-permute-start.16 = (bf16[6,64,128]{2,1,0:T(8,128)(2,1)S(1)}, bf16[6,64,128]{2,1,0:T(8,128)(2,1)S(1)}, u32[]{:S(2)}, u32[]{:S(2)}) collective-permute-start(bf16[6,64,128]{2,1,0:T(8,128)(2,1)S(1)} %gather_fusion.13), channel_id=1, source_target_pairs={{31,0},{0,1},{1,2},{2,3},{3,4},{4,5},{5,6},{6,7},{7,8},{8,9},{9,10... | collective-permute-start | bytes 294920 | tf_op jit(solution)/shard_map/ppermute | solution.py:68
  77.8 6.3 %collective-permute-start.17 = (bf16[6,64,128]{2,1,0:T(8,128)(2,1)S(1)}, bf16[6,64,128]{2,1,0:T(8,128)(2,1)S(1)}, u32[]{:S(2)}, u32[]{:S(2)}) collective-permute-start(bf16[6,64,128]{2,1,0:T(8,128)(2,1)S(1)} %gather_fusion.14), channel_id=1, source_target_pairs={{2,0},{3,1},{4,2},{5,3},{6,4},{7,5},{8,6},{9,7},{10,8},{11,9},{12,... | collective-permute-start | bytes 294920 | tf_op jit(solution)/shard_map/ppermute | solution.py:68
  84.1 4.2 %collective-permute-start.19 = (bf16[6,64,128]{2,1,0:T(8,128)(2,1)S(1)}, bf16[6,64,128]{2,1,0:T(8,128)(2,1)S(1)}, u32[]{:S(2)}, u32[]{:S(2)}) collective-permute-start(bf16[6,64,128]{2,1,0:T(8,128)(2,1)S(1)} %gather_fusion.16), channel_id=1, source_target_pairs={{16,0},{17,1},{18,2},{19,3},{20,4},{21,5},{22,6},{23,7},{24,8},{25... | collective-permute-start | bytes 294920 | tf_op jit(solution)/shard_map/ppermute | solution.py:68
  91.1 1.0 collective-permute-done.18
  93.4 2.1 %gather_fusion.17 = bf16[120,64,128]{2,1,0:T(8,128)(2,1)S(1)} fusion(bf16[54,64,128]{2,1,0:T(8,128)(2,1)} %constant_dynamic-update-slice_fusion.12, s32[1024]{0:T(1024)S(1)} %pad_clamp_fusion), kind=kCustom, calls=%fused_computation.17 | custom fusion | bytes 3932640 | tf_op jit(solution)/shard_map/gather | solution.py:25
  95.5 3.2 %convolution_bitcast_fusion = f32[24,64,128]{2,1,0:T(8,128)S(1)} fusion(bf16[24,5,64,128]{3,2,1,0:T(8,128)(2,1)S(1)} %bitcast.139, bf16[24,5,128,128]{3,2,1,0:T(8,128)(2,1)} %param.7), kind=kOutput, calls=%fused_computation.18 | convolution fusion | flops 251658240 | bytes 6684672 | tf_op jit(solution)/shard_map/nscb,nsbd->ncd/dot_general | solution.py:29
  103.6 7.3 %collective-permute-start.20 = (f32[4,2,4,24,128]{4,3,2,1,0:T(8,128)S(1)}, f32[4,2,4,24,128]{4,3,2,1,0:T(8,128)S(1)}, u32[]{:S(2)}, u32[]{:S(2)}) collective-permute-start(f32[4,2,4,24,128]{4,3,2,1,0:T(8,128)S(1)} %bitcast.155), channel_id=1, source_target_pairs={{0,32},{32,0},{64,96},{96,64},{128,160},{160,128},{192,224},{224,1... | collective-permute-start | bytes 1179656 | tf_op jit(solution)/shard_map/ppermute | solution.py:111
  110.9 1.3 %collective-permute-done.20 = f32[4,2,4,24,128]{4,3,2,1,0:T(8,128)S(1)} collective-permute-done((f32[4,2,4,24,128]{4,3,2,1,0:T(8,128)S(1)}, f32[4,2,4,24,128]{4,3,2,1,0:T(8,128)S(1)}, u32[]{:S(2)}, u32[]{:S(2)}) %collective-permute-start.20) | collective-permute-done | bytes 393248 | tf_op jit(solution)/shard_map/ppermute | solution.py:111
  112.5 2.8 %collective-permute-start.23 = (f32[2,4,24,128]{3,2,1,0:T(8,128)S(1)}, f32[2,4,24,128]{3,2,1,0:T(8,128)S(1)}, u32[]{:S(2)}, u32[]{:S(2)}) collective-permute-start(f32[2,4,24,128]{3,2,1,0:T(8,128)S(1)} %get-tuple-element.46), channel_id=1, source_target_pairs={{0,192},{32,224},{64,0},{96,32},{128,64},{160,96},{192,128},{224,1... | collective-permute-start | bytes 294920 | tf_op jit(solution)/shard_map/ppermute | solution.py:116
  116.3 2.7 %collective-permute-done.23 = f32[2,4,24,128]{3,2,1,0:T(8,128)S(1)} collective-permute-done((f32[2,4,24,128]{3,2,1,0:T(8,128)S(1)}, f32[2,4,24,128]{3,2,1,0:T(8,128)S(1)}, u32[]{:S(2)}, u32[]{:S(2)}) %collective-permute-start.23) | collective-permute-done | bytes 98336 | tf_op jit(solution)/shard_map/ppermute | solution.py:116
  119.0 1.3 %collective-permute-done.22 = f32[2,4,24,128]{3,2,1,0:T(8,128)S(1)} collective-permute-done((f32[2,4,24,128]{3,2,1,0:T(8,128)S(1)}, f32[2,4,24,128]{3,2,1,0:T(8,128)S(1)}, u32[]{:S(2)}, u32[]{:S(2)}) %collective-permute-start.22) | collective-permute-done | bytes 98336 | tf_op jit(solution)/shard_map/ppermute | solution.py:116
  120.3 3.1 %collective-permute-done.21 = f32[2,4,24,128]{3,2,1,0:T(8,128)S(1)} collective-permute-done((f32[2,4,24,128]{3,2,1,0:T(8,128)S(1)}, f32[2,4,24,128]{3,2,1,0:T(8,128)S(1)}, u32[]{:S(2)}, u32[]{:S(2)}) %collective-permute-start.21) | collective-permute-done | bytes 98336 | tf_op jit(solution)/shard_map/ppermute | solution.py:116
  (145 shorter events, 32.2 us)
Async XLA Ops:
  0.0 38.0 %copy-start = (bf16[1,2,24,128,128]{4,3,2,1,0:T(8,128)(2,1)S(1)}, bf16[1,2,24,128,128]{4,3,2,1,0:T(8,128)(2,1)}, u32[]{:S(2)}) copy-start(bf16[1,2,24,128,128]{4,3,2,1,0:T(8,128)(2,1)} %param.8) | copy-start | bytes 4718596
  0.0 18.4 %copy-start.10 = (bf16[32,24,128]{2,1,0:T(8,128)(2,1)S(1)}, bf16[32,24,128]{2,1,0:T(8,128)(2,1)}, u32[]{:S(2)}) copy-start(bf16[32,24,128]{2,1,0:T(8,128)(2,1)} %param.5) | copy-start | bytes 589828
  4.2 14.4 %collective-permute-start = (s32[6]{0:T(128)S(1)}, s32[6]{0:T(128)S(1)}, u32[]{:S(2)}, u32[]{:S(2)}) collective-permute-start(s32[6]{0:T(128)S(1)} %get-tuple-element.19), channel_id=1, source_target_pairs={{0,1},{1,2},{2,3},{3,4},{4,5},{5,6},{6,7},{7,8},{8,9},{9,10},{10,1... | collective-permute-start | bytes 80 | tf_op jit(solution)/shard_map/ppermute | solution.py:62
  5.4 14.9 %collective-permute-start.4 = (s32[6]{0:T(128)S(1)}, s32[6]{0:T(128)S(1)}, u32[]{:S(2)}, u32[]{:S(2)}) collective-permute-start(s32[6]{0:T(128)S(1)} %get-tuple-element.17), channel_id=1, source_target_pairs={{0,2},{1,3},{2,4},{3,5},{4,6},{5,7},{6,8},{7,9},{8,10},{9,11},{10,... | collective-permute-start | bytes 80 | tf_op jit(solution)/shard_map/ppermute | solution.py:62
  7.6 12.7 %collective-permute-start.2 = (s32[6]{0:T(128)S(1)}, s32[6]{0:T(128)S(1)}, u32[]{:S(2)}, u32[]{:S(2)}) collective-permute-start(s32[6]{0:T(128)S(1)} %get-tuple-element.16), channel_id=1, source_target_pairs={{0,31},{1,0},{2,1},{3,2},{4,3},{5,4},{6,5},{7,6},{8,7},{9,8},{10,9... | collective-permute-start | bytes 80 | tf_op jit(solution)/shard_map/ppermute | solution.py:62
  8.1 18.0 %collective-permute-start.8 = (s32[6]{0:T(128)S(1)}, s32[6]{0:T(128)S(1)}, u32[]{:S(2)}, u32[]{:S(2)}) collective-permute-start(s32[6]{0:T(128)S(1)} %get-tuple-element.15), channel_id=1, source_target_pairs={{0,16},{1,17},{2,18},{3,19},{4,20},{5,21},{6,22},{7,23},{8,24},{9,... | collective-permute-start | bytes 80 | tf_op jit(solution)/shard_map/ppermute | solution.py:62
  15.1 11.1 %collective-permute-start.6 = (s32[6]{0:T(128)S(1)}, s32[6]{0:T(128)S(1)}, u32[]{:S(2)}, u32[]{:S(2)}) collective-permute-start(s32[6]{0:T(128)S(1)} %get-tuple-element.18), channel_id=1, source_target_pairs={{0,30},{1,31},{2,0},{3,1},{4,2},{5,3},{6,4},{7,5},{8,6},{9,7},{10,... | collective-permute-start | bytes 80 | tf_op jit(solution)/shard_map/ppermute | solution.py:62
  19.2 11.9 %collective-permute-start.1 = (bf16[6,32,128]{2,1,0:T(8,128)(2,1)S(1)}, bf16[6,32,128]{2,1,0:T(8,128)(2,1)S(1)}, u32[]{:S(2)}, u32[]{:S(2)}) collective-permute-start(bf16[6,32,128]{2,1,0:T(8,128)(2,1)S(1)} %gather_fusion), channel_id=1, source_target_pairs={{1,0},{2,1},{3,2},{4,3},{5,4},{6,5},{7,6},{8,7},{9,8},{10,9},{11,1... | collective-permute-start | bytes 147464 | tf_op jit(solution)/shard_map/ppermute | solution.py:68
  20.9 10.1 %collective-permute-start.3 = (bf16[6,32,128]{2,1,0:T(8,128)(2,1)S(1)}, bf16[6,32,128]{2,1,0:T(8,128)(2,1)S(1)}, u32[]{:S(2)}, u32[]{:S(2)}) collective-permute-start(bf16[6,32,128]{2,1,0:T(8,128)(2,1)S(1)} %gather_fusion.1), channel_id=1, source_target_pairs={{31,0},{0,1},{1,2},{2,3},{3,4},{4,5},{5,6},{6,7},{7,8},{8,9},{9,10... | collective-permute-start | bytes 147464 | tf_op jit(solution)/shard_map/ppermute | solution.py:68
  22.6 8.5 %collective-permute-start.5 = (bf16[6,32,128]{2,1,0:T(8,128)(2,1)S(1)}, bf16[6,32,128]{2,1,0:T(8,128)(2,1)S(1)}, u32[]{:S(2)}, u32[]{:S(2)}) collective-permute-start(bf16[6,32,128]{2,1,0:T(8,128)(2,1)S(1)} %gather_fusion.2), channel_id=1, source_target_pairs={{2,0},{3,1},{4,2},{5,3},{6,4},{7,5},{8,6},{9,7},{10,8},{11,9},{12,... | collective-permute-start | bytes 147464 | tf_op jit(solution)/shard_map/ppermute | solution.py:68
  26.2 15.9 %copy-start.11 = (s32[1024]{0:T(1024)}, s32[1024]{0:T(1024)S(1)}, u32[]{:S(2)}) copy-start(s32[1024]{0:T(1024)S(1)} %pad_clamp_fusion.2) | copy-start | bytes 12292
  26.8 6.6 %collective-permute-start.7 = (bf16[6,32,128]{2,1,0:T(8,128)(2,1)S(1)}, bf16[6,32,128]{2,1,0:T(8,128)(2,1)S(1)}, u32[]{:S(2)}, u32[]{:S(2)}) collective-permute-start(bf16[6,32,128]{2,1,0:T(8,128)(2,1)S(1)} %gather_fusion.3), channel_id=1, source_target_pairs={{30,0},{31,1},{0,2},{1,3},{2,4},{3,5},{4,6},{5,7},{6,8},{7,9},{8,1... | collective-permute-start | bytes 147464 | tf_op jit(solution)/shard_map/ppermute | solution.py:68
  26.9 15.8 %copy-start.12 = (s32[1024]{0:T(1024)}, s32[1024]{0:T(1024)S(1)}, u32[]{:S(2)}) copy-start(s32[1024]{0:T(1024)S(1)} %pad_clamp_fusion.1) | copy-start | bytes 12292
  27.4 6.9 %collective-permute-start.9 = (bf16[6,32,128]{2,1,0:T(8,128)(2,1)S(1)}, bf16[6,32,128]{2,1,0:T(8,128)(2,1)S(1)}, u32[]{:S(2)}, u32[]{:S(2)}) collective-permute-start(bf16[6,32,128]{2,1,0:T(8,128)(2,1)S(1)} %gather_fusion.4), channel_id=1, source_target_pairs={{16,0},{17,1},{18,2},{19,3},{20,4},{21,5},{22,6},{23,7},{24,8},{25... | collective-permute-start | bytes 147464 | tf_op jit(solution)/shard_map/ppermute | solution.py:68
  38.0 2.1 %copy-start.6 = (f32[24,32,128]{2,1,0:T(8,128)}, f32[24,32,128]{2,1,0:T(8,128)S(1)}, u32[]{:S(2)}) copy-start(f32[24,32,128]{2,1,0:T(8,128)S(1)} %convolution_bitcast_fusion.4) | copy-start | bytes 1179652
  40.7 16.5 %collective-permute-start.10 = (bf16[6,64,128]{2,1,0:T(8,128)(2,1)S(1)}, bf16[6,64,128]{2,1,0:T(8,128)(2,1)S(1)}, u32[]{:S(2)}, u32[]{:S(2)}) collective-permute-start(bf16[6,64,128]{2,1,0:T(8,128)(2,1)S(1)} %gather_fusion.6), channel_id=1, source_target_pairs={{1,0},{2,1},{3,2},{4,3},{5,4},{6,5},{7,6},{8,7},{9,8},{10,9},{11,1... | collective-permute-start | bytes 294920 | tf_op jit(solution)/shard_map/ppermute | solution.py:68
  43.3 14.6 %collective-permute-start.11 = (bf16[6,64,128]{2,1,0:T(8,128)(2,1)S(1)}, bf16[6,64,128]{2,1,0:T(8,128)(2,1)S(1)}, u32[]{:S(2)}, u32[]{:S(2)}) collective-permute-start(bf16[6,64,128]{2,1,0:T(8,128)(2,1)S(1)} %gather_fusion.7), channel_id=1, source_target_pairs={{31,0},{0,1},{1,2},{2,3},{3,4},{4,5},{5,6},{6,7},{7,8},{8,9},{9,10... | collective-permute-start | bytes 294920 | tf_op jit(solution)/shard_map/ppermute | solution.py:68
  45.3 13.2 %collective-permute-start.12 = (bf16[6,64,128]{2,1,0:T(8,128)(2,1)S(1)}, bf16[6,64,128]{2,1,0:T(8,128)(2,1)S(1)}, u32[]{:S(2)}, u32[]{:S(2)}) collective-permute-start(bf16[6,64,128]{2,1,0:T(8,128)(2,1)S(1)} %gather_fusion.8), channel_id=1, source_target_pairs={{2,0},{3,1},{4,2},{5,3},{6,4},{7,5},{8,6},{9,7},{10,8},{11,9},{12,... | collective-permute-start | bytes 294920 | tf_op jit(solution)/shard_map/ppermute | solution.py:68
  53.8 8.9 %collective-permute-start.13 = (bf16[6,64,128]{2,1,0:T(8,128)(2,1)S(1)}, bf16[6,64,128]{2,1,0:T(8,128)(2,1)S(1)}, u32[]{:S(2)}, u32[]{:S(2)}) collective-permute-start(bf16[6,64,128]{2,1,0:T(8,128)(2,1)S(1)} %gather_fusion.9), channel_id=1, source_target_pairs={{30,0},{31,1},{0,2},{1,3},{2,4},{3,5},{4,6},{5,7},{6,8},{7,9},{8,1... | collective-permute-start | bytes 294920 | tf_op jit(solution)/shard_map/ppermute | solution.py:68
  53.8 9.6 %collective-permute-start.14 = (bf16[6,64,128]{2,1,0:T(8,128)(2,1)S(1)}, bf16[6,64,128]{2,1,0:T(8,128)(2,1)S(1)}, u32[]{:S(2)}, u32[]{:S(2)}) collective-permute-start(bf16[6,64,128]{2,1,0:T(8,128)(2,1)S(1)} %gather_fusion.10), channel_id=1, source_target_pairs={{16,0},{17,1},{18,2},{19,3},{20,4},{21,5},{22,6},{23,7},{24,8},{25... | collective-permute-start | bytes 294920 | tf_op jit(solution)/shard_map/ppermute | solution.py:68
  66.1 3.3 %copy-start.2 = (bf16[24,5,128,128]{3,2,1,0:T(8,128)(2,1)S(1)}, bf16[24,5,128,128]{3,2,1,0:T(8,128)(2,1)}, u32[]{:S(2)}) copy-start(bf16[24,5,128,128]{3,2,1,0:T(8,128)(2,1)} %param.7) | copy-start | bytes 11796484
  76.3 12.9 %collective-permute-start.15 = (bf16[6,64,128]{2,1,0:T(8,128)(2,1)S(1)}, bf16[6,64,128]{2,1,0:T(8,128)(2,1)S(1)}, u32[]{:S(2)}, u32[]{:S(2)}) collective-permute-start(bf16[6,64,128]{2,1,0:T(8,128)(2,1)S(1)} %gather_fusion.12), channel_id=1, source_target_pairs={{1,0},{2,1},{3,2},{4,3},{5,4},{6,5},{7,6},{8,7},{9,8},{10,9},{11,1... | collective-permute-start | bytes 294920 | tf_op jit(solution)/shard_map/ppermute | solution.py:68
  76.4 13.4 %collective-permute-start.16 = (bf16[6,64,128]{2,1,0:T(8,128)(2,1)S(1)}, bf16[6,64,128]{2,1,0:T(8,128)(2,1)S(1)}, u32[]{:S(2)}, u32[]{:S(2)}) collective-permute-start(bf16[6,64,128]{2,1,0:T(8,128)(2,1)S(1)} %gather_fusion.13), channel_id=1, source_target_pairs={{31,0},{0,1},{1,2},{2,3},{3,4},{4,5},{5,6},{6,7},{7,8},{8,9},{9,10... | collective-permute-start | bytes 294920 | tf_op jit(solution)/shard_map/ppermute | solution.py:68
  77.8 12.6 %collective-permute-start.17 = (bf16[6,64,128]{2,1,0:T(8,128)(2,1)S(1)}, bf16[6,64,128]{2,1,0:T(8,128)(2,1)S(1)}, u32[]{:S(2)}, u32[]{:S(2)}) collective-permute-start(bf16[6,64,128]{2,1,0:T(8,128)(2,1)S(1)} %gather_fusion.14), channel_id=1, source_target_pairs={{2,0},{3,1},{4,2},{5,3},{6,4},{7,5},{8,6},{9,7},{10,8},{11,9},{12,... | collective-permute-start | bytes 294920 | tf_op jit(solution)/shard_map/ppermute | solution.py:68
  84.1 8.0 %collective-permute-start.18 = (bf16[6,64,128]{2,1,0:T(8,128)(2,1)S(1)}, bf16[6,64,128]{2,1,0:T(8,128)(2,1)S(1)}, u32[]{:S(2)}, u32[]{:S(2)}) collective-permute-start(bf16[6,64,128]{2,1,0:T(8,128)(2,1)S(1)} %gather_fusion.15), channel_id=1, source_target_pairs={{30,0},{31,1},{0,2},{1,3},{2,4},{3,5},{4,6},{5,7},{6,8},{7,9},{8,1... | collective-permute-start | bytes 294920 | tf_op jit(solution)/shard_map/ppermute | solution.py:68
  84.1 8.6 %collective-permute-start.19 = (bf16[6,64,128]{2,1,0:T(8,128)(2,1)S(1)}, bf16[6,64,128]{2,1,0:T(8,128)(2,1)S(1)}, u32[]{:S(2)}, u32[]{:S(2)}) collective-permute-start(bf16[6,64,128]{2,1,0:T(8,128)(2,1)S(1)} %gather_fusion.16), channel_id=1, source_target_pairs={{16,0},{17,1},{18,2},{19,3},{20,4},{21,5},{22,6},{23,7},{24,8},{25... | collective-permute-start | bytes 294920 | tf_op jit(solution)/shard_map/ppermute | solution.py:68
  95.5 3.3 %copy-start.1 = (bf16[24,5,128,128]{3,2,1,0:T(8,128)(2,1)S(1)}, bf16[24,5,128,128]{3,2,1,0:T(8,128)(2,1)}, u32[]{:S(2)}) copy-start(bf16[24,5,128,128]{3,2,1,0:T(8,128)(2,1)} %param.6) | copy-start | bytes 11796484
  100.6 1.4 %copy-start.9 = (f32[24,64,128]{2,1,0:T(8,128)S(1)}, f32[24,64,128]{2,1,0:T(8,128)}, u32[]{:S(2)}) copy-start(f32[24,64,128]{2,1,0:T(8,128)} %get-tuple-element.44) | copy-start | bytes 2359300
  103.6 8.7 %collective-permute-start.20 = (f32[4,2,4,24,128]{4,3,2,1,0:T(8,128)S(1)}, f32[4,2,4,24,128]{4,3,2,1,0:T(8,128)S(1)}, u32[]{:S(2)}, u32[]{:S(2)}) collective-permute-start(f32[4,2,4,24,128]{4,3,2,1,0:T(8,128)S(1)} %bitcast.155), channel_id=1, source_target_pairs={{0,32},{32,0},{64,96},{96,64},{128,160},{160,128},{192,224},{224,1... | collective-permute-start | bytes 1179656 | tf_op jit(solution)/shard_map/ppermute | solution.py:111
  112.5 6.6 %collective-permute-start.23 = (f32[2,4,24,128]{3,2,1,0:T(8,128)S(1)}, f32[2,4,24,128]{3,2,1,0:T(8,128)S(1)}, u32[]{:S(2)}, u32[]{:S(2)}) collective-permute-start(f32[2,4,24,128]{3,2,1,0:T(8,128)S(1)} %get-tuple-element.46), channel_id=1, source_target_pairs={{0,192},{32,224},{64,0},{96,32},{128,64},{160,96},{192,128},{224,1... | collective-permute-start | bytes 294920 | tf_op jit(solution)/shard_map/ppermute | solution.py:116
  115.3 5.1 %collective-permute-start.22 = (f32[2,4,24,128]{3,2,1,0:T(8,128)S(1)}, f32[2,4,24,128]{3,2,1,0:T(8,128)S(1)}, u32[]{:S(2)}, u32[]{:S(2)}) collective-permute-start(f32[2,4,24,128]{3,2,1,0:T(8,128)S(1)} %get-tuple-element.47), channel_id=1, source_target_pairs={{0,128},{32,160},{64,192},{96,224},{128,0},{160,32},{192,64},{224,... | collective-permute-start | bytes 294920 | tf_op jit(solution)/shard_map/ppermute | solution.py:116
  115.6 7.8 %collective-permute-start.21 = (f32[2,4,24,128]{3,2,1,0:T(8,128)S(1)}, f32[2,4,24,128]{3,2,1,0:T(8,128)S(1)}, u32[]{:S(2)}, u32[]{:S(2)}) collective-permute-start(f32[2,4,24,128]{3,2,1,0:T(8,128)S(1)} %get-tuple-element.45), channel_id=1, source_target_pairs={{0,64},{32,96},{64,128},{96,160},{128,192},{160,224},{192,0},{224,... | collective-permute-start | bytes 294920 | tf_op jit(solution)/shard_map/ppermute | solution.py:116
  (5 other events, 5.2 us)

commit v10 on v2

--- a/solution.py
+++ b/solution.py
@@ -101,12 +101,17 @@
         ]
     )
     weighted = jnp.transpose(weighted / node_count, (2, 0, 3, 1, 4))
-    total = lax.dynamic_index_in_dim(weighted, node_index, 0, keepdims=False)
-    for offset in range(1, node_count):
-        chunk = lax.dynamic_index_in_dim(weighted, (node_index + offset) % node_count, 0, keepdims=False)
-        perm = [(j, (j + offset) % node_count) for j in range(node_count)]
-        total = total + lax.ppermute(chunk, "node", perm)
-    return total
+    bit_count = node_count.bit_length() - 1
+    data = weighted.reshape((2,) * bit_count + weighted.shape[1:])
+    axis_bits = list(reversed(range(bit_count)))
+    for bit in [0] + list(reversed(range(1, bit_count))):
+        axis = axis_bits.index(bit)
+        mine = (node_index // (2 ** bit)) % 2
+        keep = lax.dynamic_index_in_dim(data, mine, axis, keepdims=False)
+        other = lax.dynamic_index_in_dim(data, 1 - mine, axis, keepdims=False)
+        data = keep + lax.ppermute(other, "node", [(j, j ^ (2 ** bit)) for j in range(node_count)])
+        axis_bits.pop(axis)
+    return data
 
 
 def solution(mesh):

time: 117 us -> 117 us (level); the launches traced: 117 us -> 115 us
  starting transfers between devices: 57.2 us -> 52.8 us
  waiting for transfers between devices: 12.4 us -> 15.4 us
    ppermute x7 -> x3, starting transfers between devices: 15.8 us -> 11.4 us  [per_device(): lax.ppermute(other, 'node', [(j, j ^ 2 ** bit) for j in range(node_count)])]
    ppermute x7 -> x3, waiting for transfers between devices: 5.25 us -> 8.21 us  [per_device(): lax.ppermute(other, 'node', [(j, j ^ 2 ** bit) for j in range(node_count)])]
  transfers between devices with their start and end apart: 27 -> 23, of which waited for: 6 -> 6; matrix products, arithmetic and copies ran while one was open for 12% -> 12% of each run, Pallas kernels for 0% -> 0%
where the time goes in v10:
time: 117 us; the launch traced here: 115 us
  starting transfers between devices  52.8 us (45%)
  local copies, waits for them, and re-layouts  29.2 us (25%)
  waiting for transfers between devices  15.4 us (13%)
  matrix products  12.2 us (10%)
  other arithmetic  4.81 us (4%)
    ppermute x15, starting transfers between devices, fetch_halo(): lax.ppermute(vector[asked_for[which]], 'rows', from_partner(offset))  29.1 us
    ppermute x5, starting transfers between devices, per_device(): lax.ppermute(wanted[which], 'rows', to_partner(offset))  12.3 us
    ppermute x3, starting transfers between devices, per_device(): lax.ppermute(other, 'node', [(j, j ^ 2 ** bit) for j in range(node_count)])  11.4 us
    unnamed x42, local copies, waits for them, and re-layouts  10.8 us
    gather x15, local copies, waits for them, and re-layouts, fetch_halo(): vector[asked_for[which]]  8.7 us
    ppermute x3, waiting for transfers between devices, per_device(): lax.ppermute(other, 'node', [(j, j ^ 2 ** bit) for j in range(node_count)])  8.21 us
    ppermute x15, waiting for transfers between devices, fetch_halo(): lax.ppermute(vector[asked_for[which]], 'rows', from_partner(offset))  7.15 us
    dot_general x3, matrix products, apply_pair(): jnp.einsum('nscb,nsbd->ncd', picked, first, preferred_element_type=jnp.fl...  6.96 us
  transfers between devices with their start and end apart: 23, of which 6 were waited for; matrix products, arithmetic and copies ran while one was open for 12% of the time, Pallas kernels for 0%

profile of v10, /device:TPU:3, one launch (start us, length us, event | category | flops | bytes accessed | tf_op | source)
XLA Modules:
  0.0 115.1 jit_solution(15226476872053511210)
XLA Ops:
  0.0 0.9 copy.76
  4.2 7.7 %collective-permute-start.8 = (s32[6]{0:T(128)S(1)}, s32[6]{0:T(128)S(1)}, u32[]{:S(2)}, u32[]{:S(2)}) collective-permute-start(s32[6]{0:T(128)S(1)} %get-tuple-element.15), channel_id=1, source_target_pairs={{0,30},{1,31},{2,0},{3,1},{4,2},{5,3},{6,4},{7,5},{8,6},{9,7},{10,... | collective-permute-start | bytes 80 | tf_op jit(solution)/shard_map/ppermute | solution.py:61
  11.9 2.4 %collective-permute-start.4 = (s32[6]{0:T(128)S(1)}, s32[6]{0:T(128)S(1)}, u32[]{:S(2)}, u32[]{:S(2)}) collective-permute-start(s32[6]{0:T(128)S(1)} %get-tuple-element.17), channel_id=1, source_target_pairs={{0,16},{1,17},{2,18},{3,19},{4,20},{5,21},{6,22},{7,23},{8,24},{9,... | collective-permute-start | bytes 80 | tf_op jit(solution)/shard_map/ppermute | solution.py:61
  14.4 2.1 %collective-permute-start = (s32[6]{0:T(128)S(1)}, s32[6]{0:T(128)S(1)}, u32[]{:S(2)}, u32[]{:S(2)}) collective-permute-start(s32[6]{0:T(128)S(1)} %get-tuple-element.19), channel_id=1, source_target_pairs={{0,1},{1,2},{2,3},{3,4},{4,5},{5,6},{6,7},{7,8},{8,9},{9,10},{10,1... | collective-permute-start | bytes 80 | tf_op jit(solution)/shard_map/ppermute | solution.py:61
  16.5 1.0 copy.124
  18.2 1.3 %collective-permute-start.7 = (bf16[6,32,128]{2,1,0:T(8,128)(2,1)S(1)}, bf16[6,32,128]{2,1,0:T(8,128)(2,1)S(1)}, u32[]{:S(2)}, u32[]{:S(2)}) collective-permute-start(bf16[6,32,128]{2,1,0:T(8,128)(2,1)S(1)} %gather_fusion.3), channel_id=1, source_target_pairs={{31,0},{0,1},{1,2},{2,3},{3,4},{4,5},{5,6},{6,7},{7,8},{8,9},{9,10... | collective-permute-start | bytes 147464 | tf_op jit(solution)/shard_map/ppermute | solution.py:67
  20.1 3.9 %collective-permute-start.3 = (bf16[6,32,128]{2,1,0:T(8,128)(2,1)S(1)}, bf16[6,32,128]{2,1,0:T(8,128)(2,1)S(1)}, u32[]{:S(2)}, u32[]{:S(2)}) collective-permute-start(bf16[6,32,128]{2,1,0:T(8,128)(2,1)S(1)} %gather_fusion.1), channel_id=1, source_target_pairs={{2,0},{3,1},{4,2},{5,3},{6,4},{7,5},{8,6},{9,7},{10,8},{11,9},{12,... | collective-permute-start | bytes 147464 | tf_op jit(solution)/shard_map/ppermute | solution.py:67
  24.6 0.9 collective-permute-start.1
  26.1 4.3 %collective-permute-start.5 = (bf16[6,32,128]{2,1,0:T(8,128)(2,1)S(1)}, bf16[6,32,128]{2,1,0:T(8,128)(2,1)S(1)}, u32[]{:S(2)}, u32[]{:S(2)}) collective-permute-start(bf16[6,32,128]{2,1,0:T(8,128)(2,1)S(1)} %gather_fusion.2), channel_id=1, source_target_pairs={{16,0},{17,1},{18,2},{19,3},{20,4},{21,5},{22,6},{23,7},{24,8},{25... | collective-permute-start | bytes 147464 | tf_op jit(solution)/shard_map/ppermute | solution.py:67
  31.1 2.1 %collective-permute-done.5 = bf16[6,32,128]{2,1,0:T(8,128)(2,1)S(1)} collective-permute-done((bf16[6,32,128]{2,1,0:T(8,128)(2,1)S(1)}, bf16[6,32,128]{2,1,0:T(8,128)(2,1)S(1)}, u32[]{:S(2)}, u32[]{:S(2)}) %collective-permute-start.5) | collective-permute-done | bytes 49184 | tf_op jit(solution)/shard_map/ppermute | solution.py:67
  33.2 4.3 %collective-permute-done.9 = bf16[6,32,128]{2,1,0:T(8,128)(2,1)S(1)} collective-permute-done((bf16[6,32,128]{2,1,0:T(8,128)(2,1)S(1)}, bf16[6,32,128]{2,1,0:T(8,128)(2,1)S(1)}, u32[]{:S(2)}, u32[]{:S(2)}) %collective-permute-start.9) | collective-permute-done | bytes 49184 | tf_op jit(solution)/shard_map/ppermute | solution.py:67
  38.3 2.8 %convolution_bitcast_fusion.4 = f32[24,32,128]{2,1,0:T(8,128)S(1)} fusion(bf16[24,5,32,128]{3,2,1,0:T(8,128)(2,1)S(1)} %bitcast.142, bf16[24,5,128,128]{3,2,1,0:T(8,128)(2,1)} %param.6), kind=kOutput, calls=%fused_computation.22 | convolution fusion | flops 125829120 | bytes 5308416 | tf_op jit(solution)/shard_map/nscb,nsbd->ncd/dot_general | solution.py:25
  41.6 0.9 copy-done.3
  46.5 1.9 %collective-permute-start.12 = (bf16[6,64,128]{2,1,0:T(8,128)(2,1)S(1)}, bf16[6,64,128]{2,1,0:T(8,128)(2,1)S(1)}, u32[]{:S(2)}, u32[]{:S(2)}) collective-permute-start(bf16[6,64,128]{2,1,0:T(8,128)(2,1)S(1)} %gather_fusion.8), channel_id=1, source_target_pairs={{16,0},{17,1},{18,2},{19,3},{20,4},{21,5},{22,6},{23,7},{24,8},{25... | collective-permute-start | bytes 294920 | tf_op jit(solution)/shard_map/ppermute | solution.py:67
  48.4 1.2 %collective-permute-start.13 = (bf16[6,64,128]{2,1,0:T(8,128)(2,1)S(1)}, bf16[6,64,128]{2,1,0:T(8,128)(2,1)S(1)}, u32[]{:S(2)}, u32[]{:S(2)}) collective-permute-start(bf16[6,64,128]{2,1,0:T(8,128)(2,1)S(1)} %gather_fusion.9), channel_id=1, source_target_pairs={{31,0},{0,1},{1,2},{2,3},{3,4},{4,5},{5,6},{6,7},{7,8},{8,9},{9,10... | collective-permute-start | bytes 294920 | tf_op jit(solution)/shard_map/ppermute | solution.py:67
  49.6 4.1 %collective-permute-start.14 = (bf16[6,64,128]{2,1,0:T(8,128)(2,1)S(1)}, bf16[6,64,128]{2,1,0:T(8,128)(2,1)S(1)}, u32[]{:S(2)}, u32[]{:S(2)}) collective-permute-start(bf16[6,64,128]{2,1,0:T(8,128)(2,1)S(1)} %gather_fusion.10), channel_id=1, source_target_pairs={{30,0},{31,1},{0,2},{1,3},{2,4},{3,5},{4,6},{5,7},{6,8},{7,9},{8,1... | collective-permute-start | bytes 294920 | tf_op jit(solution)/shard_map/ppermute | solution.py:67
  57.5 2.1 %gather_fusion.11 = bf16[120,64,128]{2,1,0:T(8,128)(2,1)S(1)} fusion(bf16[54,64,128]{2,1,0:T(8,128)(2,1)} %constant_dynamic-update-slice_fusion.6, s32[1024]{0:T(1024)S(1)} %pad_clamp_fusion), kind=kCustom, calls=%fused_computation.11 | custom fusion | bytes 3932640 | tf_op jit(solution)/shard_map/gather | solution.py:24
  59.6 3.2 %convolution_bitcast_fusion.3 = f32[24,64,128]{2,1,0:T(8,128)S(1)} fusion(bf16[24,5,64,128]{3,2,1,0:T(8,128)(2,1)S(1)} %bitcast.136, bf16[24,5,128,128]{3,2,1,0:T(8,128)(2,1)} %param.6), kind=kOutput, calls=%fused_computation.21 | convolution fusion | flops 251658240 | bytes 6684672 | tf_op jit(solution)/shard_map/nscb,nsbd->ncd/dot_general | solution.py:25
  64.7 1.0 copy-done.4
  69.0 2.1 %collective-permute-start.16 = (bf16[6,64,128]{2,1,0:T(8,128)(2,1)S(1)}, bf16[6,64,128]{2,1,0:T(8,128)(2,1)S(1)}, u32[]{:S(2)}, u32[]{:S(2)}) collective-permute-start(bf16[6,64,128]{2,1,0:T(8,128)(2,1)S(1)} %gather_fusion.13), channel_id=1, source_target_pairs={{2,0},{3,1},{4,2},{5,3},{6,4},{7,5},{8,6},{9,7},{10,8},{11,9},{12,... | collective-permute-start | bytes 294920 | tf_op jit(solution)/shard_map/ppermute | solution.py:67
  71.8 3.0 %collective-permute-start.17 = (bf16[6,64,128]{2,1,0:T(8,128)(2,1)S(1)}, bf16[6,64,128]{2,1,0:T(8,128)(2,1)S(1)}, u32[]{:S(2)}, u32[]{:S(2)}) collective-permute-start(bf16[6,64,128]{2,1,0:T(8,128)(2,1)S(1)} %gather_fusion.14), channel_id=1, source_target_pairs={{16,0},{17,1},{18,2},{19,3},{20,4},{21,5},{22,6},{23,7},{24,8},{25... | collective-permute-start | bytes 294920 | tf_op jit(solution)/shard_map/ppermute | solution.py:67
  74.8 1.1 collective-permute-start.18
  76.0 4.3 %collective-permute-start.19 = (bf16[6,64,128]{2,1,0:T(8,128)(2,1)S(1)}, bf16[6,64,128]{2,1,0:T(8,128)(2,1)S(1)}, u32[]{:S(2)}, u32[]{:S(2)}) collective-permute-start(bf16[6,64,128]{2,1,0:T(8,128)(2,1)S(1)} %gather_fusion.16), channel_id=1, source_target_pairs={{30,0},{31,1},{0,2},{1,3},{2,4},{3,5},{4,6},{5,7},{6,8},{7,9},{8,1... | collective-permute-start | bytes 294920 | tf_op jit(solution)/shard_map/ppermute | solution.py:67
  80.3 1.4 %copy.91 = f32[24,64,128]{2,0,1:T(8,128)} copy(f32[24,64,128]{2,1,0:T(8,128)S(1)} %get-tuple-element.39) | data formatting | bytes 1572864 | tf_op jit(solution)/shard_map/concatenate | solution.py:93
  85.6 2.1 %gather_fusion.17 = bf16[120,64,128]{2,1,0:T(8,128)(2,1)S(1)} fusion(bf16[54,64,128]{2,1,0:T(8,128)(2,1)} %constant_dynamic-update-slice_fusion.12, s32[1024]{0:T(1024)S(1)} %pad_clamp_fusion), kind=kCustom, calls=%fused_computation.17 | custom fusion | bytes 3932640 | tf_op jit(solution)/shard_map/gather | solution.py:24
  87.7 3.2 %convolution_bitcast_fusion = f32[24,64,128]{2,1,0:T(8,128)S(1)} fusion(bf16[24,5,64,128]{3,2,1,0:T(8,128)(2,1)S(1)} %bitcast.134, bf16[24,5,128,128]{3,2,1,0:T(8,128)(2,1)} %param.7), kind=kOutput, calls=%fused_computation.18 | convolution fusion | flops 251658240 | bytes 6684672 | tf_op jit(solution)/shard_map/nscb,nsbd->ncd/dot_general | solution.py:28
  94.8 7.0 %collective-permute-start.20 = (f32[2,2,2,4,24,128]{5,4,3,2,1,0:T(8,128)S(1)}, f32[2,2,2,4,24,128]{5,4,3,2,1,0:T(8,128)S(1)}, u32[]{:S(2)}, u32[]{:S(2)}) collective-permute-start(f32[2,2,2,4,24,128]{5,4,3,2,1,0:T(8,128)S(1)} %dynamic-slice_bitcast_fusion), channel_id=1, source_target_pairs={{0,32},{32,0},{64,96},{96,64},{128,160},{160,128},{192,224},{224,1... | collective-permute-start | bytes 1179656 | tf_op jit(solution)/shard_map/ppermute | solution.py:112
  101.8 1.3 %collective-permute-done.20 = f32[2,2,2,4,24,128]{5,4,3,2,1,0:T(8,128)S(1)} collective-permute-done((f32[2,2,2,4,24,128]{5,4,3,2,1,0:T(8,128)S(1)}, f32[2,2,2,4,24,128]{5,4,3,2,1,0:T(8,128)S(1)}, u32[]{:S(2)}, u32[]{:S(2)}) %collective-permute-start.20) | collective-permute-done | bytes 393248 | tf_op jit(solution)/shard_map/ppermute | solution.py:112
  103.2 3.0 %collective-permute-start.21 = (f32[2,2,4,24,128]{4,3,2,1,0:T(8,128)S(1)}, f32[2,2,4,24,128]{4,3,2,1,0:T(8,128)S(1)}, u32[]{:S(2)}, u32[]{:S(2)}) collective-permute-start(f32[2,2,4,24,128]{4,3,2,1,0:T(8,128)S(1)} %dynamic-slice_bitcast_fusion.1), channel_id=1, source_target_pairs={{0,128},{32,160},{64,192},{96,224},{128,0},{160,32},{192,64},{224,... | collective-permute-start | bytes 589832 | tf_op jit(solution)/shard_map/ppermute | solution.py:112
  106.2 4.7 %collective-permute-done.21 = f32[2,2,4,24,128]{4,3,2,1,0:T(8,128)S(1)} collective-permute-done((f32[2,2,4,24,128]{4,3,2,1,0:T(8,128)S(1)}, f32[2,2,4,24,128]{4,3,2,1,0:T(8,128)S(1)}, u32[]{:S(2)}, u32[]{:S(2)}) %collective-permute-start.21) | collective-permute-done | bytes 196640 | tf_op jit(solution)/shard_map/ppermute | solution.py:112
  110.9 1.4 %collective-permute-start.22 = (f32[2,4,24,128]{3,2,1,0:T(8,128)S(1)}, f32[2,4,24,128]{3,2,1,0:T(8,128)S(1)}, u32[]{:S(2)}, u32[]{:S(2)}) collective-permute-start(f32[2,4,24,128]{3,2,1,0:T(8,128)S(1)} %dynamic-slice_bitcast_fusion.2), channel_id=1, source_target_pairs={{0,64},{32,96},{64,0},{96,32},{128,192},{160,224},{192,128},{224,1... | collective-permute-start | bytes 294920 | tf_op jit(solution)/shard_map/ppermute | solution.py:112
  112.3 2.2 %collective-permute-done.22 = f32[2,4,24,128]{3,2,1,0:T(8,128)S(1)} collective-permute-done((f32[2,4,24,128]{3,2,1,0:T(8,128)S(1)}, f32[2,4,24,128]{3,2,1,0:T(8,128)S(1)}, u32[]{:S(2)}, u32[]{:S(2)}) %collective-permute-start.22) | collective-permute-done | bytes 98336 | tf_op jit(solution)/shard_map/ppermute | solution.py:112
  (144 shorter events, 29.5 us)
Async XLA Ops:
  0.0 41.2 %copy-start = (bf16[1,2,24,128,128]{4,3,2,1,0:T(8,128)(2,1)S(1)}, bf16[1,2,24,128,128]{4,3,2,1,0:T(8,128)(2,1)}, u32[]{:S(2)}) copy-start(bf16[1,2,24,128,128]{4,3,2,1,0:T(8,128)(2,1)} %param.8) | copy-start | bytes 4718596
  0.0 17.4 %copy-start.10 = (bf16[32,24,128]{2,1,0:T(8,128)(2,1)S(1)}, bf16[32,24,128]{2,1,0:T(8,128)(2,1)}, u32[]{:S(2)}) copy-start(bf16[32,24,128]{2,1,0:T(8,128)(2,1)} %param.5) | copy-start | bytes 589828
  4.2 13.4 %collective-permute-start.6 = (s32[6]{0:T(128)S(1)}, s32[6]{0:T(128)S(1)}, u32[]{:S(2)}, u32[]{:S(2)}) collective-permute-start(s32[6]{0:T(128)S(1)} %get-tuple-element.18), channel_id=1, source_target_pairs={{0,31},{1,0},{2,1},{3,2},{4,3},{5,4},{6,5},{7,6},{8,7},{9,8},{10,9... | collective-permute-start | bytes 80 | tf_op jit(solution)/shard_map/ppermute | solution.py:61
  4.2 13.4 %collective-permute-start.8 = (s32[6]{0:T(128)S(1)}, s32[6]{0:T(128)S(1)}, u32[]{:S(2)}, u32[]{:S(2)}) collective-permute-start(s32[6]{0:T(128)S(1)} %get-tuple-element.15), channel_id=1, source_target_pairs={{0,30},{1,31},{2,0},{3,1},{4,2},{5,3},{6,4},{7,5},{8,6},{9,7},{10,... | collective-permute-start | bytes 80 | tf_op jit(solution)/shard_map/ppermute | solution.py:61
  11.9 7.6 %collective-permute-start.2 = (s32[6]{0:T(128)S(1)}, s32[6]{0:T(128)S(1)}, u32[]{:S(2)}, u32[]{:S(2)}) collective-permute-start(s32[6]{0:T(128)S(1)} %get-tuple-element.16), channel_id=1, source_target_pairs={{0,2},{1,3},{2,4},{3,5},{4,6},{5,7},{6,8},{7,9},{8,10},{9,11},{10,... | collective-permute-start | bytes 80 | tf_op jit(solution)/shard_map/ppermute | solution.py:61
  11.9 7.6 %collective-permute-start.4 = (s32[6]{0:T(128)S(1)}, s32[6]{0:T(128)S(1)}, u32[]{:S(2)}, u32[]{:S(2)}) collective-permute-start(s32[6]{0:T(128)S(1)} %get-tuple-element.17), channel_id=1, source_target_pairs={{0,16},{1,17},{2,18},{3,19},{4,20},{5,21},{6,22},{7,23},{8,24},{9,... | collective-permute-start | bytes 80 | tf_op jit(solution)/shard_map/ppermute | solution.py:61
  14.4 9.6 %collective-permute-start = (s32[6]{0:T(128)S(1)}, s32[6]{0:T(128)S(1)}, u32[]{:S(2)}, u32[]{:S(2)}) collective-permute-start(s32[6]{0:T(128)S(1)} %get-tuple-element.19), channel_id=1, source_target_pairs={{0,1},{1,2},{2,3},{3,4},{4,5},{5,6},{6,7},{7,8},{8,9},{9,10},{10,1... | collective-permute-start | bytes 80 | tf_op jit(solution)/shard_map/ppermute | solution.py:61
  18.2 15.0 %collective-permute-start.7 = (bf16[6,32,128]{2,1,0:T(8,128)(2,1)S(1)}, bf16[6,32,128]{2,1,0:T(8,128)(2,1)S(1)}, u32[]{:S(2)}, u32[]{:S(2)}) collective-permute-start(bf16[6,32,128]{2,1,0:T(8,128)(2,1)S(1)} %gather_fusion.3), channel_id=1, source_target_pairs={{31,0},{0,1},{1,2},{2,3},{3,4},{4,5},{5,6},{6,7},{7,8},{8,9},{9,10... | collective-permute-start | bytes 147464 | tf_op jit(solution)/shard_map/ppermute | solution.py:67
  20.1 11.0 %collective-permute-start.3 = (bf16[6,32,128]{2,1,0:T(8,128)(2,1)S(1)}, bf16[6,32,128]{2,1,0:T(8,128)(2,1)S(1)}, u32[]{:S(2)}, u32[]{:S(2)}) collective-permute-start(bf16[6,32,128]{2,1,0:T(8,128)(2,1)S(1)} %gather_fusion.1), channel_id=1, source_target_pairs={{2,0},{3,1},{4,2},{5,3},{6,4},{7,5},{8,6},{9,7},{10,8},{11,9},{12,... | collective-permute-start | bytes 147464 | tf_op jit(solution)/shard_map/ppermute | solution.py:67
  24.6 6.5 %collective-permute-start.1 = (bf16[6,32,128]{2,1,0:T(8,128)(2,1)S(1)}, bf16[6,32,128]{2,1,0:T(8,128)(2,1)S(1)}, u32[]{:S(2)}, u32[]{:S(2)}) collective-permute-start(bf16[6,32,128]{2,1,0:T(8,128)(2,1)S(1)} %gather_fusion), channel_id=1, source_target_pairs={{1,0},{2,1},{3,2},{4,3},{5,4},{6,5},{7,6},{8,7},{9,8},{10,9},{11,1... | collective-permute-start | bytes 147464 | tf_op jit(solution)/shard_map/ppermute | solution.py:67
  25.5 18.7 %copy-start.11 = (s32[1024]{0:T(1024)}, s32[1024]{0:T(1024)S(1)}, u32[]{:S(2)}) copy-start(s32[1024]{0:T(1024)S(1)} %pad_clamp_fusion.3) | copy-start | bytes 12292
  26.1 7.1 %collective-permute-start.5 = (bf16[6,32,128]{2,1,0:T(8,128)(2,1)S(1)}, bf16[6,32,128]{2,1,0:T(8,128)(2,1)S(1)}, u32[]{:S(2)}, u32[]{:S(2)}) collective-permute-start(bf16[6,32,128]{2,1,0:T(8,128)(2,1)S(1)} %gather_fusion.2), channel_id=1, source_target_pairs={{16,0},{17,1},{18,2},{19,3},{20,4},{21,5},{22,6},{23,7},{24,8},{25... | collective-permute-start | bytes 147464 | tf_op jit(solution)/shard_map/ppermute | solution.py:67
  30.4 15.5 %copy-start.12 = (s32[1024]{0:T(1024)}, s32[1024]{0:T(1024)S(1)}, u32[]{:S(2)}) copy-start(s32[1024]{0:T(1024)S(1)} %pad_clamp_fusion.1) | copy-start | bytes 12292
  30.9 6.6 %collective-permute-start.9 = (bf16[6,32,128]{2,1,0:T(8,128)(2,1)S(1)}, bf16[6,32,128]{2,1,0:T(8,128)(2,1)S(1)}, u32[]{:S(2)}, u32[]{:S(2)}) collective-permute-start(bf16[6,32,128]{2,1,0:T(8,128)(2,1)S(1)} %gather_fusion.4), channel_id=1, source_target_pairs={{30,0},{31,1},{0,2},{1,3},{2,4},{3,5},{4,6},{5,7},{6,8},{7,9},{8,1... | collective-permute-start | bytes 147464 | tf_op jit(solution)/shard_map/ppermute | solution.py:67
  41.2 2.1 %copy-start.6 = (f32[24,32,128]{2,1,0:T(8,128)}, f32[24,32,128]{2,1,0:T(8,128)S(1)}, u32[]{:S(2)}) copy-start(f32[24,32,128]{2,1,0:T(8,128)S(1)} %convolution_bitcast_fusion.4) | copy-start | bytes 1179652
  43.9 9.8 %collective-permute-start.10 = (bf16[6,64,128]{2,1,0:T(8,128)(2,1)S(1)}, bf16[6,64,128]{2,1,0:T(8,128)(2,1)S(1)}, u32[]{:S(2)}, u32[]{:S(2)}) collective-permute-start(bf16[6,64,128]{2,1,0:T(8,128)(2,1)S(1)} %gather_fusion.6), channel_id=1, source_target_pairs={{1,0},{2,1},{3,2},{4,3},{5,4},{6,5},{7,6},{8,7},{9,8},{10,9},{11,1... | collective-permute-start | bytes 294920 | tf_op jit(solution)/shard_map/ppermute | solution.py:67
  46.5 8.5 %collective-permute-start.12 = (bf16[6,64,128]{2,1,0:T(8,128)(2,1)S(1)}, bf16[6,64,128]{2,1,0:T(8,128)(2,1)S(1)}, u32[]{:S(2)}, u32[]{:S(2)}) collective-permute-start(bf16[6,64,128]{2,1,0:T(8,128)(2,1)S(1)} %gather_fusion.8), channel_id=1, source_target_pairs={{16,0},{17,1},{18,2},{19,3},{20,4},{21,5},{22,6},{23,7},{24,8},{25... | collective-permute-start | bytes 294920 | tf_op jit(solution)/shard_map/ppermute | solution.py:67
  48.4 5.9 %collective-permute-start.11 = (bf16[6,64,128]{2,1,0:T(8,128)(2,1)S(1)}, bf16[6,64,128]{2,1,0:T(8,128)(2,1)S(1)}, u32[]{:S(2)}, u32[]{:S(2)}) collective-permute-start(bf16[6,64,128]{2,1,0:T(8,128)(2,1)S(1)} %gather_fusion.7), channel_id=1, source_target_pairs={{2,0},{3,1},{4,2},{5,3},{6,4},{7,5},{8,6},{9,7},{10,8},{11,9},{12,... | collective-permute-start | bytes 294920 | tf_op jit(solution)/shard_map/ppermute | solution.py:67
  48.4 7.2 %collective-permute-start.13 = (bf16[6,64,128]{2,1,0:T(8,128)(2,1)S(1)}, bf16[6,64,128]{2,1,0:T(8,128)(2,1)S(1)}, u32[]{:S(2)}, u32[]{:S(2)}) collective-permute-start(bf16[6,64,128]{2,1,0:T(8,128)(2,1)S(1)} %gather_fusion.9), channel_id=1, source_target_pairs={{31,0},{0,1},{1,2},{2,3},{3,4},{4,5},{5,6},{6,7},{7,8},{8,9},{9,10... | collective-permute-start | bytes 294920 | tf_op jit(solution)/shard_map/ppermute | solution.py:67
  49.6 7.3 %collective-permute-start.14 = (bf16[6,64,128]{2,1,0:T(8,128)(2,1)S(1)}, bf16[6,64,128]{2,1,0:T(8,128)(2,1)S(1)}, u32[]{:S(2)}, u32[]{:S(2)}) collective-permute-start(bf16[6,64,128]{2,1,0:T(8,128)(2,1)S(1)} %gather_fusion.10), channel_id=1, source_target_pairs={{30,0},{31,1},{0,2},{1,3},{2,4},{3,5},{4,6},{5,7},{6,8},{7,9},{8,1... | collective-permute-start | bytes 294920 | tf_op jit(solution)/shard_map/ppermute | solution.py:67
  59.6 3.3 %copy-start.2 = (bf16[24,5,128,128]{3,2,1,0:T(8,128)(2,1)S(1)}, bf16[24,5,128,128]{3,2,1,0:T(8,128)(2,1)}, u32[]{:S(2)}) copy-start(bf16[24,5,128,128]{3,2,1,0:T(8,128)(2,1)} %param.7) | copy-start | bytes 11796484
  64.5 1.1 copy-start.4
  69.0 14.1 %collective-permute-start.16 = (bf16[6,64,128]{2,1,0:T(8,128)(2,1)S(1)}, bf16[6,64,128]{2,1,0:T(8,128)(2,1)S(1)}, u32[]{:S(2)}, u32[]{:S(2)}) collective-permute-start(bf16[6,64,128]{2,1,0:T(8,128)(2,1)S(1)} %gather_fusion.13), channel_id=1, source_target_pairs={{2,0},{3,1},{4,2},{5,3},{6,4},{7,5},{8,6},{9,7},{10,8},{11,9},{12,... | collective-permute-start | bytes 294920 | tf_op jit(solution)/shard_map/ppermute | solution.py:67
  71.0 11.4 %collective-permute-start.15 = (bf16[6,64,128]{2,1,0:T(8,128)(2,1)S(1)}, bf16[6,64,128]{2,1,0:T(8,128)(2,1)S(1)}, u32[]{:S(2)}, u32[]{:S(2)}) collective-permute-start(bf16[6,64,128]{2,1,0:T(8,128)(2,1)S(1)} %gather_fusion.12), channel_id=1, source_target_pairs={{1,0},{2,1},{3,2},{4,3},{5,4},{6,5},{7,6},{8,7},{9,8},{10,9},{11,1... | collective-permute-start | bytes 294920 | tf_op jit(solution)/shard_map/ppermute | solution.py:67
  71.8 11.9 %collective-permute-start.17 = (bf16[6,64,128]{2,1,0:T(8,128)(2,1)S(1)}, bf16[6,64,128]{2,1,0:T(8,128)(2,1)S(1)}, u32[]{:S(2)}, u32[]{:S(2)}) collective-permute-start(bf16[6,64,128]{2,1,0:T(8,128)(2,1)S(1)} %gather_fusion.14), channel_id=1, source_target_pairs={{16,0},{17,1},{18,2},{19,3},{20,4},{21,5},{22,6},{23,7},{24,8},{25... | collective-permute-start | bytes 294920 | tf_op jit(solution)/shard_map/ppermute | solution.py:67
  74.8 9.5 %collective-permute-start.18 = (bf16[6,64,128]{2,1,0:T(8,128)(2,1)S(1)}, bf16[6,64,128]{2,1,0:T(8,128)(2,1)S(1)}, u32[]{:S(2)}, u32[]{:S(2)}) collective-permute-start(bf16[6,64,128]{2,1,0:T(8,128)(2,1)S(1)} %gather_fusion.15), channel_id=1, source_target_pairs={{31,0},{0,1},{1,2},{2,3},{3,4},{4,5},{5,6},{6,7},{7,8},{8,9},{9,10... | collective-permute-start | bytes 294920 | tf_op jit(solution)/shard_map/ppermute | solution.py:67
  76.0 9.0 %collective-permute-start.19 = (bf16[6,64,128]{2,1,0:T(8,128)(2,1)S(1)}, bf16[6,64,128]{2,1,0:T(8,128)(2,1)S(1)}, u32[]{:S(2)}, u32[]{:S(2)}) collective-permute-start(bf16[6,64,128]{2,1,0:T(8,128)(2,1)S(1)} %gather_fusion.16), channel_id=1, source_target_pairs={{30,0},{31,1},{0,2},{1,3},{2,4},{3,5},{4,6},{5,7},{6,8},{7,9},{8,1... | collective-permute-start | bytes 294920 | tf_op jit(solution)/shard_map/ppermute | solution.py:67
  87.7 3.3 %copy-start.1 = (bf16[24,5,128,128]{3,2,1,0:T(8,128)(2,1)S(1)}, bf16[24,5,128,128]{3,2,1,0:T(8,128)(2,1)}, u32[]{:S(2)}) copy-start(bf16[24,5,128,128]{3,2,1,0:T(8,128)(2,1)} %param.6) | copy-start | bytes 11796484
  92.7 1.4 %copy-start.9 = (f32[24,64,128]{2,0,1:T(8,128)S(1)}, f32[24,64,128]{2,0,1:T(8,128)}, u32[]{:S(2)}) copy-start(f32[24,64,128]{2,0,1:T(8,128)} %copy.91) | copy-start | bytes 2359300
  94.8 8.3 %collective-permute-start.20 = (f32[2,2,2,4,24,128]{5,4,3,2,1,0:T(8,128)S(1)}, f32[2,2,2,4,24,128]{5,4,3,2,1,0:T(8,128)S(1)}, u32[]{:S(2)}, u32[]{:S(2)}) collective-permute-start(f32[2,2,2,4,24,128]{5,4,3,2,1,0:T(8,128)S(1)} %dynamic-slice_bitcast_fusion), channel_id=1, source_target_pairs={{0,32},{32,0},{64,96},{96,64},{128,160},{160,128},{192,224},{224,1... | collective-permute-start | bytes 1179656 | tf_op jit(solution)/shard_map/ppermute | solution.py:112
  103.2 7.7 %collective-permute-start.21 = (f32[2,2,4,24,128]{4,3,2,1,0:T(8,128)S(1)}, f32[2,2,4,24,128]{4,3,2,1,0:T(8,128)S(1)}, u32[]{:S(2)}, u32[]{:S(2)}) collective-permute-start(f32[2,2,4,24,128]{4,3,2,1,0:T(8,128)S(1)} %dynamic-slice_bitcast_fusion.1), channel_id=1, source_target_pairs={{0,128},{32,160},{64,192},{96,224},{128,0},{160,32},{192,64},{224,... | collective-permute-start | bytes 589832 | tf_op jit(solution)/shard_map/ppermute | solution.py:112
  110.9 3.6 %collective-permute-start.22 = (f32[2,4,24,128]{3,2,1,0:T(8,128)S(1)}, f32[2,4,24,128]{3,2,1,0:T(8,128)S(1)}, u32[]{:S(2)}, u32[]{:S(2)}) collective-permute-start(f32[2,4,24,128]{3,2,1,0:T(8,128)S(1)} %dynamic-slice_bitcast_fusion.2), channel_id=1, source_target_pairs={{0,64},{32,96},{64,0},{96,32},{128,192},{160,224},{192,128},{224,1... | collective-permute-start | bytes 294920 | tf_op jit(solution)/shard_map/ppermute | solution.py:112
  (4 other events, 4.0 us)

commit v11 on v7

--- a/solution.py
+++ b/solution.py
@@ -68,7 +68,7 @@
         return jnp.concatenate(pieces, axis=0)
 
     e_mats = pencil_e
-    a_mats = pencil_a
+    both_mats = jnp.concatenate([pencil_e, pencil_a], axis=-1)
     cols_major = jnp.transpose(columns, (1, 0, 2))
     rhs_full, _ = apply_pair(fetch_halo(cols_major), slot_index, e_mats, None)
     node_count = lax.axis_size("node")
@@ -81,7 +81,8 @@
     iterate = start.reshape(dev_rows, 2 * col_count, -1)
     for sweep_step in range(SWEEPS):
         rounded = iterate.astype(jnp.bfloat16)
-        with_e, with_a = apply_pair(fetch_halo(rounded), slot_index, e_mats, a_mats)
+        with_both, _ = apply_pair(fetch_halo(rounded), slot_index, both_mats, None)
+        with_e, with_a = with_both[..., : pencil_e.shape[-1]], with_both[..., pencil_e.shape[-1] :]
         e_real, e_imag = with_e[:, :col_count], with_e[:, col_count:]
         applied_real = node_real * e_real - node_imag * e_imag - with_a[:, :col_count]
         applied_imag = node_real * e_imag + node_imag * e_real - with_a[:, col_count:]

time: 116 us -> 132 us (1.14)
  local copies, waits for them, and re-layouts: 28.1 us -> 37.5 us
  matrix products: 12.2 us -> 14.7 us
  starting transfers between devices: 52 us -> 54.4 us
    gather x15, local copies, waits for them, and re-layouts: 8.7 us -> 17 us  [fetch_halo(): vector[asked_for[which]]]
    dot_general x3, matrix products: 6.97 us -> 13.6 us  [apply_pair(): jnp.einsum('nscb,nsbd->ncd', picked, first, preferred_element_type=jnp.fl...]
    ppermute x15, waiting for transfers between devices: 7.42 us -> 12.1 us  [fetch_halo(): lax.ppermute(vector[asked_for[which]], 'rows', from_partner(offset))]
    concatenate x0 -> x1, local copies, waits for them, and re-layouts: none -> 4.58 us  [per_device(): both_mats = jnp.concatenate([pencil_e, pencil_a], axis=-1)]
    dot_general x2 -> x0, matrix products: 4.11 us -> none  [apply_pair(): jnp.einsum('nscb,nsbd->ncd', picked, second, preferred_element_type=jnp.f...]
    ppermute x3, waiting for transfers between devices: 7.15 us -> 3.55 us  [per_device(): total = total + lax.ppermute(chunk, 'node', perm)]
    ppermute x15, starting transfers between devices: 26.4 us -> 29.2 us  [fetch_halo(): lax.ppermute(vector[asked_for[which]], 'rows', from_partner(offset))]
    unnamed x43 -> x36, local copies, waits for them, and re-layouts: 10.5 us -> 8.11 us
  transfers between devices with their start and end apart: 24 -> 24, of which waited for: 7 -> 8; matrix products, arithmetic and copies ran while one was open for 10% -> 17% of each run, Pallas kernels for 0% -> 0%
where the time goes in v11:
time: 132 us; the launch traced here: 131 us
  starting transfers between devices  54.4 us (41%)
  local copies, waits for them, and re-layouts  37.5 us (28%)
  waiting for transfers between devices  17.1 us (13%)
  matrix products  14.7 us (11%)
  other arithmetic  6.43 us (5%)
    ppermute x15, starting transfers between devices, fetch_halo(): lax.ppermute(vector[asked_for[which]], 'rows', from_partner(offset))  29.2 us
    gather x15, local copies, waits for them, and re-layouts, fetch_halo(): vector[asked_for[which]]  17 us
    dot_general x3, matrix products, apply_pair(): jnp.einsum('nscb,nsbd->ncd', picked, first, preferred_element_type=jnp.fl...  13.6 us
    ppermute x5, starting transfers between devices, per_device(): lax.ppermute(wanted[which], 'rows', to_partner(offset))  12.3 us
    ppermute x15, waiting for transfers between devices, fetch_halo(): lax.ppermute(vector[asked_for[which]], 'rows', from_partner(offset))  12.1 us
    unnamed x36, local copies, waits for them, and re-layouts  8.11 us
    ppermute x1, starting transfers between devices, per_device(): lax.ppermute(other, 'node', [(j, j ^ 1) for j in range(node_count)])  7.78 us
    gather x3, local copies, waits for them, and re-layouts, apply_pair(): picked = extended[slot_index]  5.1 us
  transfers between devices with their start and end apart: 24, of which 8 were waited for; matrix products, arithmetic and copies ran while one was open for 17% of the time, Pallas kernels for 0%

profile of v11, /device:TPU:3, one launch (start us, length us, event | category | flops | bytes accessed | tf_op | source)
XLA Modules:
  0.0 130.8 jit_solution(16121620176536589376)
XLA Ops:
  4.2 7.7 %collective-permute-start.8 = (s32[6]{0:T(128)S(1)}, s32[6]{0:T(128)S(1)}, u32[]{:S(2)}, u32[]{:S(2)}) collective-permute-start(s32[6]{0:T(128)S(1)} %get-tuple-element.15), channel_id=1, source_target_pairs={{0,30},{1,31},{2,0},{3,1},{4,2},{5,3},{6,4},{7,5},{8,6},{9,7},{10,... | collective-permute-start | bytes 80 | tf_op jit(solution)/shard_map/ppermute | solution.py:61
  11.9 2.4 %collective-permute-start.4 = (s32[6]{0:T(128)S(1)}, s32[6]{0:T(128)S(1)}, u32[]{:S(2)}, u32[]{:S(2)}) collective-permute-start(s32[6]{0:T(128)S(1)} %get-tuple-element.17), channel_id=1, source_target_pairs={{0,16},{1,17},{2,18},{3,19},{4,20},{5,21},{6,22},{7,23},{8,24},{9,... | collective-permute-start | bytes 80 | tf_op jit(solution)/shard_map/ppermute | solution.py:61
  14.4 2.1 %collective-permute-start = (s32[6]{0:T(128)S(1)}, s32[6]{0:T(128)S(1)}, u32[]{:S(2)}, u32[]{:S(2)}) collective-permute-start(s32[6]{0:T(128)S(1)} %get-tuple-element.19), channel_id=1, source_target_pairs={{0,1},{1,2},{2,3},{3,4},{4,5},{5,6},{6,7},{7,8},{8,9},{9,10},{10,1... | collective-permute-start | bytes 80 | tf_op jit(solution)/shard_map/ppermute | solution.py:61
  17.6 4.7 %constant_dynamic-update-slice_fusion.13 = bf16[24,5,128,256]{3,2,1,0:T(8,128)(2,1)} fusion(bf16[24,5,128,128]{3,2,1,0:T(8,128)(2,1)} %param.6), kind=kLoop, calls=%fused_computation.104 | loop fusion | bytes 7864320
  24.8 2.7 %collective-permute-start.3 = (bf16[6,32,128]{2,1,0:T(8,128)(2,1)S(1)}, bf16[6,32,128]{2,1,0:T(8,128)(2,1)S(1)}, u32[]{:S(2)}, u32[]{:S(2)}) collective-permute-start(bf16[6,32,128]{2,1,0:T(8,128)(2,1)S(1)} %gather_fusion.1), channel_id=1, source_target_pairs={{2,0},{3,1},{4,2},{5,3},{6,4},{7,5},{8,6},{9,7},{10,8},{11,9},{12,... | collective-permute-start | bytes 147464 | tf_op jit(solution)/shard_map/ppermute | solution.py:67
  28.1 2.1 %collective-permute-start.1 = (bf16[6,32,128]{2,1,0:T(8,128)(2,1)S(1)}, bf16[6,32,128]{2,1,0:T(8,128)(2,1)S(1)}, u32[]{:S(2)}, u32[]{:S(2)}) collective-permute-start(bf16[6,32,128]{2,1,0:T(8,128)(2,1)S(1)} %gather_fusion), channel_id=1, source_target_pairs={{1,0},{2,1},{3,2},{4,3},{5,4},{6,5},{7,6},{8,7},{9,8},{10,9},{11,1... | collective-permute-start | bytes 147464 | tf_op jit(solution)/shard_map/ppermute | solution.py:67
  30.7 4.3 %collective-permute-start.5 = (bf16[6,32,128]{2,1,0:T(8,128)(2,1)S(1)}, bf16[6,32,128]{2,1,0:T(8,128)(2,1)S(1)}, u32[]{:S(2)}, u32[]{:S(2)}) collective-permute-start(bf16[6,32,128]{2,1,0:T(8,128)(2,1)S(1)} %gather_fusion.2), channel_id=1, source_target_pairs={{16,0},{17,1},{18,2},{19,3},{20,4},{21,5},{22,6},{23,7},{24,8},{25... | collective-permute-start | bytes 147464 | tf_op jit(solution)/shard_map/ppermute | solution.py:67
  35.8 1.9 %collective-permute-done.5 = bf16[6,32,128]{2,1,0:T(8,128)(2,1)S(1)} collective-permute-done((bf16[6,32,128]{2,1,0:T(8,128)(2,1)S(1)}, bf16[6,32,128]{2,1,0:T(8,128)(2,1)S(1)}, u32[]{:S(2)}, u32[]{:S(2)}) %collective-permute-start.5) | collective-permute-done | bytes 49184 | tf_op jit(solution)/shard_map/ppermute | solution.py:67
  37.7 4.5 %collective-permute-done.9 = bf16[6,32,128]{2,1,0:T(8,128)(2,1)S(1)} collective-permute-done((bf16[6,32,128]{2,1,0:T(8,128)(2,1)S(1)}, bf16[6,32,128]{2,1,0:T(8,128)(2,1)S(1)}, u32[]{:S(2)}, u32[]{:S(2)}) %collective-permute-start.9) | collective-permute-done | bytes 49184 | tf_op jit(solution)/shard_map/ppermute | solution.py:67
  43.0 2.8 %convolution_bitcast_fusion.2 = f32[24,32,128]{2,1,0:T(8,128)S(1)} fusion(bf16[24,5,32,128]{3,2,1,0:T(8,128)(2,1)S(1)} %bitcast.134, bf16[24,5,128,128]{3,2,1,0:T(8,128)(2,1)} %param.6), kind=kOutput, calls=%fused_computation.20 | convolution fusion | flops 125829120 | bytes 5308416 | tf_op jit(solution)/shard_map/nscb,nsbd->ncd/dot_general | solution.py:25
  47.1 1.6 %gather_fusion.6 = bf16[6,64,128]{2,1,0:T(8,128)(2,1)S(1)} fusion(bf16[24,64,128]{2,1,0:T(8,128)(2,1)} %get-tuple-element.57, s32[1024]{0:T(1024)S(1)} %pad_clamp_fusion.5), kind=kCustom, calls=%fused_computation.6 | custom fusion | bytes 196632 | tf_op jit(solution)/shard_map/gather | solution.py:67
  48.8 4.6 %constant_dynamic-update-slice_fusion.12 = bf16[24,5,128,256]{3,2,1,0:T(8,128)(2,1)} fusion(bf16[24,5,128,256]{3,2,1,0:T(8,128)(2,1)} %constant_dynamic-update-slice_fusion.13, bf16[24,5,128,128]{3,2,1,0:T(8,128)(2,1)} %param.7), kind=kLoop, calls=%fused_computation.103 | loop fusion | bytes 7864320 | tf_op jit(solution)/shard_map/concatenate | solution.py:71
  53.6 2.2 %gather_fusion.8 = bf16[6,64,128]{2,1,0:T(8,128)(2,1)} fusion(bf16[24,64,128]{2,1,0:T(8,128)(2,1)} %get-tuple-element.57, s32[1024]{0:T(1024)S(1)} %pad_clamp_fusion.3), kind=kCustom, calls=%fused_computation.8 | custom fusion | bytes 196632 | tf_op jit(solution)/shard_map/gather | solution.py:67
  55.8 2.2 %gather_fusion.7 = bf16[6,64,128]{2,1,0:T(8,128)(2,1)} fusion(bf16[24,64,128]{2,1,0:T(8,128)(2,1)} %get-tuple-element.57, s32[1024]{0:T(1024)S(1)} %pad_clamp_fusion.4), kind=kCustom, calls=%fused_computation.7 | custom fusion | bytes 196632 | tf_op jit(solution)/shard_map/gather | solution.py:67
  58.0 2.2 %gather_fusion.9 = bf16[6,64,128]{2,1,0:T(8,128)(2,1)} fusion(bf16[24,64,128]{2,1,0:T(8,128)(2,1)} %get-tuple-element.57, s32[1024]{0:T(1024)S(1)} %pad_clamp_fusion.2), kind=kCustom, calls=%fused_computation.9 | custom fusion | bytes 196632 | tf_op jit(solution)/shard_map/gather | solution.py:67
  60.2 1.7 %gather_fusion.10 = bf16[6,64,128]{2,1,0:T(8,128)(2,1)S(1)} fusion(bf16[24,64,128]{2,1,0:T(8,128)(2,1)} %get-tuple-element.57, s32[1024]{0:T(1024)} %copy-done.8), kind=kCustom, calls=%fused_computation.10 | custom fusion | bytes 196632 | tf_op jit(solution)/shard_map/gather | solution.py:67
  61.9 1.5 %collective-permute-start.12 = (bf16[6,64,128]{2,1,0:T(8,128)(2,1)}, bf16[6,64,128]{2,1,0:T(8,128)(2,1)S(1)}, u32[]{:S(2)}, u32[]{:S(2)}) collective-permute-start(bf16[6,64,128]{2,1,0:T(8,128)(2,1)} %gather_fusion.8), channel_id=1, source_target_pairs={{16,0},{17,1},{18,2},{19,3},{20,4},{21,5},{22,6},{23,7},{24,8},{25... | collective-permute-start | bytes 294920 | tf_op jit(solution)/shard_map/ppermute | solution.py:67
  63.4 1.6 %collective-permute-start.13 = (bf16[6,64,128]{2,1,0:T(8,128)(2,1)}, bf16[6,64,128]{2,1,0:T(8,128)(2,1)S(1)}, u32[]{:S(2)}, u32[]{:S(2)}) collective-permute-start(bf16[6,64,128]{2,1,0:T(8,128)(2,1)} %gather_fusion.9), channel_id=1, source_target_pairs={{31,0},{0,1},{1,2},{2,3},{3,4},{4,5},{5,6},{6,7},{7,8},{8,9},{9,10... | collective-permute-start | bytes 294920 | tf_op jit(solution)/shard_map/ppermute | solution.py:67
  65.0 4.2 %collective-permute-start.14 = (bf16[6,64,128]{2,1,0:T(8,128)(2,1)S(1)}, bf16[6,64,128]{2,1,0:T(8,128)(2,1)S(1)}, u32[]{:S(2)}, u32[]{:S(2)}) collective-permute-start(bf16[6,64,128]{2,1,0:T(8,128)(2,1)S(1)} %gather_fusion.10), channel_id=1, source_target_pairs={{30,0},{31,1},{0,2},{1,3},{2,4},{3,5},{4,6},{5,7},{6,8},{7,9},{8,1... | collective-permute-start | bytes 294920 | tf_op jit(solution)/shard_map/ppermute | solution.py:67
  69.8 2.3 %collective-permute-done.14 = bf16[6,64,128]{2,1,0:T(8,128)(2,1)S(1)} collective-permute-done((bf16[6,64,128]{2,1,0:T(8,128)(2,1)S(1)}, bf16[6,64,128]{2,1,0:T(8,128)(2,1)S(1)}, u32[]{:S(2)}, u32[]{:S(2)}) %collective-permute-start.14) | collective-permute-done | bytes 98336 | tf_op jit(solution)/shard_map/ppermute | solution.py:67
  72.2 2.2 %gather_fusion.11 = bf16[120,64,128]{2,1,0:T(8,128)(2,1)} fusion(bf16[54,64,128]{2,1,0:T(8,128)(2,1)S(1)} %constant_dynamic-update-slice_fusion.6, s32[1024]{0:T(1024)S(1)} %pad_clamp_fusion), kind=kCustom, calls=%fused_computation.11 | custom fusion | bytes 3932640 | tf_op jit(solution)/shard_map/gather | solution.py:24
  74.4 5.4 %convolution_bitcast_fusion.1 = f32[24,64,256]{2,1,0:T(8,128)S(1)} fusion(bf16[24,5,64,128]{3,2,1,0:T(8,128)(2,1)} %bitcast.131, bf16[24,5,128,256]{3,2,1,0:T(8,128)(2,1)} %constant_dynamic-update-slice_fusion.12), kind=kOutput, calls=%fused_computation.19 | convolution fusion | flops 503316480 | bytes 11403264 | tf_op jit(solution)/shard_map/nscb,nsbd->ncd/dot_general | solution.py:25
  87.8 3.6 %collective-permute-start.17 = (bf16[6,64,128]{2,1,0:T(8,128)(2,1)S(1)}, bf16[6,64,128]{2,1,0:T(8,128)(2,1)S(1)}, u32[]{:S(2)}, u32[]{:S(2)}) collective-permute-start(bf16[6,64,128]{2,1,0:T(8,128)(2,1)S(1)} %gather_fusion.14), channel_id=1, source_target_pairs={{16,0},{17,1},{18,2},{19,3},{20,4},{21,5},{22,6},{23,7},{24,8},{25... | collective-permute-start | bytes 294920 | tf_op jit(solution)/shard_map/ppermute | solution.py:67
  91.4 1.5 %collective-permute-start.18 = (bf16[6,64,128]{2,1,0:T(8,128)(2,1)S(1)}, bf16[6,64,128]{2,1,0:T(8,128)(2,1)S(1)}, u32[]{:S(2)}, u32[]{:S(2)}) collective-permute-start(bf16[6,64,128]{2,1,0:T(8,128)(2,1)S(1)} %gather_fusion.15), channel_id=1, source_target_pairs={{31,0},{0,1},{1,2},{2,3},{3,4},{4,5},{5,6},{6,7},{7,8},{8,9},{9,10... | collective-permute-start | bytes 294920 | tf_op jit(solution)/shard_map/ppermute | solution.py:67
  92.8 4.3 %collective-permute-start.19 = (bf16[6,64,128]{2,1,0:T(8,128)(2,1)S(1)}, bf16[6,64,128]{2,1,0:T(8,128)(2,1)S(1)}, u32[]{:S(2)}, u32[]{:S(2)}) collective-permute-start(bf16[6,64,128]{2,1,0:T(8,128)(2,1)S(1)} %gather_fusion.16), channel_id=1, source_target_pairs={{30,0},{31,1},{0,2},{1,3},{2,4},{3,5},{4,6},{5,7},{6,8},{7,9},{8,1... | collective-permute-start | bytes 294920 | tf_op jit(solution)/shard_map/ppermute | solution.py:67
  98.3 2.8 %collective-permute-done.19 = bf16[6,64,128]{2,1,0:T(8,128)(2,1)S(1)} collective-permute-done((bf16[6,64,128]{2,1,0:T(8,128)(2,1)S(1)}, bf16[6,64,128]{2,1,0:T(8,128)(2,1)S(1)}, u32[]{:S(2)}, u32[]{:S(2)}) %collective-permute-start.19) | collective-permute-done | bytes 98336 | tf_op jit(solution)/shard_map/ppermute | solution.py:67
  101.1 2.2 %gather_fusion.17 = bf16[120,64,128]{2,1,0:T(8,128)(2,1)} fusion(bf16[54,64,128]{2,1,0:T(8,128)(2,1)S(1)} %constant_dynamic-update-slice_fusion.14, s32[1024]{0:T(1024)S(1)} %pad_clamp_fusion), kind=kCustom, calls=%fused_computation.17 | custom fusion | bytes 3932640 | tf_op jit(solution)/shard_map/gather | solution.py:24
  103.3 5.4 %convolution_bitcast_fusion = f32[24,64,256]{2,1,0:T(8,128)S(1)} fusion(bf16[24,5,64,128]{3,2,1,0:T(8,128)(2,1)} %bitcast.130, bf16[24,5,128,256]{3,2,1,0:T(8,128)(2,1)} %constant_dynamic-update-slice_fusion.12), kind=kOutput, calls=%fused_computation.18 | convolution fusion | flops 503316480 | bytes 11403264 | tf_op jit(solution)/shard_map/nscb,nsbd->ncd/dot_general | solution.py:25
  112.2 7.8 %collective-permute-start.20 = (f32[4,2,4,24,128]{4,3,2,1,0:T(8,128)S(1)}, f32[4,2,4,24,128]{4,3,2,1,0:T(8,128)S(1)}, u32[]{:S(2)}, u32[]{:S(2)}) collective-permute-start(f32[4,2,4,24,128]{4,3,2,1,0:T(8,128)S(1)} %bitcast.143), channel_id=1, source_target_pairs={{0,32},{32,0},{64,96},{96,64},{128,160},{160,128},{192,224},{224,1... | collective-permute-start | bytes 1179656 | tf_op jit(solution)/shard_map/ppermute | solution.py:111
  121.5 1.4 %collective-permute-start.21 = (f32[2,4,24,128]{3,2,1,0:T(8,128)S(1)}, f32[2,4,24,128]{3,2,1,0:T(8,128)S(1)}, u32[]{:S(2)}, u32[]{:S(2)}) collective-permute-start(f32[2,4,24,128]{3,2,1,0:T(8,128)S(1)} %get-tuple-element.45), channel_id=1, source_target_pairs={{0,64},{32,96},{64,128},{96,160},{128,192},{160,224},{192,0},{224,... | collective-permute-start | bytes 294920 | tf_op jit(solution)/shard_map/ppermute | solution.py:116
  122.9 2.6 %collective-permute-start.22 = (f32[2,4,24,128]{3,2,1,0:T(8,128)S(1)}, f32[2,4,24,128]{3,2,1,0:T(8,128)S(1)}, u32[]{:S(2)}, u32[]{:S(2)}) collective-permute-start(f32[2,4,24,128]{3,2,1,0:T(8,128)S(1)} %get-tuple-element.47), channel_id=1, source_target_pairs={{0,128},{32,160},{64,192},{96,224},{128,0},{160,32},{192,64},{224,... | collective-permute-start | bytes 294920 | tf_op jit(solution)/shard_map/ppermute | solution.py:116
  126.9 3.2 %collective-permute-done.22 = f32[2,4,24,128]{3,2,1,0:T(8,128)S(1)} collective-permute-done((f32[2,4,24,128]{3,2,1,0:T(8,128)S(1)}, f32[2,4,24,128]{3,2,1,0:T(8,128)S(1)}, u32[]{:S(2)}, u32[]{:S(2)}) %collective-permute-start.22) | collective-permute-done | bytes 98336 | tf_op jit(solution)/shard_map/ppermute | solution.py:116
  (137 shorter events, 28.3 us)
Async XLA Ops:
  0.0 45.9 %copy-start = (bf16[1,2,24,128,128]{4,3,2,1,0:T(8,128)(2,1)S(1)}, bf16[1,2,24,128,128]{4,3,2,1,0:T(8,128)(2,1)}, u32[]{:S(2)}) copy-start(bf16[1,2,24,128,128]{4,3,2,1,0:T(8,128)(2,1)} %param.8) | copy-start | bytes 4718596
  0.0 17.4 %copy-start.6 = (bf16[32,24,128]{2,1,0:T(8,128)(2,1)S(1)}, bf16[32,24,128]{2,1,0:T(8,128)(2,1)}, u32[]{:S(2)}) copy-start(bf16[32,24,128]{2,1,0:T(8,128)(2,1)} %param.5) | copy-start | bytes 589828
  4.2 18.1 %collective-permute-start.6 = (s32[6]{0:T(128)S(1)}, s32[6]{0:T(128)S(1)}, u32[]{:S(2)}, u32[]{:S(2)}) collective-permute-start(s32[6]{0:T(128)S(1)} %get-tuple-element.18), channel_id=1, source_target_pairs={{0,31},{1,0},{2,1},{3,2},{4,3},{5,4},{6,5},{7,6},{8,7},{9,8},{10,9... | collective-permute-start | bytes 80 | tf_op jit(solution)/shard_map/ppermute | solution.py:61
  4.2 18.1 %collective-permute-start.8 = (s32[6]{0:T(128)S(1)}, s32[6]{0:T(128)S(1)}, u32[]{:S(2)}, u32[]{:S(2)}) collective-permute-start(s32[6]{0:T(128)S(1)} %get-tuple-element.15), channel_id=1, source_target_pairs={{0,30},{1,31},{2,0},{3,1},{4,2},{5,3},{6,4},{7,5},{8,6},{9,7},{10,... | collective-permute-start | bytes 80 | tf_op jit(solution)/shard_map/ppermute | solution.py:61
  11.9 12.3 %collective-permute-start.2 = (s32[6]{0:T(128)S(1)}, s32[6]{0:T(128)S(1)}, u32[]{:S(2)}, u32[]{:S(2)}) collective-permute-start(s32[6]{0:T(128)S(1)} %get-tuple-element.16), channel_id=1, source_target_pairs={{0,2},{1,3},{2,4},{3,5},{4,6},{5,7},{6,8},{7,9},{8,10},{9,11},{10,... | collective-permute-start | bytes 80 | tf_op jit(solution)/shard_map/ppermute | solution.py:61
  11.9 12.3 %collective-permute-start.4 = (s32[6]{0:T(128)S(1)}, s32[6]{0:T(128)S(1)}, u32[]{:S(2)}, u32[]{:S(2)}) collective-permute-start(s32[6]{0:T(128)S(1)} %get-tuple-element.17), channel_id=1, source_target_pairs={{0,16},{1,17},{2,18},{3,19},{4,20},{5,21},{6,22},{7,23},{8,24},{9,... | collective-permute-start | bytes 80 | tf_op jit(solution)/shard_map/ppermute | solution.py:61
  14.4 13.1 %collective-permute-start = (s32[6]{0:T(128)S(1)}, s32[6]{0:T(128)S(1)}, u32[]{:S(2)}, u32[]{:S(2)}) collective-permute-start(s32[6]{0:T(128)S(1)} %get-tuple-element.19), channel_id=1, source_target_pairs={{0,1},{1,2},{2,3},{3,4},{4,5},{5,6},{6,7},{7,8},{8,9},{9,10},{10,1... | collective-permute-start | bytes 80 | tf_op jit(solution)/shard_map/ppermute | solution.py:61
  22.9 14.8 %collective-permute-start.7 = (bf16[6,32,128]{2,1,0:T(8,128)(2,1)S(1)}, bf16[6,32,128]{2,1,0:T(8,128)(2,1)S(1)}, u32[]{:S(2)}, u32[]{:S(2)}) collective-permute-start(bf16[6,32,128]{2,1,0:T(8,128)(2,1)S(1)} %gather_fusion.3), channel_id=1, source_target_pairs={{31,0},{0,1},{1,2},{2,3},{3,4},{4,5},{5,6},{6,7},{7,8},{8,9},{9,10... | collective-permute-start | bytes 147464 | tf_op jit(solution)/shard_map/ppermute | solution.py:67
  24.8 11.0 %collective-permute-start.3 = (bf16[6,32,128]{2,1,0:T(8,128)(2,1)S(1)}, bf16[6,32,128]{2,1,0:T(8,128)(2,1)S(1)}, u32[]{:S(2)}, u32[]{:S(2)}) collective-permute-start(bf16[6,32,128]{2,1,0:T(8,128)(2,1)S(1)} %gather_fusion.1), channel_id=1, source_target_pairs={{2,0},{3,1},{4,2},{5,3},{6,4},{7,5},{8,6},{9,7},{10,8},{11,9},{12,... | collective-permute-start | bytes 147464 | tf_op jit(solution)/shard_map/ppermute | solution.py:67
  28.1 7.7 %collective-permute-start.1 = (bf16[6,32,128]{2,1,0:T(8,128)(2,1)S(1)}, bf16[6,32,128]{2,1,0:T(8,128)(2,1)S(1)}, u32[]{:S(2)}, u32[]{:S(2)}) collective-permute-start(bf16[6,32,128]{2,1,0:T(8,128)(2,1)S(1)} %gather_fusion), channel_id=1, source_target_pairs={{1,0},{2,1},{3,2},{4,3},{5,4},{6,5},{7,6},{8,7},{9,8},{10,9},{11,1... | collective-permute-start | bytes 147464 | tf_op jit(solution)/shard_map/ppermute | solution.py:67
  30.2 23.4 %copy-start.7 = (s32[1024]{0:T(1024)}, s32[1024]{0:T(1024)S(1)}, u32[]{:S(2)}) copy-start(s32[1024]{0:T(1024)S(1)} %pad_clamp_fusion.3) | copy-start | bytes 12292
  30.7 6.9 %collective-permute-start.5 = (bf16[6,32,128]{2,1,0:T(8,128)(2,1)S(1)}, bf16[6,32,128]{2,1,0:T(8,128)(2,1)S(1)}, u32[]{:S(2)}, u32[]{:S(2)}) collective-permute-start(bf16[6,32,128]{2,1,0:T(8,128)(2,1)S(1)} %gather_fusion.2), channel_id=1, source_target_pairs={{16,0},{17,1},{18,2},{19,3},{20,4},{21,5},{22,6},{23,7},{24,8},{25... | collective-permute-start | bytes 147464 | tf_op jit(solution)/shard_map/ppermute | solution.py:67
  35.1 10.8 %copy-start.8 = (s32[1024]{0:T(1024)}, s32[1024]{0:T(1024)S(1)}, u32[]{:S(2)}) copy-start(s32[1024]{0:T(1024)S(1)} %pad_clamp_fusion.1) | copy-start | bytes 12292
  35.6 6.6 %collective-permute-start.9 = (bf16[6,32,128]{2,1,0:T(8,128)(2,1)S(1)}, bf16[6,32,128]{2,1,0:T(8,128)(2,1)S(1)}, u32[]{:S(2)}, u32[]{:S(2)}) collective-permute-start(bf16[6,32,128]{2,1,0:T(8,128)(2,1)S(1)} %gather_fusion.4), channel_id=1, source_target_pairs={{30,0},{31,1},{0,2},{1,3},{2,4},{3,5},{4,6},{5,7},{6,8},{7,9},{8,1... | collective-permute-start | bytes 147464 | tf_op jit(solution)/shard_map/ppermute | solution.py:67
  45.9 1.2 copy-start.1
  48.7 20.5 %collective-permute-start.10 = (bf16[6,64,128]{2,1,0:T(8,128)(2,1)S(1)}, bf16[6,64,128]{2,1,0:T(8,128)(2,1)S(1)}, u32[]{:S(2)}, u32[]{:S(2)}) collective-permute-start(bf16[6,64,128]{2,1,0:T(8,128)(2,1)S(1)} %gather_fusion.6), channel_id=1, source_target_pairs={{1,0},{2,1},{3,2},{4,3},{5,4},{6,5},{7,6},{8,7},{9,8},{10,9},{11,1... | collective-permute-start | bytes 294920 | tf_op jit(solution)/shard_map/ppermute | solution.py:67
  61.9 7.9 %collective-permute-start.12 = (bf16[6,64,128]{2,1,0:T(8,128)(2,1)}, bf16[6,64,128]{2,1,0:T(8,128)(2,1)S(1)}, u32[]{:S(2)}, u32[]{:S(2)}) collective-permute-start(bf16[6,64,128]{2,1,0:T(8,128)(2,1)} %gather_fusion.8), channel_id=1, source_target_pairs={{16,0},{17,1},{18,2},{19,3},{20,4},{21,5},{22,6},{23,7},{24,8},{25... | collective-permute-start | bytes 294920 | tf_op jit(solution)/shard_map/ppermute | solution.py:67
  63.4 5.8 %collective-permute-start.11 = (bf16[6,64,128]{2,1,0:T(8,128)(2,1)}, bf16[6,64,128]{2,1,0:T(8,128)(2,1)S(1)}, u32[]{:S(2)}, u32[]{:S(2)}) collective-permute-start(bf16[6,64,128]{2,1,0:T(8,128)(2,1)} %gather_fusion.7), channel_id=1, source_target_pairs={{2,0},{3,1},{4,2},{5,3},{6,4},{7,5},{8,6},{9,7},{10,8},{11,9},{12,... | collective-permute-start | bytes 294920 | tf_op jit(solution)/shard_map/ppermute | solution.py:67
  63.4 6.4 %collective-permute-start.13 = (bf16[6,64,128]{2,1,0:T(8,128)(2,1)}, bf16[6,64,128]{2,1,0:T(8,128)(2,1)S(1)}, u32[]{:S(2)}, u32[]{:S(2)}) collective-permute-start(bf16[6,64,128]{2,1,0:T(8,128)(2,1)} %gather_fusion.9), channel_id=1, source_target_pairs={{31,0},{0,1},{1,2},{2,3},{3,4},{4,5},{5,6},{6,7},{7,8},{8,9},{9,10... | collective-permute-start | bytes 294920 | tf_op jit(solution)/shard_map/ppermute | solution.py:67
  65.0 7.1 %collective-permute-start.14 = (bf16[6,64,128]{2,1,0:T(8,128)(2,1)S(1)}, bf16[6,64,128]{2,1,0:T(8,128)(2,1)S(1)}, u32[]{:S(2)}, u32[]{:S(2)}) collective-permute-start(bf16[6,64,128]{2,1,0:T(8,128)(2,1)S(1)} %gather_fusion.10), channel_id=1, source_target_pairs={{30,0},{31,1},{0,2},{1,3},{2,4},{3,5},{4,6},{5,7},{6,8},{7,9},{8,1... | collective-permute-start | bytes 294920 | tf_op jit(solution)/shard_map/ppermute | solution.py:67
  74.4 5.4 %copy-start.2 = (f32[24,32,128]{2,1,0:T(8,128)S(1)}, f32[24,32,128]{2,1,0:T(8,128)}, u32[]{:S(2)}) copy-start(f32[24,32,128]{2,1,0:T(8,128)} %copy-done.1) | copy-start | bytes 1179652
  81.5 11.4 %copy-start.4 = (bf16[24,64,128]{2,1,0:T(8,128)(2,1)}, bf16[24,64,128]{2,1,0:T(8,128)(2,1)S(1)}, u32[]{:S(2)}) copy-start(bf16[24,64,128]{2,1,0:T(8,128)(2,1)S(1)} %get-tuple-element.43) | copy-start | bytes 1179652
  85.8 12.3 %collective-permute-start.16 = (bf16[6,64,128]{2,1,0:T(8,128)(2,1)}, bf16[6,64,128]{2,1,0:T(8,128)(2,1)S(1)}, u32[]{:S(2)}, u32[]{:S(2)}) collective-permute-start(bf16[6,64,128]{2,1,0:T(8,128)(2,1)} %gather_fusion.13), channel_id=1, source_target_pairs={{2,0},{3,1},{4,2},{5,3},{6,4},{7,5},{8,6},{9,7},{10,8},{11,9},{12,... | collective-permute-start | bytes 294920 | tf_op jit(solution)/shard_map/ppermute | solution.py:67
  87.2 11.0 %collective-permute-start.15 = (bf16[6,64,128]{2,1,0:T(8,128)(2,1)}, bf16[6,64,128]{2,1,0:T(8,128)(2,1)S(1)}, u32[]{:S(2)}, u32[]{:S(2)}) collective-permute-start(bf16[6,64,128]{2,1,0:T(8,128)(2,1)} %gather_fusion.12), channel_id=1, source_target_pairs={{1,0},{2,1},{3,2},{4,3},{5,4},{6,5},{7,6},{8,7},{9,8},{10,9},{11,1... | collective-permute-start | bytes 294920 | tf_op jit(solution)/shard_map/ppermute | solution.py:67
  87.8 10.4 %collective-permute-start.17 = (bf16[6,64,128]{2,1,0:T(8,128)(2,1)S(1)}, bf16[6,64,128]{2,1,0:T(8,128)(2,1)S(1)}, u32[]{:S(2)}, u32[]{:S(2)}) collective-permute-start(bf16[6,64,128]{2,1,0:T(8,128)(2,1)S(1)} %gather_fusion.14), channel_id=1, source_target_pairs={{16,0},{17,1},{18,2},{19,3},{20,4},{21,5},{22,6},{23,7},{24,8},{25... | collective-permute-start | bytes 294920 | tf_op jit(solution)/shard_map/ppermute | solution.py:67
  91.4 6.9 %collective-permute-start.18 = (bf16[6,64,128]{2,1,0:T(8,128)(2,1)S(1)}, bf16[6,64,128]{2,1,0:T(8,128)(2,1)S(1)}, u32[]{:S(2)}, u32[]{:S(2)}) collective-permute-start(bf16[6,64,128]{2,1,0:T(8,128)(2,1)S(1)} %gather_fusion.15), channel_id=1, source_target_pairs={{31,0},{0,1},{1,2},{2,3},{3,4},{4,5},{5,6},{6,7},{7,8},{8,9},{9,10... | collective-permute-start | bytes 294920 | tf_op jit(solution)/shard_map/ppermute | solution.py:67
  92.8 8.3 %collective-permute-start.19 = (bf16[6,64,128]{2,1,0:T(8,128)(2,1)S(1)}, bf16[6,64,128]{2,1,0:T(8,128)(2,1)S(1)}, u32[]{:S(2)}, u32[]{:S(2)}) collective-permute-start(bf16[6,64,128]{2,1,0:T(8,128)(2,1)S(1)} %gather_fusion.16), channel_id=1, source_target_pairs={{30,0},{31,1},{0,2},{1,3},{2,4},{3,5},{4,6},{5,7},{6,8},{7,9},{8,1... | collective-permute-start | bytes 294920 | tf_op jit(solution)/shard_map/ppermute | solution.py:67
  103.3 5.4 %copy-start.3 = (f32[24,32,128]{2,1,0:T(8,128)S(1)}, f32[24,32,128]{2,1,0:T(8,128)}, u32[]{:S(2)}) copy-start(f32[24,32,128]{2,1,0:T(8,128)} %copy-done.1) | copy-start | bytes 1179652
  112.2 9.1 %collective-permute-start.20 = (f32[4,2,4,24,128]{4,3,2,1,0:T(8,128)S(1)}, f32[4,2,4,24,128]{4,3,2,1,0:T(8,128)S(1)}, u32[]{:S(2)}, u32[]{:S(2)}) collective-permute-start(f32[4,2,4,24,128]{4,3,2,1,0:T(8,128)S(1)} %bitcast.143), channel_id=1, source_target_pairs={{0,32},{32,0},{64,96},{96,64},{128,160},{160,128},{192,224},{224,1... | collective-permute-start | bytes 1179656 | tf_op jit(solution)/shard_map/ppermute | solution.py:111
  121.5 5.4 %collective-permute-start.21 = (f32[2,4,24,128]{3,2,1,0:T(8,128)S(1)}, f32[2,4,24,128]{3,2,1,0:T(8,128)S(1)}, u32[]{:S(2)}, u32[]{:S(2)}) collective-permute-start(f32[2,4,24,128]{3,2,1,0:T(8,128)S(1)} %get-tuple-element.45), channel_id=1, source_target_pairs={{0,64},{32,96},{64,128},{96,160},{128,192},{160,224},{192,0},{224,... | collective-permute-start | bytes 294920 | tf_op jit(solution)/shard_map/ppermute | solution.py:116
  122.9 7.3 %collective-permute-start.22 = (f32[2,4,24,128]{3,2,1,0:T(8,128)S(1)}, f32[2,4,24,128]{3,2,1,0:T(8,128)S(1)}, u32[]{:S(2)}, u32[]{:S(2)}) collective-permute-start(f32[2,4,24,128]{3,2,1,0:T(8,128)S(1)} %get-tuple-element.47), channel_id=1, source_target_pairs={{0,128},{32,160},{64,192},{96,224},{128,0},{160,32},{192,64},{224,... | collective-permute-start | bytes 294920 | tf_op jit(solution)/shard_map/ppermute | solution.py:116
  125.5 4.6 %collective-permute-start.23 = (f32[2,4,24,128]{3,2,1,0:T(8,128)S(1)}, f32[2,4,24,128]{3,2,1,0:T(8,128)S(1)}, u32[]{:S(2)}, u32[]{:S(2)}) collective-permute-start(f32[2,4,24,128]{3,2,1,0:T(8,128)S(1)} %get-tuple-element.46), channel_id=1, source_target_pairs={{0,192},{32,224},{64,0},{96,32},{128,64},{160,96},{192,128},{224,1... | collective-permute-start | bytes 294920 | tf_op jit(solution)/shard_map/ppermute | solution.py:116
  (1 other events, 1.1 us)

commit v12 on v7

--- a/solution.py
+++ b/solution.py
@@ -105,15 +105,14 @@
     core = node_index % 2
     group = node_index // 2
     paired = weighted.reshape((groups, 2) + weighted.shape[1:])
-    keep = lax.dynamic_index_in_dim(paired, core, 1, keepdims=False)
-    other = lax.dynamic_index_in_dim(paired, 1 - core, 1, keepdims=False)
-    partial = keep + lax.ppermute(other, "node", [(j, j ^ 1) for j in range(node_count)])
-    total = lax.dynamic_index_in_dim(partial, group, 0, keepdims=False)
+    partial = lax.dynamic_index_in_dim(paired, group, 0, keepdims=False)
     for offset in range(1, groups):
-        chunk = lax.dynamic_index_in_dim(partial, (group + offset) % groups, 0, keepdims=False)
+        chunk = lax.dynamic_index_in_dim(paired, (group + offset) % groups, 0, keepdims=False)
         perm = [(j, ((j // 2 + offset) % groups) * 2 + j % 2) for j in range(node_count)]
-        total = total + lax.ppermute(chunk, "node", perm)
-    return total
+        partial = partial + lax.ppermute(chunk, "node", perm)
+    keep = lax.dynamic_index_in_dim(partial, core, 0, keepdims=False)
+    other = lax.dynamic_index_in_dim(partial, 1 - core, 0, keepdims=False)
+    return keep + lax.ppermute(other, "node", [(j, j ^ 1) for j in range(node_count)])
 
 
 def solution(mesh):

time: 116 us -> 117 us (level)
  starting transfers between devices: 52 us -> 53.6 us
    ppermute x1, starting transfers between devices: 8.19 us -> 9.63 us  [per_device(): lax.ppermute(other, 'node', [(j, j ^ 1) for j in range(node_count)])]
    unnamed x43 -> x45, local copies, waits for them, and re-layouts: 10.5 us -> 10.6 us
where the time goes in v12:
time: 117 us; the launch traced here: 116 us
  starting transfers between devices  53.6 us (46%)
  local copies, waits for them, and re-layouts  27.6 us (24%)
  waiting for transfers between devices  15.3 us (13%)
  matrix products  12.2 us (10%)
  other arithmetic  6.49 us (6%)
    ppermute x15, starting transfers between devices, fetch_halo(): lax.ppermute(vector[asked_for[which]], 'rows', from_partner(offset))  26.4 us
    ppermute x5, starting transfers between devices, per_device(): lax.ppermute(wanted[which], 'rows', to_partner(offset))  13.5 us
    unnamed x45, local copies, waits for them, and re-layouts  10.6 us
    ppermute x1, starting transfers between devices, per_device(): lax.ppermute(other, 'node', [(j, j ^ 1) for j in range(node_count)])  9.63 us
    gather x15, local copies, waits for them, and re-layouts, fetch_halo(): vector[asked_for[which]]  8.7 us
    ppermute x15, waiting for transfers between devices, fetch_halo(): lax.ppermute(vector[asked_for[which]], 'rows', from_partner(offset))  7.42 us
    ppermute x3, waiting for transfers between devices, per_device(): partial = partial + lax.ppermute(chunk, 'node', perm)  6.97 us
    dot_general x3, matrix products, apply_pair(): jnp.einsum('nscb,nsbd->ncd', picked, first, preferred_element_type=jnp.fl...  6.95 us
  transfers between devices with their start and end apart: 24, of which 7 were waited for; matrix products, arithmetic and copies ran while one was open for 10% of the time, Pallas kernels for 0%

profile of v12, /device:TPU:3, one launch (start us, length us, event | category | flops | bytes accessed | tf_op | source)
XLA Modules:
  0.0 116.1 jit_solution(14138584633065127487)
XLA Ops:
  0.0 0.9 copy.145
  4.2 1.3 %collective-permute-start = (s32[6]{0:T(128)S(1)}, s32[6]{0:T(128)S(1)}, u32[]{:S(2)}, u32[]{:S(2)}) collective-permute-start(s32[6]{0:T(128)S(1)} %get-tuple-element.19), channel_id=1, source_target_pairs={{0,1},{1,2},{2,3},{3,4},{4,5},{5,6},{6,7},{7,8},{8,9},{9,10},{10,1... | collective-permute-start | bytes 80 | tf_op jit(solution)/shard_map/ppermute | solution.py:61
  5.4 6.9 %collective-permute-start.4 = (s32[6]{0:T(128)S(1)}, s32[6]{0:T(128)S(1)}, u32[]{:S(2)}, u32[]{:S(2)}) collective-permute-start(s32[6]{0:T(128)S(1)} %get-tuple-element.17), channel_id=1, source_target_pairs={{0,16},{1,17},{2,18},{3,19},{4,20},{5,21},{6,22},{7,23},{8,24},{9,... | collective-permute-start | bytes 80 | tf_op jit(solution)/shard_map/ppermute | solution.py:61
  12.4 1.3 %collective-permute-start.2 = (s32[6]{0:T(128)S(1)}, s32[6]{0:T(128)S(1)}, u32[]{:S(2)}, u32[]{:S(2)}) collective-permute-start(s32[6]{0:T(128)S(1)} %get-tuple-element.16), channel_id=1, source_target_pairs={{0,2},{1,3},{2,4},{3,5},{4,6},{5,7},{6,8},{7,9},{8,10},{9,11},{10,... | collective-permute-start | bytes 80 | tf_op jit(solution)/shard_map/ppermute | solution.py:61
  13.6 3.8 %collective-permute-start.8 = (s32[6]{0:T(128)S(1)}, s32[6]{0:T(128)S(1)}, u32[]{:S(2)}, u32[]{:S(2)}) collective-permute-start(s32[6]{0:T(128)S(1)} %get-tuple-element.15), channel_id=1, source_target_pairs={{0,30},{1,31},{2,0},{3,1},{4,2},{5,3},{6,4},{7,5},{8,6},{9,7},{10,... | collective-permute-start | bytes 80 | tf_op jit(solution)/shard_map/ppermute | solution.py:61
  17.7 1.0 constant_dynamic-update-slice_fusion.5
  19.4 1.5 %collective-permute-start.1 = (bf16[6,32,128]{2,1,0:T(8,128)(2,1)S(1)}, bf16[6,32,128]{2,1,0:T(8,128)(2,1)S(1)}, u32[]{:S(2)}, u32[]{:S(2)}) collective-permute-start(bf16[6,32,128]{2,1,0:T(8,128)(2,1)S(1)} %gather_fusion), channel_id=1, source_target_pairs={{1,0},{2,1},{3,2},{4,3},{5,4},{6,5},{7,6},{8,7},{9,8},{10,9},{11,1... | collective-permute-start | bytes 147464 | tf_op jit(solution)/shard_map/ppermute | solution.py:67
  22.2 3.5 %collective-permute-start.5 = (bf16[6,32,128]{2,1,0:T(8,128)(2,1)S(1)}, bf16[6,32,128]{2,1,0:T(8,128)(2,1)S(1)}, u32[]{:S(2)}, u32[]{:S(2)}) collective-permute-start(bf16[6,32,128]{2,1,0:T(8,128)(2,1)S(1)} %gather_fusion.2), channel_id=1, source_target_pairs={{16,0},{17,1},{18,2},{19,3},{20,4},{21,5},{22,6},{23,7},{24,8},{25... | collective-permute-start | bytes 147464 | tf_op jit(solution)/shard_map/ppermute | solution.py:67
  27.6 1.6 %collective-permute-start.9 = (bf16[6,32,128]{2,1,0:T(8,128)(2,1)S(1)}, bf16[6,32,128]{2,1,0:T(8,128)(2,1)S(1)}, u32[]{:S(2)}, u32[]{:S(2)}) collective-permute-start(bf16[6,32,128]{2,1,0:T(8,128)(2,1)S(1)} %gather_fusion.4), channel_id=1, source_target_pairs={{30,0},{31,1},{0,2},{1,3},{2,4},{3,5},{4,6},{5,7},{6,8},{7,9},{8,1... | collective-permute-start | bytes 147464 | tf_op jit(solution)/shard_map/ppermute | solution.py:67
  29.4 4.9 %collective-permute-done.9 = bf16[6,32,128]{2,1,0:T(8,128)(2,1)S(1)} collective-permute-done((bf16[6,32,128]{2,1,0:T(8,128)(2,1)S(1)}, bf16[6,32,128]{2,1,0:T(8,128)(2,1)S(1)}, u32[]{:S(2)}, u32[]{:S(2)}) %collective-permute-start.9) | collective-permute-done | bytes 49184 | tf_op jit(solution)/shard_map/ppermute | solution.py:67
  35.0 2.8 %convolution_bitcast_fusion.4 = f32[24,32,128]{2,1,0:T(8,128)S(1)} fusion(bf16[24,5,32,128]{3,2,1,0:T(8,128)(2,1)S(1)} %bitcast.148, bf16[24,5,128,128]{3,2,1,0:T(8,128)(2,1)} %param.6), kind=kOutput, calls=%fused_computation.22 | convolution fusion | flops 125829120 | bytes 5308416 | tf_op jit(solution)/shard_map/nscb,nsbd->ncd/dot_general | solution.py:25
  40.6 1.1 collective-permute-start.10
  44.2 1.3 %collective-permute-start.11 = (bf16[6,64,128]{2,1,0:T(8,128)(2,1)S(1)}, bf16[6,64,128]{2,1,0:T(8,128)(2,1)S(1)}, u32[]{:S(2)}, u32[]{:S(2)}) collective-permute-start(bf16[6,64,128]{2,1,0:T(8,128)(2,1)S(1)} %gather_fusion.7), channel_id=1, source_target_pairs={{2,0},{3,1},{4,2},{5,3},{6,4},{7,5},{8,6},{9,7},{10,8},{11,9},{12,... | collective-permute-start | bytes 294920 | tf_op jit(solution)/shard_map/ppermute | solution.py:67
  45.5 1.5 %collective-permute-start.12 = (bf16[6,64,128]{2,1,0:T(8,128)(2,1)S(1)}, bf16[6,64,128]{2,1,0:T(8,128)(2,1)S(1)}, u32[]{:S(2)}, u32[]{:S(2)}) collective-permute-start(bf16[6,64,128]{2,1,0:T(8,128)(2,1)S(1)} %gather_fusion.8), channel_id=1, source_target_pairs={{16,0},{17,1},{18,2},{19,3},{20,4},{21,5},{22,6},{23,7},{24,8},{25... | collective-permute-start | bytes 294920 | tf_op jit(solution)/shard_map/ppermute | solution.py:67
  46.9 2.1 %collective-permute-start.13 = (bf16[6,64,128]{2,1,0:T(8,128)(2,1)S(1)}, bf16[6,64,128]{2,1,0:T(8,128)(2,1)S(1)}, u32[]{:S(2)}, u32[]{:S(2)}) collective-permute-start(bf16[6,64,128]{2,1,0:T(8,128)(2,1)S(1)} %gather_fusion.9), channel_id=1, source_target_pairs={{31,0},{0,1},{1,2},{2,3},{3,4},{4,5},{5,6},{6,7},{7,8},{8,9},{9,10... | collective-permute-start | bytes 294920 | tf_op jit(solution)/shard_map/ppermute | solution.py:67
  49.0 3.3 %collective-permute-start.14 = (bf16[6,64,128]{2,1,0:T(8,128)(2,1)S(1)}, bf16[6,64,128]{2,1,0:T(8,128)(2,1)S(1)}, u32[]{:S(2)}, u32[]{:S(2)}) collective-permute-start(bf16[6,64,128]{2,1,0:T(8,128)(2,1)S(1)} %gather_fusion.10), channel_id=1, source_target_pairs={{30,0},{31,1},{0,2},{1,3},{2,4},{3,5},{4,6},{5,7},{6,8},{7,9},{8,1... | collective-permute-start | bytes 294920 | tf_op jit(solution)/shard_map/ppermute | solution.py:67
  54.9 2.4 %collective-permute-done.14 = bf16[6,64,128]{2,1,0:T(8,128)(2,1)S(1)} collective-permute-done((bf16[6,64,128]{2,1,0:T(8,128)(2,1)S(1)}, bf16[6,64,128]{2,1,0:T(8,128)(2,1)S(1)}, u32[]{:S(2)}, u32[]{:S(2)}) %collective-permute-start.14) | collective-permute-done | bytes 98336 | tf_op jit(solution)/shard_map/ppermute | solution.py:67
  57.9 2.1 %gather_fusion.11 = bf16[120,64,128]{2,1,0:T(8,128)(2,1)S(1)} fusion(bf16[54,64,128]{2,1,0:T(8,128)(2,1)} %constant_dynamic-update-slice_fusion.6, s32[1024]{0:T(1024)S(1)} %pad_clamp_fusion), kind=kCustom, calls=%fused_computation.11 | custom fusion | bytes 3932640 | tf_op jit(solution)/shard_map/gather | solution.py:24
  60.0 3.2 %convolution_bitcast_fusion.3 = f32[24,64,128]{2,1,0:T(8,128)S(1)} fusion(bf16[24,5,64,128]{3,2,1,0:T(8,128)(2,1)S(1)} %bitcast.143, bf16[24,5,128,128]{3,2,1,0:T(8,128)(2,1)} %param.6), kind=kOutput, calls=%fused_computation.21 | convolution fusion | flops 251658240 | bytes 6684672 | tf_op jit(solution)/shard_map/nscb,nsbd->ncd/dot_general | solution.py:25
  65.1 1.0 copy-done.4
  66.0 1.0 fusion.6
  70.9 3.3 %collective-permute-start.17 = (bf16[6,64,128]{2,1,0:T(8,128)(2,1)S(1)}, bf16[6,64,128]{2,1,0:T(8,128)(2,1)S(1)}, u32[]{:S(2)}, u32[]{:S(2)}) collective-permute-start(bf16[6,64,128]{2,1,0:T(8,128)(2,1)S(1)} %gather_fusion.14), channel_id=1, source_target_pairs={{16,0},{17,1},{18,2},{19,3},{20,4},{21,5},{22,6},{23,7},{24,8},{25... | collective-permute-start | bytes 294920 | tf_op jit(solution)/shard_map/ppermute | solution.py:67
  74.3 1.5 %collective-permute-start.18 = (bf16[6,64,128]{2,1,0:T(8,128)(2,1)S(1)}, bf16[6,64,128]{2,1,0:T(8,128)(2,1)S(1)}, u32[]{:S(2)}, u32[]{:S(2)}) collective-permute-start(bf16[6,64,128]{2,1,0:T(8,128)(2,1)S(1)} %gather_fusion.15), channel_id=1, source_target_pairs={{31,0},{0,1},{1,2},{2,3},{3,4},{4,5},{5,6},{6,7},{7,8},{8,9},{9,10... | collective-permute-start | bytes 294920 | tf_op jit(solution)/shard_map/ppermute | solution.py:67
  75.8 4.2 %collective-permute-start.19 = (bf16[6,64,128]{2,1,0:T(8,128)(2,1)S(1)}, bf16[6,64,128]{2,1,0:T(8,128)(2,1)S(1)}, u32[]{:S(2)}, u32[]{:S(2)}) collective-permute-start(bf16[6,64,128]{2,1,0:T(8,128)(2,1)S(1)} %gather_fusion.16), channel_id=1, source_target_pairs={{30,0},{31,1},{0,2},{1,3},{2,4},{3,5},{4,6},{5,7},{6,8},{7,9},{8,1... | collective-permute-start | bytes 294920 | tf_op jit(solution)/shard_map/ppermute | solution.py:67
  84.0 2.1 %gather_fusion.17 = bf16[120,64,128]{2,1,0:T(8,128)(2,1)S(1)} fusion(bf16[54,64,128]{2,1,0:T(8,128)(2,1)} %constant_dynamic-update-slice_fusion.12, s32[1024]{0:T(1024)S(1)} %pad_clamp_fusion), kind=kCustom, calls=%fused_computation.17 | custom fusion | bytes 3932640 | tf_op jit(solution)/shard_map/gather | solution.py:24
  86.1 3.2 %convolution_bitcast_fusion = f32[24,64,128]{2,1,0:T(8,128)S(1)} fusion(bf16[24,5,64,128]{3,2,1,0:T(8,128)(2,1)S(1)} %bitcast.141, bf16[24,5,128,128]{3,2,1,0:T(8,128)(2,1)} %param.7), kind=kOutput, calls=%fused_computation.18 | convolution fusion | flops 251658240 | bytes 6684672 | tf_op jit(solution)/shard_map/nscb,nsbd->ncd/dot_general | solution.py:28
  93.7 2.8 %collective-permute-start.22 = (f32[2,2,4,24,128]{4,3,2,1,0:T(8,128)S(1)}, f32[2,2,4,24,128]{4,3,2,1,0:T(8,128)S(1)}, u32[]{:S(2)}, u32[]{:S(2)}) collective-permute-start(f32[2,2,4,24,128]{4,3,2,1,0:T(8,128)S(1)} %bitcast.157), channel_id=1, source_target_pairs={{0,192},{32,224},{64,0},{96,32},{128,64},{160,96},{192,128},{224,1... | collective-permute-start | bytes 589832 | tf_op jit(solution)/shard_map/ppermute | solution.py:112
  97.8 3.4 %collective-permute-done.22 = f32[2,2,4,24,128]{4,3,2,1,0:T(8,128)S(1)} collective-permute-done((f32[2,2,4,24,128]{4,3,2,1,0:T(8,128)S(1)}, f32[2,2,4,24,128]{4,3,2,1,0:T(8,128)S(1)}, u32[]{:S(2)}, u32[]{:S(2)}) %collective-permute-start.22) | collective-permute-done | bytes 196640 | tf_op jit(solution)/shard_map/ppermute | solution.py:112
  101.2 1.5 %collective-permute-done.21 = f32[2,2,4,24,128]{4,3,2,1,0:T(8,128)S(1)} collective-permute-done((f32[2,2,4,24,128]{4,3,2,1,0:T(8,128)S(1)}, f32[2,2,4,24,128]{4,3,2,1,0:T(8,128)S(1)}, u32[]{:S(2)}, u32[]{:S(2)}) %collective-permute-start.21) | collective-permute-done | bytes 196640 | tf_op jit(solution)/shard_map/ppermute | solution.py:112
  102.8 2.0 %collective-permute-done.20 = f32[2,2,4,24,128]{4,3,2,1,0:T(8,128)S(1)} collective-permute-done((f32[2,2,4,24,128]{4,3,2,1,0:T(8,128)S(1)}, f32[2,2,4,24,128]{4,3,2,1,0:T(8,128)S(1)}, u32[]{:S(2)}, u32[]{:S(2)}) %collective-permute-start.20) | collective-permute-done | bytes 196640 | tf_op jit(solution)/shard_map/ppermute | solution.py:112
  104.9 9.6 %collective-permute-start.23 = (f32[2,4,24,128]{3,2,1,0:T(8,128)S(1)}, f32[2,4,24,128]{3,2,1,0:T(8,128)S(1)}, u32[]{:S(2)}, u32[]{:S(2)}) collective-permute-start(f32[2,4,24,128]{3,2,1,0:T(8,128)S(1)} %dynamic-slice_bitcast_fusion), channel_id=1, source_target_pairs={{0,32},{32,0},{64,96},{96,64},{128,160},{160,128},{192,224},{224,1... | collective-permute-start | bytes 294920 | tf_op jit(solution)/shard_map/ppermute | solution.py:115
  114.5 0.9 collective-permute-done.23
  (147 shorter events, 32.1 us)
Async XLA Ops:
  0.0 37.9 %copy-start = (bf16[1,2,24,128,128]{4,3,2,1,0:T(8,128)(2,1)S(1)}, bf16[1,2,24,128,128]{4,3,2,1,0:T(8,128)(2,1)}, u32[]{:S(2)}) copy-start(bf16[1,2,24,128,128]{4,3,2,1,0:T(8,128)(2,1)} %param.8) | copy-start | bytes 4718596
  0.0 18.6 %copy-start.10 = (bf16[32,24,128]{2,1,0:T(8,128)(2,1)S(1)}, bf16[32,24,128]{2,1,0:T(8,128)(2,1)}, u32[]{:S(2)}) copy-start(bf16[32,24,128]{2,1,0:T(8,128)(2,1)} %param.5) | copy-start | bytes 589828
  4.2 14.6 %collective-permute-start = (s32[6]{0:T(128)S(1)}, s32[6]{0:T(128)S(1)}, u32[]{:S(2)}, u32[]{:S(2)}) collective-permute-start(s32[6]{0:T(128)S(1)} %get-tuple-element.19), channel_id=1, source_target_pairs={{0,1},{1,2},{2,3},{3,4},{4,5},{5,6},{6,7},{7,8},{8,9},{9,10},{10,1... | collective-permute-start | bytes 80 | tf_op jit(solution)/shard_map/ppermute | solution.py:61
  5.4 15.5 %collective-permute-start.4 = (s32[6]{0:T(128)S(1)}, s32[6]{0:T(128)S(1)}, u32[]{:S(2)}, u32[]{:S(2)}) collective-permute-start(s32[6]{0:T(128)S(1)} %get-tuple-element.17), channel_id=1, source_target_pairs={{0,16},{1,17},{2,18},{3,19},{4,20},{5,21},{6,22},{7,23},{8,24},{9,... | collective-permute-start | bytes 80 | tf_op jit(solution)/shard_map/ppermute | solution.py:61
  12.4 8.6 %collective-permute-start.2 = (s32[6]{0:T(128)S(1)}, s32[6]{0:T(128)S(1)}, u32[]{:S(2)}, u32[]{:S(2)}) collective-permute-start(s32[6]{0:T(128)S(1)} %get-tuple-element.16), channel_id=1, source_target_pairs={{0,2},{1,3},{2,4},{3,5},{4,6},{5,7},{6,8},{7,9},{8,10},{9,11},{10,... | collective-permute-start | bytes 80 | tf_op jit(solution)/shard_map/ppermute | solution.py:61
  13.6 12.1 %collective-permute-start.8 = (s32[6]{0:T(128)S(1)}, s32[6]{0:T(128)S(1)}, u32[]{:S(2)}, u32[]{:S(2)}) collective-permute-start(s32[6]{0:T(128)S(1)} %get-tuple-element.15), channel_id=1, source_target_pairs={{0,30},{1,31},{2,0},{3,1},{4,2},{5,3},{6,4},{7,5},{8,6},{9,7},{10,... | collective-permute-start | bytes 80 | tf_op jit(solution)/shard_map/ppermute | solution.py:61
  17.4 8.3 %collective-permute-start.6 = (s32[6]{0:T(128)S(1)}, s32[6]{0:T(128)S(1)}, u32[]{:S(2)}, u32[]{:S(2)}) collective-permute-start(s32[6]{0:T(128)S(1)} %get-tuple-element.18), channel_id=1, source_target_pairs={{0,31},{1,0},{2,1},{3,2},{4,3},{5,4},{6,5},{7,6},{8,7},{9,8},{10,9... | collective-permute-start | bytes 80 | tf_op jit(solution)/shard_map/ppermute | solution.py:61
  19.4 9.8 %collective-permute-start.1 = (bf16[6,32,128]{2,1,0:T(8,128)(2,1)S(1)}, bf16[6,32,128]{2,1,0:T(8,128)(2,1)S(1)}, u32[]{:S(2)}, u32[]{:S(2)}) collective-permute-start(bf16[6,32,128]{2,1,0:T(8,128)(2,1)S(1)} %gather_fusion), channel_id=1, source_target_pairs={{1,0},{2,1},{3,2},{4,3},{5,4},{6,5},{7,6},{8,7},{9,8},{10,9},{11,1... | collective-permute-start | bytes 147464 | tf_op jit(solution)/shard_map/ppermute | solution.py:67
  21.5 7.7 %collective-permute-start.3 = (bf16[6,32,128]{2,1,0:T(8,128)(2,1)S(1)}, bf16[6,32,128]{2,1,0:T(8,128)(2,1)S(1)}, u32[]{:S(2)}, u32[]{:S(2)}) collective-permute-start(bf16[6,32,128]{2,1,0:T(8,128)(2,1)S(1)} %gather_fusion.1), channel_id=1, source_target_pairs={{2,0},{3,1},{4,2},{5,3},{6,4},{7,5},{8,6},{9,7},{10,8},{11,9},{12,... | collective-permute-start | bytes 147464 | tf_op jit(solution)/shard_map/ppermute | solution.py:67
  22.2 7.0 %collective-permute-start.5 = (bf16[6,32,128]{2,1,0:T(8,128)(2,1)S(1)}, bf16[6,32,128]{2,1,0:T(8,128)(2,1)S(1)}, u32[]{:S(2)}, u32[]{:S(2)}) collective-permute-start(bf16[6,32,128]{2,1,0:T(8,128)(2,1)S(1)} %gather_fusion.2), channel_id=1, source_target_pairs={{16,0},{17,1},{18,2},{19,3},{20,4},{21,5},{22,6},{23,7},{24,8},{25... | collective-permute-start | bytes 147464 | tf_op jit(solution)/shard_map/ppermute | solution.py:67
  25.8 17.3 %copy-start.11 = (s32[1024]{0:T(1024)}, s32[1024]{0:T(1024)S(1)}, u32[]{:S(2)}) copy-start(s32[1024]{0:T(1024)S(1)} %pad_clamp_fusion.2) | copy-start | bytes 12292
  26.3 3.0 %collective-permute-start.7 = (bf16[6,32,128]{2,1,0:T(8,128)(2,1)S(1)}, bf16[6,32,128]{2,1,0:T(8,128)(2,1)S(1)}, u32[]{:S(2)}, u32[]{:S(2)}) collective-permute-start(bf16[6,32,128]{2,1,0:T(8,128)(2,1)S(1)} %gather_fusion.3), channel_id=1, source_target_pairs={{31,0},{0,1},{1,2},{2,3},{3,4},{4,5},{5,6},{6,7},{7,8},{8,9},{9,10... | collective-permute-start | bytes 147464 | tf_op jit(solution)/shard_map/ppermute | solution.py:67
  27.1 16.6 %copy-start.12 = (s32[1024]{0:T(1024)}, s32[1024]{0:T(1024)S(1)}, u32[]{:S(2)}) copy-start(s32[1024]{0:T(1024)S(1)} %pad_clamp_fusion.1) | copy-start | bytes 12292
  27.6 6.6 %collective-permute-start.9 = (bf16[6,32,128]{2,1,0:T(8,128)(2,1)S(1)}, bf16[6,32,128]{2,1,0:T(8,128)(2,1)S(1)}, u32[]{:S(2)}, u32[]{:S(2)}) collective-permute-start(bf16[6,32,128]{2,1,0:T(8,128)(2,1)S(1)} %gather_fusion.4), channel_id=1, source_target_pairs={{30,0},{31,1},{0,2},{1,3},{2,4},{3,5},{4,6},{5,7},{6,8},{7,9},{8,1... | collective-permute-start | bytes 147464 | tf_op jit(solution)/shard_map/ppermute | solution.py:67
  37.9 2.1 %copy-start.6 = (f32[24,32,128]{2,1,0:T(8,128)}, f32[24,32,128]{2,1,0:T(8,128)S(1)}, u32[]{:S(2)}) copy-start(f32[24,32,128]{2,1,0:T(8,128)S(1)} %convolution_bitcast_fusion.4) | copy-start | bytes 1179652
  40.6 11.7 %collective-permute-start.10 = (bf16[6,64,128]{2,1,0:T(8,128)(2,1)S(1)}, bf16[6,64,128]{2,1,0:T(8,128)(2,1)S(1)}, u32[]{:S(2)}, u32[]{:S(2)}) collective-permute-start(bf16[6,64,128]{2,1,0:T(8,128)(2,1)S(1)} %gather_fusion.6), channel_id=1, source_target_pairs={{1,0},{2,1},{3,2},{4,3},{5,4},{6,5},{7,6},{8,7},{9,8},{10,9},{11,1... | collective-permute-start | bytes 294920 | tf_op jit(solution)/shard_map/ppermute | solution.py:67
  44.2 8.7 %collective-permute-start.11 = (bf16[6,64,128]{2,1,0:T(8,128)(2,1)S(1)}, bf16[6,64,128]{2,1,0:T(8,128)(2,1)S(1)}, u32[]{:S(2)}, u32[]{:S(2)}) collective-permute-start(bf16[6,64,128]{2,1,0:T(8,128)(2,1)S(1)} %gather_fusion.7), channel_id=1, source_target_pairs={{2,0},{3,1},{4,2},{5,3},{6,4},{7,5},{8,6},{9,7},{10,8},{11,9},{12,... | collective-permute-start | bytes 294920 | tf_op jit(solution)/shard_map/ppermute | solution.py:67
  45.5 8.1 %collective-permute-start.12 = (bf16[6,64,128]{2,1,0:T(8,128)(2,1)S(1)}, bf16[6,64,128]{2,1,0:T(8,128)(2,1)S(1)}, u32[]{:S(2)}, u32[]{:S(2)}) collective-permute-start(bf16[6,64,128]{2,1,0:T(8,128)(2,1)S(1)} %gather_fusion.8), channel_id=1, source_target_pairs={{16,0},{17,1},{18,2},{19,3},{20,4},{21,5},{22,6},{23,7},{24,8},{25... | collective-permute-start | bytes 294920 | tf_op jit(solution)/shard_map/ppermute | solution.py:67
  46.9 7.3 %collective-permute-start.13 = (bf16[6,64,128]{2,1,0:T(8,128)(2,1)S(1)}, bf16[6,64,128]{2,1,0:T(8,128)(2,1)S(1)}, u32[]{:S(2)}, u32[]{:S(2)}) collective-permute-start(bf16[6,64,128]{2,1,0:T(8,128)(2,1)S(1)} %gather_fusion.9), channel_id=1, source_target_pairs={{31,0},{0,1},{1,2},{2,3},{3,4},{4,5},{5,6},{6,7},{7,8},{8,9},{9,10... | collective-permute-start | bytes 294920 | tf_op jit(solution)/shard_map/ppermute | solution.py:67
  49.0 8.3 %collective-permute-start.14 = (bf16[6,64,128]{2,1,0:T(8,128)(2,1)S(1)}, bf16[6,64,128]{2,1,0:T(8,128)(2,1)S(1)}, u32[]{:S(2)}, u32[]{:S(2)}) collective-permute-start(bf16[6,64,128]{2,1,0:T(8,128)(2,1)S(1)} %gather_fusion.10), channel_id=1, source_target_pairs={{30,0},{31,1},{0,2},{1,3},{2,4},{3,5},{4,6},{5,7},{6,8},{7,9},{8,1... | collective-permute-start | bytes 294920 | tf_op jit(solution)/shard_map/ppermute | solution.py:67
  60.0 3.3 %copy-start.2 = (bf16[24,5,128,128]{3,2,1,0:T(8,128)(2,1)S(1)}, bf16[24,5,128,128]{3,2,1,0:T(8,128)(2,1)}, u32[]{:S(2)}) copy-start(bf16[24,5,128,128]{3,2,1,0:T(8,128)(2,1)} %param.7) | copy-start | bytes 11796484
  70.2 10.6 %collective-permute-start.15 = (bf16[6,64,128]{2,1,0:T(8,128)(2,1)S(1)}, bf16[6,64,128]{2,1,0:T(8,128)(2,1)S(1)}, u32[]{:S(2)}, u32[]{:S(2)}) collective-permute-start(bf16[6,64,128]{2,1,0:T(8,128)(2,1)S(1)} %gather_fusion.12), channel_id=1, source_target_pairs={{1,0},{2,1},{3,2},{4,3},{5,4},{6,5},{7,6},{8,7},{9,8},{10,9},{11,1... | collective-permute-start | bytes 294920 | tf_op jit(solution)/shard_map/ppermute | solution.py:67
  70.6 10.8 %collective-permute-start.16 = (bf16[6,64,128]{2,1,0:T(8,128)(2,1)S(1)}, bf16[6,64,128]{2,1,0:T(8,128)(2,1)S(1)}, u32[]{:S(2)}, u32[]{:S(2)}) collective-permute-start(bf16[6,64,128]{2,1,0:T(8,128)(2,1)S(1)} %gather_fusion.13), channel_id=1, source_target_pairs={{2,0},{3,1},{4,2},{5,3},{6,4},{7,5},{8,6},{9,7},{10,8},{11,9},{12,... | collective-permute-start | bytes 294920 | tf_op jit(solution)/shard_map/ppermute | solution.py:67
  70.9 11.1 %collective-permute-start.17 = (bf16[6,64,128]{2,1,0:T(8,128)(2,1)S(1)}, bf16[6,64,128]{2,1,0:T(8,128)(2,1)S(1)}, u32[]{:S(2)}, u32[]{:S(2)}) collective-permute-start(bf16[6,64,128]{2,1,0:T(8,128)(2,1)S(1)} %gather_fusion.14), channel_id=1, source_target_pairs={{16,0},{17,1},{18,2},{19,3},{20,4},{21,5},{22,6},{23,7},{24,8},{25... | collective-permute-start | bytes 294920 | tf_op jit(solution)/shard_map/ppermute | solution.py:67
  74.3 8.5 %collective-permute-start.18 = (bf16[6,64,128]{2,1,0:T(8,128)(2,1)S(1)}, bf16[6,64,128]{2,1,0:T(8,128)(2,1)S(1)}, u32[]{:S(2)}, u32[]{:S(2)}) collective-permute-start(bf16[6,64,128]{2,1,0:T(8,128)(2,1)S(1)} %gather_fusion.15), channel_id=1, source_target_pairs={{31,0},{0,1},{1,2},{2,3},{3,4},{4,5},{5,6},{6,7},{7,8},{8,9},{9,10... | collective-permute-start | bytes 294920 | tf_op jit(solution)/shard_map/ppermute | solution.py:67
  75.8 7.6 %collective-permute-start.19 = (bf16[6,64,128]{2,1,0:T(8,128)(2,1)S(1)}, bf16[6,64,128]{2,1,0:T(8,128)(2,1)S(1)}, u32[]{:S(2)}, u32[]{:S(2)}) collective-permute-start(bf16[6,64,128]{2,1,0:T(8,128)(2,1)S(1)} %gather_fusion.16), channel_id=1, source_target_pairs={{30,0},{31,1},{0,2},{1,3},{2,4},{3,5},{4,6},{5,7},{6,8},{7,9},{8,1... | collective-permute-start | bytes 294920 | tf_op jit(solution)/shard_map/ppermute | solution.py:67
  86.1 3.3 %copy-start.1 = (bf16[24,5,128,128]{3,2,1,0:T(8,128)(2,1)S(1)}, bf16[24,5,128,128]{3,2,1,0:T(8,128)(2,1)}, u32[]{:S(2)}) copy-start(bf16[24,5,128,128]{3,2,1,0:T(8,128)(2,1)} %param.6) | copy-start | bytes 11796484
  91.2 1.4 %copy-start.9 = (f32[24,64,128]{2,1,0:T(8,128)S(1)}, f32[24,64,128]{2,1,0:T(8,128)}, u32[]{:S(2)}) copy-start(f32[24,64,128]{2,1,0:T(8,128)} %get-tuple-element.46) | copy-start | bytes 2359300
  93.7 7.5 %collective-permute-start.22 = (f32[2,2,4,24,128]{4,3,2,1,0:T(8,128)S(1)}, f32[2,2,4,24,128]{4,3,2,1,0:T(8,128)S(1)}, u32[]{:S(2)}, u32[]{:S(2)}) collective-permute-start(f32[2,2,4,24,128]{4,3,2,1,0:T(8,128)S(1)} %bitcast.157), channel_id=1, source_target_pairs={{0,192},{32,224},{64,0},{96,32},{128,64},{160,96},{192,128},{224,1... | collective-permute-start | bytes 589832 | tf_op jit(solution)/shard_map/ppermute | solution.py:112
  96.5 6.2 %collective-permute-start.21 = (f32[2,2,4,24,128]{4,3,2,1,0:T(8,128)S(1)}, f32[2,2,4,24,128]{4,3,2,1,0:T(8,128)S(1)}, u32[]{:S(2)}, u32[]{:S(2)}) collective-permute-start(f32[2,2,4,24,128]{4,3,2,1,0:T(8,128)S(1)} %bitcast.158), channel_id=1, source_target_pairs={{0,128},{32,160},{64,192},{96,224},{128,0},{160,32},{192,64},{224,... | collective-permute-start | bytes 589832 | tf_op jit(solution)/shard_map/ppermute | solution.py:112
  97.0 7.7 %collective-permute-start.20 = (f32[2,2,4,24,128]{4,3,2,1,0:T(8,128)S(1)}, f32[2,2,4,24,128]{4,3,2,1,0:T(8,128)S(1)}, u32[]{:S(2)}, u32[]{:S(2)}) collective-permute-start(f32[2,2,4,24,128]{4,3,2,1,0:T(8,128)S(1)} %bitcast.159), channel_id=1, source_target_pairs={{0,64},{32,96},{64,128},{96,160},{128,192},{160,224},{192,0},{224,... | collective-permute-start | bytes 589832 | tf_op jit(solution)/shard_map/ppermute | solution.py:112
  104.9 10.6 %collective-permute-start.23 = (f32[2,4,24,128]{3,2,1,0:T(8,128)S(1)}, f32[2,4,24,128]{3,2,1,0:T(8,128)S(1)}, u32[]{:S(2)}, u32[]{:S(2)}) collective-permute-start(f32[2,4,24,128]{3,2,1,0:T(8,128)S(1)} %dynamic-slice_bitcast_fusion), channel_id=1, source_target_pairs={{0,32},{32,0},{64,96},{96,64},{128,160},{160,128},{192,224},{224,1... | collective-permute-start | bytes 294920 | tf_op jit(solution)/shard_map/ppermute | solution.py:115
  (5 other events, 5.2 us)

commit v13 on v7

--- a/solution.py
+++ b/solution.py
@@ -61,10 +61,14 @@
         lax.ppermute(wanted[which], "rows", to_partner(offset)) for which, offset in enumerate(offsets)
     ]
 
+    asked_all = jnp.concatenate(asked_for)
+
     def fetch_halo(vector):
         pieces = [vector]
+        outgoing = vector[asked_all]
         for which, offset in enumerate(offsets):
-            pieces.append(lax.ppermute(vector[asked_for[which]], "rows", from_partner(offset)))
+            piece = outgoing[which * HMAX : (which + 1) * HMAX]
+            pieces.append(lax.ppermute(piece, "rows", from_partner(offset)))
         return jnp.concatenate(pieces, axis=0)
 
     e_mats = pencil_e

time: 116 us -> 112 us (0.966)
  local copies, waits for them, and re-layouts: 28.1 us -> 21.4 us
  waiting for transfers between devices: 15.9 us -> 20 us
  starting transfers between devices: 52 us -> 50.1 us
    gather x15 -> x3, local copies, waits for them, and re-layouts: 8.7 us -> 1.87 us  [fetch_halo(): outgoing = vector[asked_all]]
    ppermute x15, waiting for transfers between devices: 7.42 us -> 11.1 us  [fetch_halo(): pieces.append(lax.ppermute(piece, 'rows', from_partner(offset)))]
    ppermute x1, starting transfers between devices: 8.19 us -> 6.17 us  [per_device(): lax.ppermute(other, 'node', [(j, j ^ 1) for j in range(node_count)])]
    unnamed x43 -> x39, local copies, waits for them, and re-layouts: 10.5 us -> 10.5 us
  transfers between devices with their start and end apart: 24 -> 24, of which waited for: 7 -> 10; matrix products, arithmetic and copies ran while one was open for 10% -> 6% of each run, Pallas kernels for 0% -> 0%
where the time goes in v13:
time: 112 us; the launch traced here: 111 us
  starting transfers between devices  50.1 us (45%)
  local copies, waits for them, and re-layouts  21.4 us (19%)
  waiting for transfers between devices  20 us (18%)
  matrix products  12.2 us (11%)
  other arithmetic  6.42 us (6%)
    ppermute x15, starting transfers between devices, fetch_halo(): pieces.append(lax.ppermute(piece, 'rows', from_partner(offset)))  26.8 us
    ppermute x5, starting transfers between devices, per_device(): lax.ppermute(wanted[which], 'rows', to_partner(offset))  13.3 us
    ppermute x15, waiting for transfers between devices, fetch_halo(): pieces.append(lax.ppermute(piece, 'rows', from_partner(offset)))  11.1 us
    unnamed x39, local copies, waits for them, and re-layouts  10.5 us
    ppermute x3, waiting for transfers between devices, per_device(): total = total + lax.ppermute(chunk, 'node', perm)  7.15 us
    dot_general x3, matrix products, apply_pair(): jnp.einsum('nscb,nsbd->ncd', picked, first, preferred_element_type=jnp.fl...  6.97 us
    ppermute x1, starting transfers between devices, per_device(): lax.ppermute(other, 'node', [(j, j ^ 1) for j in range(node_count)])  6.17 us
    gather x3, local copies, waits for them, and re-layouts, apply_pair(): picked = extended[slot_index]  4.94 us
  transfers between devices with their start and end apart: 24, of which 10 were waited for; matrix products, arithmetic and copies ran while one was open for 6% of the time, Pallas kernels for 0%

profile of v13, /device:TPU:3, one launch (start us, length us, event | category | flops | bytes accessed | tf_op | source)
XLA Modules:
  0.0 110.7 jit_solution(3583803540449858782)
XLA Ops:
  4.0 1.3 %collective-permute-start = (s32[6]{0:T(128)S(1)}, s32[6]{0:T(128)S(1)}, u32[]{:S(2)}, u32[]{:S(2)}) collective-permute-start(s32[6]{0:T(128)S(1)} %get-tuple-element.19), channel_id=1, source_target_pairs={{0,1},{1,2},{2,3},{3,4},{4,5},{5,6},{6,7},{7,8},{8,9},{9,10},{10,1... | collective-permute-start | bytes 80 | tf_op jit(solution)/shard_map/ppermute | solution.py:61
  5.3 2.2 %collective-permute-start.1 = (s32[6]{0:T(128)S(1)}, s32[6]{0:T(128)S(1)}, u32[]{:S(2)}, u32[]{:S(2)}) collective-permute-start(s32[6]{0:T(128)S(1)} %get-tuple-element.16), channel_id=1, source_target_pairs={{0,2},{1,3},{2,4},{3,5},{4,6},{5,7},{6,8},{7,9},{8,10},{9,11},{10,... | collective-permute-start | bytes 80 | tf_op jit(solution)/shard_map/ppermute | solution.py:61
  7.5 6.0 %collective-permute-start.2 = (s32[6]{0:T(128)S(1)}, s32[6]{0:T(128)S(1)}, u32[]{:S(2)}, u32[]{:S(2)}) collective-permute-start(s32[6]{0:T(128)S(1)} %get-tuple-element.17), channel_id=1, source_target_pairs={{0,16},{1,17},{2,18},{3,19},{4,20},{5,21},{6,22},{7,23},{8,24},{9,... | collective-permute-start | bytes 80 | tf_op jit(solution)/shard_map/ppermute | solution.py:61
  13.5 1.4 %collective-permute-start.3 = (s32[6]{0:T(128)S(1)}, s32[6]{0:T(128)S(1)}, u32[]{:S(2)}, u32[]{:S(2)}) collective-permute-start(s32[6]{0:T(128)S(1)} %get-tuple-element.18), channel_id=1, source_target_pairs={{0,31},{1,0},{2,1},{3,2},{4,3},{5,4},{6,5},{7,6},{8,7},{9,8},{10,9... | collective-permute-start | bytes 80 | tf_op jit(solution)/shard_map/ppermute | solution.py:61
  14.9 2.4 %collective-permute-start.4 = (s32[6]{0:T(128)S(1)}, s32[6]{0:T(128)S(1)}, u32[]{:S(2)}, u32[]{:S(2)}) collective-permute-start(s32[6]{0:T(128)S(1)} %get-tuple-element.15), channel_id=1, source_target_pairs={{0,30},{1,31},{2,0},{3,1},{4,2},{5,3},{6,4},{7,5},{8,6},{9,7},{10,... | collective-permute-start | bytes 80 | tf_op jit(solution)/shard_map/ppermute | solution.py:61
  19.6 3.3 %collective-permute-start.5 = (bf16[6,32,128]{2,1,0:T(8,128)(2,1)S(1)}, bf16[6,32,128]{2,1,0:T(8,128)(2,1)S(1)}, u32[]{:S(2)}, u32[]{:S(2)}) collective-permute-start(bf16[6,32,128]{2,1,0:T(8,128)(2,1)S(1)} %get-tuple-element.62), channel_id=1, source_target_pairs={{1,0},{2,1},{3,2},{4,3},{5,4},{6,5},{7,6},{8,7},{9,8},{10,9},{11,1... | collective-permute-start | bytes 147464 | tf_op jit(solution)/shard_map/ppermute | solution.py:71
  22.9 1.7 %collective-permute-start.6 = (bf16[6,32,128]{2,1,0:T(8,128)(2,1)S(1)}, bf16[6,32,128]{2,1,0:T(8,128)(2,1)S(1)}, u32[]{:S(2)}, u32[]{:S(2)}) collective-permute-start(bf16[6,32,128]{2,1,0:T(8,128)(2,1)S(1)} %get-tuple-element.61), channel_id=1, source_target_pairs={{2,0},{3,1},{4,2},{5,3},{6,4},{7,5},{8,6},{9,7},{10,8},{11,9},{12,... | collective-permute-start | bytes 147464 | tf_op jit(solution)/shard_map/ppermute | solution.py:71
  24.6 1.5 %collective-permute-start.7 = (bf16[6,32,128]{2,1,0:T(8,128)(2,1)S(1)}, bf16[6,32,128]{2,1,0:T(8,128)(2,1)S(1)}, u32[]{:S(2)}, u32[]{:S(2)}) collective-permute-start(bf16[6,32,128]{2,1,0:T(8,128)(2,1)S(1)} %get-tuple-element.60), channel_id=1, source_target_pairs={{16,0},{17,1},{18,2},{19,3},{20,4},{21,5},{22,6},{23,7},{24,8},{25... | collective-permute-start | bytes 147464 | tf_op jit(solution)/shard_map/ppermute | solution.py:71
  27.4 4.1 %collective-permute-done.7 = bf16[6,32,128]{2,1,0:T(8,128)(2,1)S(1)} collective-permute-done((bf16[6,32,128]{2,1,0:T(8,128)(2,1)S(1)}, bf16[6,32,128]{2,1,0:T(8,128)(2,1)S(1)}, u32[]{:S(2)}, u32[]{:S(2)}) %collective-permute-start.7) | collective-permute-done | bytes 49184 | tf_op jit(solution)/shard_map/ppermute | solution.py:71
  31.5 2.0 %collective-permute-done.9 = bf16[6,32,128]{2,1,0:T(8,128)(2,1)S(1)} collective-permute-done((bf16[6,32,128]{2,1,0:T(8,128)(2,1)S(1)}, bf16[6,32,128]{2,1,0:T(8,128)(2,1)S(1)}, u32[]{:S(2)}, u32[]{:S(2)}) %collective-permute-start.9) | collective-permute-done | bytes 49184 | tf_op jit(solution)/shard_map/ppermute | solution.py:71
  34.3 2.8 %convolution_bitcast_fusion.4 = f32[24,32,128]{2,1,0:T(8,128)S(1)} fusion(bf16[24,5,32,128]{3,2,1,0:T(8,128)(2,1)S(1)} %bitcast.153, bf16[24,5,128,128]{3,2,1,0:T(8,128)(2,1)} %param.6), kind=kOutput, calls=%fused_computation.10 | convolution fusion | flops 125829120 | bytes 5308416 | tf_op jit(solution)/shard_map/nscb,nsbd->ncd/dot_general | solution.py:25
  40.0 1.8 %collective-permute-start.10 = (bf16[6,64,128]{2,1,0:T(8,128)(2,1)S(1)}, bf16[6,64,128]{2,1,0:T(8,128)(2,1)S(1)}, u32[]{:S(2)}, u32[]{:S(2)}) collective-permute-start(bf16[6,64,128]{2,1,0:T(8,128)(2,1)S(1)} %get-tuple-element.54), channel_id=1, source_target_pairs={{1,0},{2,1},{3,2},{4,3},{5,4},{6,5},{7,6},{8,7},{9,8},{10,9},{11,1... | collective-permute-start | bytes 294920 | tf_op jit(solution)/shard_map/ppermute | solution.py:71
  42.3 3.8 %collective-permute-start.12 = (bf16[6,64,128]{2,1,0:T(8,128)(2,1)S(1)}, bf16[6,64,128]{2,1,0:T(8,128)(2,1)S(1)}, u32[]{:S(2)}, u32[]{:S(2)}) collective-permute-start(bf16[6,64,128]{2,1,0:T(8,128)(2,1)S(1)} %get-tuple-element.52), channel_id=1, source_target_pairs={{16,0},{17,1},{18,2},{19,3},{20,4},{21,5},{22,6},{23,7},{24,8},{25... | collective-permute-start | bytes 294920 | tf_op jit(solution)/shard_map/ppermute | solution.py:71
  46.1 2.1 %collective-permute-start.13 = (bf16[6,64,128]{2,1,0:T(8,128)(2,1)S(1)}, bf16[6,64,128]{2,1,0:T(8,128)(2,1)S(1)}, u32[]{:S(2)}, u32[]{:S(2)}) collective-permute-start(bf16[6,64,128]{2,1,0:T(8,128)(2,1)S(1)} %get-tuple-element.51), channel_id=1, source_target_pairs={{31,0},{0,1},{1,2},{2,3},{3,4},{4,5},{5,6},{6,7},{7,8},{8,9},{9,10... | collective-permute-start | bytes 294920 | tf_op jit(solution)/shard_map/ppermute | solution.py:71
  48.2 2.6 %collective-permute-start.14 = (bf16[6,64,128]{2,1,0:T(8,128)(2,1)S(1)}, bf16[6,64,128]{2,1,0:T(8,128)(2,1)S(1)}, u32[]{:S(2)}, u32[]{:S(2)}) collective-permute-start(bf16[6,64,128]{2,1,0:T(8,128)(2,1)S(1)} %get-tuple-element.50), channel_id=1, source_target_pairs={{30,0},{31,1},{0,2},{1,3},{2,4},{3,5},{4,6},{5,7},{6,8},{7,9},{8,1... | collective-permute-start | bytes 294920 | tf_op jit(solution)/shard_map/ppermute | solution.py:71
  53.4 2.2 %collective-permute-done.14 = bf16[6,64,128]{2,1,0:T(8,128)(2,1)S(1)} collective-permute-done((bf16[6,64,128]{2,1,0:T(8,128)(2,1)S(1)}, bf16[6,64,128]{2,1,0:T(8,128)(2,1)S(1)}, u32[]{:S(2)}, u32[]{:S(2)}) %collective-permute-start.14) | collective-permute-done | bytes 98336 | tf_op jit(solution)/shard_map/ppermute | solution.py:71
  56.2 2.1 %gather_fusion.3 = bf16[120,64,128]{2,1,0:T(8,128)(2,1)S(1)} fusion(bf16[54,64,128]{2,1,0:T(8,128)(2,1)} %constant_dynamic-update-slice_fusion.6, s32[1024]{0:T(1024)S(1)} %pad_clamp_fusion), kind=kCustom, calls=%fused_computation.3 | custom fusion | bytes 3932640 | tf_op jit(solution)/shard_map/gather | solution.py:24
  58.3 3.2 %convolution_bitcast_fusion.3 = f32[24,64,128]{2,1,0:T(8,128)S(1)} fusion(bf16[24,5,64,128]{3,2,1,0:T(8,128)(2,1)S(1)} %bitcast.148, bf16[24,5,128,128]{3,2,1,0:T(8,128)(2,1)} %param.6), kind=kOutput, calls=%fused_computation.9 | convolution fusion | flops 251658240 | bytes 6684672 | tf_op jit(solution)/shard_map/nscb,nsbd->ncd/dot_general | solution.py:25
  63.4 1.0 copy-done.4
  64.3 1.0 fusion.6
  67.1 3.4 %collective-permute-start.17 = (bf16[6,64,128]{2,1,0:T(8,128)(2,1)S(1)}, bf16[6,64,128]{2,1,0:T(8,128)(2,1)S(1)}, u32[]{:S(2)}, u32[]{:S(2)}) collective-permute-start(bf16[6,64,128]{2,1,0:T(8,128)(2,1)S(1)} %get-tuple-element.47), channel_id=1, source_target_pairs={{16,0},{17,1},{18,2},{19,3},{20,4},{21,5},{22,6},{23,7},{24,8},{25... | collective-permute-start | bytes 294920 | tf_op jit(solution)/shard_map/ppermute | solution.py:71
  70.5 2.0 %collective-permute-start.18 = (bf16[6,64,128]{2,1,0:T(8,128)(2,1)S(1)}, bf16[6,64,128]{2,1,0:T(8,128)(2,1)S(1)}, u32[]{:S(2)}, u32[]{:S(2)}) collective-permute-start(bf16[6,64,128]{2,1,0:T(8,128)(2,1)S(1)} %get-tuple-element.46), channel_id=1, source_target_pairs={{31,0},{0,1},{1,2},{2,3},{3,4},{4,5},{5,6},{6,7},{7,8},{8,9},{9,10... | collective-permute-start | bytes 294920 | tf_op jit(solution)/shard_map/ppermute | solution.py:71
  72.5 2.2 %collective-permute-start.19 = (bf16[6,64,128]{2,1,0:T(8,128)(2,1)S(1)}, bf16[6,64,128]{2,1,0:T(8,128)(2,1)S(1)}, u32[]{:S(2)}, u32[]{:S(2)}) collective-permute-start(bf16[6,64,128]{2,1,0:T(8,128)(2,1)S(1)} %get-tuple-element.45), channel_id=1, source_target_pairs={{30,0},{31,1},{0,2},{1,3},{2,4},{3,5},{4,6},{5,7},{6,8},{7,9},{8,1... | collective-permute-start | bytes 294920 | tf_op jit(solution)/shard_map/ppermute | solution.py:71
  78.1 2.4 %collective-permute-done.19 = bf16[6,64,128]{2,1,0:T(8,128)(2,1)S(1)} collective-permute-done((bf16[6,64,128]{2,1,0:T(8,128)(2,1)S(1)}, bf16[6,64,128]{2,1,0:T(8,128)(2,1)S(1)}, u32[]{:S(2)}, u32[]{:S(2)}) %collective-permute-start.19) | collective-permute-done | bytes 98336 | tf_op jit(solution)/shard_map/ppermute | solution.py:71
  81.1 2.1 %gather_fusion.5 = bf16[120,64,128]{2,1,0:T(8,128)(2,1)S(1)} fusion(bf16[54,64,128]{2,1,0:T(8,128)(2,1)} %constant_dynamic-update-slice_fusion.12, s32[1024]{0:T(1024)S(1)} %pad_clamp_fusion), kind=kCustom, calls=%fused_computation.5 | custom fusion | bytes 3932640 | tf_op jit(solution)/shard_map/gather | solution.py:24
  83.2 3.2 %convolution_bitcast_fusion = f32[24,64,128]{2,1,0:T(8,128)S(1)} fusion(bf16[24,5,64,128]{3,2,1,0:T(8,128)(2,1)S(1)} %bitcast.146, bf16[24,5,128,128]{3,2,1,0:T(8,128)(2,1)} %param.7), kind=kOutput, calls=%fused_computation.6 | convolution fusion | flops 251658240 | bytes 6684672 | tf_op jit(solution)/shard_map/nscb,nsbd->ncd/dot_general | solution.py:28
  91.3 6.2 %collective-permute-start.20 = (f32[4,2,4,24,128]{4,3,2,1,0:T(8,128)S(1)}, f32[4,2,4,24,128]{4,3,2,1,0:T(8,128)S(1)}, u32[]{:S(2)}, u32[]{:S(2)}) collective-permute-start(f32[4,2,4,24,128]{4,3,2,1,0:T(8,128)S(1)} %bitcast.158), channel_id=1, source_target_pairs={{0,32},{32,0},{64,96},{96,64},{128,160},{160,128},{192,224},{224,1... | collective-permute-start | bytes 1179656 | tf_op jit(solution)/shard_map/ppermute | solution.py:114
  97.5 1.3 %collective-permute-done.20 = f32[4,2,4,24,128]{4,3,2,1,0:T(8,128)S(1)} collective-permute-done((f32[4,2,4,24,128]{4,3,2,1,0:T(8,128)S(1)}, f32[4,2,4,24,128]{4,3,2,1,0:T(8,128)S(1)}, u32[]{:S(2)}, u32[]{:S(2)}) %collective-permute-start.20) | collective-permute-done | bytes 393248 | tf_op jit(solution)/shard_map/ppermute | solution.py:114
  99.0 2.8 %collective-permute-start.23 = (f32[2,4,24,128]{3,2,1,0:T(8,128)S(1)}, f32[2,4,24,128]{3,2,1,0:T(8,128)S(1)}, u32[]{:S(2)}, u32[]{:S(2)}) collective-permute-start(f32[2,4,24,128]{3,2,1,0:T(8,128)S(1)} %get-tuple-element.56), channel_id=1, source_target_pairs={{0,192},{32,224},{64,0},{96,32},{128,64},{160,96},{192,128},{224,1... | collective-permute-start | bytes 294920 | tf_op jit(solution)/shard_map/ppermute | solution.py:119
  102.9 2.7 %collective-permute-done.23 = f32[2,4,24,128]{3,2,1,0:T(8,128)S(1)} collective-permute-done((f32[2,4,24,128]{3,2,1,0:T(8,128)S(1)}, f32[2,4,24,128]{3,2,1,0:T(8,128)S(1)}, u32[]{:S(2)}, u32[]{:S(2)}) %collective-permute-start.23) | collective-permute-done | bytes 98336 | tf_op jit(solution)/shard_map/ppermute | solution.py:119
  105.6 1.3 %collective-permute-done.22 = f32[2,4,24,128]{3,2,1,0:T(8,128)S(1)} collective-permute-done((f32[2,4,24,128]{3,2,1,0:T(8,128)S(1)}, f32[2,4,24,128]{3,2,1,0:T(8,128)S(1)}, u32[]{:S(2)}, u32[]{:S(2)}) %collective-permute-start.22) | collective-permute-done | bytes 98336 | tf_op jit(solution)/shard_map/ppermute | solution.py:119
  106.9 3.1 %collective-permute-done.21 = f32[2,4,24,128]{3,2,1,0:T(8,128)S(1)} collective-permute-done((f32[2,4,24,128]{3,2,1,0:T(8,128)S(1)}, f32[2,4,24,128]{3,2,1,0:T(8,128)S(1)}, u32[]{:S(2)}, u32[]{:S(2)}) %collective-permute-start.21) | collective-permute-done | bytes 98336 | tf_op jit(solution)/shard_map/ppermute | solution.py:119
  (125 shorter events, 28.6 us)
Async XLA Ops:
  0.0 37.2 %copy-start = (bf16[1,2,24,128,128]{4,3,2,1,0:T(8,128)(2,1)S(1)}, bf16[1,2,24,128,128]{4,3,2,1,0:T(8,128)(2,1)}, u32[]{:S(2)}) copy-start(bf16[1,2,24,128,128]{4,3,2,1,0:T(8,128)(2,1)} %param.8) | copy-start | bytes 4718596
  0.0 18.2 %copy-start.10 = (bf16[32,24,128]{2,1,0:T(8,128)(2,1)S(1)}, bf16[32,24,128]{2,1,0:T(8,128)(2,1)}, u32[]{:S(2)}) copy-start(bf16[32,24,128]{2,1,0:T(8,128)(2,1)} %param.5) | copy-start | bytes 589828
  4.0 14.4 %collective-permute-start = (s32[6]{0:T(128)S(1)}, s32[6]{0:T(128)S(1)}, u32[]{:S(2)}, u32[]{:S(2)}) collective-permute-start(s32[6]{0:T(128)S(1)} %get-tuple-element.19), channel_id=1, source_target_pairs={{0,1},{1,2},{2,3},{3,4},{4,5},{5,6},{6,7},{7,8},{8,9},{9,10},{10,1... | collective-permute-start | bytes 80 | tf_op jit(solution)/shard_map/ppermute | solution.py:61
  5.3 13.1 %collective-permute-start.1 = (s32[6]{0:T(128)S(1)}, s32[6]{0:T(128)S(1)}, u32[]{:S(2)}, u32[]{:S(2)}) collective-permute-start(s32[6]{0:T(128)S(1)} %get-tuple-element.16), channel_id=1, source_target_pairs={{0,2},{1,3},{2,4},{3,5},{4,6},{5,7},{6,8},{7,9},{8,10},{9,11},{10,... | collective-permute-start | bytes 80 | tf_op jit(solution)/shard_map/ppermute | solution.py:61
  7.5 10.9 %collective-permute-start.2 = (s32[6]{0:T(128)S(1)}, s32[6]{0:T(128)S(1)}, u32[]{:S(2)}, u32[]{:S(2)}) collective-permute-start(s32[6]{0:T(128)S(1)} %get-tuple-element.17), channel_id=1, source_target_pairs={{0,16},{1,17},{2,18},{3,19},{4,20},{5,21},{6,22},{7,23},{8,24},{9,... | collective-permute-start | bytes 80 | tf_op jit(solution)/shard_map/ppermute | solution.py:61
  13.5 4.9 %collective-permute-start.3 = (s32[6]{0:T(128)S(1)}, s32[6]{0:T(128)S(1)}, u32[]{:S(2)}, u32[]{:S(2)}) collective-permute-start(s32[6]{0:T(128)S(1)} %get-tuple-element.18), channel_id=1, source_target_pairs={{0,31},{1,0},{2,1},{3,2},{4,3},{5,4},{6,5},{7,6},{8,7},{9,8},{10,9... | collective-permute-start | bytes 80 | tf_op jit(solution)/shard_map/ppermute | solution.py:61
  14.9 3.9 %collective-permute-start.4 = (s32[6]{0:T(128)S(1)}, s32[6]{0:T(128)S(1)}, u32[]{:S(2)}, u32[]{:S(2)}) collective-permute-start(s32[6]{0:T(128)S(1)} %get-tuple-element.15), channel_id=1, source_target_pairs={{0,30},{1,31},{2,0},{3,1},{4,2},{5,3},{6,4},{7,5},{8,6},{9,7},{10,... | collective-permute-start | bytes 80 | tf_op jit(solution)/shard_map/ppermute | solution.py:61
  19.6 7.4 %collective-permute-start.5 = (bf16[6,32,128]{2,1,0:T(8,128)(2,1)S(1)}, bf16[6,32,128]{2,1,0:T(8,128)(2,1)S(1)}, u32[]{:S(2)}, u32[]{:S(2)}) collective-permute-start(bf16[6,32,128]{2,1,0:T(8,128)(2,1)S(1)} %get-tuple-element.62), channel_id=1, source_target_pairs={{1,0},{2,1},{3,2},{4,3},{5,4},{6,5},{7,6},{8,7},{9,8},{10,9},{11,1... | collective-permute-start | bytes 147464 | tf_op jit(solution)/shard_map/ppermute | solution.py:71
  22.9 4.4 %collective-permute-start.6 = (bf16[6,32,128]{2,1,0:T(8,128)(2,1)S(1)}, bf16[6,32,128]{2,1,0:T(8,128)(2,1)S(1)}, u32[]{:S(2)}, u32[]{:S(2)}) collective-permute-start(bf16[6,32,128]{2,1,0:T(8,128)(2,1)S(1)} %get-tuple-element.61), channel_id=1, source_target_pairs={{2,0},{3,1},{4,2},{5,3},{6,4},{7,5},{8,6},{9,7},{10,8},{11,9},{12,... | collective-permute-start | bytes 147464 | tf_op jit(solution)/shard_map/ppermute | solution.py:71
  24.6 6.8 %collective-permute-start.7 = (bf16[6,32,128]{2,1,0:T(8,128)(2,1)S(1)}, bf16[6,32,128]{2,1,0:T(8,128)(2,1)S(1)}, u32[]{:S(2)}, u32[]{:S(2)}) collective-permute-start(bf16[6,32,128]{2,1,0:T(8,128)(2,1)S(1)} %get-tuple-element.60), channel_id=1, source_target_pairs={{16,0},{17,1},{18,2},{19,3},{20,4},{21,5},{22,6},{23,7},{24,8},{25... | collective-permute-start | bytes 147464 | tf_op jit(solution)/shard_map/ppermute | solution.py:71
  26.2 5.3 %collective-permute-start.8 = (bf16[6,32,128]{2,1,0:T(8,128)(2,1)S(1)}, bf16[6,32,128]{2,1,0:T(8,128)(2,1)S(1)}, u32[]{:S(2)}, u32[]{:S(2)}) collective-permute-start(bf16[6,32,128]{2,1,0:T(8,128)(2,1)S(1)} %get-tuple-element.59), channel_id=1, source_target_pairs={{31,0},{0,1},{1,2},{2,3},{3,4},{4,5},{5,6},{6,7},{7,8},{8,9},{9,10... | collective-permute-start | bytes 147464 | tf_op jit(solution)/shard_map/ppermute | solution.py:71
  27.0 6.6 %collective-permute-start.9 = (bf16[6,32,128]{2,1,0:T(8,128)(2,1)S(1)}, bf16[6,32,128]{2,1,0:T(8,128)(2,1)S(1)}, u32[]{:S(2)}, u32[]{:S(2)}) collective-permute-start(bf16[6,32,128]{2,1,0:T(8,128)(2,1)S(1)} %get-tuple-element.58), channel_id=1, source_target_pairs={{30,0},{31,1},{0,2},{1,3},{2,4},{3,5},{4,6},{5,7},{6,8},{7,9},{8,1... | collective-permute-start | bytes 147464 | tf_op jit(solution)/shard_map/ppermute | solution.py:71
  37.2 2.1 %copy-start.6 = (f32[24,32,128]{2,1,0:T(8,128)}, f32[24,32,128]{2,1,0:T(8,128)S(1)}, u32[]{:S(2)}) copy-start(f32[24,32,128]{2,1,0:T(8,128)S(1)} %convolution_bitcast_fusion.4) | copy-start | bytes 1179652
  40.0 10.9 %collective-permute-start.10 = (bf16[6,64,128]{2,1,0:T(8,128)(2,1)S(1)}, bf16[6,64,128]{2,1,0:T(8,128)(2,1)S(1)}, u32[]{:S(2)}, u32[]{:S(2)}) collective-permute-start(bf16[6,64,128]{2,1,0:T(8,128)(2,1)S(1)} %get-tuple-element.54), channel_id=1, source_target_pairs={{1,0},{2,1},{3,2},{4,3},{5,4},{6,5},{7,6},{8,7},{9,8},{10,9},{11,1... | collective-permute-start | bytes 294920 | tf_op jit(solution)/shard_map/ppermute | solution.py:71
  41.9 9.5 %collective-permute-start.11 = (bf16[6,64,128]{2,1,0:T(8,128)(2,1)S(1)}, bf16[6,64,128]{2,1,0:T(8,128)(2,1)S(1)}, u32[]{:S(2)}, u32[]{:S(2)}) collective-permute-start(bf16[6,64,128]{2,1,0:T(8,128)(2,1)S(1)} %get-tuple-element.53), channel_id=1, source_target_pairs={{2,0},{3,1},{4,2},{5,3},{6,4},{7,5},{8,6},{9,7},{10,8},{11,9},{12,... | collective-permute-start | bytes 294920 | tf_op jit(solution)/shard_map/ppermute | solution.py:71
  42.3 9.8 %collective-permute-start.12 = (bf16[6,64,128]{2,1,0:T(8,128)(2,1)S(1)}, bf16[6,64,128]{2,1,0:T(8,128)(2,1)S(1)}, u32[]{:S(2)}, u32[]{:S(2)}) collective-permute-start(bf16[6,64,128]{2,1,0:T(8,128)(2,1)S(1)} %get-tuple-element.52), channel_id=1, source_target_pairs={{16,0},{17,1},{18,2},{19,3},{20,4},{21,5},{22,6},{23,7},{24,8},{25... | collective-permute-start | bytes 294920 | tf_op jit(solution)/shard_map/ppermute | solution.py:71
  46.1 6.6 %collective-permute-start.13 = (bf16[6,64,128]{2,1,0:T(8,128)(2,1)S(1)}, bf16[6,64,128]{2,1,0:T(8,128)(2,1)S(1)}, u32[]{:S(2)}, u32[]{:S(2)}) collective-permute-start(bf16[6,64,128]{2,1,0:T(8,128)(2,1)S(1)} %get-tuple-element.51), channel_id=1, source_target_pairs={{31,0},{0,1},{1,2},{2,3},{3,4},{4,5},{5,6},{6,7},{7,8},{8,9},{9,10... | collective-permute-start | bytes 294920 | tf_op jit(solution)/shard_map/ppermute | solution.py:71
  48.2 7.4 %collective-permute-start.14 = (bf16[6,64,128]{2,1,0:T(8,128)(2,1)S(1)}, bf16[6,64,128]{2,1,0:T(8,128)(2,1)S(1)}, u32[]{:S(2)}, u32[]{:S(2)}) collective-permute-start(bf16[6,64,128]{2,1,0:T(8,128)(2,1)S(1)} %get-tuple-element.50), channel_id=1, source_target_pairs={{30,0},{31,1},{0,2},{1,3},{2,4},{3,5},{4,6},{5,7},{6,8},{7,9},{8,1... | collective-permute-start | bytes 294920 | tf_op jit(solution)/shard_map/ppermute | solution.py:71
  58.3 3.3 %copy-start.2 = (bf16[24,5,128,128]{3,2,1,0:T(8,128)(2,1)S(1)}, bf16[24,5,128,128]{3,2,1,0:T(8,128)(2,1)}, u32[]{:S(2)}) copy-start(bf16[24,5,128,128]{3,2,1,0:T(8,128)(2,1)} %param.7) | copy-start | bytes 11796484
  63.2 1.1 %copy-start.4 = (f32[24,32,2,128]{3,1,2,0:T(8,128)S(1)}, f32[24,32,2,128]{3,1,2,0:T(8,128)}, u32[]{:S(2)}) copy-start(f32[24,32,2,128]{3,1,2,0:T(8,128)} %copy-done.3) | copy-start | bytes 2359300
  66.1 9.4 %collective-permute-start.15 = (bf16[6,64,128]{2,1,0:T(8,128)(2,1)S(1)}, bf16[6,64,128]{2,1,0:T(8,128)(2,1)S(1)}, u32[]{:S(2)}, u32[]{:S(2)}) collective-permute-start(bf16[6,64,128]{2,1,0:T(8,128)(2,1)S(1)} %get-tuple-element.49), channel_id=1, source_target_pairs={{1,0},{2,1},{3,2},{4,3},{5,4},{6,5},{7,6},{8,7},{9,8},{10,9},{11,1... | collective-permute-start | bytes 294920 | tf_op jit(solution)/shard_map/ppermute | solution.py:71
  66.6 9.6 %collective-permute-start.16 = (bf16[6,64,128]{2,1,0:T(8,128)(2,1)S(1)}, bf16[6,64,128]{2,1,0:T(8,128)(2,1)S(1)}, u32[]{:S(2)}, u32[]{:S(2)}) collective-permute-start(bf16[6,64,128]{2,1,0:T(8,128)(2,1)S(1)} %get-tuple-element.48), channel_id=1, source_target_pairs={{2,0},{3,1},{4,2},{5,3},{6,4},{7,5},{8,6},{9,7},{10,8},{11,9},{12,... | collective-permute-start | bytes 294920 | tf_op jit(solution)/shard_map/ppermute | solution.py:71
  67.1 9.7 %collective-permute-start.17 = (bf16[6,64,128]{2,1,0:T(8,128)(2,1)S(1)}, bf16[6,64,128]{2,1,0:T(8,128)(2,1)S(1)}, u32[]{:S(2)}, u32[]{:S(2)}) collective-permute-start(bf16[6,64,128]{2,1,0:T(8,128)(2,1)S(1)} %get-tuple-element.47), channel_id=1, source_target_pairs={{16,0},{17,1},{18,2},{19,3},{20,4},{21,5},{22,6},{23,7},{24,8},{25... | collective-permute-start | bytes 294920 | tf_op jit(solution)/shard_map/ppermute | solution.py:71
  70.5 6.9 %collective-permute-start.18 = (bf16[6,64,128]{2,1,0:T(8,128)(2,1)S(1)}, bf16[6,64,128]{2,1,0:T(8,128)(2,1)S(1)}, u32[]{:S(2)}, u32[]{:S(2)}) collective-permute-start(bf16[6,64,128]{2,1,0:T(8,128)(2,1)S(1)} %get-tuple-element.46), channel_id=1, source_target_pairs={{31,0},{0,1},{1,2},{2,3},{3,4},{4,5},{5,6},{6,7},{7,8},{8,9},{9,10... | collective-permute-start | bytes 294920 | tf_op jit(solution)/shard_map/ppermute | solution.py:71
  72.5 8.0 %collective-permute-start.19 = (bf16[6,64,128]{2,1,0:T(8,128)(2,1)S(1)}, bf16[6,64,128]{2,1,0:T(8,128)(2,1)S(1)}, u32[]{:S(2)}, u32[]{:S(2)}) collective-permute-start(bf16[6,64,128]{2,1,0:T(8,128)(2,1)S(1)} %get-tuple-element.45), channel_id=1, source_target_pairs={{30,0},{31,1},{0,2},{1,3},{2,4},{3,5},{4,6},{5,7},{6,8},{7,9},{8,1... | collective-permute-start | bytes 294920 | tf_op jit(solution)/shard_map/ppermute | solution.py:71
  83.2 3.3 %copy-start.1 = (bf16[24,5,128,128]{3,2,1,0:T(8,128)(2,1)S(1)}, bf16[24,5,128,128]{3,2,1,0:T(8,128)(2,1)}, u32[]{:S(2)}) copy-start(bf16[24,5,128,128]{3,2,1,0:T(8,128)(2,1)} %param.6) | copy-start | bytes 11796484
  88.3 1.1 %copy-start.5 = (f32[24,32,2,128]{3,1,2,0:T(8,128)S(1)}, f32[24,32,2,128]{3,1,2,0:T(8,128)}, u32[]{:S(2)}) copy-start(f32[24,32,2,128]{3,1,2,0:T(8,128)} %copy-done.3) | copy-start | bytes 2359300
  88.3 1.4 %copy-start.9 = (f32[24,64,128]{2,1,0:T(8,128)S(1)}, f32[24,64,128]{2,1,0:T(8,128)}, u32[]{:S(2)}) copy-start(f32[24,64,128]{2,1,0:T(8,128)} %get-tuple-element.44) | copy-start | bytes 2359300
  91.3 7.5 %collective-permute-start.20 = (f32[4,2,4,24,128]{4,3,2,1,0:T(8,128)S(1)}, f32[4,2,4,24,128]{4,3,2,1,0:T(8,128)S(1)}, u32[]{:S(2)}, u32[]{:S(2)}) collective-permute-start(f32[4,2,4,24,128]{4,3,2,1,0:T(8,128)S(1)} %bitcast.158), channel_id=1, source_target_pairs={{0,32},{32,0},{64,96},{96,64},{128,160},{160,128},{192,224},{224,1... | collective-permute-start | bytes 1179656 | tf_op jit(solution)/shard_map/ppermute | solution.py:114
  99.0 6.6 %collective-permute-start.23 = (f32[2,4,24,128]{3,2,1,0:T(8,128)S(1)}, f32[2,4,24,128]{3,2,1,0:T(8,128)S(1)}, u32[]{:S(2)}, u32[]{:S(2)}) collective-permute-start(f32[2,4,24,128]{3,2,1,0:T(8,128)S(1)} %get-tuple-element.56), channel_id=1, source_target_pairs={{0,192},{32,224},{64,0},{96,32},{128,64},{160,96},{192,128},{224,1... | collective-permute-start | bytes 294920 | tf_op jit(solution)/shard_map/ppermute | solution.py:119
  101.8 5.1 %collective-permute-start.22 = (f32[2,4,24,128]{3,2,1,0:T(8,128)S(1)}, f32[2,4,24,128]{3,2,1,0:T(8,128)S(1)}, u32[]{:S(2)}, u32[]{:S(2)}) collective-permute-start(f32[2,4,24,128]{3,2,1,0:T(8,128)S(1)} %get-tuple-element.57), channel_id=1, source_target_pairs={{0,128},{32,160},{64,192},{96,224},{128,0},{160,32},{192,64},{224,... | collective-permute-start | bytes 294920 | tf_op jit(solution)/shard_map/ppermute | solution.py:119
  102.2 7.8 %collective-permute-start.21 = (f32[2,4,24,128]{3,2,1,0:T(8,128)S(1)}, f32[2,4,24,128]{3,2,1,0:T(8,128)S(1)}, u32[]{:S(2)}, u32[]{:S(2)}) collective-permute-start(f32[2,4,24,128]{3,2,1,0:T(8,128)S(1)} %get-tuple-element.55), channel_id=1, source_target_pairs={{0,64},{32,96},{64,128},{96,160},{128,192},{160,224},{192,0},{224,... | collective-permute-start | bytes 294920 | tf_op jit(solution)/shard_map/ppermute | solution.py:119
  (3 other events, 2.9 us)

commit v14 on v13

--- a/solution.py
+++ b/solution.py
@@ -40,15 +40,14 @@
     relative = (owners - my_index) % peer_count
     flat_rel = relative.reshape(-1)
     flat_local = local_ids.reshape(-1)
-    slot_flat = flat_local
-    wanted = []
-    rank_range = jnp.arange(HMAX)
-    for which, offset in enumerate(offsets):
-        hit = flat_rel == offset
-        rank = jnp.cumsum(hit.astype(jnp.int32)) - 1
-        slot_flat = jnp.where(hit, dev_rows + which * HMAX + rank, slot_flat)
-        matched = hit[None, :] & (rank[None, :] == rank_range[:, None])
-        wanted.append(jnp.sum(jnp.where(matched, flat_local[None, :], 0), axis=1))
+    partner_ids = jnp.array(offsets, jnp.int32)
+    hit = flat_rel[None, :] == partner_ids[:, None]
+    rank = jnp.cumsum(hit.astype(jnp.int32), axis=1) - 1
+    base = dev_rows + jnp.arange(len(offsets), dtype=jnp.int32)[:, None] * HMAX
+    slot_flat = jnp.where(jnp.any(hit, axis=0), jnp.sum(jnp.where(hit, base + rank, 0), axis=0), flat_local)
+    matched = hit[:, None, :] & (rank[:, None, :] == jnp.arange(HMAX)[None, :, None])
+    wanted_all = jnp.sum(jnp.where(matched, flat_local[None, None, :], 0), axis=2)
+    wanted = [wanted_all[which] for which in range(len(offsets))]
     slot_index = slot_flat.reshape(dev_rows, SLOTS)
 
     def to_partner(offset):

time: 112 us -> 112 us (level)
    unnamed x39 -> x37, local copies, waits for them, and re-layouts: 10.5 us -> 11.6 us
  transfers between devices with their start and end apart: 24 -> 24, of which waited for: 10 -> 9; matrix products, arithmetic and copies ran while one was open for 6% -> 7% of each run, Pallas kernels for 0% -> 0%
where the time goes in v14:
time: 112 us; the launch traced here: 110 us
  starting transfers between devices  49.2 us (44%)
  local copies, waits for them, and re-layouts  21.3 us (19%)
  waiting for transfers between devices  19.8 us (18%)
  matrix products  12.2 us (11%)
  other arithmetic  6.95 us (6%)
    ppermute x15, starting transfers between devices, fetch_halo(): pieces.append(lax.ppermute(piece, 'rows', from_partner(offset)))  26.2 us
    ppermute x5, starting transfers between devices, per_device(): lax.ppermute(wanted[which], 'rows', to_partner(offset))  13.3 us
    unnamed x37, local copies, waits for them, and re-layouts  11.6 us
    ppermute x15, waiting for transfers between devices, fetch_halo(): pieces.append(lax.ppermute(piece, 'rows', from_partner(offset)))  11.3 us
    ppermute x3, waiting for transfers between devices, per_device(): total = total + lax.ppermute(chunk, 'node', perm)  7.15 us
    dot_general x3, matrix products, apply_pair(): jnp.einsum('nscb,nsbd->ncd', picked, first, preferred_element_type=jnp.fl...  6.96 us
    ppermute x1, starting transfers between devices, per_device(): lax.ppermute(other, 'node', [(j, j ^ 1) for j in range(node_count)])  5.85 us
    gather x3, local copies, waits for them, and re-layouts, apply_pair(): picked = extended[slot_index]  4.94 us
  transfers between devices with their start and end apart: 24, of which 9 were waited for; matrix products, arithmetic and copies ran while one was open for 7% of the time, Pallas kernels for 0%

profile of v14, /device:TPU:3, one launch (start us, length us, event | category | flops | bytes accessed | tf_op | source)
XLA Modules:
  0.0 110.0 jit_solution(4942265166803917782)
XLA Ops:
  3.3 1.3 %collective-permute-start = (s32[6]{0:T(128)S(1)}, s32[6]{0:T(128)S(1)}, u32[]{:S(2)}, u32[]{:S(2)}) collective-permute-start(s32[6]{0:T(128)S(1)} %get-tuple-element.45), channel_id=1, source_target_pairs={{0,1},{1,2},{2,3},{3,4},{4,5},{5,6},{6,7},{7,8},{8,9},{9,10},{10,1... | collective-permute-start | bytes 80 | tf_op jit(solution)/shard_map/ppermute | solution.py:60
  4.6 2.2 %collective-permute-start.1 = (s32[6]{0:T(128)S(1)}, s32[6]{0:T(128)S(1)}, u32[]{:S(2)}, u32[]{:S(2)}) collective-permute-start(s32[6]{0:T(128)S(1)} %get-tuple-element.44), channel_id=1, source_target_pairs={{0,2},{1,3},{2,4},{3,5},{4,6},{5,7},{6,8},{7,9},{8,10},{9,11},{10,... | collective-permute-start | bytes 80 | tf_op jit(solution)/shard_map/ppermute | solution.py:60
  6.8 6.0 %collective-permute-start.2 = (s32[6]{0:T(128)S(1)}, s32[6]{0:T(128)S(1)}, u32[]{:S(2)}, u32[]{:S(2)}) collective-permute-start(s32[6]{0:T(128)S(1)} %get-tuple-element.43), channel_id=1, source_target_pairs={{0,16},{1,17},{2,18},{3,19},{4,20},{5,21},{6,22},{7,23},{8,24},{9,... | collective-permute-start | bytes 80 | tf_op jit(solution)/shard_map/ppermute | solution.py:60
  12.8 1.4 %collective-permute-start.3 = (s32[6]{0:T(128)S(1)}, s32[6]{0:T(128)S(1)}, u32[]{:S(2)}, u32[]{:S(2)}) collective-permute-start(s32[6]{0:T(128)S(1)} %get-tuple-element.42), channel_id=1, source_target_pairs={{0,31},{1,0},{2,1},{3,2},{4,3},{5,4},{6,5},{7,6},{8,7},{9,8},{10,9... | collective-permute-start | bytes 80 | tf_op jit(solution)/shard_map/ppermute | solution.py:60
  14.2 2.4 %collective-permute-start.4 = (s32[6]{0:T(128)S(1)}, s32[6]{0:T(128)S(1)}, u32[]{:S(2)}, u32[]{:S(2)}) collective-permute-start(s32[6]{0:T(128)S(1)} %get-tuple-element.41), channel_id=1, source_target_pairs={{0,30},{1,31},{2,0},{3,1},{4,2},{5,3},{6,4},{7,5},{8,6},{9,7},{10,... | collective-permute-start | bytes 80 | tf_op jit(solution)/shard_map/ppermute | solution.py:60
  19.4 2.8 %collective-permute-start.5 = (bf16[6,32,128]{2,1,0:T(8,128)(2,1)S(1)}, bf16[6,32,128]{2,1,0:T(8,128)(2,1)S(1)}, u32[]{:S(2)}, u32[]{:S(2)}) collective-permute-start(bf16[6,32,128]{2,1,0:T(8,128)(2,1)S(1)} %get-tuple-element.36), channel_id=1, source_target_pairs={{1,0},{2,1},{3,2},{4,3},{5,4},{6,5},{7,6},{8,7},{9,8},{10,9},{11,1... | collective-permute-start | bytes 147464 | tf_op jit(solution)/shard_map/ppermute | solution.py:70
  22.2 1.7 %collective-permute-start.6 = (bf16[6,32,128]{2,1,0:T(8,128)(2,1)S(1)}, bf16[6,32,128]{2,1,0:T(8,128)(2,1)S(1)}, u32[]{:S(2)}, u32[]{:S(2)}) collective-permute-start(bf16[6,32,128]{2,1,0:T(8,128)(2,1)S(1)} %get-tuple-element.35), channel_id=1, source_target_pairs={{2,0},{3,1},{4,2},{5,3},{6,4},{7,5},{8,6},{9,7},{10,8},{11,9},{12,... | collective-permute-start | bytes 147464 | tf_op jit(solution)/shard_map/ppermute | solution.py:70
  23.9 1.5 %collective-permute-start.7 = (bf16[6,32,128]{2,1,0:T(8,128)(2,1)S(1)}, bf16[6,32,128]{2,1,0:T(8,128)(2,1)S(1)}, u32[]{:S(2)}, u32[]{:S(2)}) collective-permute-start(bf16[6,32,128]{2,1,0:T(8,128)(2,1)S(1)} %get-tuple-element.34), channel_id=1, source_target_pairs={{16,0},{17,1},{18,2},{19,3},{20,4},{21,5},{22,6},{23,7},{24,8},{25... | collective-permute-start | bytes 147464 | tf_op jit(solution)/shard_map/ppermute | solution.py:70
  27.1 3.7 %collective-permute-done.7 = bf16[6,32,128]{2,1,0:T(8,128)(2,1)S(1)} collective-permute-done((bf16[6,32,128]{2,1,0:T(8,128)(2,1)S(1)}, bf16[6,32,128]{2,1,0:T(8,128)(2,1)S(1)}, u32[]{:S(2)}, u32[]{:S(2)}) %collective-permute-start.7) | collective-permute-done | bytes 49184 | tf_op jit(solution)/shard_map/ppermute | solution.py:70
  30.8 2.0 %collective-permute-done.9 = bf16[6,32,128]{2,1,0:T(8,128)(2,1)S(1)} collective-permute-done((bf16[6,32,128]{2,1,0:T(8,128)(2,1)S(1)}, bf16[6,32,128]{2,1,0:T(8,128)(2,1)S(1)}, u32[]{:S(2)}, u32[]{:S(2)}) %collective-permute-start.9) | collective-permute-done | bytes 49184 | tf_op jit(solution)/shard_map/ppermute | solution.py:70
  33.6 2.8 %convolution_bitcast_fusion.4 = f32[24,32,128]{2,1,0:T(8,128)S(1)} fusion(bf16[24,5,32,128]{3,2,1,0:T(8,128)(2,1)S(1)} %bitcast.163, bf16[24,5,128,128]{3,2,1,0:T(8,128)(2,1)} %param.7), kind=kOutput, calls=%fused_computation.10 | convolution fusion | flops 125829120 | bytes 5308416 | tf_op jit(solution)/shard_map/nscb,nsbd->ncd/dot_general | solution.py:25
  39.3 1.8 %collective-permute-start.10 = (bf16[6,64,128]{2,1,0:T(8,128)(2,1)S(1)}, bf16[6,64,128]{2,1,0:T(8,128)(2,1)S(1)}, u32[]{:S(2)}, u32[]{:S(2)}) collective-permute-start(bf16[6,64,128]{2,1,0:T(8,128)(2,1)S(1)} %get-tuple-element.28), channel_id=1, source_target_pairs={{1,0},{2,1},{3,2},{4,3},{5,4},{6,5},{7,6},{8,7},{9,8},{10,9},{11,1... | collective-permute-start | bytes 294920 | tf_op jit(solution)/shard_map/ppermute | solution.py:70
  41.8 3.7 %collective-permute-start.12 = (bf16[6,64,128]{2,1,0:T(8,128)(2,1)S(1)}, bf16[6,64,128]{2,1,0:T(8,128)(2,1)S(1)}, u32[]{:S(2)}, u32[]{:S(2)}) collective-permute-start(bf16[6,64,128]{2,1,0:T(8,128)(2,1)S(1)} %get-tuple-element.26), channel_id=1, source_target_pairs={{16,0},{17,1},{18,2},{19,3},{20,4},{21,5},{22,6},{23,7},{24,8},{25... | collective-permute-start | bytes 294920 | tf_op jit(solution)/shard_map/ppermute | solution.py:70
  45.5 2.1 %collective-permute-start.13 = (bf16[6,64,128]{2,1,0:T(8,128)(2,1)S(1)}, bf16[6,64,128]{2,1,0:T(8,128)(2,1)S(1)}, u32[]{:S(2)}, u32[]{:S(2)}) collective-permute-start(bf16[6,64,128]{2,1,0:T(8,128)(2,1)S(1)} %get-tuple-element.25), channel_id=1, source_target_pairs={{31,0},{0,1},{1,2},{2,3},{3,4},{4,5},{5,6},{6,7},{7,8},{8,9},{9,10... | collective-permute-start | bytes 294920 | tf_op jit(solution)/shard_map/ppermute | solution.py:70
  47.5 2.6 %collective-permute-start.14 = (bf16[6,64,128]{2,1,0:T(8,128)(2,1)S(1)}, bf16[6,64,128]{2,1,0:T(8,128)(2,1)S(1)}, u32[]{:S(2)}, u32[]{:S(2)}) collective-permute-start(bf16[6,64,128]{2,1,0:T(8,128)(2,1)S(1)} %get-tuple-element.24), channel_id=1, source_target_pairs={{30,0},{31,1},{0,2},{1,3},{2,4},{3,5},{4,6},{5,7},{6,8},{7,9},{8,1... | collective-permute-start | bytes 294920 | tf_op jit(solution)/shard_map/ppermute | solution.py:70
  52.8 2.1 %collective-permute-done.14 = bf16[6,64,128]{2,1,0:T(8,128)(2,1)S(1)} collective-permute-done((bf16[6,64,128]{2,1,0:T(8,128)(2,1)S(1)}, bf16[6,64,128]{2,1,0:T(8,128)(2,1)S(1)}, u32[]{:S(2)}, u32[]{:S(2)}) %collective-permute-start.14) | collective-permute-done | bytes 98336 | tf_op jit(solution)/shard_map/ppermute | solution.py:70
  55.5 2.1 %gather_fusion.3 = bf16[120,64,128]{2,1,0:T(8,128)(2,1)S(1)} fusion(bf16[54,64,128]{2,1,0:T(8,128)(2,1)} %constant_dynamic-update-slice_fusion.6, s32[1024]{0:T(1024)S(1)} %pad_clamp_fusion), kind=kCustom, calls=%fused_computation.3 | custom fusion | bytes 3932640 | tf_op jit(solution)/shard_map/gather | solution.py:24
  57.7 3.2 %convolution_bitcast_fusion.3 = f32[24,64,128]{2,1,0:T(8,128)S(1)} fusion(bf16[24,5,64,128]{3,2,1,0:T(8,128)(2,1)S(1)} %bitcast.158, bf16[24,5,128,128]{3,2,1,0:T(8,128)(2,1)} %param.7), kind=kOutput, calls=%fused_computation.9 | convolution fusion | flops 251658240 | bytes 6684672 | tf_op jit(solution)/shard_map/nscb,nsbd->ncd/dot_general | solution.py:25
  62.7 1.0 copy-done.4
  63.7 1.0 fusion.6
  66.3 3.4 %collective-permute-start.17 = (bf16[6,64,128]{2,1,0:T(8,128)(2,1)S(1)}, bf16[6,64,128]{2,1,0:T(8,128)(2,1)S(1)}, u32[]{:S(2)}, u32[]{:S(2)}) collective-permute-start(bf16[6,64,128]{2,1,0:T(8,128)(2,1)S(1)} %get-tuple-element.21), channel_id=1, source_target_pairs={{16,0},{17,1},{18,2},{19,3},{20,4},{21,5},{22,6},{23,7},{24,8},{25... | collective-permute-start | bytes 294920 | tf_op jit(solution)/shard_map/ppermute | solution.py:70
  69.8 2.0 %collective-permute-start.18 = (bf16[6,64,128]{2,1,0:T(8,128)(2,1)S(1)}, bf16[6,64,128]{2,1,0:T(8,128)(2,1)S(1)}, u32[]{:S(2)}, u32[]{:S(2)}) collective-permute-start(bf16[6,64,128]{2,1,0:T(8,128)(2,1)S(1)} %get-tuple-element.20), channel_id=1, source_target_pairs={{31,0},{0,1},{1,2},{2,3},{3,4},{4,5},{5,6},{6,7},{7,8},{8,9},{9,10... | collective-permute-start | bytes 294920 | tf_op jit(solution)/shard_map/ppermute | solution.py:70
  71.7 2.2 %collective-permute-start.19 = (bf16[6,64,128]{2,1,0:T(8,128)(2,1)S(1)}, bf16[6,64,128]{2,1,0:T(8,128)(2,1)S(1)}, u32[]{:S(2)}, u32[]{:S(2)}) collective-permute-start(bf16[6,64,128]{2,1,0:T(8,128)(2,1)S(1)} %get-tuple-element.19), channel_id=1, source_target_pairs={{30,0},{31,1},{0,2},{1,3},{2,4},{3,5},{4,6},{5,7},{6,8},{7,9},{8,1... | collective-permute-start | bytes 294920 | tf_op jit(solution)/shard_map/ppermute | solution.py:70
  77.4 2.7 %collective-permute-done.19 = bf16[6,64,128]{2,1,0:T(8,128)(2,1)S(1)} collective-permute-done((bf16[6,64,128]{2,1,0:T(8,128)(2,1)S(1)}, bf16[6,64,128]{2,1,0:T(8,128)(2,1)S(1)}, u32[]{:S(2)}, u32[]{:S(2)}) %collective-permute-start.19) | collective-permute-done | bytes 98336 | tf_op jit(solution)/shard_map/ppermute | solution.py:70
  80.8 2.1 %gather_fusion.5 = bf16[120,64,128]{2,1,0:T(8,128)(2,1)S(1)} fusion(bf16[54,64,128]{2,1,0:T(8,128)(2,1)} %constant_dynamic-update-slice_fusion.12, s32[1024]{0:T(1024)S(1)} %pad_clamp_fusion), kind=kCustom, calls=%fused_computation.5 | custom fusion | bytes 3932640 | tf_op jit(solution)/shard_map/gather | solution.py:24
  82.9 3.2 %convolution_bitcast_fusion = f32[24,64,128]{2,1,0:T(8,128)S(1)} fusion(bf16[24,5,64,128]{3,2,1,0:T(8,128)(2,1)S(1)} %bitcast.156, bf16[24,5,128,128]{3,2,1,0:T(8,128)(2,1)} %param.8), kind=kOutput, calls=%fused_computation.6 | convolution fusion | flops 251658240 | bytes 6684672 | tf_op jit(solution)/shard_map/nscb,nsbd->ncd/dot_general | solution.py:28
  91.0 5.8 %collective-permute-start.20 = (f32[4,2,4,24,128]{4,3,2,1,0:T(8,128)S(1)}, f32[4,2,4,24,128]{4,3,2,1,0:T(8,128)S(1)}, u32[]{:S(2)}, u32[]{:S(2)}) collective-permute-start(f32[4,2,4,24,128]{4,3,2,1,0:T(8,128)S(1)} %bitcast.168), channel_id=1, source_target_pairs={{0,32},{32,0},{64,96},{96,64},{128,160},{160,128},{192,224},{224,1... | collective-permute-start | bytes 1179656 | tf_op jit(solution)/shard_map/ppermute | solution.py:113
  96.8 1.3 %collective-permute-done.20 = f32[4,2,4,24,128]{4,3,2,1,0:T(8,128)S(1)} collective-permute-done((f32[4,2,4,24,128]{4,3,2,1,0:T(8,128)S(1)}, f32[4,2,4,24,128]{4,3,2,1,0:T(8,128)S(1)}, u32[]{:S(2)}, u32[]{:S(2)}) %collective-permute-start.20) | collective-permute-done | bytes 393248 | tf_op jit(solution)/shard_map/ppermute | solution.py:113
  98.4 2.8 %collective-permute-start.23 = (f32[2,4,24,128]{3,2,1,0:T(8,128)S(1)}, f32[2,4,24,128]{3,2,1,0:T(8,128)S(1)}, u32[]{:S(2)}, u32[]{:S(2)}) collective-permute-start(f32[2,4,24,128]{3,2,1,0:T(8,128)S(1)} %get-tuple-element.30), channel_id=1, source_target_pairs={{0,192},{32,224},{64,0},{96,32},{128,64},{160,96},{192,128},{224,1... | collective-permute-start | bytes 294920 | tf_op jit(solution)/shard_map/ppermute | solution.py:118
  102.2 2.7 %collective-permute-done.23 = f32[2,4,24,128]{3,2,1,0:T(8,128)S(1)} collective-permute-done((f32[2,4,24,128]{3,2,1,0:T(8,128)S(1)}, f32[2,4,24,128]{3,2,1,0:T(8,128)S(1)}, u32[]{:S(2)}, u32[]{:S(2)}) %collective-permute-start.23) | collective-permute-done | bytes 98336 | tf_op jit(solution)/shard_map/ppermute | solution.py:118
  104.9 1.3 %collective-permute-done.22 = f32[2,4,24,128]{3,2,1,0:T(8,128)S(1)} collective-permute-done((f32[2,4,24,128]{3,2,1,0:T(8,128)S(1)}, f32[2,4,24,128]{3,2,1,0:T(8,128)S(1)}, u32[]{:S(2)}, u32[]{:S(2)}) %collective-permute-start.22) | collective-permute-done | bytes 98336 | tf_op jit(solution)/shard_map/ppermute | solution.py:118
  106.3 3.1 %collective-permute-done.21 = f32[2,4,24,128]{3,2,1,0:T(8,128)S(1)} collective-permute-done((f32[2,4,24,128]{3,2,1,0:T(8,128)S(1)}, f32[2,4,24,128]{3,2,1,0:T(8,128)S(1)}, u32[]{:S(2)}, u32[]{:S(2)}) %collective-permute-start.21) | collective-permute-done | bytes 98336 | tf_op jit(solution)/shard_map/ppermute | solution.py:118
  (106 shorter events, 29.1 us)
Async XLA Ops:
  0.0 36.5 %copy-start = (bf16[1,2,24,128,128]{4,3,2,1,0:T(8,128)(2,1)S(1)}, bf16[1,2,24,128,128]{4,3,2,1,0:T(8,128)(2,1)}, u32[]{:S(2)}) copy-start(bf16[1,2,24,128,128]{4,3,2,1,0:T(8,128)(2,1)} %param.9) | copy-start | bytes 4718596
  3.3 15.3 %collective-permute-start = (s32[6]{0:T(128)S(1)}, s32[6]{0:T(128)S(1)}, u32[]{:S(2)}, u32[]{:S(2)}) collective-permute-start(s32[6]{0:T(128)S(1)} %get-tuple-element.45), channel_id=1, source_target_pairs={{0,1},{1,2},{2,3},{3,4},{4,5},{5,6},{6,7},{7,8},{8,9},{9,10},{10,1... | collective-permute-start | bytes 80 | tf_op jit(solution)/shard_map/ppermute | solution.py:60
  4.6 14.0 %collective-permute-start.1 = (s32[6]{0:T(128)S(1)}, s32[6]{0:T(128)S(1)}, u32[]{:S(2)}, u32[]{:S(2)}) collective-permute-start(s32[6]{0:T(128)S(1)} %get-tuple-element.44), channel_id=1, source_target_pairs={{0,2},{1,3},{2,4},{3,5},{4,6},{5,7},{6,8},{7,9},{8,10},{9,11},{10,... | collective-permute-start | bytes 80 | tf_op jit(solution)/shard_map/ppermute | solution.py:60
  6.8 11.8 %collective-permute-start.2 = (s32[6]{0:T(128)S(1)}, s32[6]{0:T(128)S(1)}, u32[]{:S(2)}, u32[]{:S(2)}) collective-permute-start(s32[6]{0:T(128)S(1)} %get-tuple-element.43), channel_id=1, source_target_pairs={{0,16},{1,17},{2,18},{3,19},{4,20},{5,21},{6,22},{7,23},{8,24},{9,... | collective-permute-start | bytes 80 | tf_op jit(solution)/shard_map/ppermute | solution.py:60
  12.8 5.8 %collective-permute-start.3 = (s32[6]{0:T(128)S(1)}, s32[6]{0:T(128)S(1)}, u32[]{:S(2)}, u32[]{:S(2)}) collective-permute-start(s32[6]{0:T(128)S(1)} %get-tuple-element.42), channel_id=1, source_target_pairs={{0,31},{1,0},{2,1},{3,2},{4,3},{5,4},{6,5},{7,6},{8,7},{9,8},{10,9... | collective-permute-start | bytes 80 | tf_op jit(solution)/shard_map/ppermute | solution.py:60
  14.2 4.4 %collective-permute-start.4 = (s32[6]{0:T(128)S(1)}, s32[6]{0:T(128)S(1)}, u32[]{:S(2)}, u32[]{:S(2)}) collective-permute-start(s32[6]{0:T(128)S(1)} %get-tuple-element.41), channel_id=1, source_target_pairs={{0,30},{1,31},{2,0},{3,1},{4,2},{5,3},{6,4},{7,5},{8,6},{9,7},{10,... | collective-permute-start | bytes 80 | tf_op jit(solution)/shard_map/ppermute | solution.py:60
  19.4 6.9 %collective-permute-start.5 = (bf16[6,32,128]{2,1,0:T(8,128)(2,1)S(1)}, bf16[6,32,128]{2,1,0:T(8,128)(2,1)S(1)}, u32[]{:S(2)}, u32[]{:S(2)}) collective-permute-start(bf16[6,32,128]{2,1,0:T(8,128)(2,1)S(1)} %get-tuple-element.36), channel_id=1, source_target_pairs={{1,0},{2,1},{3,2},{4,3},{5,4},{6,5},{7,6},{8,7},{9,8},{10,9},{11,1... | collective-permute-start | bytes 147464 | tf_op jit(solution)/shard_map/ppermute | solution.py:70
  22.2 4.9 %collective-permute-start.6 = (bf16[6,32,128]{2,1,0:T(8,128)(2,1)S(1)}, bf16[6,32,128]{2,1,0:T(8,128)(2,1)S(1)}, u32[]{:S(2)}, u32[]{:S(2)}) collective-permute-start(bf16[6,32,128]{2,1,0:T(8,128)(2,1)S(1)} %get-tuple-element.35), channel_id=1, source_target_pairs={{2,0},{3,1},{4,2},{5,3},{6,4},{7,5},{8,6},{9,7},{10,8},{11,9},{12,... | collective-permute-start | bytes 147464 | tf_op jit(solution)/shard_map/ppermute | solution.py:70
  23.9 6.8 %collective-permute-start.7 = (bf16[6,32,128]{2,1,0:T(8,128)(2,1)S(1)}, bf16[6,32,128]{2,1,0:T(8,128)(2,1)S(1)}, u32[]{:S(2)}, u32[]{:S(2)}) collective-permute-start(bf16[6,32,128]{2,1,0:T(8,128)(2,1)S(1)} %get-tuple-element.34), channel_id=1, source_target_pairs={{16,0},{17,1},{18,2},{19,3},{20,4},{21,5},{22,6},{23,7},{24,8},{25... | collective-permute-start | bytes 147464 | tf_op jit(solution)/shard_map/ppermute | solution.py:70
  25.5 5.3 %collective-permute-start.8 = (bf16[6,32,128]{2,1,0:T(8,128)(2,1)S(1)}, bf16[6,32,128]{2,1,0:T(8,128)(2,1)S(1)}, u32[]{:S(2)}, u32[]{:S(2)}) collective-permute-start(bf16[6,32,128]{2,1,0:T(8,128)(2,1)S(1)} %get-tuple-element.33), channel_id=1, source_target_pairs={{31,0},{0,1},{1,2},{2,3},{3,4},{4,5},{5,6},{6,7},{7,8},{8,9},{9,10... | collective-permute-start | bytes 147464 | tf_op jit(solution)/shard_map/ppermute | solution.py:70
  26.3 6.6 %collective-permute-start.9 = (bf16[6,32,128]{2,1,0:T(8,128)(2,1)S(1)}, bf16[6,32,128]{2,1,0:T(8,128)(2,1)S(1)}, u32[]{:S(2)}, u32[]{:S(2)}) collective-permute-start(bf16[6,32,128]{2,1,0:T(8,128)(2,1)S(1)} %get-tuple-element.32), channel_id=1, source_target_pairs={{30,0},{31,1},{0,2},{1,3},{2,4},{3,5},{4,6},{5,7},{6,8},{7,9},{8,1... | collective-permute-start | bytes 147464 | tf_op jit(solution)/shard_map/ppermute | solution.py:70
  36.5 2.1 %copy-start.6 = (f32[24,32,128]{2,1,0:T(8,128)}, f32[24,32,128]{2,1,0:T(8,128)S(1)}, u32[]{:S(2)}) copy-start(f32[24,32,128]{2,1,0:T(8,128)S(1)} %convolution_bitcast_fusion.4) | copy-start | bytes 1179652
  39.3 10.9 %collective-permute-start.10 = (bf16[6,64,128]{2,1,0:T(8,128)(2,1)S(1)}, bf16[6,64,128]{2,1,0:T(8,128)(2,1)S(1)}, u32[]{:S(2)}, u32[]{:S(2)}) collective-permute-start(bf16[6,64,128]{2,1,0:T(8,128)(2,1)S(1)} %get-tuple-element.28), channel_id=1, source_target_pairs={{1,0},{2,1},{3,2},{4,3},{5,4},{6,5},{7,6},{8,7},{9,8},{10,9},{11,1... | collective-permute-start | bytes 294920 | tf_op jit(solution)/shard_map/ppermute | solution.py:70
  41.3 9.6 %collective-permute-start.11 = (bf16[6,64,128]{2,1,0:T(8,128)(2,1)S(1)}, bf16[6,64,128]{2,1,0:T(8,128)(2,1)S(1)}, u32[]{:S(2)}, u32[]{:S(2)}) collective-permute-start(bf16[6,64,128]{2,1,0:T(8,128)(2,1)S(1)} %get-tuple-element.27), channel_id=1, source_target_pairs={{2,0},{3,1},{4,2},{5,3},{6,4},{7,5},{8,6},{9,7},{10,8},{11,9},{12,... | collective-permute-start | bytes 294920 | tf_op jit(solution)/shard_map/ppermute | solution.py:70
  41.8 9.7 %collective-permute-start.12 = (bf16[6,64,128]{2,1,0:T(8,128)(2,1)S(1)}, bf16[6,64,128]{2,1,0:T(8,128)(2,1)S(1)}, u32[]{:S(2)}, u32[]{:S(2)}) collective-permute-start(bf16[6,64,128]{2,1,0:T(8,128)(2,1)S(1)} %get-tuple-element.26), channel_id=1, source_target_pairs={{16,0},{17,1},{18,2},{19,3},{20,4},{21,5},{22,6},{23,7},{24,8},{25... | collective-permute-start | bytes 294920 | tf_op jit(solution)/shard_map/ppermute | solution.py:70
  45.5 6.7 %collective-permute-start.13 = (bf16[6,64,128]{2,1,0:T(8,128)(2,1)S(1)}, bf16[6,64,128]{2,1,0:T(8,128)(2,1)S(1)}, u32[]{:S(2)}, u32[]{:S(2)}) collective-permute-start(bf16[6,64,128]{2,1,0:T(8,128)(2,1)S(1)} %get-tuple-element.25), channel_id=1, source_target_pairs={{31,0},{0,1},{1,2},{2,3},{3,4},{4,5},{5,6},{6,7},{7,8},{8,9},{9,10... | collective-permute-start | bytes 294920 | tf_op jit(solution)/shard_map/ppermute | solution.py:70
  47.5 7.4 %collective-permute-start.14 = (bf16[6,64,128]{2,1,0:T(8,128)(2,1)S(1)}, bf16[6,64,128]{2,1,0:T(8,128)(2,1)S(1)}, u32[]{:S(2)}, u32[]{:S(2)}) collective-permute-start(bf16[6,64,128]{2,1,0:T(8,128)(2,1)S(1)} %get-tuple-element.24), channel_id=1, source_target_pairs={{30,0},{31,1},{0,2},{1,3},{2,4},{3,5},{4,6},{5,7},{6,8},{7,9},{8,1... | collective-permute-start | bytes 294920 | tf_op jit(solution)/shard_map/ppermute | solution.py:70
  57.6 3.3 %copy-start.2 = (bf16[24,5,128,128]{3,2,1,0:T(8,128)(2,1)S(1)}, bf16[24,5,128,128]{3,2,1,0:T(8,128)(2,1)}, u32[]{:S(2)}) copy-start(bf16[24,5,128,128]{3,2,1,0:T(8,128)(2,1)} %param.8) | copy-start | bytes 11796484
  62.5 1.1 %copy-start.4 = (f32[24,32,2,128]{3,1,2,0:T(8,128)S(1)}, f32[24,32,2,128]{3,1,2,0:T(8,128)}, u32[]{:S(2)}) copy-start(f32[24,32,2,128]{3,1,2,0:T(8,128)} %copy-done.3) | copy-start | bytes 2359300
  65.4 9.4 %collective-permute-start.15 = (bf16[6,64,128]{2,1,0:T(8,128)(2,1)S(1)}, bf16[6,64,128]{2,1,0:T(8,128)(2,1)S(1)}, u32[]{:S(2)}, u32[]{:S(2)}) collective-permute-start(bf16[6,64,128]{2,1,0:T(8,128)(2,1)S(1)} %get-tuple-element.23), channel_id=1, source_target_pairs={{1,0},{2,1},{3,2},{4,3},{5,4},{6,5},{7,6},{8,7},{9,8},{10,9},{11,1... | collective-permute-start | bytes 294920 | tf_op jit(solution)/shard_map/ppermute | solution.py:70
  65.9 9.5 %collective-permute-start.16 = (bf16[6,64,128]{2,1,0:T(8,128)(2,1)S(1)}, bf16[6,64,128]{2,1,0:T(8,128)(2,1)S(1)}, u32[]{:S(2)}, u32[]{:S(2)}) collective-permute-start(bf16[6,64,128]{2,1,0:T(8,128)(2,1)S(1)} %get-tuple-element.22), channel_id=1, source_target_pairs={{2,0},{3,1},{4,2},{5,3},{6,4},{7,5},{8,6},{9,7},{10,8},{11,9},{12,... | collective-permute-start | bytes 294920 | tf_op jit(solution)/shard_map/ppermute | solution.py:70
  66.3 9.7 %collective-permute-start.17 = (bf16[6,64,128]{2,1,0:T(8,128)(2,1)S(1)}, bf16[6,64,128]{2,1,0:T(8,128)(2,1)S(1)}, u32[]{:S(2)}, u32[]{:S(2)}) collective-permute-start(bf16[6,64,128]{2,1,0:T(8,128)(2,1)S(1)} %get-tuple-element.21), channel_id=1, source_target_pairs={{16,0},{17,1},{18,2},{19,3},{20,4},{21,5},{22,6},{23,7},{24,8},{25... | collective-permute-start | bytes 294920 | tf_op jit(solution)/shard_map/ppermute | solution.py:70
  69.8 7.0 %collective-permute-start.18 = (bf16[6,64,128]{2,1,0:T(8,128)(2,1)S(1)}, bf16[6,64,128]{2,1,0:T(8,128)(2,1)S(1)}, u32[]{:S(2)}, u32[]{:S(2)}) collective-permute-start(bf16[6,64,128]{2,1,0:T(8,128)(2,1)S(1)} %get-tuple-element.20), channel_id=1, source_target_pairs={{31,0},{0,1},{1,2},{2,3},{3,4},{4,5},{5,6},{6,7},{7,8},{8,9},{9,10... | collective-permute-start | bytes 294920 | tf_op jit(solution)/shard_map/ppermute | solution.py:70
  71.7 8.4 %collective-permute-start.19 = (bf16[6,64,128]{2,1,0:T(8,128)(2,1)S(1)}, bf16[6,64,128]{2,1,0:T(8,128)(2,1)S(1)}, u32[]{:S(2)}, u32[]{:S(2)}) collective-permute-start(bf16[6,64,128]{2,1,0:T(8,128)(2,1)S(1)} %get-tuple-element.19), channel_id=1, source_target_pairs={{30,0},{31,1},{0,2},{1,3},{2,4},{3,5},{4,6},{5,7},{6,8},{7,9},{8,1... | collective-permute-start | bytes 294920 | tf_op jit(solution)/shard_map/ppermute | solution.py:70
  82.9 3.3 %copy-start.1 = (bf16[24,5,128,128]{3,2,1,0:T(8,128)(2,1)S(1)}, bf16[24,5,128,128]{3,2,1,0:T(8,128)(2,1)}, u32[]{:S(2)}) copy-start(bf16[24,5,128,128]{3,2,1,0:T(8,128)(2,1)} %param.7) | copy-start | bytes 11796484
  86.2 1.0 copy-start.8
  87.9 1.1 %copy-start.5 = (f32[24,32,2,128]{3,1,2,0:T(8,128)S(1)}, f32[24,32,2,128]{3,1,2,0:T(8,128)}, u32[]{:S(2)}) copy-start(f32[24,32,2,128]{3,1,2,0:T(8,128)} %copy-done.3) | copy-start | bytes 2359300
  87.9 1.4 %copy-start.9 = (f32[24,64,128]{2,1,0:T(8,128)S(1)}, f32[24,64,128]{2,1,0:T(8,128)}, u32[]{:S(2)}) copy-start(f32[24,64,128]{2,1,0:T(8,128)} %get-tuple-element.18) | copy-start | bytes 2359300
  91.0 7.2 %collective-permute-start.20 = (f32[4,2,4,24,128]{4,3,2,1,0:T(8,128)S(1)}, f32[4,2,4,24,128]{4,3,2,1,0:T(8,128)S(1)}, u32[]{:S(2)}, u32[]{:S(2)}) collective-permute-start(f32[4,2,4,24,128]{4,3,2,1,0:T(8,128)S(1)} %bitcast.168), channel_id=1, source_target_pairs={{0,32},{32,0},{64,96},{96,64},{128,160},{160,128},{192,224},{224,1... | collective-permute-start | bytes 1179656 | tf_op jit(solution)/shard_map/ppermute | solution.py:113
  98.4 6.6 %collective-permute-start.23 = (f32[2,4,24,128]{3,2,1,0:T(8,128)S(1)}, f32[2,4,24,128]{3,2,1,0:T(8,128)S(1)}, u32[]{:S(2)}, u32[]{:S(2)}) collective-permute-start(f32[2,4,24,128]{3,2,1,0:T(8,128)S(1)} %get-tuple-element.30), channel_id=1, source_target_pairs={{0,192},{32,224},{64,0},{96,32},{128,64},{160,96},{192,128},{224,1... | collective-permute-start | bytes 294920 | tf_op jit(solution)/shard_map/ppermute | solution.py:118
  101.2 5.1 %collective-permute-start.22 = (f32[2,4,24,128]{3,2,1,0:T(8,128)S(1)}, f32[2,4,24,128]{3,2,1,0:T(8,128)S(1)}, u32[]{:S(2)}, u32[]{:S(2)}) collective-permute-start(f32[2,4,24,128]{3,2,1,0:T(8,128)S(1)} %get-tuple-element.31), channel_id=1, source_target_pairs={{0,128},{32,160},{64,192},{96,224},{128,0},{160,32},{192,64},{224,... | collective-permute-start | bytes 294920 | tf_op jit(solution)/shard_map/ppermute | solution.py:118
  101.5 7.8 %collective-permute-start.21 = (f32[2,4,24,128]{3,2,1,0:T(8,128)S(1)}, f32[2,4,24,128]{3,2,1,0:T(8,128)S(1)}, u32[]{:S(2)}, u32[]{:S(2)}) collective-permute-start(f32[2,4,24,128]{3,2,1,0:T(8,128)S(1)} %get-tuple-element.29), channel_id=1, source_target_pairs={{0,64},{32,96},{64,128},{96,160},{128,192},{160,224},{192,0},{224,... | collective-permute-start | bytes 294920 | tf_op jit(solution)/shard_map/ppermute | solution.py:118
  (2 other events, 1.9 us)
